TPU v7x, 32 devices: a whole 2x2x4 slice. The times are simulated.
32 devices in a mesh: beam: 8 (over z, y), cross: 4 (over x, core).
Axes of the slice: x: 2, y: 2, z: 4, core: 2. Of those that a mesh axis runs over, the one named last changes fastest.
Arguments:
- xenon_spin_polarization: float32 [64, 128, 128], P('beam', 'cross'), may hold values from 0 to 0.6
- heat_ratio: float32 [64, 128, 128], P('beam', 'cross'), may hold values from 1 to 1.12
- rubidium_polarization_old: float32 [64, 128, 128], P('beam', 'cross'), may hold values from 0.1 to 0.9
- earlier_spectral_power: bfloat16 [64, 64, 128, 128], P(None, 'beam', 'cross'), may hold values from 0 to 2
- entry_spectral_power: float32 [64, 128, 128], P(None, 'cross'), may hold values from 0.3 to 3
- spectral_attenuation_section: float32 [64], replicated, may hold values from 0.3 to 20
- flow_rate_forward: float32 [128, 128], P('cross'), may hold values from 0.3 to 1
- solid_pillar_flags: int32 [64, 128], P('beam', 'cross'), may hold values from 0 to 1, as said below
Outputs:
- spectral_power: bfloat16 [64, 64, 128, 128], P(None, 'beam', 'cross')
- xenon_next: float32 [64, 128, 128], P('beam', 'cross')
- temperature_next: float32 [64, 128, 128], P('beam', 'cross')
- rubidium_polarization_new: float32 [64, 128, 128], P('beam', 'cross')
Inputs may be any that keep to these rules, and one draw needn't show every extreme that they name: `solid_pillar_flags`: constant on aligned tiles of 4 x 4 grid columns; at least one tile is glass.
All inputs are finite; a program needn't handle non-finite values.
Results may differ from a plain program's by a relative error of at most 0.001.
Values sent between devices are 32-bit elements; how exact they have to be, the bound alone decides.
No kernel may reach another device: no remote copies, remote signals or barrier semaphores. Data moves between devices by JAX's collectives and lax.ppermute only.
A program may use at most 128 MiB of HBM per device.

v0:
```python
import jax
import jax.numpy as jnp
from jax import lax
from jax.sharding import PartitionSpec as P

SUBSTEPS = 2


rubidium_amount_slope = 23.25
rubidium_amount_center = 0.95
absorb_scale = 1.0
glass_depth = 0.07
saturation = 1.0
pump_scale = 0.015625
spin_decay = 0.5
exchange_rate = 0.05
xenon_relax = 0.02
heat_gain = 0.05
cooling = 0.02
xenon_diffusion = 0.09
conduction = 0.09
flow_scale = 0.2
boundary_kelvin = 1.0
neighbor_offsets = ((1, 0, 0), (-1, 0, 0), (0, 1, 0), (0, -1, 0), (0, 0, 1), (0, 0, -1))


def padded(block, sides, width):
    for axis, dim in sides:
        count = lax.axis_size(axis)
        forward = [(i, i + 1) for i in range(count - 1)]
        backward = [(target, source) for source, target in forward]
        low = lax.ppermute(
            lax.slice_in_dim(block, block.shape[dim] - width, None, axis=dim), axis, forward
        )
        high = lax.ppermute(lax.slice_in_dim(block, 0, width, axis=dim), axis, backward)
        block = jnp.concatenate([low, block, high], axis=dim)
    return block


def window(source, step_beam, step_cross, step_depth):
    return source[
        ...,
        1 + step_beam : source.shape[-3] - 1 + step_beam,
        1 + step_cross : source.shape[-2] - 1 + step_cross,
        1 + step_depth : source.shape[-1] - 1 + step_depth,
    ]


def advance(
    bordered, rubidium_number_amount, spin_ratio, heating, drift_speed, fluid_occupied_sites
):
    center = window(bordered, 0, 0, 0)
    complete_heat_ratio = bordered[1] + boundary_kelvin
    coefficients = jnp.stack(
        [xenon_diffusion * complete_heat_ratio**1.5, conduction * complete_heat_ratio**0.7]
    )
    coeff_center = window(coefficients, 0, 0, 0)
    diffused = jnp.zeros_like(center)
    for step_beam, step_cross, step_depth in neighbor_offsets:
        neighbor = window(bordered, step_beam, step_cross, step_depth)
        face_coeff = 0.5 * (coeff_center + window(coefficients, step_beam, step_cross, step_depth))
        diffused = diffused + face_coeff * (neighbor - center)
    upstream = window(bordered, -1, 0, 0)
    transport = diffused - drift_speed * (center - upstream)
    xenon_new = (
        center[0]
        + transport[0]
        + exchange_rate * rubidium_number_amount * (spin_ratio - center[0])
        - xenon_relax * center[0]
    )
    deviation = center[1] + transport[1] + heat_gain * heating - cooling * center[1]
    return jnp.stack([xenon_new * fluid_occupied_sites, deviation * fluid_occupied_sites])


def exclusive_prefix(source):
    length = source.shape[1]
    strictly_lower = (jnp.arange(length)[None, :] < jnp.arange(length)[:, None]).astype(jnp.float32)
    return jnp.einsum("ab,lbcz->lacz", strictly_lower, source, precision=lax.Precision.HIGHEST)


def local(
    xenon_spin_polarization,
    heat_ratio,
    rubidium_polarization_old,
    earlier_spectral_power,
    entry_spectral_power,
    spectral_attenuation_section,
    flow_rate_forward,
    solid_pillar_flags,
):
    total_rows = earlier_spectral_power.shape[1] * lax.axis_size("beam")
    glass_cells = solid_pillar_flags.astype(jnp.float32)[:, :, None]
    fluid_occupied_sites = 1.0 - glass_cells
    rubidium_number_amount = fluid_occupied_sites * jnp.exp(
        rubidium_amount_slope * (rubidium_amount_center - 1.0 / heat_ratio)
    )
    absorber = (
        absorb_scale / total_rows * rubidium_number_amount * (1.0 - rubidium_polarization_old)
    )
    glass_term = glass_depth * glass_cells
    weight = spectral_attenuation_section[:, None, None, None] / (
        1.0 + earlier_spectral_power.astype(jnp.float32) / saturation
    )
    optical_depth = absorber[None] * weight + glass_term[None]
    summed = exclusive_prefix(
        lax.all_to_all(optical_depth, "beam", split_axis=0, concat_axis=1, tiled=True)
    )
    column = lax.all_to_all(summed, "beam", split_axis=1, concat_axis=0, tiled=True)
    radiance = entry_spectral_power[:, None] * jnp.exp(-column)
    spectral_power = radiance.astype(jnp.bfloat16)
    pumping = pump_scale * jnp.sum(weight * radiance, axis=0)
    heating = jnp.sum(radiance * (1.0 - jnp.exp(-optical_depth)), axis=0)
    spin_ratio = pumping / (pumping + spin_decay * (1.0 + rubidium_number_amount))
    rubidium_polarization_new = fluid_occupied_sites * spin_ratio
    drift_speed = flow_scale * flow_rate_forward
    physical_quantities = jnp.stack([xenon_spin_polarization, heat_ratio - boundary_kelvin])
    for substep in range(SUBSTEPS):
        bordered = padded(physical_quantities, (("beam", 1), ("cross", 2)), 1)
        bordered = jnp.pad(bordered, ((0, 0), (0, 0), (0, 0), (1, 1)))
        physical_quantities = advance(
            bordered, rubidium_number_amount, spin_ratio, heating, drift_speed, fluid_occupied_sites
        )
    return (
        spectral_power,
        physical_quantities[0],
        physical_quantities[1] + boundary_kelvin,
        rubidium_polarization_new,
    )


def solution(mesh):
    in_specs = (
        P("beam", "cross", None),
        P("beam", "cross", None),
        P("beam", "cross", None),
        P(None, "beam", "cross", None),
        P(None, "cross", None),
        P(),
        P("cross", None),
        P("beam", "cross"),
    )
    out_specs = (
        P(None, "beam", "cross", None),
        P("beam", "cross", None),
        P("beam", "cross", None),
        P("beam", "cross", None),
    )
    return jax.shard_map(local, mesh=mesh, in_specs=in_specs, out_specs=out_specs, check_vma=False)
```

profile of v0, /device:TPU:9, one launch (start us, length us, event | category | flops | bytes accessed | tf_op | source)
XLA Modules:
  0.0 437.8 jit_solution(12544853171271203784)
XLA Ops:
  0.6 0.7 convert_subtract_fusion
  1.3 1.1 add_bitcast_fusion
  2.4 3.5 multiply_add_fusion
  5.9 186.7 %all_to_all.27 = f32[64,8,32,128]{3,2,1,0:T(8,128)S(1)} all-to-all(f32[64,8,32,128]{3,2,1,0:T(8,128)S(1)} %multiply_add_fusion), channel_id=1, replica_groups=mesh['beam'=8,'cross'=4] {'beam'}, dimensions={0} | all-to-all | bytes 16777216 | tf_op jit(solution)/shard_map/all_to_all | solution.py:106
  192.6 9.8 %fusion.4 = f32[8,64,32,128]{3,1,2,0:T(8,128)S(1)} fusion(f32[8,8,8,32,128]{4,3,2,1,0:T(8,128)S(1)} %bitcast.83), kind=kOutput, calls=%fused_computation.10 | convolution fusion | flops 1610616832 | bytes 16777216 | tf_op jit(solution)/shard_map/ab,lbcz->lacz/dot_general | solution.py:78
  202.4 8.3 %copy.15 = f32[8,64,32,128]{3,2,0,1:T(8,128)} copy(f32[8,64,32,128]{3,1,2,0:T(8,128)S(1)} %fusion.4) | data formatting | bytes 16777216 | tf_op jit(solution)/shard_map/ab,lbcz->lacz/transpose | solution.py:78
  210.7 0.0 copy-start.1
  210.7 0.0 copy-start.4
  210.7 6.0 %all-to-all-start.1 = ((f32[8,64,32,128]{3,2,0,1:T(8,128)}), f32[8,64,32,128]{3,2,0,1:T(8,128)}, u32[]{:S(2)}, u32[]{:S(2)}) async-start(f32[8,64,32,128]{3,2,0,1:T(8,128)} %copy.15), calls=%async_computation.1 | async-start | bytes 16777216 | tf_op jit(solution)/shard_map/all_to_all | solution.py:108
  216.7 0.0 copy-done.1
  216.7 3.1 collective-permute-start.1
  219.8 2.2 collective-permute-start
  222.0 61.3 %collective-permute-done.1 = f32[2,1,32,128]{3,2,1,0:T(8,128)S(1)} collective-permute-done((f32[2,1,32,128]{3,2,1,0:T(8,128)S(1)}, f32[2,1,32,128]{3,2,1,0:T(8,128)S(1)}, u32[]{:S(2)}, u32[]{:S(2)}) %collective-permute-start.1) | collective-permute-done | bytes 32800 | tf_op jit(solution)/shard_map/ppermute | solution.py:35
  283.3 70.0 %collective-permute-done = f32[2,1,32,128]{3,2,1,0:T(8,128)S(1)} collective-permute-done((f32[2,1,32,128]{3,2,1,0:T(8,128)S(1)}, f32[2,1,32,128]{3,2,1,0:T(8,128)S(1)}, u32[]{:S(2)}, u32[]{:S(2)}) %collective-permute-start) | collective-permute-done | bytes 32800 | tf_op jit(solution)/shard_map/ppermute | solution.py:32
  353.3 4.5 %collective-permute-start.3 = (f32[2,10,1,128]{3,2,1,0:T(1,128)S(1)}, f32[2,10,1,128]{3,2,1,0:T(1,128)S(1)}, u32[]{:S(2)}, u32[]{:S(2)}) collective-permute-start(f32[2,10,1,128]{3,2,1,0:T(1,128)S(1)} %get-tuple-element.18), channel_id=1, source_target_pairs={{1,0},{2,1},{3,2},{5,4},{6,5},{7,6},{9,8},{10,9},{11,10},{13,12},{... | collective-permute-start | bytes 30728 | tf_op jit(solution)/shard_map/ppermute | solution.py:35
  357.8 3.0 collective-permute-start.2
  360.8 0.0 copy-done.4
  360.8 0.0 collective-permute-done.3
  360.8 0.8 collective-permute-done.2
  361.6 0.4 select_maximum_fusion.5
  362.0 0.4 power_multiply_fusion.2
  362.4 0.7 fusion.41
  363.1 35.0 %all-to-all-done.1 = f32[8,64,32,128]{3,2,0,1:T(8,128)} async-done(((f32[8,64,32,128]{3,2,0,1:T(8,128)}), f32[8,64,32,128]{3,2,0,1:T(8,128)}, u32[]{:S(2)}, u32[]{:S(2)}) %all-to-all-start.1) | async-done | bytes 8388640 | tf_op jit(solution)/shard_map/all_to_all | solution.py:108
  398.0 4.5 %negate_exponential_fusion = f32[8,64,32,128]{3,2,0,1:T(8,128)S(1)} fusion(f32[8,64,32,128]{3,2,0,1:T(8,128)} %all-to-all-done.1), kind=kLoop, calls=%fused_computation.6 | loop fusion | flops 2097152 | bytes 16777216 | tf_op jit(solution)/shard_map/exp | solution.py:109
  402.5 0.0 copy-start
  402.5 0.0 copy-start.3
  402.5 0.0 copy-start.5
  402.5 1.4 copy.16
  404.0 0.7 copy-done
  404.7 0.3 copy-done.3
  405.0 0.0 copy-done.5
  405.0 0.0 copy-start.2
  405.0 6.4 %multiply_reduce_fusion = (f32[8,32,128]{2,1,0:T(8,128)S(1)}, f32[8,32,128]{2,1,0:T(8,128)S(1)}, bf16[64,8,32,128]{3,2,1,0:T(8,128)(2,1)}) fusion(f32[8,8,8,32,128]{4,3,2,1,0:T(8,128)S(1)} %copy.16, f32[64,32,128]{2,1,0:T(8,128)S(1)} %copy-done.3, f32[8,32]{1,0:T(8,128)S(1)} %get-tuple-element.27, bf16[64,8,32,128]{3,2,1,0:T(8,128)(2,1)S(1)} %copy-done, ...), kind=kLoop, calls=%fused_computation.4 | loop fusion | flops 27197440 | bytes 18220288 | tf_op jit(solution)/shard_map/reduce_sum | solution.py:112
  411.4 0.0 copy-done.2
  411.4 0.8 fusion.103
  412.2 4.1 collective-permute-start.5
  416.3 10.3 %collective-permute-start.4 = (f32[2,1,32,128]{3,2,1,0:T(8,128)S(1)}, f32[2,1,32,128]{3,2,1,0:T(8,128)S(1)}, u32[]{:S(2)}, u32[]{:S(2)}) collective-permute-start(f32[2,1,32,128]{3,2,1,0:T(8,128)S(1)} %get-tuple-element.20), channel_id=1, source_target_pairs={{0,4},{4,8},{8,12},{12,16},{16,20},{20,24},{24,28},{1,5},{5,9},{9,... | collective-permute-start | bytes 98312 | tf_op jit(solution)/shard_map/ppermute | solution.py:32
  426.6 0.0 collective-permute-done.5
  426.6 1.1 collective-permute-done.4
  427.8 2.1 collective-permute-start.7
  429.9 4.7 %collective-permute-start.6 = (f32[2,10,1,128]{3,2,1,0:T(1,128)S(1)}, f32[2,10,1,128]{3,2,1,0:T(1,128)S(1)}, u32[]{:S(2)}, u32[]{:S(2)}) collective-permute-start(f32[2,10,1,128]{3,2,1,0:T(1,128)S(1)} %get-tuple-element.15), channel_id=1, source_target_pairs={{0,1},{1,2},{2,3},{4,5},{5,6},{6,7},{8,9},{9,10},{10,11},{12,13},{... | collective-permute-start | bytes 30728 | tf_op jit(solution)/shard_map/ppermute | solution.py:32
  434.6 0.0 collective-permute-done.7
  434.7 0.8 collective-permute-done.6
  435.4 0.4 select_maximum_fusion
  435.8 0.4 power_multiply_fusion
  436.2 0.7 fusion.14
  436.9 0.9 fusion.84
  (5 shorter events, 0.1 us)
Async XLA Ops:
  210.7 6.0 %copy-start.1 = (f32[8,32,128]{2,1,0:T(8,128)S(1)}, f32[8,32,128]{2,1,0:T(8,128)}, u32[]{:S(2)}) copy-start(f32[8,32,128]{2,1,0:T(8,128)} %param.8) | copy-start | bytes 393220
  210.7 150.1 %copy-start.4 = (f32[32,128]{1,0:T(8,128)S(1)}, f32[32,128]{1,0:T(8,128)}, u32[]{:S(2)}) copy-start(f32[32,128]{1,0:T(8,128)} %param.14) | copy-start | bytes 49156
  210.7 187.3 %all-to-all-start.1 = ((f32[8,64,32,128]{3,2,0,1:T(8,128)}), f32[8,64,32,128]{3,2,0,1:T(8,128)}, u32[]{:S(2)}, u32[]{:S(2)}) async-start(f32[8,64,32,128]{3,2,0,1:T(8,128)} %copy.15), calls=%async_computation.1 | async-start | bytes 16777216 | tf_op jit(solution)/shard_map/all_to_all | solution.py:108
  216.7 66.6 %collective-permute-start.1 = (f32[2,1,32,128]{3,2,1,0:T(8,128)S(1)}, f32[2,1,32,128]{3,2,1,0:T(8,128)S(1)}, u32[]{:S(2)}, u32[]{:S(2)}) collective-permute-start(f32[2,1,32,128]{3,2,1,0:T(8,128)S(1)} %get-tuple-element.23), channel_id=1, source_target_pairs={{4,0},{8,4},{12,8},{16,12},{20,16},{24,20},{28,24},{5,1},{9,5},{13... | collective-permute-start | bytes 98312 | tf_op jit(solution)/shard_map/ppermute | solution.py:35
  219.8 133.5 %collective-permute-start = (f32[2,1,32,128]{3,2,1,0:T(8,128)S(1)}, f32[2,1,32,128]{3,2,1,0:T(8,128)S(1)}, u32[]{:S(2)}, u32[]{:S(2)}) collective-permute-start(f32[2,1,32,128]{3,2,1,0:T(8,128)S(1)} %get-tuple-element.22), channel_id=1, source_target_pairs={{0,4},{4,8},{8,12},{12,16},{16,20},{20,24},{24,28},{1,5},{5,9},{9,... | collective-permute-start | bytes 98312 | tf_op jit(solution)/shard_map/ppermute | solution.py:32
  353.3 7.5 %collective-permute-start.3 = (f32[2,10,1,128]{3,2,1,0:T(1,128)S(1)}, f32[2,10,1,128]{3,2,1,0:T(1,128)S(1)}, u32[]{:S(2)}, u32[]{:S(2)}) collective-permute-start(f32[2,10,1,128]{3,2,1,0:T(1,128)S(1)} %get-tuple-element.18), channel_id=1, source_target_pairs={{1,0},{2,1},{3,2},{5,4},{6,5},{7,6},{9,8},{10,9},{11,10},{13,12},{... | collective-permute-start | bytes 30728 | tf_op jit(solution)/shard_map/ppermute | solution.py:35
  357.8 3.8 collective-permute-start.2
  402.5 2.2 copy-start
  402.5 2.5 copy-start.3
  402.5 2.5 copy-start.5
  405.0 6.4 %copy-start.2 = (f32[8,32,128]{2,1,0:T(8,128)S(1)}, f32[8,32,128]{2,1,0:T(8,128)}, u32[]{:S(2)}) copy-start(f32[8,32,128]{2,1,0:T(8,128)} %param.9) | copy-start | bytes 393220
  412.2 14.5 %collective-permute-start.5 = (f32[2,1,32,128]{3,2,1,0:T(8,128)S(1)}, f32[2,1,32,128]{3,2,1,0:T(8,128)S(1)}, u32[]{:S(2)}, u32[]{:S(2)}) collective-permute-start(f32[2,1,32,128]{3,2,1,0:T(8,128)S(1)} %get-tuple-element.21), channel_id=1, source_target_pairs={{4,0},{8,4},{12,8},{16,12},{20,16},{24,20},{28,24},{5,1},{9,5},{13... | collective-permute-start | bytes 98312 | tf_op jit(solution)/shard_map/ppermute | solution.py:35
  416.3 11.5 %collective-permute-start.4 = (f32[2,1,32,128]{3,2,1,0:T(8,128)S(1)}, f32[2,1,32,128]{3,2,1,0:T(8,128)S(1)}, u32[]{:S(2)}, u32[]{:S(2)}) collective-permute-start(f32[2,1,32,128]{3,2,1,0:T(8,128)S(1)} %get-tuple-element.20), channel_id=1, source_target_pairs={{0,4},{4,8},{8,12},{12,16},{16,20},{20,24},{24,28},{1,5},{5,9},{9,... | collective-permute-start | bytes 98312 | tf_op jit(solution)/shard_map/ppermute | solution.py:32
  427.8 6.8 %collective-permute-start.7 = (f32[2,10,1,128]{3,2,1,0:T(1,128)S(1)}, f32[2,10,1,128]{3,2,1,0:T(1,128)S(1)}, u32[]{:S(2)}, u32[]{:S(2)}) collective-permute-start(f32[2,10,1,128]{3,2,1,0:T(1,128)S(1)} %get-tuple-element.16), channel_id=1, source_target_pairs={{1,0},{2,1},{3,2},{5,4},{6,5},{7,6},{9,8},{10,9},{11,10},{13,12},{... | collective-permute-start | bytes 30728 | tf_op jit(solution)/shard_map/ppermute | solution.py:35
  429.9 5.5 %collective-permute-start.6 = (f32[2,10,1,128]{3,2,1,0:T(1,128)S(1)}, f32[2,10,1,128]{3,2,1,0:T(1,128)S(1)}, u32[]{:S(2)}, u32[]{:S(2)}) collective-permute-start(f32[2,10,1,128]{3,2,1,0:T(1,128)S(1)} %get-tuple-element.15), channel_id=1, source_target_pairs={{0,1},{1,2},{2,3},{4,5},{5,6},{6,7},{8,9},{9,10},{10,11},{12,13},{... | collective-permute-start | bytes 30728 | tf_op jit(solution)/shard_map/ppermute | solution.py:32
where the time goes:
time: 442 us; the launch traced here: 438 us
  blocking collectives  187 us (42%)
  waiting for transfers between devices  169 us (38%)
  starting transfers between devices  40 us (9%)
  other arithmetic  20.8 us (5%)
  local copies, waits for them, and re-layouts  10.7 us (2%)
  matrix products  9.82 us (2%)
    all_to_all x1, blocking collectives, local(): lax.all_to_all(optical_depth, 'beam', split_axis=0, concat_axis=1, tiled=...  187 us
    ppermute x4, waiting for transfers between devices, padded(): lax.ppermute(lax.slice_in_dim(block, block.shape[dim] - width, None, axis...  72.7 us
    ppermute x4, waiting for transfers between devices, padded(): lax.ppermute(lax.slice_in_dim(block, 0, width, axis=dim), axis, backward)  61.3 us
    all_to_all x1, waiting for transfers between devices, local(): lax.all_to_all(summed, 'beam', split_axis=1, concat_axis=0, tiled=True)  35 us
    ppermute x4, starting transfers between devices, padded(): lax.ppermute(lax.slice_in_dim(block, block.shape[dim] - width, None, axis...  20.3 us
    ppermute x4, starting transfers between devices, padded(): lax.ppermute(lax.slice_in_dim(block, 0, width, axis=dim), axis, backward)  13.8 us
    dot_general x1, matrix products, exclusive_prefix(): jnp.einsum('ab,lbcz->lacz', strictly_lower, source, precision=lax.Precisi...  9.82 us
  transfers between devices with their start and end apart: 9, of which 6 were waited for; matrix products, arithmetic and copies ran while one was open for 0% of the time, Pallas kernels for 0%

commit v1 on v0

--- a/solution.py
+++ b/solution.py
@@ -24,17 +24,43 @@
 neighbor_offsets = ((1, 0, 0), (-1, 0, 0), (0, 1, 0), (0, -1, 0), (0, 0, 1), (0, 0, -1))
 
 
-def padded(block, sides, width):
-    for axis, dim in sides:
-        count = lax.axis_size(axis)
-        forward = [(i, i + 1) for i in range(count - 1)]
-        backward = [(target, source) for source, target in forward]
-        low = lax.ppermute(
-            lax.slice_in_dim(block, block.shape[dim] - width, None, axis=dim), axis, forward
-        )
-        high = lax.ppermute(lax.slice_in_dim(block, 0, width, axis=dim), axis, backward)
-        block = jnp.concatenate([low, block, high], axis=dim)
-    return block
+def shifted(block, axis, shift):
+    count = lax.axis_size(axis)
+    if shift > 0:
+        pairs = [(i, i + shift) for i in range(count - shift)]
+    else:
+        pairs = [(i - shift, i) for i in range(count + shift)]
+    return lax.ppermute(block, axis, pairs)
+
+
+def bordered_fields(block):
+    _, rows, columns, _ = block.shape
+    low_beam = shifted(block[:, rows - 1 :], "beam", 1)
+    high_beam = shifted(block[:, :1], "beam", -1)
+    low_cross = shifted(block[:, :, columns - 1 :], "cross", 1)
+    high_cross = shifted(block[:, :, :1], "cross", -1)
+    middle = jnp.concatenate([low_cross, block, high_cross], axis=2)
+    zeros = jnp.zeros_like(low_beam[:, :, :1])
+    low_beam = jnp.concatenate([zeros, low_beam, zeros], axis=2)
+    high_beam = jnp.concatenate([zeros, high_beam, zeros], axis=2)
+    bordered = jnp.concatenate([low_beam, middle, high_beam], axis=1)
+    return jnp.pad(bordered, ((0, 0), (0, 0), (0, 0), (1, 1)))
+
+
+def exclusive_scan(totals, axis):
+    count = lax.axis_size(axis)
+    if count == 1:
+        return jnp.zeros_like(totals)
+    before = shifted(totals, axis, 1)
+    through = totals + before
+    step = 2
+    while step < count:
+        arrived = shifted(through, axis, step)
+        before = before + arrived
+        step *= 2
+        if step < count:
+            through = through + arrived
+    return before
 
 
 def window(source, step_beam, step_cross, step_depth):
@@ -72,12 +98,6 @@
     return jnp.stack([xenon_new * fluid_occupied_sites, deviation * fluid_occupied_sites])
 
 
-def exclusive_prefix(source):
-    length = source.shape[1]
-    strictly_lower = (jnp.arange(length)[None, :] < jnp.arange(length)[:, None]).astype(jnp.float32)
-    return jnp.einsum("ab,lbcz->lacz", strictly_lower, source, precision=lax.Precision.HIGHEST)
-
-
 def local(
     xenon_spin_polarization,
     heat_ratio,
@@ -88,7 +108,10 @@
     flow_rate_forward,
     solid_pillar_flags,
 ):
-    total_rows = earlier_spectral_power.shape[1] * lax.axis_size("beam")
+    rows = earlier_spectral_power.shape[1]
+    total_rows = rows * lax.axis_size("beam")
+    physical_quantities = jnp.stack([xenon_spin_polarization, heat_ratio - boundary_kelvin])
+    first_border = bordered_fields(physical_quantities)
     glass_cells = solid_pillar_flags.astype(jnp.float32)[:, :, None]
     fluid_occupied_sites = 1.0 - glass_cells
     rubidium_number_amount = fluid_occupied_sites * jnp.exp(
@@ -102,10 +125,13 @@
         1.0 + earlier_spectral_power.astype(jnp.float32) / saturation
     )
     optical_depth = absorber[None] * weight + glass_term[None]
-    summed = exclusive_prefix(
-        lax.all_to_all(optical_depth, "beam", split_axis=0, concat_axis=1, tiled=True)
-    )
-    column = lax.all_to_all(summed, "beam", split_axis=1, concat_axis=0, tiled=True)
+    running = jnp.zeros_like(optical_depth[:, 0])
+    prefix = []
+    for row in range(rows):
+        prefix.append(running)
+        running = running + optical_depth[:, row]
+    local_column = jnp.stack(prefix, axis=1)
+    column = exclusive_scan(running, "beam")[:, None] + local_column
     radiance = entry_spectral_power[:, None] * jnp.exp(-column)
     spectral_power = radiance.astype(jnp.bfloat16)
     pumping = pump_scale * jnp.sum(weight * radiance, axis=0)
@@ -113,10 +139,8 @@
     spin_ratio = pumping / (pumping + spin_decay * (1.0 + rubidium_number_amount))
     rubidium_polarization_new = fluid_occupied_sites * spin_ratio
     drift_speed = flow_scale * flow_rate_forward
-    physical_quantities = jnp.stack([xenon_spin_polarization, heat_ratio - boundary_kelvin])
     for substep in range(SUBSTEPS):
-        bordered = padded(physical_quantities, (("beam", 1), ("cross", 2)), 1)
-        bordered = jnp.pad(bordered, ((0, 0), (0, 0), (0, 0), (1, 1)))
+        bordered = first_border if substep == 0 else bordered_fields(physical_quantities)
         physical_quantities = advance(
             bordered, rubidium_number_amount, spin_ratio, heating, drift_speed, fluid_occupied_sites
         )

time: 442 us -> 135 us (0.31)
  blocking collectives: 187 us -> 0 us
  waiting for transfers between devices: 169 us -> 78.1 us
  local copies, waits for them, and re-layouts: 10.7 us -> 0.4 us
  matrix products: 9.82 us -> 0 us
  starting transfers between devices: 40 us -> 35.4 us
    all_to_all x1 -> x0, blocking collectives: 187 us -> none  [local(): lax.all_to_all(optical_depth, 'beam', split_axis=0, concat_axis=1, tiled=...]
    ppermute x8 -> x11, waiting for transfers between devices: 134 us -> 78.1 us  [shifted(): return lax.ppermute(block, axis, pairs)]
    all_to_all x1 -> x0, waiting for transfers between devices: 35 us -> none  [local(): lax.all_to_all(summed, 'beam', split_axis=1, concat_axis=0, tiled=True)]
    dot_general x1 -> x0, matrix products: 9.82 us -> none  [exclusive_prefix(): jnp.einsum('ab,lbcz->lacz', strictly_lower, source, precision=lax.Precisi...]
    transpose x1 -> x0, local copies, waits for them, and re-layouts: 8.26 us -> none  [exclusive_prefix(): jnp.einsum('ab,lbcz->lacz', strictly_lower, source, precision=lax.Precisi...]
    all_to_all x1 -> x0, starting transfers between devices: 5.96 us -> none  [local(): lax.all_to_all(summed, 'beam', split_axis=1, concat_axis=0, tiled=True)]
    exp x1 -> x0, other arithmetic: 4.47 us -> none  [local(): radiance = entry_spectral_power[:, None] * jnp.exp(-column)]
    ppermute x8 -> x11, starting transfers between devices: 34 us -> 35.4 us  [shifted(): return lax.ppermute(block, axis, pairs)]
  transfers between devices with their start and end apart: 9 -> 11, of which waited for: 6 -> 4; matrix products, arithmetic and copies ran while one was open for 0% -> 2% of each run, Pallas kernels for 0% -> 0%
where the time goes in v1:
time: 135 us; the launch traced here: 133 us
  waiting for transfers between devices  78.1 us (58%)
  starting transfers between devices  35.4 us (26%)
  other arithmetic  18.6 us (14%)
    ppermute x11, waiting for transfers between devices, shifted(): return lax.ppermute(block, axis, pairs)  78.1 us
    ppermute x11, starting transfers between devices, shifted(): return lax.ppermute(block, axis, pairs)  35.4 us
    reduce_sum x1, other arithmetic, local(): heating = jnp.sum(radiance * (1.0 - jnp.exp(-optical_depth)), axis=0)  6.6 us
    add x1, other arithmetic, local(): optical_depth = absorber[None] * weight + glass_term[None]  3.48 us
  transfers between devices with their start and end apart: 11, of which 4 were waited for; matrix products, arithmetic and copies ran while one was open for 2% of the time, Pallas kernels for 0%

profile of v1, /device:TPU:9, one launch (start us, length us, event | category | flops | bytes accessed | tf_op | source)
XLA Modules:
  0.0 133.4 jit_solution(2425869515450083519)
XLA Ops:
  0.6 0.1 broadcast_dynamic-update-slice_fusion
  0.8 0.7 convert_subtract_fusion
  1.4 1.1 add_bitcast_fusion
  2.5 3.5 %multiply_add_fusion = f32[64,8,32,128]{3,2,1,0:T(8,128)S(1)} fusion(bf16[64,8,32,128]{3,2,1,0:T(8,128)(2,1)} %param.11, f32[8,32]{1,0:T(8,128)S(1)} %get-tuple-element.31, f32[64]{0:T(128)} %param.13, f32[8,32,128]{2,1,0:T(8,128)S(1)} %get-tuple-element.29), kind=kLoop, calls=%fused_computation.3 | loop fusion | flops 10485760 | bytes 12715264 | tf_op jit(solution)/shard_map/add | solution.py:127
  6.0 0.1 slice_dynamic-update-slice_fusion
  6.1 0.2 constant_dynamic-update-slice_fusion.2
  6.3 0.0 copy-start.1
  6.3 1.0 fusion.1
  7.4 0.0 copy-start.4
  7.4 3.1 %collective-permute-start = (f32[64,32,128]{2,1,0:T(8,128)S(1)}, f32[64,32,128]{2,1,0:T(8,128)S(1)}, u32[]{:S(2)}, u32[]{:S(2)}) collective-permute-start(f32[64,32,128]{2,1,0:T(8,128)S(1)} %get-tuple-element.6), channel_id=1, source_target_pairs={{0,4},{4,8},{8,12},{12,16},{16,20},{20,24},{24,28},{1,5},{5,9},{9,... | collective-permute-start | bytes 3145736 | tf_op jit(solution)/shard_map/ppermute | solution.py:33
  10.5 23.7 %collective-permute-done = f32[64,32,128]{2,1,0:T(8,128)S(1)} collective-permute-done((f32[64,32,128]{2,1,0:T(8,128)S(1)}, f32[64,32,128]{2,1,0:T(8,128)S(1)}, u32[]{:S(2)}, u32[]{:S(2)}) %collective-permute-start) | collective-permute-done | bytes 1048608 | tf_op jit(solution)/shard_map/ppermute | solution.py:33
  34.2 0.2 add.208
  34.4 3.2 %collective-permute-start.1 = (f32[64,32,128]{2,1,0:T(8,128)S(1)}, f32[64,32,128]{2,1,0:T(8,128)S(1)}, u32[]{:S(2)}, u32[]{:S(2)}) collective-permute-start(f32[64,32,128]{2,1,0:T(8,128)S(1)} %add.208), channel_id=1, source_target_pairs={{0,8},{4,12},{8,16},{12,20},{16,24},{20,28},{1,9},{5,13},{9,17},{1... | collective-permute-start | bytes 3145736 | tf_op jit(solution)/shard_map/ppermute | solution.py:33
  37.6 0.0 copy-done.1
  37.6 2.2 %collective-permute-start.3 = (f32[2,1,32,128]{3,2,1,0:T(8,128)S(1)}, f32[2,1,32,128]{3,2,1,0:T(8,128)S(1)}, u32[]{:S(2)}, u32[]{:S(2)}) collective-permute-start(f32[2,1,32,128]{3,2,1,0:T(8,128)S(1)} %get-tuple-element.24), channel_id=1, source_target_pairs={{0,4},{4,8},{8,12},{12,16},{16,20},{20,24},{24,28},{1,5},{5,9},{9,... | collective-permute-start | bytes 98312 | tf_op jit(solution)/shard_map/ppermute | solution.py:33
  39.9 3.9 %collective-permute-start.6 = (f32[2,1,32,128]{3,2,1,0:T(8,128)S(1)}, f32[2,1,32,128]{3,2,1,0:T(8,128)S(1)}, u32[]{:S(2)}, u32[]{:S(2)}) collective-permute-start(f32[2,1,32,128]{3,2,1,0:T(8,128)S(1)} %get-tuple-element.25), channel_id=1, source_target_pairs={{4,0},{8,4},{12,8},{16,12},{20,16},{24,20},{28,24},{5,1},{9,5},{13... | collective-permute-start | bytes 98312 | tf_op jit(solution)/shard_map/ppermute | solution.py:33
  43.9 5.4 %collective-permute-start.4 = (f32[2,8,1,128]{3,2,1,0:T(1,128)S(1)}, f32[2,8,1,128]{3,2,1,0:T(1,128)S(1)}, u32[]{:S(2)}, u32[]{:S(2)}) collective-permute-start(f32[2,8,1,128]{3,2,1,0:T(1,128)S(1)} %get-tuple-element.26), channel_id=1, source_target_pairs={{0,1},{1,2},{2,3},{4,5},{5,6},{6,7},{8,9},{9,10},{10,11},{12,13},{... | collective-permute-start | bytes 24584 | tf_op jit(solution)/shard_map/ppermute | solution.py:33
  49.3 1.9 %collective-permute-start.5 = (f32[2,8,1,128]{3,2,1,0:T(1,128)S(1)}, f32[2,8,1,128]{3,2,1,0:T(1,128)S(1)}, u32[]{:S(2)}, u32[]{:S(2)}) collective-permute-start(f32[2,8,1,128]{3,2,1,0:T(1,128)S(1)} %get-tuple-element.27), channel_id=1, source_target_pairs={{1,0},{2,1},{3,2},{5,4},{6,5},{7,6},{9,8},{10,9},{11,10},{13,12},{... | collective-permute-start | bytes 24584 | tf_op jit(solution)/shard_map/ppermute | solution.py:33
  51.2 0.1 constant_dynamic-update-slice_fusion.1
  51.3 0.2 fusion.9
  51.5 0.0 copy-start
  51.5 0.0 copy-start.3
  51.5 0.0 copy-start.5
  51.5 0.1 constant_dynamic-update-slice_fusion
  51.6 7.8 %collective-permute-done.1 = f32[64,32,128]{2,1,0:T(8,128)S(1)} collective-permute-done((f32[64,32,128]{2,1,0:T(8,128)S(1)}, f32[64,32,128]{2,1,0:T(8,128)S(1)}, u32[]{:S(2)}, u32[]{:S(2)}) %collective-permute-start.1) | collective-permute-done | bytes 1048608 | tf_op jit(solution)/shard_map/ppermute | solution.py:33
  59.4 0.2 add.210
  59.6 4.3 %collective-permute-start.2 = (f32[64,32,128]{2,1,0:T(8,128)S(1)}, f32[64,32,128]{2,1,0:T(8,128)S(1)}, u32[]{:S(2)}, u32[]{:S(2)}) collective-permute-start(f32[64,32,128]{2,1,0:T(8,128)S(1)} %add.210), channel_id=1, source_target_pairs={{0,16},{4,20},{8,24},{12,28},{1,17},{5,21},{9,25},{13,29},{2,18},{... | collective-permute-start | bytes 3145736 | tf_op jit(solution)/shard_map/ppermute | solution.py:33
  63.9 0.2 fusion.10
  64.1 0.0 copy-done.4
  64.1 0.0 collective-permute-done.4
  64.1 0.0 collective-permute-done.5
  64.2 0.0 collective-permute-done.3
  64.2 0.0 collective-permute-done.6
  64.2 0.1 fusion.3
  64.2 0.5 power_multiply_fusion.2
  64.8 0.7 fusion.19
  65.5 43.6 %collective-permute-done.2 = f32[64,32,128]{2,1,0:T(8,128)S(1)} collective-permute-done((f32[64,32,128]{2,1,0:T(8,128)S(1)}, f32[64,32,128]{2,1,0:T(8,128)S(1)}, u32[]{:S(2)}, u32[]{:S(2)}) %collective-permute-start.2) | collective-permute-done | bytes 1048608 | tf_op jit(solution)/shard_map/ppermute | solution.py:33
  109.0 0.3 add_add_fusion
  109.4 0.0 copy-done
  109.4 0.0 copy-done.3
  109.4 0.0 copy-done.5
  109.4 0.0 copy-start.2
  109.4 6.6 %multiply_reduce_fusion = (f32[8,32,128]{2,1,0:T(8,128)S(1)}, f32[8,32,128]{2,1,0:T(8,128)S(1)}, bf16[64,8,32,128]{3,2,1,0:T(8,128)(2,1)}) fusion(f32[64,8,32,128]{3,2,1,0:T(8,128)S(1)} %fusion.10, f32[64,32,128]{2,1,0:T(8,128)S(1)} %add_add_fusion, f32[64,32,128]{2,1,0:T(8,128)S(1)} %copy-done.3, f32[8,32]{1,0:T(8,128)S(1)} %get-tuple-element.31, ...), kind=kLoop, calls=%fused_computation | loop fusion | flops 31391744 | bytes 19268864 | tf_op jit(solution)/shard_map/reduce_sum | solution.py:138
  116.0 0.0 copy-done.2
  116.0 0.8 fusion.116
  116.9 1.9 %collective-permute-start.10 = (f32[2,1,32,128]{3,2,1,0:T(8,128)S(1)}, f32[2,1,32,128]{3,2,1,0:T(8,128)S(1)}, u32[]{:S(2)}, u32[]{:S(2)}) collective-permute-start(f32[2,1,32,128]{3,2,1,0:T(8,128)S(1)} %get-tuple-element.21), channel_id=1, source_target_pairs={{4,0},{8,4},{12,8},{16,12},{20,16},{24,20},{28,24},{5,1},{9,5},{13... | collective-permute-start | bytes 98312 | tf_op jit(solution)/shard_map/ppermute | solution.py:33
  118.8 3.4 %collective-permute-start.7 = (f32[2,1,32,128]{3,2,1,0:T(8,128)S(1)}, f32[2,1,32,128]{3,2,1,0:T(8,128)S(1)}, u32[]{:S(2)}, u32[]{:S(2)}) collective-permute-start(f32[2,1,32,128]{3,2,1,0:T(8,128)S(1)} %get-tuple-element.20), channel_id=1, source_target_pairs={{0,4},{4,8},{8,12},{12,16},{16,20},{20,24},{24,28},{1,5},{5,9},{9,... | collective-permute-start | bytes 98312 | tf_op jit(solution)/shard_map/ppermute | solution.py:33
  122.2 4.1 %collective-permute-start.8 = (f32[2,8,1,128]{3,2,1,0:T(1,128)S(1)}, f32[2,8,1,128]{3,2,1,0:T(1,128)S(1)}, u32[]{:S(2)}, u32[]{:S(2)}) collective-permute-start(f32[2,8,1,128]{3,2,1,0:T(1,128)S(1)} %get-tuple-element.22), channel_id=1, source_target_pairs={{0,1},{1,2},{2,3},{4,5},{5,6},{6,7},{8,9},{9,10},{10,11},{12,13},{... | collective-permute-start | bytes 24584 | tf_op jit(solution)/shard_map/ppermute | solution.py:33
  126.2 1.9 %collective-permute-start.9 = (f32[2,8,1,128]{3,2,1,0:T(1,128)S(1)}, f32[2,8,1,128]{3,2,1,0:T(1,128)S(1)}, u32[]{:S(2)}, u32[]{:S(2)}) collective-permute-start(f32[2,8,1,128]{3,2,1,0:T(1,128)S(1)} %get-tuple-element.23), channel_id=1, source_target_pairs={{1,0},{2,1},{3,2},{5,4},{6,5},{7,6},{9,8},{10,9},{11,10},{13,12},{... | collective-permute-start | bytes 24584 | tf_op jit(solution)/shard_map/ppermute | solution.py:33
  128.2 0.0 collective-permute-done.8
  128.2 3.0 %collective-permute-done.9 = f32[2,8,1,128]{3,2,1,0:T(1,128)S(1)} collective-permute-done((f32[2,8,1,128]{3,2,1,0:T(1,128)S(1)}, f32[2,8,1,128]{3,2,1,0:T(1,128)S(1)}, u32[]{:S(2)}, u32[]{:S(2)}) %collective-permute-start.9) | collective-permute-done | bytes 8224 | tf_op jit(solution)/shard_map/ppermute | solution.py:33
  131.2 0.0 collective-permute-done.10
  131.2 0.0 collective-permute-done.7
  131.2 0.1 fusion.5
  131.3 0.5 power_multiply_fusion
  131.8 0.7 fusion.28
  132.5 0.9 fusion.95
  (6 shorter events, 0.0 us)
Async XLA Ops:
  6.3 31.3 %copy-start.1 = (f32[8,32,128]{2,1,0:T(8,128)S(1)}, f32[8,32,128]{2,1,0:T(8,128)}, u32[]{:S(2)}) copy-start(f32[8,32,128]{2,1,0:T(8,128)} %param.8) | copy-start | bytes 393220
  7.4 56.8 %copy-start.4 = (f32[32,128]{1,0:T(8,128)S(1)}, f32[32,128]{1,0:T(8,128)}, u32[]{:S(2)}) copy-start(f32[32,128]{1,0:T(8,128)} %param.14) | copy-start | bytes 49156
  7.4 26.8 %collective-permute-start = (f32[64,32,128]{2,1,0:T(8,128)S(1)}, f32[64,32,128]{2,1,0:T(8,128)S(1)}, u32[]{:S(2)}, u32[]{:S(2)}) collective-permute-start(f32[64,32,128]{2,1,0:T(8,128)S(1)} %get-tuple-element.6), channel_id=1, source_target_pairs={{0,4},{4,8},{8,12},{12,16},{16,20},{20,24},{24,28},{1,5},{5,9},{9,... | collective-permute-start | bytes 3145736 | tf_op jit(solution)/shard_map/ppermute | solution.py:33
  34.4 25.0 %collective-permute-start.1 = (f32[64,32,128]{2,1,0:T(8,128)S(1)}, f32[64,32,128]{2,1,0:T(8,128)S(1)}, u32[]{:S(2)}, u32[]{:S(2)}) collective-permute-start(f32[64,32,128]{2,1,0:T(8,128)S(1)} %add.208), channel_id=1, source_target_pairs={{0,8},{4,12},{8,16},{12,20},{16,24},{20,28},{1,9},{5,13},{9,17},{1... | collective-permute-start | bytes 3145736 | tf_op jit(solution)/shard_map/ppermute | solution.py:33
  37.6 26.5 %collective-permute-start.3 = (f32[2,1,32,128]{3,2,1,0:T(8,128)S(1)}, f32[2,1,32,128]{3,2,1,0:T(8,128)S(1)}, u32[]{:S(2)}, u32[]{:S(2)}) collective-permute-start(f32[2,1,32,128]{3,2,1,0:T(8,128)S(1)} %get-tuple-element.24), channel_id=1, source_target_pairs={{0,4},{4,8},{8,12},{12,16},{16,20},{20,24},{24,28},{1,5},{5,9},{9,... | collective-permute-start | bytes 98312 | tf_op jit(solution)/shard_map/ppermute | solution.py:33
  39.9 24.3 %collective-permute-start.6 = (f32[2,1,32,128]{3,2,1,0:T(8,128)S(1)}, f32[2,1,32,128]{3,2,1,0:T(8,128)S(1)}, u32[]{:S(2)}, u32[]{:S(2)}) collective-permute-start(f32[2,1,32,128]{3,2,1,0:T(8,128)S(1)} %get-tuple-element.25), channel_id=1, source_target_pairs={{4,0},{8,4},{12,8},{16,12},{20,16},{24,20},{28,24},{5,1},{9,5},{13... | collective-permute-start | bytes 98312 | tf_op jit(solution)/shard_map/ppermute | solution.py:33
  43.9 20.3 %collective-permute-start.4 = (f32[2,8,1,128]{3,2,1,0:T(1,128)S(1)}, f32[2,8,1,128]{3,2,1,0:T(1,128)S(1)}, u32[]{:S(2)}, u32[]{:S(2)}) collective-permute-start(f32[2,8,1,128]{3,2,1,0:T(1,128)S(1)} %get-tuple-element.26), channel_id=1, source_target_pairs={{0,1},{1,2},{2,3},{4,5},{5,6},{6,7},{8,9},{9,10},{10,11},{12,13},{... | collective-permute-start | bytes 24584 | tf_op jit(solution)/shard_map/ppermute | solution.py:33
  49.3 14.9 %collective-permute-start.5 = (f32[2,8,1,128]{3,2,1,0:T(1,128)S(1)}, f32[2,8,1,128]{3,2,1,0:T(1,128)S(1)}, u32[]{:S(2)}, u32[]{:S(2)}) collective-permute-start(f32[2,8,1,128]{3,2,1,0:T(1,128)S(1)} %get-tuple-element.27), channel_id=1, source_target_pairs={{1,0},{2,1},{3,2},{5,4},{6,5},{7,6},{9,8},{10,9},{11,10},{13,12},{... | collective-permute-start | bytes 24584 | tf_op jit(solution)/shard_map/ppermute | solution.py:33
  51.5 57.9 %copy-start = (bf16[64,8,32,128]{3,2,1,0:T(8,128)(2,1)S(1)}, bf16[64,8,32,128]{3,2,1,0:T(8,128)(2,1)}, u32[]{:S(2)}) copy-start(bf16[64,8,32,128]{3,2,1,0:T(8,128)(2,1)} %param.11) | copy-start | bytes 12582916
  51.5 57.9 %copy-start.3 = (f32[64,32,128]{2,1,0:T(8,128)S(1)}, f32[64,32,128]{2,1,0:T(8,128)}, u32[]{:S(2)}) copy-start(f32[64,32,128]{2,1,0:T(8,128)} %param.12) | copy-start | bytes 3145732
  51.5 57.9 %copy-start.5 = (f32[64]{0:T(128)S(1)}, f32[64]{0:T(128)}, u32[]{:S(2)}) copy-start(f32[64]{0:T(128)} %param.13) | copy-start | bytes 772
  59.6 49.4 %collective-permute-start.2 = (f32[64,32,128]{2,1,0:T(8,128)S(1)}, f32[64,32,128]{2,1,0:T(8,128)S(1)}, u32[]{:S(2)}, u32[]{:S(2)}) collective-permute-start(f32[64,32,128]{2,1,0:T(8,128)S(1)} %add.210), channel_id=1, source_target_pairs={{0,16},{4,20},{8,24},{12,28},{1,17},{5,21},{9,25},{13,29},{2,18},{... | collective-permute-start | bytes 3145736 | tf_op jit(solution)/shard_map/ppermute | solution.py:33
  109.4 6.6 %copy-start.2 = (f32[8,32,128]{2,1,0:T(8,128)S(1)}, f32[8,32,128]{2,1,0:T(8,128)}, u32[]{:S(2)}) copy-start(f32[8,32,128]{2,1,0:T(8,128)} %param.9) | copy-start | bytes 393220
  116.9 14.3 %collective-permute-start.10 = (f32[2,1,32,128]{3,2,1,0:T(8,128)S(1)}, f32[2,1,32,128]{3,2,1,0:T(8,128)S(1)}, u32[]{:S(2)}, u32[]{:S(2)}) collective-permute-start(f32[2,1,32,128]{3,2,1,0:T(8,128)S(1)} %get-tuple-element.21), channel_id=1, source_target_pairs={{4,0},{8,4},{12,8},{16,12},{20,16},{24,20},{28,24},{5,1},{9,5},{13... | collective-permute-start | bytes 98312 | tf_op jit(solution)/shard_map/ppermute | solution.py:33
  118.8 12.4 %collective-permute-start.7 = (f32[2,1,32,128]{3,2,1,0:T(8,128)S(1)}, f32[2,1,32,128]{3,2,1,0:T(8,128)S(1)}, u32[]{:S(2)}, u32[]{:S(2)}) collective-permute-start(f32[2,1,32,128]{3,2,1,0:T(8,128)S(1)} %get-tuple-element.20), channel_id=1, source_target_pairs={{0,4},{4,8},{8,12},{12,16},{16,20},{20,24},{24,28},{1,5},{5,9},{9,... | collective-permute-start | bytes 98312 | tf_op jit(solution)/shard_map/ppermute | solution.py:33
  122.2 6.0 %collective-permute-start.8 = (f32[2,8,1,128]{3,2,1,0:T(1,128)S(1)}, f32[2,8,1,128]{3,2,1,0:T(1,128)S(1)}, u32[]{:S(2)}, u32[]{:S(2)}) collective-permute-start(f32[2,8,1,128]{3,2,1,0:T(1,128)S(1)} %get-tuple-element.22), channel_id=1, source_target_pairs={{0,1},{1,2},{2,3},{4,5},{5,6},{6,7},{8,9},{9,10},{10,11},{12,13},{... | collective-permute-start | bytes 24584 | tf_op jit(solution)/shard_map/ppermute | solution.py:33
  126.2 5.0 %collective-permute-start.9 = (f32[2,8,1,128]{3,2,1,0:T(1,128)S(1)}, f32[2,8,1,128]{3,2,1,0:T(1,128)S(1)}, u32[]{:S(2)}, u32[]{:S(2)}) collective-permute-start(f32[2,8,1,128]{3,2,1,0:T(1,128)S(1)} %get-tuple-element.23), channel_id=1, source_target_pairs={{1,0},{2,1},{3,2},{5,4},{6,5},{7,6},{9,8},{10,9},{11,10},{13,12},{... | collective-permute-start | bytes 24584 | tf_op jit(solution)/shard_map/ppermute | solution.py:33

commit v2 on v1

--- a/solution.py
+++ b/solution.py
@@ -47,20 +47,37 @@
     return jnp.pad(bordered, ((0, 0), (0, 0), (0, 0), (1, 1)))
 
 
-def exclusive_scan(totals, axis):
-    count = lax.axis_size(axis)
+def exclusive_scan(totals, axis, stride=1):
+    count = lax.axis_size(axis) // stride
     if count == 1:
         return jnp.zeros_like(totals)
-    before = shifted(totals, axis, 1)
+    before = shifted(totals, axis, stride)
     through = totals + before
     step = 2
     while step < count:
-        arrived = shifted(through, axis, step)
+        arrived = shifted(through, axis, step * stride)
         before = before + arrived
         step *= 2
         if step < count:
             through = through + arrived
     return before
+
+
+def paired_scan(totals, axis):
+    count = lax.axis_size(axis)
+    half = totals.shape[0] // 2
+    if count % 2 or totals.shape[0] % 2 or count == 2:
+        return exclusive_scan(totals, axis)
+    is_low = lax.axis_index(axis) % 2 == 0
+    first, second = totals[:half], totals[half:]
+    mine = jnp.where(is_low, first, second)
+    swap = [(i, i ^ 1) for i in range(count)]
+    got = lax.ppermute(jnp.where(is_low, second, first), axis, swap)
+    before = exclusive_scan(mine + got, axis, stride=2)
+    back = lax.ppermute(jnp.where(is_low, before + mine, before), axis, swap)
+    low_result = jnp.concatenate([before, back])
+    high_result = jnp.concatenate([back, before + got])
+    return jnp.where(is_low, low_result, high_result)
 
 
 def window(source, step_beam, step_cross, step_depth):
@@ -131,7 +148,7 @@
         prefix.append(running)
         running = running + optical_depth[:, row]
     local_column = jnp.stack(prefix, axis=1)
-    column = exclusive_scan(running, "beam")[:, None] + local_column
+    column = paired_scan(running, "beam")[:, None] + local_column
     radiance = entry_spectral_power[:, None] * jnp.exp(-column)
     spectral_power = radiance.astype(jnp.bfloat16)
     pumping = pump_scale * jnp.sum(weight * radiance, axis=0)

time: 135 us -> 108 us (0.80)
  waiting for transfers between devices: 78.1 us -> 39.9 us
  other arithmetic: 18.6 us -> 28.6 us
  local copies, waits for them, and re-layouts: 0.4 us -> 5.57 us
  starting transfers between devices: 35.4 us -> 32 us
    ppermute x11 -> x10, waiting for transfers between devices: 78.1 us -> 16.9 us  [shifted(): return lax.ppermute(block, axis, pairs)]
    ppermute x0 -> x2, waiting for transfers between devices: none -> 23 us  [the longest x1 11.6 us: paired_scan(): got = lax.ppermute(jnp.where(is_low, second, first), axis, swap)]
    unnamed x16 -> x18, local copies, waits for them, and re-layouts: 0.4 us -> 5.57 us
    ppermute x11 -> x10, starting transfers between devices: 35.4 us -> 30.7 us  [shifted(): return lax.ppermute(block, axis, pairs)]
    unnamed x2, other arithmetic: 0.42 us -> 4.19 us
    another operation x1, other arithmetic: 0.21 us -> 3.24 us  [local(): local_column = jnp.stack(prefix, axis=1)]
    reduce_sum x1, other arithmetic: 6.6 us -> 8.82 us  [local(): heating = jnp.sum(radiance * (1.0 - jnp.exp(-optical_depth)), axis=0)]
    ppermute x0 -> x2, starting transfers between devices: none -> 1.38 us  [the longest x1 1.3 us: paired_scan(): got = lax.ppermute(jnp.where(is_low, second, first), axis, swap)]
  transfers between devices with their start and end apart: 11 -> 12, of which waited for: 4 -> 4; matrix products, arithmetic and copies ran while one was open for 2% -> 9% of each run, Pallas kernels for 0% -> 0%
where the time goes in v2:
time: 108 us; the launch traced here: 107 us
  waiting for transfers between devices  39.9 us (37%)
  starting transfers between devices  32 us (30%)
  other arithmetic  28.6 us (26%)
  local copies, waits for them, and re-layouts  5.57 us (5%)
    ppermute x10, starting transfers between devices, shifted(): return lax.ppermute(block, axis, pairs)  30.7 us
    ppermute x10, waiting for transfers between devices, shifted(): return lax.ppermute(block, axis, pairs)  16.9 us
    ppermute x1, waiting for transfers between devices, paired_scan(): got = lax.ppermute(jnp.where(is_low, second, first), axis, swap)  11.6 us
    ppermute x1, waiting for transfers between devices, paired_scan(): back = lax.ppermute(jnp.where(is_low, before + mine, before), axis, swap)  11.4 us
    reduce_sum x1, other arithmetic, local(): heating = jnp.sum(radiance * (1.0 - jnp.exp(-optical_depth)), axis=0)  8.82 us
    unnamed x18, local copies, waits for them, and re-layouts  5.57 us
    unnamed x2, other arithmetic  4.19 us
    add x1, other arithmetic, local(): optical_depth = absorber[None] * weight + glass_term[None]  3.48 us
  transfers between devices with their start and end apart: 12, of which 4 were waited for; matrix products, arithmetic and copies ran while one was open for 9% of the time, Pallas kernels for 0%

profile of v2, /device:TPU:9, one launch (start us, length us, event | category | flops | bytes accessed | tf_op | source)
XLA Modules:
  0.0 107.1 jit_solution(2704497355271643232)
XLA Ops:
  0.6 1.1 %broadcast_dynamic-update-slice_fusion = f32[64,8,32,128]{3,2,1,0:T(8,128)} fusion(), kind=kLoop, calls=%fused_computation.58 | loop fusion | bytes 1048576
  1.7 0.7 convert_subtract_fusion
  2.4 1.1 add_bitcast_fusion
  3.5 3.5 %multiply_add_fusion = f32[64,8,32,128]{3,2,1,0:T(8,128)S(1)} fusion(bf16[64,8,32,128]{3,2,1,0:T(8,128)(2,1)} %param.11, f32[8,32]{1,0:T(8,128)S(1)} %get-tuple-element.33, f32[64]{0:T(128)} %param.13, f32[8,32,128]{2,1,0:T(8,128)S(1)} %get-tuple-element.31), kind=kLoop, calls=%fused_computation.3 | loop fusion | flops 10485760 | bytes 12715264 | tf_op jit(solution)/shard_map/add | solution.py:144
  7.0 0.0 copy-start
  7.0 1.1 %slice_dynamic-update-slice_fusion = f32[64,8,32,128]{3,2,1,0:T(8,128)} fusion(f32[64,8,32,128]{3,2,1,0:T(8,128)} %broadcast_dynamic-update-slice_fusion, f32[64,8,32,128]{3,2,1,0:T(8,128)S(1)} %multiply_add_fusion), kind=kLoop, calls=%fused_computation.44 | loop fusion | bytes 2097152
  8.1 1.7 %constant_dynamic-update-slice_fusion.2 = f32[64,8,32,128]{3,2,1,0:T(8,128)} fusion(f32[64,8,32,128]{3,2,1,0:T(8,128)} %slice_dynamic-update-slice_fusion, f32[64,8,32,128]{3,2,1,0:T(8,128)S(1)} %multiply_add_fusion), kind=kLoop, calls=%fused_computation.232 | loop fusion | flops 262144 | bytes 3145728
  9.8 1.1 %copy-done = f32[64,8,32,128]{3,2,1,0:T(8,128)} copy-done((f32[64,8,32,128]{3,2,1,0:T(8,128)}, f32[64,8,32,128]{3,2,1,0:T(8,128)S(1)}, u32[]{:S(2)}) %copy-start) | copy-done | bytes 8388632
  10.9 0.0 copy-start.2
  10.9 2.0 %slice_add_fusion = (f32[64,1,32,128]{3,2,1,0:T(8,128)S(1)}, f32[64,1,32,128]{3,2,1,0:T(8,128)S(1)}, f32[64,1,32,128]{3,2,1,0:T(8,128)S(1)}, f32[64,8,32,128]{3,2,1,0:T(8,128)}) fusion(f32[64,8,32,128]{3,2,1,0:T(8,128)S(1)} %multiply_add_fusion, f32[64,8,32,128]{3,2,1,0:T(8,128)} %constant_dynamic-update-slice_fusion.2), kind=kLoop, calls=%fused_computation.36 | loop fusion | flops 1835008 | bytes 12582912 | tf_op jit(solution)/shard_map/add | solution.py:149
  13.0 0.1 fusion.1
  13.0 1.3 %collective-permute-start = (f32[32,32,128]{2,1,0:T(8,128)S(1)}, f32[32,32,128]{2,1,0:T(8,128)S(1)}, u32[]{:S(2)}, u32[]{:S(2)}) collective-permute-start(f32[32,32,128]{2,1,0:T(8,128)S(1)} %fusion.1), channel_id=1, source_target_pairs={{0,4},{4,0},{8,12},{12,8},{16,20},{20,16},{24,28},{28,24},{1,5},{5... | collective-permute-start | bytes 1572872 | tf_op jit(solution)/shard_map/ppermute | solution.py:75
  14.3 11.6 %collective-permute-done = f32[32,32,128]{2,1,0:T(8,128)S(1)} collective-permute-done((f32[32,32,128]{2,1,0:T(8,128)S(1)}, f32[32,32,128]{2,1,0:T(8,128)S(1)}, u32[]{:S(2)}, u32[]{:S(2)}) %collective-permute-start) | collective-permute-done | bytes 524320 | tf_op jit(solution)/shard_map/ppermute | solution.py:75
  25.9 0.1 bitcast_add_fusion
  26.0 3.2 %collective-permute-start.1 = (f32[32,32,128]{2,1,0:T(8,128)S(1)}, f32[32,32,128]{2,1,0:T(8,128)S(1)}, u32[]{:S(2)}, u32[]{:S(2)}) collective-permute-start(f32[32,32,128]{2,1,0:T(8,128)S(1)} %bitcast_add_fusion), channel_id=1, source_target_pairs={{0,8},{4,12},{8,16},{12,20},{16,24},{20,28},{1,9},{5,13},{9,17},{1... | collective-permute-start | bytes 1572872 | tf_op jit(solution)/shard_map/ppermute | solution.py:33
  29.3 0.0 copy-done.2
  29.3 3.1 %collective-permute-start.7 = (f32[2,1,32,128]{3,2,1,0:T(8,128)S(1)}, f32[2,1,32,128]{3,2,1,0:T(8,128)S(1)}, u32[]{:S(2)}, u32[]{:S(2)}) collective-permute-start(f32[2,1,32,128]{3,2,1,0:T(8,128)S(1)} %get-tuple-element.27), channel_id=1, source_target_pairs={{4,0},{8,4},{12,8},{16,12},{20,16},{24,20},{28,24},{5,1},{9,5},{13... | collective-permute-start | bytes 98312 | tf_op jit(solution)/shard_map/ppermute | solution.py:33
  32.4 4.0 %collective-permute-start.6 = (f32[2,8,1,128]{3,2,1,0:T(1,128)S(1)}, f32[2,8,1,128]{3,2,1,0:T(1,128)S(1)}, u32[]{:S(2)}, u32[]{:S(2)}) collective-permute-start(f32[2,8,1,128]{3,2,1,0:T(1,128)S(1)} %get-tuple-element.29), channel_id=1, source_target_pairs={{1,0},{2,1},{3,2},{5,4},{6,5},{7,6},{9,8},{10,9},{11,10},{13,12},{... | collective-permute-start | bytes 24584 | tf_op jit(solution)/shard_map/ppermute | solution.py:33
  36.4 3.0 %collective-permute-start.5 = (f32[2,8,1,128]{3,2,1,0:T(1,128)S(1)}, f32[2,8,1,128]{3,2,1,0:T(1,128)S(1)}, u32[]{:S(2)}, u32[]{:S(2)}) collective-permute-start(f32[2,8,1,128]{3,2,1,0:T(1,128)S(1)} %get-tuple-element.28), channel_id=1, source_target_pairs={{0,1},{1,2},{2,3},{4,5},{5,6},{6,7},{8,9},{9,10},{10,11},{12,13},{... | collective-permute-start | bytes 24584 | tf_op jit(solution)/shard_map/ppermute | solution.py:33
  39.4 2.2 %collective-permute-start.4 = (f32[2,1,32,128]{3,2,1,0:T(8,128)S(1)}, f32[2,1,32,128]{3,2,1,0:T(8,128)S(1)}, u32[]{:S(2)}, u32[]{:S(2)}) collective-permute-start(f32[2,1,32,128]{3,2,1,0:T(8,128)S(1)} %get-tuple-element.26), channel_id=1, source_target_pairs={{0,4},{4,8},{8,12},{12,16},{16,20},{20,24},{24,28},{1,5},{5,9},{9,... | collective-permute-start | bytes 98312 | tf_op jit(solution)/shard_map/ppermute | solution.py:33
  41.6 0.0 copy-start.5
  41.7 1.1 %constant_dynamic-update-slice_fusion.1 = f32[64,8,32,128]{3,2,1,0:T(8,128)} fusion(f32[64,8,32,128]{3,2,1,0:T(8,128)} %get-tuple-element.12, f32[64,1,32,128]{3,2,1,0:T(8,128)S(1)} %get-tuple-element.10), kind=kLoop, calls=%fused_computation.231 | loop fusion | bytes 2097152
  42.8 0.0 collective-permute-done.1
  42.8 0.1 add.217
  42.8 3.9 %collective-permute-start.2 = (f32[32,32,128]{2,1,0:T(8,128)S(1)}, f32[32,32,128]{2,1,0:T(8,128)S(1)}, u32[]{:S(2)}, u32[]{:S(2)}) collective-permute-start(f32[32,32,128]{2,1,0:T(8,128)S(1)} %add.217), channel_id=1, source_target_pairs={{0,16},{4,20},{8,24},{12,28},{1,17},{5,21},{9,25},{13,29},{2,18},{... | collective-permute-start | bytes 1572872 | tf_op jit(solution)/shard_map/ppermute | solution.py:33
  46.8 2.5 %fusion.9 = f32[64,8,32,128]{3,2,1,0:T(8,128)} fusion(f32[64,8,32,128]{3,2,1,0:T(8,128)} %constant_dynamic-update-slice_fusion.1, f32[64,1,32,128]{3,2,1,0:T(8,128)S(1)} %get-tuple-element.10, f32[64,8,32,128]{3,2,1,0:T(8,128)} %copy-done), kind=kLoop, calls=%fused_computation.88 | loop fusion | flops 262144 | bytes 3145728
  49.3 0.0 copy-start.1
  49.3 0.0 copy-start.4
  49.3 0.0 copy-start.6
  49.3 1.1 %constant_dynamic-update-slice_fusion = f32[64,8,32,128]{3,2,1,0:T(8,128)} fusion(f32[64,8,32,128]{3,2,1,0:T(8,128)} %fusion.9, f32[64,1,32,128]{3,2,1,0:T(8,128)S(1)} %get-tuple-element.9), kind=kLoop, calls=%fused_computation.230 | loop fusion | bytes 2097152
  50.4 3.2 %fusion.10 = f32[64,8,32,128]{3,2,1,0:T(8,128)} fusion(f32[64,8,32,128]{3,2,1,0:T(8,128)} %constant_dynamic-update-slice_fusion, f32[64,1,32,128]{3,2,1,0:T(8,128)S(1)} %get-tuple-element.9, f32[64,8,32,128]{3,2,1,0:T(8,128)} %copy-done), kind=kLoop, calls=%fused_computation.89 | loop fusion | flops 262144 | bytes 3145728 | tf_op jit(solution)/shard_map/stack | solution.py:150
  53.6 15.8 %collective-permute-done.2 = f32[32,32,128]{2,1,0:T(8,128)S(1)} collective-permute-done((f32[32,32,128]{2,1,0:T(8,128)S(1)}, f32[32,32,128]{2,1,0:T(8,128)S(1)}, u32[]{:S(2)}, u32[]{:S(2)}) %collective-permute-start.2) | collective-permute-done | bytes 524320 | tf_op jit(solution)/shard_map/ppermute | solution.py:33
  69.4 0.1 fusion.118
  69.6 0.2 add_select_fusion
  69.7 0.1 collective-permute-start.3
  69.8 0.0 copy-done.5
  69.8 0.0 collective-permute-done.6
  69.8 0.0 collective-permute-done.5
  69.8 0.0 collective-permute-done.7
  69.9 0.0 collective-permute-done.4
  69.9 0.1 fusion.3
  69.9 0.5 power_multiply_fusion.2
  70.5 0.7 fusion.19
  71.2 11.4 %collective-permute-done.3 = f32[32,32,128]{2,1,0:T(8,128)S(1)} collective-permute-done((f32[32,32,128]{2,1,0:T(8,128)S(1)}, f32[32,32,128]{2,1,0:T(8,128)S(1)}, u32[]{:S(2)}, u32[]{:S(2)}) %collective-permute-start.3) | collective-permute-done | bytes 524320 | tf_op jit(solution)/shard_map/ppermute | solution.py:77
  82.6 0.2 maximum_select_fusion
  82.8 0.0 copy-done.1
  82.8 0.0 copy-done.4
  82.8 0.0 copy-done.6
  82.8 0.0 copy-start.3
  82.8 8.8 %multiply_reduce_fusion = (f32[8,32,128]{2,1,0:T(8,128)S(1)}, f32[8,32,128]{2,1,0:T(8,128)S(1)}, bf16[64,8,32,128]{3,2,1,0:T(8,128)(2,1)}) fusion(f32[64,8,32,128]{3,2,1,0:T(8,128)} %fusion.10, f32[64,32,128]{2,1,0:T(8,128)S(1)} %maximum_select_fusion, f32[64,32,128]{2,1,0:T(8,128)S(1)} %copy-done.4, f32[8,32]{1,0:T(8,128)S(1)} %get-tuple-element.33, ...), kind=kLoop, calls=%fused_computation | loop fusion | flops 31391744 | bytes 19268864 | tf_op jit(solution)/shard_map/reduce_sum | solution.py:155
  91.6 0.0 copy-done.3
  91.6 0.8 fusion.116
  92.4 1.9 %collective-permute-start.11 = (f32[2,1,32,128]{3,2,1,0:T(8,128)S(1)}, f32[2,1,32,128]{3,2,1,0:T(8,128)S(1)}, u32[]{:S(2)}, u32[]{:S(2)}) collective-permute-start(f32[2,1,32,128]{3,2,1,0:T(8,128)S(1)} %get-tuple-element.23), channel_id=1, source_target_pairs={{4,0},{8,4},{12,8},{16,12},{20,16},{24,20},{28,24},{5,1},{9,5},{13... | collective-permute-start | bytes 98312 | tf_op jit(solution)/shard_map/ppermute | solution.py:33
  94.4 3.4 %collective-permute-start.8 = (f32[2,1,32,128]{3,2,1,0:T(8,128)S(1)}, f32[2,1,32,128]{3,2,1,0:T(8,128)S(1)}, u32[]{:S(2)}, u32[]{:S(2)}) collective-permute-start(f32[2,1,32,128]{3,2,1,0:T(8,128)S(1)} %get-tuple-element.22), channel_id=1, source_target_pairs={{0,4},{4,8},{8,12},{12,16},{16,20},{20,24},{24,28},{1,5},{5,9},{9,... | collective-permute-start | bytes 98312 | tf_op jit(solution)/shard_map/ppermute | solution.py:33
  97.7 4.0 %collective-permute-start.10 = (f32[2,8,1,128]{3,2,1,0:T(1,128)S(1)}, f32[2,8,1,128]{3,2,1,0:T(1,128)S(1)}, u32[]{:S(2)}, u32[]{:S(2)}) collective-permute-start(f32[2,8,1,128]{3,2,1,0:T(1,128)S(1)} %get-tuple-element.25), channel_id=1, source_target_pairs={{1,0},{2,1},{3,2},{5,4},{6,5},{7,6},{9,8},{10,9},{11,10},{13,12},{... | collective-permute-start | bytes 24584 | tf_op jit(solution)/shard_map/ppermute | solution.py:33
  101.8 1.9 %collective-permute-start.9 = (f32[2,8,1,128]{3,2,1,0:T(1,128)S(1)}, f32[2,8,1,128]{3,2,1,0:T(1,128)S(1)}, u32[]{:S(2)}, u32[]{:S(2)}) collective-permute-start(f32[2,8,1,128]{3,2,1,0:T(1,128)S(1)} %get-tuple-element.24), channel_id=1, source_target_pairs={{0,1},{1,2},{2,3},{4,5},{5,6},{6,7},{8,9},{9,10},{10,11},{12,13},{... | collective-permute-start | bytes 24584 | tf_op jit(solution)/shard_map/ppermute | solution.py:33
  103.7 0.0 collective-permute-done.10
  103.7 1.1 %collective-permute-done.9 = f32[2,8,1,128]{3,2,1,0:T(1,128)S(1)} collective-permute-done((f32[2,8,1,128]{3,2,1,0:T(1,128)S(1)}, f32[2,8,1,128]{3,2,1,0:T(1,128)S(1)}, u32[]{:S(2)}, u32[]{:S(2)}) %collective-permute-start.9) | collective-permute-done | bytes 8224 | tf_op jit(solution)/shard_map/ppermute | solution.py:33
  104.9 0.0 collective-permute-done.11
  104.9 0.0 collective-permute-done.8
  104.9 0.1 fusion.5
  104.9 0.5 power_multiply_fusion
  105.5 0.7 fusion.28
  106.1 0.9 fusion.95
  (6 shorter events, 0.0 us)
Async XLA Ops:
  7.0 3.9 %copy-start = (f32[64,8,32,128]{3,2,1,0:T(8,128)}, f32[64,8,32,128]{3,2,1,0:T(8,128)S(1)}, u32[]{:S(2)}) copy-start(f32[64,8,32,128]{3,2,1,0:T(8,128)S(1)} %multiply_add_fusion) | copy-start | bytes 25165828
  10.9 18.3 %copy-start.2 = (f32[8,32,128]{2,1,0:T(8,128)S(1)}, f32[8,32,128]{2,1,0:T(8,128)}, u32[]{:S(2)}) copy-start(f32[8,32,128]{2,1,0:T(8,128)} %param.8) | copy-start | bytes 393220
  13.0 12.9 %collective-permute-start = (f32[32,32,128]{2,1,0:T(8,128)S(1)}, f32[32,32,128]{2,1,0:T(8,128)S(1)}, u32[]{:S(2)}, u32[]{:S(2)}) collective-permute-start(f32[32,32,128]{2,1,0:T(8,128)S(1)} %fusion.1), channel_id=1, source_target_pairs={{0,4},{4,0},{8,12},{12,8},{16,20},{20,16},{24,28},{28,24},{1,5},{5... | collective-permute-start | bytes 1572872 | tf_op jit(solution)/shard_map/ppermute | solution.py:75
  26.0 16.7 %collective-permute-start.1 = (f32[32,32,128]{2,1,0:T(8,128)S(1)}, f32[32,32,128]{2,1,0:T(8,128)S(1)}, u32[]{:S(2)}, u32[]{:S(2)}) collective-permute-start(f32[32,32,128]{2,1,0:T(8,128)S(1)} %bitcast_add_fusion), channel_id=1, source_target_pairs={{0,8},{4,12},{8,16},{12,20},{16,24},{20,28},{1,9},{5,13},{9,17},{1... | collective-permute-start | bytes 1572872 | tf_op jit(solution)/shard_map/ppermute | solution.py:33
  29.3 40.6 %collective-permute-start.7 = (f32[2,1,32,128]{3,2,1,0:T(8,128)S(1)}, f32[2,1,32,128]{3,2,1,0:T(8,128)S(1)}, u32[]{:S(2)}, u32[]{:S(2)}) collective-permute-start(f32[2,1,32,128]{3,2,1,0:T(8,128)S(1)} %get-tuple-element.27), channel_id=1, source_target_pairs={{4,0},{8,4},{12,8},{16,12},{20,16},{24,20},{28,24},{5,1},{9,5},{13... | collective-permute-start | bytes 98312 | tf_op jit(solution)/shard_map/ppermute | solution.py:33
  32.4 37.5 %collective-permute-start.6 = (f32[2,8,1,128]{3,2,1,0:T(1,128)S(1)}, f32[2,8,1,128]{3,2,1,0:T(1,128)S(1)}, u32[]{:S(2)}, u32[]{:S(2)}) collective-permute-start(f32[2,8,1,128]{3,2,1,0:T(1,128)S(1)} %get-tuple-element.29), channel_id=1, source_target_pairs={{1,0},{2,1},{3,2},{5,4},{6,5},{7,6},{9,8},{10,9},{11,10},{13,12},{... | collective-permute-start | bytes 24584 | tf_op jit(solution)/shard_map/ppermute | solution.py:33
  36.4 33.4 %collective-permute-start.5 = (f32[2,8,1,128]{3,2,1,0:T(1,128)S(1)}, f32[2,8,1,128]{3,2,1,0:T(1,128)S(1)}, u32[]{:S(2)}, u32[]{:S(2)}) collective-permute-start(f32[2,8,1,128]{3,2,1,0:T(1,128)S(1)} %get-tuple-element.28), channel_id=1, source_target_pairs={{0,1},{1,2},{2,3},{4,5},{5,6},{6,7},{8,9},{9,10},{10,11},{12,13},{... | collective-permute-start | bytes 24584 | tf_op jit(solution)/shard_map/ppermute | solution.py:33
  39.4 30.4 %collective-permute-start.4 = (f32[2,1,32,128]{3,2,1,0:T(8,128)S(1)}, f32[2,1,32,128]{3,2,1,0:T(8,128)S(1)}, u32[]{:S(2)}, u32[]{:S(2)}) collective-permute-start(f32[2,1,32,128]{3,2,1,0:T(8,128)S(1)} %get-tuple-element.26), channel_id=1, source_target_pairs={{0,4},{4,8},{8,12},{12,16},{16,20},{20,24},{24,28},{1,5},{5,9},{9,... | collective-permute-start | bytes 98312 | tf_op jit(solution)/shard_map/ppermute | solution.py:33
  41.6 28.2 %copy-start.5 = (f32[32,128]{1,0:T(8,128)S(1)}, f32[32,128]{1,0:T(8,128)}, u32[]{:S(2)}) copy-start(f32[32,128]{1,0:T(8,128)} %param.14) | copy-start | bytes 49156
  42.8 26.6 %collective-permute-start.2 = (f32[32,32,128]{2,1,0:T(8,128)S(1)}, f32[32,32,128]{2,1,0:T(8,128)S(1)}, u32[]{:S(2)}, u32[]{:S(2)}) collective-permute-start(f32[32,32,128]{2,1,0:T(8,128)S(1)} %add.217), channel_id=1, source_target_pairs={{0,16},{4,20},{8,24},{12,28},{1,17},{5,21},{9,25},{13,29},{2,18},{... | collective-permute-start | bytes 1572872 | tf_op jit(solution)/shard_map/ppermute | solution.py:33
  49.3 33.5 %copy-start.1 = (bf16[64,8,32,128]{3,2,1,0:T(8,128)(2,1)S(1)}, bf16[64,8,32,128]{3,2,1,0:T(8,128)(2,1)}, u32[]{:S(2)}) copy-start(bf16[64,8,32,128]{3,2,1,0:T(8,128)(2,1)} %param.11) | copy-start | bytes 12582916
  49.3 33.5 %copy-start.4 = (f32[64,32,128]{2,1,0:T(8,128)S(1)}, f32[64,32,128]{2,1,0:T(8,128)}, u32[]{:S(2)}) copy-start(f32[64,32,128]{2,1,0:T(8,128)} %param.12) | copy-start | bytes 3145732
  49.3 33.5 %copy-start.6 = (f32[64]{0:T(128)S(1)}, f32[64]{0:T(128)}, u32[]{:S(2)}) copy-start(f32[64]{0:T(128)} %param.13) | copy-start | bytes 772
  69.7 12.8 %collective-permute-start.3 = (f32[32,32,128]{2,1,0:T(8,128)S(1)}, f32[32,32,128]{2,1,0:T(8,128)S(1)}, u32[]{:S(2)}, u32[]{:S(2)}) collective-permute-start(f32[32,32,128]{2,1,0:T(8,128)S(1)} %add_select_fusion), channel_id=1, source_target_pairs={{0,4},{4,0},{8,12},{12,8},{16,20},{20,16},{24,28},{28,24},{1,5},{5... | collective-permute-start | bytes 1572872 | tf_op jit(solution)/shard_map/ppermute | solution.py:77
  82.8 8.8 %copy-start.3 = (f32[8,32,128]{2,1,0:T(8,128)S(1)}, f32[8,32,128]{2,1,0:T(8,128)}, u32[]{:S(2)}) copy-start(f32[8,32,128]{2,1,0:T(8,128)} %param.9) | copy-start | bytes 393220
  92.4 12.4 %collective-permute-start.11 = (f32[2,1,32,128]{3,2,1,0:T(8,128)S(1)}, f32[2,1,32,128]{3,2,1,0:T(8,128)S(1)}, u32[]{:S(2)}, u32[]{:S(2)}) collective-permute-start(f32[2,1,32,128]{3,2,1,0:T(8,128)S(1)} %get-tuple-element.23), channel_id=1, source_target_pairs={{4,0},{8,4},{12,8},{16,12},{20,16},{24,20},{28,24},{5,1},{9,5},{13... | collective-permute-start | bytes 98312 | tf_op jit(solution)/shard_map/ppermute | solution.py:33
  94.4 10.5 %collective-permute-start.8 = (f32[2,1,32,128]{3,2,1,0:T(8,128)S(1)}, f32[2,1,32,128]{3,2,1,0:T(8,128)S(1)}, u32[]{:S(2)}, u32[]{:S(2)}) collective-permute-start(f32[2,1,32,128]{3,2,1,0:T(8,128)S(1)} %get-tuple-element.22), channel_id=1, source_target_pairs={{0,4},{4,8},{8,12},{12,16},{16,20},{20,24},{24,28},{1,5},{5,9},{9,... | collective-permute-start | bytes 98312 | tf_op jit(solution)/shard_map/ppermute | solution.py:33
  97.7 6.0 %collective-permute-start.10 = (f32[2,8,1,128]{3,2,1,0:T(1,128)S(1)}, f32[2,8,1,128]{3,2,1,0:T(1,128)S(1)}, u32[]{:S(2)}, u32[]{:S(2)}) collective-permute-start(f32[2,8,1,128]{3,2,1,0:T(1,128)S(1)} %get-tuple-element.25), channel_id=1, source_target_pairs={{1,0},{2,1},{3,2},{5,4},{6,5},{7,6},{9,8},{10,9},{11,10},{13,12},{... | collective-permute-start | bytes 24584 | tf_op jit(solution)/shard_map/ppermute | solution.py:33
  101.8 3.1 %collective-permute-start.9 = (f32[2,8,1,128]{3,2,1,0:T(1,128)S(1)}, f32[2,8,1,128]{3,2,1,0:T(1,128)S(1)}, u32[]{:S(2)}, u32[]{:S(2)}) collective-permute-start(f32[2,8,1,128]{3,2,1,0:T(1,128)S(1)} %get-tuple-element.24), channel_id=1, source_target_pairs={{0,1},{1,2},{2,3},{4,5},{5,6},{6,7},{8,9},{9,10},{10,11},{12,13},{... | collective-permute-start | bytes 24584 | tf_op jit(solution)/shard_map/ppermute | solution.py:33

commit v3 on v2

--- a/solution.py
+++ b/solution.py
@@ -142,13 +142,11 @@
         1.0 + earlier_spectral_power.astype(jnp.float32) / saturation
     )
     optical_depth = absorber[None] * weight + glass_term[None]
-    running = jnp.zeros_like(optical_depth[:, 0])
-    prefix = []
-    for row in range(rows):
-        prefix.append(running)
-        running = running + optical_depth[:, row]
-    local_column = jnp.stack(prefix, axis=1)
-    column = paired_scan(running, "beam")[:, None] + local_column
+    totals = jnp.sum(optical_depth, axis=1)
+    local_column = jnp.pad(
+        jnp.cumsum(optical_depth[:, : rows - 1], axis=1), ((0, 0), (1, 0), (0, 0), (0, 0))
+    )
+    column = paired_scan(totals, "beam")[:, None] + local_column
     radiance = entry_spectral_power[:, None] * jnp.exp(-column)
     spectral_power = radiance.astype(jnp.bfloat16)
     pumping = pump_scale * jnp.sum(weight * radiance, axis=0)

time: 108 us -> 106 us (0.981)
  local copies, waits for them, and re-layouts: 5.57 us -> 0.04 us
  other arithmetic: 28.6 us -> 30.7 us
    reduce_sum x0 -> x1, other arithmetic: none -> 6.06 us  [local(): totals = jnp.sum(optical_depth, axis=1)]
    unnamed x18 -> x14, local copies, waits for them, and re-layouts: 5.57 us -> 0.04 us
    add x2 -> x0, other arithmetic: 5.52 us -> none  [the longest x1 3.48 us: local(): optical_depth = absorber[None] * weight + glass_term[None]]
    unnamed x2 -> x0, other arithmetic: 4.19 us -> none
    ppermute x10, waiting for transfers between devices: 16.9 us -> 19.2 us  [shifted(): return lax.ppermute(block, axis, pairs)]
    ppermute x1, waiting for transfers between devices: 11.4 us -> 9.3 us  [paired_scan(): back = lax.ppermute(jnp.where(is_low, before + mine, before), axis, swap)]
    reduce_sum x1, other arithmetic: 8.82 us -> 6.82 us  [local(): heating = jnp.sum(radiance * (1.0 - jnp.exp(-optical_depth)), axis=0)]
    another operation x3, other arithmetic: 1.09 us -> 2.31 us  [local(): jnp.stack([xenon_spin_polarization, heat_ratio - boundary_kelvin])]
  transfers between devices with their start and end apart: 12 -> 12, of which waited for: 4 -> 4; matrix products, arithmetic and copies ran while one was open for 9% -> 12% of each run, Pallas kernels for 0% -> 0%
where the time goes in v3:
time: 106 us; the launch traced here: 104 us
  waiting for transfers between devices  40 us (38%)
  starting transfers between devices  32.7 us (31%)
  other arithmetic  30.7 us (29%)
    ppermute x10, starting transfers between devices, shifted(): return lax.ppermute(block, axis, pairs)  31.3 us
    ppermute x10, waiting for transfers between devices, shifted(): return lax.ppermute(block, axis, pairs)  19.2 us
    ppermute x1, waiting for transfers between devices, paired_scan(): got = lax.ppermute(jnp.where(is_low, second, first), axis, swap)  11.6 us
    ppermute x1, waiting for transfers between devices, paired_scan(): back = lax.ppermute(jnp.where(is_low, before + mine, before), axis, swap)  9.3 us
    reduce_sum x1, other arithmetic, local(): heating = jnp.sum(radiance * (1.0 - jnp.exp(-optical_depth)), axis=0)  6.82 us
    reduce_sum x1, other arithmetic, local(): totals = jnp.sum(optical_depth, axis=1)  6.06 us
    another operation x1, other arithmetic, local(): jnp.cumsum(optical_depth[:, :rows - 1], axis=1)  4.16 us
    another operation x3, other arithmetic, local(): jnp.stack([xenon_spin_polarization, heat_ratio - boundary_kelvin])  2.31 us
  transfers between devices with their start and end apart: 12, of which 4 were waited for; matrix products, arithmetic and copies ran while one was open for 12% of the time, Pallas kernels for 0%

profile of v3, /device:TPU:9, one launch (start us, length us, event | category | flops | bytes accessed | tf_op | source)
XLA Modules:
  0.0 104.4 jit_solution(6744105604454326805)
XLA Ops:
  0.6 0.7 convert_subtract_fusion
  1.3 1.1 %add_bitcast_fusion = (f32[1,8,32,128]{3,2,1,0:T(8,128)S(1)}, f32[8,32,128]{2,1,0:T(8,128)S(1)}) fusion(f32[8,32,128]{2,1,0:T(8,128)} %param.9, f32[8,32,128]{2,1,0:T(8,128)} %param.10, f32[8,32]{1,0:T(8,128)S(1)} %get-tuple-element.30), kind=kLoop, calls=%fused_computation.213 | loop fusion | flops 262144 | bytes 525312 | tf_op jit(solution)/shard_map/stack | solution.py:130
  2.4 0.0 copy-start.2
  2.4 6.1 %fusion.117 = (f32[64,32,128]{2,1,0:T(8,128)S(1)}, f32[64,8,32,128]{3,2,1,0:T(8,128)}) fusion(f32[8,32]{1,0:T(8,128)S(1)} %get-tuple-element.31, bf16[64,8,32,128]{3,2,1,0:T(8,128)(2,1)} %param.11, f32[64]{0:T(128)} %param.13, f32[8,32,128]{2,1,0:T(8,128)S(1)} %get-tuple-element.29), kind=kLoop, calls=%fused_computation.228 | loop fusion | flops 12320768 | bytes 13763840 | tf_op jit(solution)/shard_map/reduce_sum | solution.py:145
  8.5 0.0 copy-start
  8.5 0.1 slice_select_fusion
  8.6 1.3 %collective-permute-start = (f32[32,32,128]{2,1,0:T(8,128)S(1)}, f32[32,32,128]{2,1,0:T(8,128)S(1)}, u32[]{:S(2)}, u32[]{:S(2)}) collective-permute-start(f32[32,32,128]{2,1,0:T(8,128)S(1)} %slice_select_fusion), channel_id=1, source_target_pairs={{0,4},{4,0},{8,12},{12,8},{16,20},{20,16},{24,28},{28,24},{1,5},{5... | collective-permute-start | bytes 1572872 | tf_op jit(solution)/shard_map/ppermute | solution.py:75
  9.9 11.6 %collective-permute-done = f32[32,32,128]{2,1,0:T(8,128)S(1)} collective-permute-done((f32[32,32,128]{2,1,0:T(8,128)S(1)}, f32[32,32,128]{2,1,0:T(8,128)S(1)}, u32[]{:S(2)}, u32[]{:S(2)}) %collective-permute-start) | collective-permute-done | bytes 524320 | tf_op jit(solution)/shard_map/ppermute | solution.py:75
  21.4 0.2 fusion.89
  21.6 3.2 %collective-permute-start.1 = (f32[32,32,128]{2,1,0:T(8,128)S(1)}, f32[32,32,128]{2,1,0:T(8,128)S(1)}, u32[]{:S(2)}, u32[]{:S(2)}) collective-permute-start(f32[32,32,128]{2,1,0:T(8,128)S(1)} %fusion.89), channel_id=1, source_target_pairs={{0,8},{4,12},{8,16},{12,20},{16,24},{20,28},{1,9},{5,13},{9,17},{1... | collective-permute-start | bytes 1572872 | tf_op jit(solution)/shard_map/ppermute | solution.py:33
  24.8 0.0 copy-done.2
  24.8 0.6 fusion.109
  25.4 3.1 %collective-permute-start.4 = (f32[2,1,32,128]{3,2,1,0:T(8,128)}, f32[2,1,32,128]{3,2,1,0:T(8,128)S(1)}, u32[]{:S(2)}, u32[]{:S(2)}) collective-permute-start(f32[2,1,32,128]{3,2,1,0:T(8,128)} %get-tuple-element.24), channel_id=1, source_target_pairs={{0,4},{4,8},{8,12},{12,16},{16,20},{20,24},{24,28},{1,5},{5,9},{9,... | collective-permute-start | bytes 98312 | tf_op jit(solution)/shard_map/ppermute | solution.py:33
  28.6 3.0 %collective-permute-start.7 = (f32[2,1,32,128]{3,2,1,0:T(8,128)}, f32[2,1,32,128]{3,2,1,0:T(8,128)}, u32[]{:S(2)}, u32[]{:S(2)}) collective-permute-start(f32[2,1,32,128]{3,2,1,0:T(8,128)} %get-tuple-element.25), channel_id=1, source_target_pairs={{4,0},{8,4},{12,8},{16,12},{20,16},{24,20},{28,24},{5,1},{9,5},{13... | collective-permute-start | bytes 98312 | tf_op jit(solution)/shard_map/ppermute | solution.py:33
  31.6 0.6 fusion.113
  32.2 5.4 %collective-permute-start.5 = (f32[2,8,1,128]{3,2,1,0:T(1,128)}, f32[2,8,1,128]{3,2,1,0:T(1,128)S(1)}, u32[]{:S(2)}, u32[]{:S(2)}) collective-permute-start(f32[2,8,1,128]{3,2,1,0:T(1,128)} %get-tuple-element.26), channel_id=1, source_target_pairs={{0,1},{1,2},{2,3},{4,5},{5,6},{6,7},{8,9},{9,10},{10,11},{12,13},{... | collective-permute-start | bytes 24584 | tf_op jit(solution)/shard_map/ppermute | solution.py:33
  37.6 1.9 %collective-permute-start.6 = (f32[2,8,1,128]{3,2,1,0:T(1,128)}, f32[2,8,1,128]{3,2,1,0:T(1,128)S(1)}, u32[]{:S(2)}, u32[]{:S(2)}) collective-permute-start(f32[2,8,1,128]{3,2,1,0:T(1,128)} %get-tuple-element.27), channel_id=1, source_target_pairs={{1,0},{2,1},{3,2},{5,4},{6,5},{7,6},{9,8},{10,9},{11,10},{13,12},{... | collective-permute-start | bytes 24584 | tf_op jit(solution)/shard_map/ppermute | solution.py:33
  39.6 0.0 collective-permute-done.1
  39.6 0.0 copy-start.3
  39.6 1.0 add.159
  40.6 3.5 %collective-permute-start.2 = (f32[32,32,128]{2,1,0:T(8,128)}, f32[32,32,128]{2,1,0:T(8,128)}, u32[]{:S(2)}, u32[]{:S(2)}) collective-permute-start(f32[32,32,128]{2,1,0:T(8,128)} %add.159), channel_id=1, source_target_pairs={{0,16},{4,20},{8,24},{12,28},{1,17},{5,21},{9,25},{13,29},{2,18},{... | collective-permute-start | bytes 1572872 | tf_op jit(solution)/shard_map/ppermute | solution.py:33
  44.1 0.0 copy-done
  44.1 0.0 copy-done.3
  44.1 4.2 %fusion = f32[64,7,32,128]{3,2,1,0:T(8,128)S(1)} fusion(f32[64,8,32,128]{3,2,1,0:T(8,128)} %get-tuple-element.10), kind=kOutput, calls=%fused_computation.5 | output fusion | flops 11010048 | bytes 14680064 | tf_op jit(solution)/shard_map/jit(cumsum)/reduce_window_sum | solution.py:147
  48.3 0.0 copy-start.1
  48.3 0.0 copy-start.5
  48.3 0.0 copy-start.6
  48.3 18.0 %collective-permute-done.2 = f32[32,32,128]{2,1,0:T(8,128)} collective-permute-done((f32[32,32,128]{2,1,0:T(8,128)}, f32[32,32,128]{2,1,0:T(8,128)}, u32[]{:S(2)}, u32[]{:S(2)}) %collective-permute-start.2) | collective-permute-done | bytes 524320 | tf_op jit(solution)/shard_map/ppermute | solution.py:33
  66.3 1.3 %fusion.118 = (f32[32,32,128]{2,1,0:T(8,128)S(1)}, f32[32,32,128]{2,1,0:T(8,128)S(1)}) fusion(f32[32,32,128]{2,1,0:T(8,128)S(1)} %collective-permute-done, f32[32,32,128]{2,1,0:T(8,128)} %copy-done.3, f32[32,32,128]{2,1,0:T(8,128)} %collective-permute-done.2), kind=kLoop, calls=%fused_computation.229 | loop fusion | flops 262144 | bytes 2621440 | tf_op jit(solution)/shard_map/add | solution.py:79
  67.7 1.4 %add_select_fusion = f32[32,32,128]{2,1,0:T(8,128)S(1)} fusion(f32[32,32,128]{2,1,0:T(8,128)S(1)} %get-tuple-element.7, pred[]{:T(512)S(6)} %eq.5, f32[64,32,128]{2,1,0:T(8,128)} %copy-done), kind=kLoop, calls=%fused_computation.39 | loop fusion | flops 393216 | bytes 2097153 | tf_op jit(solution)/shard_map/jit(_where)/select_n | solution.py:77
  69.1 0.1 collective-permute-start.3
  69.1 0.7 broadcast_multiply_fusion.1
  69.9 0.0 collective-permute-done.5
  69.9 0.0 collective-permute-done.6
  69.9 0.0 collective-permute-done.4
  69.9 0.0 collective-permute-done.7
  69.9 0.8 fusion.4
  70.7 0.5 power_multiply_fusion.2
  71.3 1.4 %fusion.17 = f32[2,8,32,128]{3,2,1,0:T(8,128)S(1)} fusion(f32[2,1,1,128]{3,2,1,0:T(1,128)S(1)} %broadcast.70, f32[2,10,34,128]{3,2,1,0:T(8,128)S(1)} %fusion.4, f32[1,10,34,130]{3,2,1,0:T(8,128)S(1)} %get-tuple-element.16, f32[1,10,34,130]{3,2,1,0:T(8,128)S(1)} %get-tuple-element.15, f32[2,8,1,128]{3,2,1,0:T(1,128)S(1)} %collective-permute-done.5, ...), kind=kLoop, calls=%fused_computation.94 | loop fusion | flops 3670016 | bytes 1325376 | tf_op jit(solution)/shard_map/sub | solution.py:107
  72.7 9.3 %collective-permute-done.3 = f32[32,32,128]{2,1,0:T(8,128)S(1)} collective-permute-done((f32[32,32,128]{2,1,0:T(8,128)S(1)}, f32[32,32,128]{2,1,0:T(8,128)S(1)}, u32[]{:S(2)}, u32[]{:S(2)}) %collective-permute-start.3) | collective-permute-done | bytes 524320 | tf_op jit(solution)/shard_map/ppermute | solution.py:77
  82.0 0.2 maximum_select_fusion
  82.2 0.0 copy-done.1
  82.2 0.0 copy-done.5
  82.2 0.0 copy-done.6
  82.2 0.0 copy-start.4
  82.2 6.8 %multiply_reduce_fusion = (f32[8,32,128]{2,1,0:T(8,128)S(1)}, f32[8,32,128]{2,1,0:T(8,128)S(1)}, bf16[64,8,32,128]{3,2,1,0:T(8,128)(2,1)}) fusion(f32[64,7,32,128]{3,2,1,0:T(8,128)S(1)} %fusion, f32[64,32,128]{2,1,0:T(8,128)S(1)} %maximum_select_fusion, f32[64,32,128]{2,1,0:T(8,128)S(1)} %copy-done.5, f32[8,32]{1,0:T(8,128)S(1)} %get-tuple-element.31, ...), kind=kLoop, calls=%fused_computation | loop fusion | flops 31391744 | bytes 18220288 | tf_op jit(solution)/shard_map/reduce_sum | solution.py:153
  89.0 0.0 copy-done.4
  89.0 0.8 fusion.115
  89.9 1.9 %collective-permute-start.11 = (f32[2,1,32,128]{3,2,1,0:T(8,128)S(1)}, f32[2,1,32,128]{3,2,1,0:T(8,128)S(1)}, u32[]{:S(2)}, u32[]{:S(2)}) collective-permute-start(f32[2,1,32,128]{3,2,1,0:T(8,128)S(1)} %get-tuple-element.21), channel_id=1, source_target_pairs={{4,0},{8,4},{12,8},{16,12},{20,16},{24,20},{28,24},{5,1},{9,5},{13... | collective-permute-start | bytes 98312 | tf_op jit(solution)/shard_map/ppermute | solution.py:33
  91.8 3.4 %collective-permute-start.8 = (f32[2,1,32,128]{3,2,1,0:T(8,128)S(1)}, f32[2,1,32,128]{3,2,1,0:T(8,128)S(1)}, u32[]{:S(2)}, u32[]{:S(2)}) collective-permute-start(f32[2,1,32,128]{3,2,1,0:T(8,128)S(1)} %get-tuple-element.20), channel_id=1, source_target_pairs={{0,4},{4,8},{8,12},{12,16},{16,20},{20,24},{24,28},{1,5},{5,9},{9,... | collective-permute-start | bytes 98312 | tf_op jit(solution)/shard_map/ppermute | solution.py:33
  95.2 3.9 %collective-permute-start.10 = (f32[2,8,1,128]{3,2,1,0:T(1,128)S(1)}, f32[2,8,1,128]{3,2,1,0:T(1,128)S(1)}, u32[]{:S(2)}, u32[]{:S(2)}) collective-permute-start(f32[2,8,1,128]{3,2,1,0:T(1,128)S(1)} %get-tuple-element.23), channel_id=1, source_target_pairs={{1,0},{2,1},{3,2},{5,4},{6,5},{7,6},{9,8},{10,9},{11,10},{13,12},{... | collective-permute-start | bytes 24584 | tf_op jit(solution)/shard_map/ppermute | solution.py:33
  99.1 1.9 %collective-permute-start.9 = (f32[2,8,1,128]{3,2,1,0:T(1,128)S(1)}, f32[2,8,1,128]{3,2,1,0:T(1,128)S(1)}, u32[]{:S(2)}, u32[]{:S(2)}) collective-permute-start(f32[2,8,1,128]{3,2,1,0:T(1,128)S(1)} %get-tuple-element.22), channel_id=1, source_target_pairs={{0,1},{1,2},{2,3},{4,5},{5,6},{6,7},{8,9},{9,10},{10,11},{12,13},{... | collective-permute-start | bytes 24584 | tf_op jit(solution)/shard_map/ppermute | solution.py:33
  101.0 0.0 collective-permute-done.10
  101.0 1.1 %collective-permute-done.9 = f32[2,8,1,128]{3,2,1,0:T(1,128)S(1)} collective-permute-done((f32[2,8,1,128]{3,2,1,0:T(1,128)S(1)}, f32[2,8,1,128]{3,2,1,0:T(1,128)S(1)}, u32[]{:S(2)}, u32[]{:S(2)}) %collective-permute-start.9) | collective-permute-done | bytes 8224 | tf_op jit(solution)/shard_map/ppermute | solution.py:33
  102.2 0.0 collective-permute-done.11
  102.2 0.0 collective-permute-done.8
  102.2 0.1 fusion.6
  102.2 0.5 power_multiply_fusion
  102.8 0.7 fusion.26
  103.5 0.9 fusion.94
  (3 shorter events, 0.0 us)
Async XLA Ops:
  2.4 22.4 %copy-start.2 = (f32[8,32,128]{2,1,0:T(8,128)S(1)}, f32[8,32,128]{2,1,0:T(8,128)}, u32[]{:S(2)}) copy-start(f32[8,32,128]{2,1,0:T(8,128)} %param.8) | copy-start | bytes 393220
  8.5 35.6 %copy-start = (f32[64,32,128]{2,1,0:T(8,128)}, f32[64,32,128]{2,1,0:T(8,128)S(1)}, u32[]{:S(2)}) copy-start(f32[64,32,128]{2,1,0:T(8,128)S(1)} %get-tuple-element.9) | copy-start | bytes 3145732
  8.6 12.9 %collective-permute-start = (f32[32,32,128]{2,1,0:T(8,128)S(1)}, f32[32,32,128]{2,1,0:T(8,128)S(1)}, u32[]{:S(2)}, u32[]{:S(2)}) collective-permute-start(f32[32,32,128]{2,1,0:T(8,128)S(1)} %slice_select_fusion), channel_id=1, source_target_pairs={{0,4},{4,0},{8,12},{12,8},{16,20},{20,16},{24,28},{28,24},{1,5},{5... | collective-permute-start | bytes 1572872 | tf_op jit(solution)/shard_map/ppermute | solution.py:75
  21.6 18.0 %collective-permute-start.1 = (f32[32,32,128]{2,1,0:T(8,128)S(1)}, f32[32,32,128]{2,1,0:T(8,128)S(1)}, u32[]{:S(2)}, u32[]{:S(2)}) collective-permute-start(f32[32,32,128]{2,1,0:T(8,128)S(1)} %fusion.89), channel_id=1, source_target_pairs={{0,8},{4,12},{8,16},{12,20},{16,24},{20,28},{1,9},{5,13},{9,17},{1... | collective-permute-start | bytes 1572872 | tf_op jit(solution)/shard_map/ppermute | solution.py:33
  25.4 44.4 %collective-permute-start.4 = (f32[2,1,32,128]{3,2,1,0:T(8,128)}, f32[2,1,32,128]{3,2,1,0:T(8,128)S(1)}, u32[]{:S(2)}, u32[]{:S(2)}) collective-permute-start(f32[2,1,32,128]{3,2,1,0:T(8,128)} %get-tuple-element.24), channel_id=1, source_target_pairs={{0,4},{4,8},{8,12},{12,16},{16,20},{20,24},{24,28},{1,5},{5,9},{9,... | collective-permute-start | bytes 98312 | tf_op jit(solution)/shard_map/ppermute | solution.py:33
  28.6 41.3 %collective-permute-start.7 = (f32[2,1,32,128]{3,2,1,0:T(8,128)}, f32[2,1,32,128]{3,2,1,0:T(8,128)}, u32[]{:S(2)}, u32[]{:S(2)}) collective-permute-start(f32[2,1,32,128]{3,2,1,0:T(8,128)} %get-tuple-element.25), channel_id=1, source_target_pairs={{4,0},{8,4},{12,8},{16,12},{20,16},{24,20},{28,24},{5,1},{9,5},{13... | collective-permute-start | bytes 98312 | tf_op jit(solution)/shard_map/ppermute | solution.py:33
  32.2 37.6 %collective-permute-start.5 = (f32[2,8,1,128]{3,2,1,0:T(1,128)}, f32[2,8,1,128]{3,2,1,0:T(1,128)S(1)}, u32[]{:S(2)}, u32[]{:S(2)}) collective-permute-start(f32[2,8,1,128]{3,2,1,0:T(1,128)} %get-tuple-element.26), channel_id=1, source_target_pairs={{0,1},{1,2},{2,3},{4,5},{5,6},{6,7},{8,9},{9,10},{10,11},{12,13},{... | collective-permute-start | bytes 24584 | tf_op jit(solution)/shard_map/ppermute | solution.py:33
  37.6 32.2 %collective-permute-start.6 = (f32[2,8,1,128]{3,2,1,0:T(1,128)}, f32[2,8,1,128]{3,2,1,0:T(1,128)S(1)}, u32[]{:S(2)}, u32[]{:S(2)}) collective-permute-start(f32[2,8,1,128]{3,2,1,0:T(1,128)} %get-tuple-element.27), channel_id=1, source_target_pairs={{1,0},{2,1},{3,2},{5,4},{6,5},{7,6},{9,8},{10,9},{11,10},{13,12},{... | collective-permute-start | bytes 24584 | tf_op jit(solution)/shard_map/ppermute | solution.py:33
  39.6 4.5 %copy-start.3 = (f32[32,32,128]{2,1,0:T(8,128)}, f32[32,32,128]{2,1,0:T(8,128)S(1)}, u32[]{:S(2)}) copy-start(f32[32,32,128]{2,1,0:T(8,128)S(1)} %collective-permute-done.1) | copy-start | bytes 1572868
  40.6 25.8 %collective-permute-start.2 = (f32[32,32,128]{2,1,0:T(8,128)}, f32[32,32,128]{2,1,0:T(8,128)}, u32[]{:S(2)}, u32[]{:S(2)}) collective-permute-start(f32[32,32,128]{2,1,0:T(8,128)} %add.159), channel_id=1, source_target_pairs={{0,16},{4,20},{8,24},{12,28},{1,17},{5,21},{9,25},{13,29},{2,18},{... | collective-permute-start | bytes 1572872 | tf_op jit(solution)/shard_map/ppermute | solution.py:33
  48.3 33.9 %copy-start.1 = (bf16[64,8,32,128]{3,2,1,0:T(8,128)(2,1)S(1)}, bf16[64,8,32,128]{3,2,1,0:T(8,128)(2,1)}, u32[]{:S(2)}) copy-start(bf16[64,8,32,128]{3,2,1,0:T(8,128)(2,1)} %param.11) | copy-start | bytes 12582916
  48.3 33.9 %copy-start.5 = (f32[64,32,128]{2,1,0:T(8,128)S(1)}, f32[64,32,128]{2,1,0:T(8,128)}, u32[]{:S(2)}) copy-start(f32[64,32,128]{2,1,0:T(8,128)} %param.12) | copy-start | bytes 3145732
  48.3 33.9 %copy-start.6 = (f32[64]{0:T(128)S(1)}, f32[64]{0:T(128)}, u32[]{:S(2)}) copy-start(f32[64]{0:T(128)} %param.13) | copy-start | bytes 772
  69.1 12.9 %collective-permute-start.3 = (f32[32,32,128]{2,1,0:T(8,128)S(1)}, f32[32,32,128]{2,1,0:T(8,128)S(1)}, u32[]{:S(2)}, u32[]{:S(2)}) collective-permute-start(f32[32,32,128]{2,1,0:T(8,128)S(1)} %add_select_fusion), channel_id=1, source_target_pairs={{0,4},{4,0},{8,12},{12,8},{16,20},{20,16},{24,28},{28,24},{1,5},{5... | collective-permute-start | bytes 1572872 | tf_op jit(solution)/shard_map/ppermute | solution.py:77
  82.2 6.8 %copy-start.4 = (f32[8,32,128]{2,1,0:T(8,128)S(1)}, f32[8,32,128]{2,1,0:T(8,128)}, u32[]{:S(2)}) copy-start(f32[8,32,128]{2,1,0:T(8,128)} %param.9) | copy-start | bytes 393220
  89.9 12.3 %collective-permute-start.11 = (f32[2,1,32,128]{3,2,1,0:T(8,128)S(1)}, f32[2,1,32,128]{3,2,1,0:T(8,128)S(1)}, u32[]{:S(2)}, u32[]{:S(2)}) collective-permute-start(f32[2,1,32,128]{3,2,1,0:T(8,128)S(1)} %get-tuple-element.21), channel_id=1, source_target_pairs={{4,0},{8,4},{12,8},{16,12},{20,16},{24,20},{28,24},{5,1},{9,5},{13... | collective-permute-start | bytes 98312 | tf_op jit(solution)/shard_map/ppermute | solution.py:33
  91.8 10.4 %collective-permute-start.8 = (f32[2,1,32,128]{3,2,1,0:T(8,128)S(1)}, f32[2,1,32,128]{3,2,1,0:T(8,128)S(1)}, u32[]{:S(2)}, u32[]{:S(2)}) collective-permute-start(f32[2,1,32,128]{3,2,1,0:T(8,128)S(1)} %get-tuple-element.20), channel_id=1, source_target_pairs={{0,4},{4,8},{8,12},{12,16},{16,20},{20,24},{24,28},{1,5},{5,9},{9,... | collective-permute-start | bytes 98312 | tf_op jit(solution)/shard_map/ppermute | solution.py:33
  95.2 5.9 %collective-permute-start.10 = (f32[2,8,1,128]{3,2,1,0:T(1,128)S(1)}, f32[2,8,1,128]{3,2,1,0:T(1,128)S(1)}, u32[]{:S(2)}, u32[]{:S(2)}) collective-permute-start(f32[2,8,1,128]{3,2,1,0:T(1,128)S(1)} %get-tuple-element.23), channel_id=1, source_target_pairs={{1,0},{2,1},{3,2},{5,4},{6,5},{7,6},{9,8},{10,9},{11,10},{13,12},{... | collective-permute-start | bytes 24584 | tf_op jit(solution)/shard_map/ppermute | solution.py:33
  99.1 3.1 %collective-permute-start.9 = (f32[2,8,1,128]{3,2,1,0:T(1,128)S(1)}, f32[2,8,1,128]{3,2,1,0:T(1,128)S(1)}, u32[]{:S(2)}, u32[]{:S(2)}) collective-permute-start(f32[2,8,1,128]{3,2,1,0:T(1,128)S(1)} %get-tuple-element.22), channel_id=1, source_target_pairs={{0,1},{1,2},{2,3},{4,5},{5,6},{6,7},{8,9},{9,10},{10,11},{12,13},{... | collective-permute-start | bytes 24584 | tf_op jit(solution)/shard_map/ppermute | solution.py:33

commit v4 on v3

--- a/solution.py
+++ b/solution.py
@@ -63,21 +63,23 @@
     return before
 
 
-def paired_scan(totals, axis):
+def paired_scan(totals, axis, rider):
     count = lax.axis_size(axis)
     half = totals.shape[0] // 2
     if count % 2 or totals.shape[0] % 2 or count == 2:
-        return exclusive_scan(totals, axis)
+        return exclusive_scan(totals, axis), rider(None)
     is_low = lax.axis_index(axis) % 2 == 0
     first, second = totals[:half], totals[half:]
     mine = jnp.where(is_low, first, second)
     swap = [(i, i ^ 1) for i in range(count)]
-    got = lax.ppermute(jnp.where(is_low, second, first), axis, swap)
+    given = jnp.where(is_low, second, first)
+    got = lax.ppermute(given, axis, swap)
+    got, carried = lax.optimization_barrier((got, rider(given)))
     before = exclusive_scan(mine + got, axis, stride=2)
     back = lax.ppermute(jnp.where(is_low, before + mine, before), axis, swap)
     low_result = jnp.concatenate([before, back])
     high_result = jnp.concatenate([back, before + got])
-    return jnp.where(is_low, low_result, high_result)
+    return jnp.where(is_low, low_result, high_result), carried
 
 
 def window(source, step_beam, step_cross, step_depth):
@@ -128,7 +130,6 @@
     rows = earlier_spectral_power.shape[1]
     total_rows = rows * lax.axis_size("beam")
     physical_quantities = jnp.stack([xenon_spin_polarization, heat_ratio - boundary_kelvin])
-    first_border = bordered_fields(physical_quantities)
     glass_cells = solid_pillar_flags.astype(jnp.float32)[:, :, None]
     fluid_occupied_sites = 1.0 - glass_cells
     rubidium_number_amount = fluid_occupied_sites * jnp.exp(
@@ -146,7 +147,14 @@
     local_column = jnp.pad(
         jnp.cumsum(optical_depth[:, : rows - 1], axis=1), ((0, 0), (1, 0), (0, 0), (0, 0))
     )
-    column = paired_scan(totals, "beam")[:, None] + local_column
+    def first_border(after):
+        fields = physical_quantities
+        if after is not None:
+            fields, _ = lax.optimization_barrier((fields, after))
+        return bordered_fields(fields)
+
+    prefix, first_bordered = paired_scan(totals, "beam", first_border)
+    column = prefix[:, None] + local_column
     radiance = entry_spectral_power[:, None] * jnp.exp(-column)
     spectral_power = radiance.astype(jnp.bfloat16)
     pumping = pump_scale * jnp.sum(weight * radiance, axis=0)
@@ -155,7 +163,7 @@
     rubidium_polarization_new = fluid_occupied_sites * spin_ratio
     drift_speed = flow_scale * flow_rate_forward
     for substep in range(SUBSTEPS):
-        bordered = first_border if substep == 0 else bordered_fields(physical_quantities)
+        bordered = first_bordered if substep == 0 else bordered_fields(physical_quantities)
         physical_quantities = advance(
             bordered, rubidium_number_amount, spin_ratio, heating, drift_speed, fluid_occupied_sites
         )

time: 106 us -> 106 us (level)
  other arithmetic: 30.7 us -> 27 us
  waiting for transfers between devices: 40 us -> 42.1 us
    ppermute x1, waiting for transfers between devices: 11.6 us -> 0.01 us  [paired_scan(): got = lax.ppermute(given, axis, swap)]
    ppermute x10, waiting for transfers between devices: 19.2 us -> 30.5 us  [shifted(): return lax.ppermute(block, axis, pairs)]
    ppermute x1, waiting for transfers between devices: 9.3 us -> 11.6 us  [paired_scan(): back = lax.ppermute(jnp.where(is_low, before + mine, before), axis, swap)]
    another operation x3 -> x2, other arithmetic: 2.31 us -> 1.09 us  [local(): jnp.stack([xenon_spin_polarization, heat_ratio - boundary_kelvin])]
  transfers between devices with their start and end apart: 12 -> 12, of which waited for: 4 -> 6; matrix products, arithmetic and copies ran while one was open for 12% -> 6% of each run, Pallas kernels for 0% -> 0%
where the time goes in v4:
time: 106 us; the launch traced here: 104 us
  waiting for transfers between devices  42.1 us (40%)
  starting transfers between devices  33.4 us (32%)
  other arithmetic  27 us (25%)
    ppermute x10, starting transfers between devices, shifted(): return lax.ppermute(block, axis, pairs)  32 us
    ppermute x10, waiting for transfers between devices, shifted(): return lax.ppermute(block, axis, pairs)  30.5 us
    ppermute x1, waiting for transfers between devices, paired_scan(): back = lax.ppermute(jnp.where(is_low, before + mine, before), axis, swap)  11.6 us
    reduce_sum x1, other arithmetic, local(): heating = jnp.sum(radiance * (1.0 - jnp.exp(-optical_depth)), axis=0)  6.82 us
    reduce_sum x1, other arithmetic, local(): totals = jnp.sum(optical_depth, axis=1)  6.08 us
    another operation x1, other arithmetic, local(): jnp.cumsum(optical_depth[:, :rows - 1], axis=1)  4.16 us
  transfers between devices with their start and end apart: 12, of which 6 were waited for; matrix products, arithmetic and copies ran while one was open for 6% of the time, Pallas kernels for 0%

profile of v4, /device:TPU:9, one launch (start us, length us, event | category | flops | bytes accessed | tf_op | source)
XLA Modules:
  0.0 104.1 jit_solution(4469213527472790026)
XLA Ops:
  0.6 0.0 copy-start.6
  0.6 0.7 convert_subtract_fusion
  1.4 1.1 %add_bitcast_fusion = (f32[1,8,32,128]{3,2,1,0:T(8,128)S(1)}, f32[8,32,128]{2,1,0:T(8,128)S(1)}) fusion(f32[8,32,128]{2,1,0:T(8,128)} %param.9, f32[8,32,128]{2,1,0:T(8,128)} %param.10, f32[8,32]{1,0:T(8,128)S(1)} %get-tuple-element.34), kind=kLoop, calls=%fused_computation.181 | loop fusion | flops 262144 | bytes 525312 | tf_op jit(solution)/shard_map/stack | solution.py:132
  2.4 6.1 %fusion.101 = (f32[64,32,128]{2,1,0:T(8,128)S(1)}, f32[64,8,32,128]{3,2,1,0:T(8,128)}) fusion(f32[8,32]{1,0:T(8,128)S(1)} %get-tuple-element.35, bf16[64,8,32,128]{3,2,1,0:T(8,128)(2,1)} %param.11, f32[64]{0:T(128)} %param.13, f32[8,32,128]{2,1,0:T(8,128)S(1)} %get-tuple-element.33), kind=kLoop, calls=%fused_computation.193 | loop fusion | flops 12320768 | bytes 13763840 | tf_op jit(solution)/shard_map/reduce_sum | solution.py:146
  8.5 0.0 copy-start
  8.5 0.1 slice_select_fusion
  8.6 1.3 %collective-permute-start = (f32[32,32,128]{2,1,0:T(8,128)S(1)}, f32[32,32,128]{2,1,0:T(8,128)S(1)}, u32[]{:S(2)}, u32[]{:S(2)}) collective-permute-start(f32[32,32,128]{2,1,0:T(8,128)S(1)} %slice_select_fusion), channel_id=1, source_target_pairs={{0,4},{4,0},{8,12},{12,8},{16,20},{20,16},{24,28},{28,24},{1,5},{5... | collective-permute-start | bytes 1572872 | tf_op jit(solution)/shard_map/ppermute | solution.py:76
  9.9 0.0 copy-done.6
  10.0 1.9 %collective-permute-start.4 = (f32[2,1,32,128]{3,2,1,0:T(8,128)S(1)}, f32[2,1,32,128]{3,2,1,0:T(8,128)S(1)}, u32[]{:S(2)}, u32[]{:S(2)}) collective-permute-start(f32[2,1,32,128]{3,2,1,0:T(8,128)S(1)} %get-tuple-element.29), channel_id=1, source_target_pairs={{4,0},{8,4},{12,8},{16,12},{20,16},{24,20},{28,24},{5,1},{9,5},{13... | collective-permute-start | bytes 98312 | tf_op jit(solution)/shard_map/ppermute | solution.py:33
  11.9 3.4 %collective-permute-start.1 = (f32[2,1,32,128]{3,2,1,0:T(8,128)S(1)}, f32[2,1,32,128]{3,2,1,0:T(8,128)S(1)}, u32[]{:S(2)}, u32[]{:S(2)}) collective-permute-start(f32[2,1,32,128]{3,2,1,0:T(8,128)S(1)} %get-tuple-element.28), channel_id=1, source_target_pairs={{0,4},{4,8},{8,12},{12,16},{16,20},{20,24},{24,28},{1,5},{5,9},{9,... | collective-permute-start | bytes 98312 | tf_op jit(solution)/shard_map/ppermute | solution.py:33
  15.3 3.4 %collective-permute-start.3 = (f32[2,8,1,128]{3,2,1,0:T(1,128)S(1)}, f32[2,8,1,128]{3,2,1,0:T(1,128)S(1)}, u32[]{:S(2)}, u32[]{:S(2)}) collective-permute-start(f32[2,8,1,128]{3,2,1,0:T(1,128)S(1)} %get-tuple-element.31), channel_id=1, source_target_pairs={{1,0},{2,1},{3,2},{5,4},{6,5},{7,6},{9,8},{10,9},{11,10},{13,12},{... | collective-permute-start | bytes 24584 | tf_op jit(solution)/shard_map/ppermute | solution.py:33
  18.7 3.0 %collective-permute-start.2 = (f32[2,8,1,128]{3,2,1,0:T(1,128)S(1)}, f32[2,8,1,128]{3,2,1,0:T(1,128)S(1)}, u32[]{:S(2)}, u32[]{:S(2)}) collective-permute-start(f32[2,8,1,128]{3,2,1,0:T(1,128)S(1)} %get-tuple-element.30), channel_id=1, source_target_pairs={{0,1},{1,2},{2,3},{4,5},{5,6},{6,7},{8,9},{9,10},{10,11},{12,13},{... | collective-permute-start | bytes 24584 | tf_op jit(solution)/shard_map/ppermute | solution.py:33
  21.7 0.0 collective-permute-done.3
  21.7 0.8 collective-permute-done.2
  22.5 0.4 collective-permute-done.4
  22.9 0.0 collective-permute-done.1
  22.9 0.0 copy-start.8
  22.9 0.3 pad.11
  23.2 0.2 copy-done.8
  23.4 0.0 collective-permute-done
  23.4 0.0 copy-start.2
  23.4 0.2 fusion.78
  23.6 3.2 %collective-permute-start.5 = (f32[32,32,128]{2,1,0:T(8,128)S(1)}, f32[32,32,128]{2,1,0:T(8,128)S(1)}, u32[]{:S(2)}, u32[]{:S(2)}) collective-permute-start(f32[32,32,128]{2,1,0:T(8,128)S(1)} %fusion.78), channel_id=1, source_target_pairs={{0,8},{4,12},{8,16},{12,20},{16,24},{20,28},{1,9},{5,13},{9,17},{1... | collective-permute-start | bytes 1572872 | tf_op jit(solution)/shard_map/ppermute | solution.py:33
  26.8 10.6 %collective-permute-done.5 = f32[32,32,128]{2,1,0:T(8,128)S(1)} collective-permute-done((f32[32,32,128]{2,1,0:T(8,128)S(1)}, f32[32,32,128]{2,1,0:T(8,128)S(1)}, u32[]{:S(2)}, u32[]{:S(2)}) %collective-permute-start.5) | collective-permute-done | bytes 524320 | tf_op jit(solution)/shard_map/ppermute | solution.py:33
  37.4 1.0 add.166
  38.4 5.0 %collective-permute-start.6 = (f32[32,32,128]{2,1,0:T(8,128)}, f32[32,32,128]{2,1,0:T(8,128)}, u32[]{:S(2)}, u32[]{:S(2)}) collective-permute-start(f32[32,32,128]{2,1,0:T(8,128)} %add.166), channel_id=1, source_target_pairs={{0,16},{4,20},{8,24},{12,28},{1,17},{5,21},{9,25},{13,29},{2,18},{... | collective-permute-start | bytes 1572872 | tf_op jit(solution)/shard_map/ppermute | solution.py:33
  43.4 0.0 copy-done
  43.4 0.0 copy-done.2
  43.4 0.0 copy-done.3
  43.4 4.2 %fusion = f32[64,7,32,128]{3,2,1,0:T(8,128)S(1)} fusion(f32[64,8,32,128]{3,2,1,0:T(8,128)} %get-tuple-element.16), kind=kOutput, calls=%fused_computation.5 | output fusion | flops 11010048 | bytes 14680064 | tf_op jit(solution)/shard_map/jit(cumsum)/reduce_window_sum | solution.py:148
  47.6 0.0 copy-start.1
  47.6 0.0 copy-start.5
  47.6 0.0 copy-start.10
  47.6 18.0 %collective-permute-done.6 = f32[32,32,128]{2,1,0:T(8,128)} collective-permute-done((f32[32,32,128]{2,1,0:T(8,128)}, f32[32,32,128]{2,1,0:T(8,128)}, u32[]{:S(2)}, u32[]{:S(2)}) %collective-permute-start.6) | collective-permute-done | bytes 524320 | tf_op jit(solution)/shard_map/ppermute | solution.py:33
  65.6 1.5 %fusion.102 = (f32[32,32,128]{2,1,0:T(8,128)S(1)}, f32[32,32,128]{2,1,0:T(8,128)S(1)}) fusion(f32[32,32,128]{2,1,0:T(8,128)} %copy-done.2, f32[32,32,128]{2,1,0:T(8,128)} %copy-done.3, f32[32,32,128]{2,1,0:T(8,128)} %collective-permute-done.6), kind=kLoop, calls=%fused_computation.194 | loop fusion | flops 262144 | bytes 2621440 | tf_op jit(solution)/shard_map/add | solution.py:81
  67.1 1.4 %add_select_fusion = f32[32,32,128]{2,1,0:T(8,128)S(1)} fusion(f32[32,32,128]{2,1,0:T(8,128)S(1)} %get-tuple-element.13, pred[]{:T(512)S(6)} %eq.5, f32[64,32,128]{2,1,0:T(8,128)} %copy-done), kind=kLoop, calls=%fused_computation.36 | loop fusion | flops 393216 | bytes 2097153 | tf_op jit(solution)/shard_map/jit(_where)/select_n | solution.py:79
  68.5 0.1 collective-permute-start.7
  68.6 0.0 copy-done.7
  68.6 0.4 power_multiply_fusion.2
  69.0 0.9 fusion.44
  69.9 11.6 %collective-permute-done.7 = f32[32,32,128]{2,1,0:T(8,128)S(1)} collective-permute-done((f32[32,32,128]{2,1,0:T(8,128)S(1)}, f32[32,32,128]{2,1,0:T(8,128)S(1)}, u32[]{:S(2)}, u32[]{:S(2)}) %collective-permute-start.7) | collective-permute-done | bytes 524320 | tf_op jit(solution)/shard_map/ppermute | solution.py:79
  81.6 0.2 maximum_select_fusion
  81.7 0.0 copy-done.1
  81.7 0.0 copy-done.5
  81.7 0.0 copy-done.10
  81.8 0.0 copy-start.4
  81.8 0.0 copy-start.9
  81.8 6.8 %multiply_reduce_fusion = (f32[8,32,128]{2,1,0:T(8,128)S(1)}, f32[8,32,128]{2,1,0:T(8,128)S(1)}, bf16[64,8,32,128]{3,2,1,0:T(8,128)(2,1)}) fusion(f32[64,7,32,128]{3,2,1,0:T(8,128)S(1)} %fusion, f32[64,32,128]{2,1,0:T(8,128)S(1)} %maximum_select_fusion, f32[64,32,128]{2,1,0:T(8,128)S(1)} %copy-done.5, f32[8,32]{1,0:T(8,128)S(1)} %get-tuple-element.35, ...), kind=kLoop, calls=%fused_computation | loop fusion | flops 31391744 | bytes 18220288 | tf_op jit(solution)/shard_map/reduce_sum | solution.py:161
  88.6 0.0 copy-done.4
  88.6 0.1 fusion.100
  88.8 0.1 fusion.94
  88.9 1.9 %collective-permute-start.11 = (f32[2,1,32,128]{3,2,1,0:T(8,128)S(1)}, f32[2,1,32,128]{3,2,1,0:T(8,128)S(1)}, u32[]{:S(2)}, u32[]{:S(2)}) collective-permute-start(f32[2,1,32,128]{3,2,1,0:T(8,128)S(1)} %get-tuple-element.25), channel_id=1, source_target_pairs={{4,0},{8,4},{12,8},{16,12},{20,16},{24,20},{28,24},{5,1},{9,5},{13... | collective-permute-start | bytes 98312 | tf_op jit(solution)/shard_map/ppermute | solution.py:33
  90.8 3.4 %collective-permute-start.8 = (f32[2,1,32,128]{3,2,1,0:T(8,128)S(1)}, f32[2,1,32,128]{3,2,1,0:T(8,128)S(1)}, u32[]{:S(2)}, u32[]{:S(2)}) collective-permute-start(f32[2,1,32,128]{3,2,1,0:T(8,128)S(1)} %get-tuple-element.24), channel_id=1, source_target_pairs={{0,4},{4,8},{8,12},{12,16},{16,20},{20,24},{24,28},{1,5},{5,9},{9,... | collective-permute-start | bytes 98312 | tf_op jit(solution)/shard_map/ppermute | solution.py:33
  94.2 3.8 %collective-permute-start.10 = (f32[2,8,1,128]{3,2,1,0:T(1,128)S(1)}, f32[2,8,1,128]{3,2,1,0:T(1,128)S(1)}, u32[]{:S(2)}, u32[]{:S(2)}) collective-permute-start(f32[2,8,1,128]{3,2,1,0:T(1,128)S(1)} %get-tuple-element.27), channel_id=1, source_target_pairs={{1,0},{2,1},{3,2},{5,4},{6,5},{7,6},{9,8},{10,9},{11,10},{13,12},{... | collective-permute-start | bytes 24584 | tf_op jit(solution)/shard_map/ppermute | solution.py:33
  98.1 3.0 %collective-permute-start.9 = (f32[2,8,1,128]{3,2,1,0:T(1,128)S(1)}, f32[2,8,1,128]{3,2,1,0:T(1,128)S(1)}, u32[]{:S(2)}, u32[]{:S(2)}) collective-permute-start(f32[2,8,1,128]{3,2,1,0:T(1,128)S(1)} %get-tuple-element.26), channel_id=1, source_target_pairs={{0,1},{1,2},{2,3},{4,5},{5,6},{6,7},{8,9},{9,10},{10,11},{12,13},{... | collective-permute-start | bytes 24584 | tf_op jit(solution)/shard_map/ppermute | solution.py:33
  101.1 0.0 collective-permute-done.10
  101.1 0.8 collective-permute-done.9
  101.8 0.0 collective-permute-done.11
  101.9 0.0 collective-permute-done.8
  101.9 0.0 copy-done.9
  101.9 0.1 fusion.6
  101.9 0.5 power_multiply_fusion
  102.5 0.7 fusion.12
  103.1 1.0 fusion.83
  (10 shorter events, 0.1 us)
Async XLA Ops:
  0.6 9.3 %copy-start.6 = (f32[8,32,128]{2,1,0:T(8,128)S(1)}, f32[8,32,128]{2,1,0:T(8,128)}, u32[]{:S(2)}) copy-start(f32[8,32,128]{2,1,0:T(8,128)} %param.8) | copy-start | bytes 393220
  8.5 34.9 %copy-start = (f32[64,32,128]{2,1,0:T(8,128)}, f32[64,32,128]{2,1,0:T(8,128)S(1)}, u32[]{:S(2)}) copy-start(f32[64,32,128]{2,1,0:T(8,128)S(1)} %get-tuple-element.15) | copy-start | bytes 3145732
  8.6 14.8 %collective-permute-start = (f32[32,32,128]{2,1,0:T(8,128)S(1)}, f32[32,32,128]{2,1,0:T(8,128)S(1)}, u32[]{:S(2)}, u32[]{:S(2)}) collective-permute-start(f32[32,32,128]{2,1,0:T(8,128)S(1)} %slice_select_fusion), channel_id=1, source_target_pairs={{0,4},{4,0},{8,12},{12,8},{16,20},{20,16},{24,28},{28,24},{1,5},{5... | collective-permute-start | bytes 1572872 | tf_op jit(solution)/shard_map/ppermute | solution.py:76
  10.0 12.9 %collective-permute-start.4 = (f32[2,1,32,128]{3,2,1,0:T(8,128)S(1)}, f32[2,1,32,128]{3,2,1,0:T(8,128)S(1)}, u32[]{:S(2)}, u32[]{:S(2)}) collective-permute-start(f32[2,1,32,128]{3,2,1,0:T(8,128)S(1)} %get-tuple-element.29), channel_id=1, source_target_pairs={{4,0},{8,4},{12,8},{16,12},{20,16},{24,20},{28,24},{5,1},{9,5},{13... | collective-permute-start | bytes 98312 | tf_op jit(solution)/shard_map/ppermute | solution.py:33
  11.9 11.0 %collective-permute-start.1 = (f32[2,1,32,128]{3,2,1,0:T(8,128)S(1)}, f32[2,1,32,128]{3,2,1,0:T(8,128)S(1)}, u32[]{:S(2)}, u32[]{:S(2)}) collective-permute-start(f32[2,1,32,128]{3,2,1,0:T(8,128)S(1)} %get-tuple-element.28), channel_id=1, source_target_pairs={{0,4},{4,8},{8,12},{12,16},{16,20},{20,24},{24,28},{1,5},{5,9},{9,... | collective-permute-start | bytes 98312 | tf_op jit(solution)/shard_map/ppermute | solution.py:33
  15.3 6.5 %collective-permute-start.3 = (f32[2,8,1,128]{3,2,1,0:T(1,128)S(1)}, f32[2,8,1,128]{3,2,1,0:T(1,128)S(1)}, u32[]{:S(2)}, u32[]{:S(2)}) collective-permute-start(f32[2,8,1,128]{3,2,1,0:T(1,128)S(1)} %get-tuple-element.31), channel_id=1, source_target_pairs={{1,0},{2,1},{3,2},{5,4},{6,5},{7,6},{9,8},{10,9},{11,10},{13,12},{... | collective-permute-start | bytes 24584 | tf_op jit(solution)/shard_map/ppermute | solution.py:33
  18.7 3.8 %collective-permute-start.2 = (f32[2,8,1,128]{3,2,1,0:T(1,128)S(1)}, f32[2,8,1,128]{3,2,1,0:T(1,128)S(1)}, u32[]{:S(2)}, u32[]{:S(2)}) collective-permute-start(f32[2,8,1,128]{3,2,1,0:T(1,128)S(1)} %get-tuple-element.30), channel_id=1, source_target_pairs={{0,1},{1,2},{2,3},{4,5},{5,6},{6,7},{8,9},{9,10},{10,11},{12,13},{... | collective-permute-start | bytes 24584 | tf_op jit(solution)/shard_map/ppermute | solution.py:33
  22.9 0.6 copy-start.8
  23.4 19.9 %copy-start.2 = (f32[32,32,128]{2,1,0:T(8,128)}, f32[32,32,128]{2,1,0:T(8,128)S(1)}, u32[]{:S(2)}) copy-start(f32[32,32,128]{2,1,0:T(8,128)S(1)} %collective-permute-done) | copy-start | bytes 1572868
  23.6 13.8 %collective-permute-start.5 = (f32[32,32,128]{2,1,0:T(8,128)S(1)}, f32[32,32,128]{2,1,0:T(8,128)S(1)}, u32[]{:S(2)}, u32[]{:S(2)}) collective-permute-start(f32[32,32,128]{2,1,0:T(8,128)S(1)} %fusion.78), channel_id=1, source_target_pairs={{0,8},{4,12},{8,16},{12,20},{16,24},{20,28},{1,9},{5,13},{9,17},{1... | collective-permute-start | bytes 1572872 | tf_op jit(solution)/shard_map/ppermute | solution.py:33
  37.4 6.0 %copy-start.3 = (f32[32,32,128]{2,1,0:T(8,128)}, f32[32,32,128]{2,1,0:T(8,128)S(1)}, u32[]{:S(2)}) copy-start(f32[32,32,128]{2,1,0:T(8,128)S(1)} %collective-permute-done.5) | copy-start | bytes 1572868
  38.4 27.3 %collective-permute-start.6 = (f32[32,32,128]{2,1,0:T(8,128)}, f32[32,32,128]{2,1,0:T(8,128)}, u32[]{:S(2)}, u32[]{:S(2)}) collective-permute-start(f32[32,32,128]{2,1,0:T(8,128)} %add.166), channel_id=1, source_target_pairs={{0,16},{4,20},{8,24},{12,28},{1,17},{5,21},{9,25},{13,29},{2,18},{... | collective-permute-start | bytes 1572872 | tf_op jit(solution)/shard_map/ppermute | solution.py:33
  43.4 25.2 %copy-start.7 = (f32[32,128]{1,0:T(8,128)S(1)}, f32[32,128]{1,0:T(8,128)}, u32[]{:S(2)}) copy-start(f32[32,128]{1,0:T(8,128)} %param.14) | copy-start | bytes 49156
  47.6 34.2 %copy-start.1 = (bf16[64,8,32,128]{3,2,1,0:T(8,128)(2,1)S(1)}, bf16[64,8,32,128]{3,2,1,0:T(8,128)(2,1)}, u32[]{:S(2)}) copy-start(bf16[64,8,32,128]{3,2,1,0:T(8,128)(2,1)} %param.11) | copy-start | bytes 12582916
  47.6 34.2 %copy-start.5 = (f32[64,32,128]{2,1,0:T(8,128)S(1)}, f32[64,32,128]{2,1,0:T(8,128)}, u32[]{:S(2)}) copy-start(f32[64,32,128]{2,1,0:T(8,128)} %param.12) | copy-start | bytes 3145732
  47.6 34.2 %copy-start.10 = (f32[64]{0:T(128)S(1)}, f32[64]{0:T(128)}, u32[]{:S(2)}) copy-start(f32[64]{0:T(128)} %param.13) | copy-start | bytes 772
  68.5 13.1 %collective-permute-start.7 = (f32[32,32,128]{2,1,0:T(8,128)S(1)}, f32[32,32,128]{2,1,0:T(8,128)S(1)}, u32[]{:S(2)}, u32[]{:S(2)}) collective-permute-start(f32[32,32,128]{2,1,0:T(8,128)S(1)} %add_select_fusion), channel_id=1, source_target_pairs={{0,4},{4,0},{8,12},{12,8},{16,20},{20,16},{24,28},{28,24},{1,5},{5... | collective-permute-start | bytes 1572872 | tf_op jit(solution)/shard_map/ppermute | solution.py:79
  81.8 6.8 %copy-start.4 = (f32[8,32,128]{2,1,0:T(8,128)S(1)}, f32[8,32,128]{2,1,0:T(8,128)}, u32[]{:S(2)}) copy-start(f32[8,32,128]{2,1,0:T(8,128)} %param.9) | copy-start | bytes 393220
  81.8 20.1 %copy-start.9 = (f32[2,1,1,128]{3,2,1,0:T(1,128)S(1)}, f32[2,1,1,128]{3,2,1,0:T(1,128)}, u32[]{:S(2)}) copy-start(f32[2,1,1,128]{3,2,1,0:T(1,128)} %copy-done.8) | copy-start | bytes 3076
  88.9 12.9 %collective-permute-start.11 = (f32[2,1,32,128]{3,2,1,0:T(8,128)S(1)}, f32[2,1,32,128]{3,2,1,0:T(8,128)S(1)}, u32[]{:S(2)}, u32[]{:S(2)}) collective-permute-start(f32[2,1,32,128]{3,2,1,0:T(8,128)S(1)} %get-tuple-element.25), channel_id=1, source_target_pairs={{4,0},{8,4},{12,8},{16,12},{20,16},{24,20},{28,24},{5,1},{9,5},{13... | collective-permute-start | bytes 98312 | tf_op jit(solution)/shard_map/ppermute | solution.py:33
  90.8 11.0 %collective-permute-start.8 = (f32[2,1,32,128]{3,2,1,0:T(8,128)S(1)}, f32[2,1,32,128]{3,2,1,0:T(8,128)S(1)}, u32[]{:S(2)}, u32[]{:S(2)}) collective-permute-start(f32[2,1,32,128]{3,2,1,0:T(8,128)S(1)} %get-tuple-element.24), channel_id=1, source_target_pairs={{0,4},{4,8},{8,12},{12,16},{16,20},{20,24},{24,28},{1,5},{5,9},{9,... | collective-permute-start | bytes 98312 | tf_op jit(solution)/shard_map/ppermute | solution.py:33
  94.2 6.8 %collective-permute-start.10 = (f32[2,8,1,128]{3,2,1,0:T(1,128)S(1)}, f32[2,8,1,128]{3,2,1,0:T(1,128)S(1)}, u32[]{:S(2)}, u32[]{:S(2)}) collective-permute-start(f32[2,8,1,128]{3,2,1,0:T(1,128)S(1)} %get-tuple-element.27), channel_id=1, source_target_pairs={{1,0},{2,1},{3,2},{5,4},{6,5},{7,6},{9,8},{10,9},{11,10},{13,12},{... | collective-permute-start | bytes 24584 | tf_op jit(solution)/shard_map/ppermute | solution.py:33
  98.1 3.8 %collective-permute-start.9 = (f32[2,8,1,128]{3,2,1,0:T(1,128)S(1)}, f32[2,8,1,128]{3,2,1,0:T(1,128)S(1)}, u32[]{:S(2)}, u32[]{:S(2)}) collective-permute-start(f32[2,8,1,128]{3,2,1,0:T(1,128)S(1)} %get-tuple-element.26), channel_id=1, source_target_pairs={{0,1},{1,2},{2,3},{4,5},{5,6},{6,7},{8,9},{9,10},{10,11},{12,13},{... | collective-permute-start | bytes 24584 | tf_op jit(solution)/shard_map/ppermute | solution.py:33

commit v5 on v4

--- a/solution.py
+++ b/solution.py
@@ -63,23 +63,28 @@
     return before
 
 
-def paired_scan(totals, axis, rider):
+def line_half(block, offset, half):
+    return lax.dynamic_slice_in_dim(block, offset, half, axis=0)
+
+
+def paired_column(depth_of, lines, axis, rider):
     count = lax.axis_size(axis)
-    half = totals.shape[0] // 2
-    if count % 2 or totals.shape[0] % 2 or count == 2:
-        return exclusive_scan(totals, axis), rider(None)
-    is_low = lax.axis_index(axis) % 2 == 0
-    first, second = totals[:half], totals[half:]
-    mine = jnp.where(is_low, first, second)
+    half = lines // 2
+    if count % 2 or lines % 2 or count == 2:
+        whole = exclusive_scan(jnp.sum(depth_of(0, lines), axis=1), axis)
+        return [(0, lines, whole)], rider(None)
+    parity = lax.axis_index(axis) % 2
+    is_low = parity == 0
+    own, other = parity * half, (1 - parity) * half
+    given = jnp.sum(depth_of(other, half), axis=1)
     swap = [(i, i ^ 1) for i in range(count)]
-    given = jnp.where(is_low, second, first)
     got = lax.ppermute(given, axis, swap)
     got, carried = lax.optimization_barrier((got, rider(given)))
+    mine = jnp.sum(depth_of(own, half), axis=1)
     before = exclusive_scan(mine + got, axis, stride=2)
     back = lax.ppermute(jnp.where(is_low, before + mine, before), axis, swap)
-    low_result = jnp.concatenate([before, back])
-    high_result = jnp.concatenate([back, before + got])
-    return jnp.where(is_low, low_result, high_result), carried
+    own_prefix = jnp.where(is_low, before, before + got)
+    return [(own, half, own_prefix), (other, half, back)], carried
 
 
 def window(source, step_beam, step_cross, step_depth):
@@ -139,26 +144,42 @@
         absorb_scale / total_rows * rubidium_number_amount * (1.0 - rubidium_polarization_old)
     )
     glass_term = glass_depth * glass_cells
-    weight = spectral_attenuation_section[:, None, None, None] / (
-        1.0 + earlier_spectral_power.astype(jnp.float32) / saturation
-    )
-    optical_depth = absorber[None] * weight + glass_term[None]
-    totals = jnp.sum(optical_depth, axis=1)
-    local_column = jnp.pad(
-        jnp.cumsum(optical_depth[:, : rows - 1], axis=1), ((0, 0), (1, 0), (0, 0), (0, 0))
-    )
+    lines = earlier_spectral_power.shape[0]
+
+    def depth_of(offset, count):
+        weight = line_half(spectral_attenuation_section, offset, count)[:, None, None, None] / (
+            1.0 + line_half(earlier_spectral_power, offset, count).astype(jnp.float32) / saturation
+        )
+        return absorber[None] * weight + glass_term[None], weight
+
     def first_border(after):
         fields = physical_quantities
         if after is not None:
             fields, _ = lax.optimization_barrier((fields, after))
         return bordered_fields(fields)
 
-    prefix, first_bordered = paired_scan(totals, "beam", first_border)
-    column = prefix[:, None] + local_column
-    radiance = entry_spectral_power[:, None] * jnp.exp(-column)
-    spectral_power = radiance.astype(jnp.bfloat16)
-    pumping = pump_scale * jnp.sum(weight * radiance, axis=0)
-    heating = jnp.sum(radiance * (1.0 - jnp.exp(-optical_depth)), axis=0)
+    pieces, first_bordered = paired_column(
+        lambda offset, count: depth_of(offset, count)[0], lines, "beam", first_border
+    )
+    spectral_power = jnp.zeros(earlier_spectral_power.shape, jnp.bfloat16)
+    pumping = None
+    for offset, count, earlier in pieces:
+        optical_depth, weight = depth_of(offset, count)
+        local_column = jnp.pad(
+            jnp.cumsum(optical_depth[:, : rows - 1], axis=1), ((0, 0), (1, 0), (0, 0), (0, 0))
+        )
+        column = earlier[:, None] + local_column
+        radiance = line_half(entry_spectral_power, offset, count)[:, None] * jnp.exp(-column)
+        spectral_power = lax.dynamic_update_slice_in_dim(
+            spectral_power, radiance.astype(jnp.bfloat16), offset, axis=0
+        )
+        part_pumping = jnp.sum(weight * radiance, axis=0)
+        part_heating = jnp.sum(radiance * (1.0 - jnp.exp(-optical_depth)), axis=0)
+        if pumping is None:
+            pumping, heating = part_pumping, part_heating
+        else:
+            pumping, heating = pumping + part_pumping, heating + part_heating
+    pumping = pump_scale * pumping
     spin_ratio = pumping / (pumping + spin_decay * (1.0 + rubidium_number_amount))
     rubidium_polarization_new = fluid_occupied_sites * spin_ratio
     drift_speed = flow_scale * flow_rate_forward

time: 106 us -> 107 us (level)
  local copies, waits for them, and re-layouts: 0.58 us -> 2.23 us
    dynamic_update_slice x0 -> x2, other arithmetic: none -> 2.35 us  [local(): lax.dynamic_update_slice_in_dim(spectral_power, radiance.astype(jnp.bfloa...]
    reduce_sum x2, other arithmetic: 12.9 us -> 10.7 us  [the longest x1 6.65 us: local(): part_heating = jnp.sum(radiance * (1.0 - jnp.exp(-optical_depth)), axis=0)]
    ppermute x10, waiting for transfers between devices: 30.5 us -> 32.4 us  [shifted(): return lax.ppermute(block, axis, pairs)]
    ppermute x2, waiting for transfers between devices: 11.6 us -> 9.9 us  [the longest x1 9.9 us: paired_column(): back = lax.ppermute(jnp.where(is_low, before + mine, before), axis, swap)]
    add x2 -> x1, other arithmetic: 1.67 us -> 0.08 us  [paired_column(): before = exclusive_scan(mine + got, axis, stride=2)]
    another operation x1 -> x2, other arithmetic: 4.16 us -> 4.72 us  [local(): jnp.cumsum(optical_depth[:, :rows - 1], axis=1)]
  transfers between devices with their start and end apart: 12 -> 12, of which waited for: 6 -> 5; matrix products, arithmetic and copies ran while one was open for 6% -> 9% of each run, Pallas kernels for 0% -> 0%
where the time goes in v5:
time: 107 us; the launch traced here: 105 us
  waiting for transfers between devices  42.3 us (40%)
  starting transfers between devices  33.2 us (31%)
  other arithmetic  26.5 us (25%)
  local copies, waits for them, and re-layouts  2.23 us (2%)
    ppermute x10, waiting for transfers between devices, shifted(): return lax.ppermute(block, axis, pairs)  32.4 us
    ppermute x10, starting transfers between devices, shifted(): return lax.ppermute(block, axis, pairs)  31.9 us
    ppermute x1, waiting for transfers between devices, paired_column(): back = lax.ppermute(jnp.where(is_low, before + mine, before), axis, swap)  9.9 us
    reduce_sum x1, other arithmetic, local(): part_heating = jnp.sum(radiance * (1.0 - jnp.exp(-optical_depth)), axis=0)  6.65 us
    another operation x2, other arithmetic, local(): jnp.cumsum(optical_depth[:, :rows - 1], axis=1)  4.72 us
    reduce_sum x1, other arithmetic, paired_column(): given = jnp.sum(depth_of(other, half), axis=1)  4.01 us
    dynamic_update_slice x2, other arithmetic, local(): lax.dynamic_update_slice_in_dim(spectral_power, radiance.astype(jnp.bfloa...  2.35 us
  transfers between devices with their start and end apart: 12, of which 5 were waited for; matrix products, arithmetic and copies ran while one was open for 9% of the time, Pallas kernels for 0%

profile of v5, /device:TPU:9, one launch (start us, length us, event | category | flops | bytes accessed | tf_op | source)
XLA Modules:
  0.0 105.3 jit_solution(17493784591186759958)
XLA Ops:
  0.6 0.7 convert_subtract_fusion
  1.3 0.8 fusion.109
  2.1 1.1 %add_bitcast_fusion = (f32[1,8,32,128]{3,2,1,0:T(8,128)S(1)}, f32[8,32,128]{2,1,0:T(8,128)S(1)}) fusion(f32[8,32,128]{2,1,0:T(8,128)} %param.9, f32[8,32,128]{2,1,0:T(8,128)} %param.10, f32[8,32]{1,0:T(8,128)S(1)} %get-tuple-element.44), kind=kLoop, calls=%fused_computation.189 | loop fusion | flops 262144 | bytes 525312 | tf_op jit(solution)/shard_map/stack | solution.py:137
  3.2 0.0 copy-start.9
  3.2 4.0 %fusion.106 = (f32[32,32,128]{2,1,0:T(8,128)S(1)}, f32[32,8,32,128]{3,2,1,0:T(8,128)S(1)}, f32[32,32,128]{2,1,0:T(8,128)S(1)}, f32[32,8,32,128]{3,2,1,0:T(8,128)S(1)}) fusion(f32[8,32]{1,0:T(8,128)S(1)} %get-tuple-element.45, bf16[64,8,32,128]{3,2,1,0:T(8,128)(2,1)} %param.11, s32[]{:T(128)S(6)} %select_n.38, f32[32]{0:T(128)S(1)} %get-tuple-element.46, ...), kind=kLoop, calls=%fused_computation.204 | loop fusion | flops 12320768 | bytes 13763848 | tf_op jit(solution)/shard_map/reduce_sum | solution.py:79
  7.2 0.0 copy-start
  7.3 0.0 copy-start.2
  7.3 1.3 %collective-permute-start = (f32[32,32,128]{2,1,0:T(8,128)S(1)}, f32[32,32,128]{2,1,0:T(8,128)S(1)}, u32[]{:S(2)}, u32[]{:S(2)}) collective-permute-start(f32[32,32,128]{2,1,0:T(8,128)S(1)} %get-tuple-element.18), channel_id=1, source_target_pairs={{0,4},{4,0},{8,12},{12,8},{16,20},{20,16},{24,28},{28,24},{1,5},{5... | collective-permute-start | bytes 1572872 | tf_op jit(solution)/shard_map/ppermute | solution.py:81
  8.6 0.0 copy-done.9
  8.6 2.1 %collective-permute-start.1 = (f32[2,1,32,128]{3,2,1,0:T(8,128)S(1)}, f32[2,1,32,128]{3,2,1,0:T(8,128)S(1)}, u32[]{:S(2)}, u32[]{:S(2)}) collective-permute-start(f32[2,1,32,128]{3,2,1,0:T(8,128)S(1)} %get-tuple-element.38), channel_id=1, source_target_pairs={{0,4},{4,8},{8,12},{12,16},{16,20},{20,24},{24,28},{1,5},{5,9},{9,... | collective-permute-start | bytes 98312 | tf_op jit(solution)/shard_map/ppermute | solution.py:33
  10.8 4.0 %collective-permute-start.4 = (f32[2,1,32,128]{3,2,1,0:T(8,128)S(1)}, f32[2,1,32,128]{3,2,1,0:T(8,128)S(1)}, u32[]{:S(2)}, u32[]{:S(2)}) collective-permute-start(f32[2,1,32,128]{3,2,1,0:T(8,128)S(1)} %get-tuple-element.39), channel_id=1, source_target_pairs={{4,0},{8,4},{12,8},{16,12},{20,16},{24,20},{28,24},{5,1},{9,5},{13... | collective-permute-start | bytes 98312 | tf_op jit(solution)/shard_map/ppermute | solution.py:33
  14.8 4.5 %collective-permute-start.2 = (f32[2,8,1,128]{3,2,1,0:T(1,128)S(1)}, f32[2,8,1,128]{3,2,1,0:T(1,128)S(1)}, u32[]{:S(2)}, u32[]{:S(2)}) collective-permute-start(f32[2,8,1,128]{3,2,1,0:T(1,128)S(1)} %get-tuple-element.40), channel_id=1, source_target_pairs={{0,1},{1,2},{2,3},{4,5},{5,6},{6,7},{8,9},{9,10},{10,11},{12,13},{... | collective-permute-start | bytes 24584 | tf_op jit(solution)/shard_map/ppermute | solution.py:33
  19.4 1.9 %collective-permute-start.3 = (f32[2,8,1,128]{3,2,1,0:T(1,128)S(1)}, f32[2,8,1,128]{3,2,1,0:T(1,128)S(1)}, u32[]{:S(2)}, u32[]{:S(2)}) collective-permute-start(f32[2,8,1,128]{3,2,1,0:T(1,128)S(1)} %get-tuple-element.41), channel_id=1, source_target_pairs={{1,0},{2,1},{3,2},{5,4},{6,5},{7,6},{9,8},{10,9},{11,10},{13,12},{... | collective-permute-start | bytes 24584 | tf_op jit(solution)/shard_map/ppermute | solution.py:33
  21.3 0.0 collective-permute-done.2
  21.3 3.0 %collective-permute-done.3 = f32[2,8,1,128]{3,2,1,0:T(1,128)S(1)} collective-permute-done((f32[2,8,1,128]{3,2,1,0:T(1,128)S(1)}, f32[2,8,1,128]{3,2,1,0:T(1,128)S(1)}, u32[]{:S(2)}, u32[]{:S(2)}) %collective-permute-start.3) | collective-permute-done | bytes 8224 | tf_op jit(solution)/shard_map/ppermute | solution.py:33
  24.3 0.0 collective-permute-done.1
  24.3 0.0 collective-permute-done.4
  24.3 0.1 fusion.9
  24.4 0.3 pad.14
  24.7 0.0 collective-permute-done
  24.7 0.1 add.228
  24.8 3.2 %collective-permute-start.5 = (f32[32,32,128]{2,1,0:T(8,128)S(1)}, f32[32,32,128]{2,1,0:T(8,128)S(1)}, u32[]{:S(2)}, u32[]{:S(2)}) collective-permute-start(f32[32,32,128]{2,1,0:T(8,128)S(1)} %add.228), channel_id=1, source_target_pairs={{0,8},{4,12},{8,16},{12,20},{16,24},{20,28},{1,9},{5,13},{9,17},{1... | collective-permute-start | bytes 1572872 | tf_op jit(solution)/shard_map/ppermute | solution.py:33
  28.0 2.3 %fusion = f32[32,7,32,128]{3,2,1,0:T(8,128)} fusion(f32[32,8,32,128]{3,2,1,0:T(8,128)S(1)} %get-tuple-element.19), kind=kOutput, calls=%fused_computation.10 | output fusion | flops 5505024 | bytes 7340032 | tf_op jit(solution)/shard_map/jit(cumsum)/reduce_window_sum | solution.py:169
  30.3 0.0 copy-done
  30.3 0.0 copy-done.2
  30.3 2.4 %fusion.2 = f32[32,7,32,128]{3,2,1,0:T(8,128)} fusion(f32[32,8,32,128]{3,2,1,0:T(8,128)S(1)} %get-tuple-element.21), kind=kOutput, calls=%fused_computation.12 | output fusion | flops 5505024 | bytes 7340032 | tf_op jit(solution)/shard_map/jit(cumsum)/reduce_window_sum | solution.py:169
  32.7 6.8 %collective-permute-done.5 = f32[32,32,128]{2,1,0:T(8,128)S(1)} collective-permute-done((f32[32,32,128]{2,1,0:T(8,128)S(1)}, f32[32,32,128]{2,1,0:T(8,128)S(1)}, u32[]{:S(2)}, u32[]{:S(2)}) %collective-permute-start.5) | collective-permute-done | bytes 524320 | tf_op jit(solution)/shard_map/ppermute | solution.py:33
  39.5 0.9 add.229
  40.4 5.0 %collective-permute-start.6 = (f32[32,32,128]{2,1,0:T(8,128)}, f32[32,32,128]{2,1,0:T(8,128)}, u32[]{:S(2)}, u32[]{:S(2)}) collective-permute-start(f32[32,32,128]{2,1,0:T(8,128)} %add.229), channel_id=1, source_target_pairs={{0,16},{4,20},{8,24},{12,28},{1,17},{5,21},{9,25},{13,29},{2,18},{... | collective-permute-start | bytes 1572872 | tf_op jit(solution)/shard_map/ppermute | solution.py:33
  45.4 0.0 copy-done.8
  45.4 0.1 constant_dynamic-slice_fusion
  45.5 0.0 copy-done.10
  45.5 0.4 power_multiply_fusion.2
  45.9 21.8 %collective-permute-done.6 = f32[32,32,128]{2,1,0:T(8,128)} collective-permute-done((f32[32,32,128]{2,1,0:T(8,128)}, f32[32,32,128]{2,1,0:T(8,128)}, u32[]{:S(2)}, u32[]{:S(2)}) %collective-permute-start.6) | collective-permute-done | bytes 524320 | tf_op jit(solution)/shard_map/ppermute | solution.py:33
  67.7 1.4 %add_select_fusion = (f32[32,32,128]{2,1,0:T(8,128)S(1)}, f32[32,32,128]{2,1,0:T(8,128)S(1)}) fusion(f32[32,32,128]{2,1,0:T(8,128)S(1)} %get-tuple-element.20, pred[]{:T(512)S(6)} %eq.5, f32[32,32,128]{2,1,0:T(8,128)S(1)} %collective-permute-done.5, f32[32,32,128]{2,1,0:T(8,128)} %collective-permute-done.6, f32[32,32,128]{2,1,0:T(8,128)S(1)} %collective-permute-done), kind=kLoop, calls=%fused_computation.45 | loop fusion | flops 655360 | bytes 3145729 | tf_op jit(solution)/shard_map/jit(_where)/select_n | solution.py:85
  69.2 0.1 collective-permute-start.7
  69.2 0.0 copy-start.4
  69.3 0.9 fusion.49
  70.2 0.0 copy-start.3
  70.2 1.0 broadcast_in_dim.2
  71.2 0.0 copy-done.5
  71.2 0.0 copy-start.1
  71.2 1.2 %fusion.7 = bf16[64,8,32,128]{3,2,1,0:T(8,128)(2,1)S(1)} fusion(bf16[64,8,32,128]{3,2,1,0:T(8,128)(2,1)S(1)} %broadcast_in_dim.2, s32[]{:T(128)S(6)} %select_n.36, f32[32,7,32,128]{3,2,1,0:T(8,128)S(1)} %copy-done.5, f32[32,32,128]{2,1,0:T(8,128)S(1)} %get-tuple-element.29, f32[32,32,128]{2,1,0:T(8,128)S(1)} %get-tuple-element.27), kind=kLoop, calls=%fused_computation.17 | loop fusion | flops 4194304 | bytes 6815748 | tf_op jit(solution)/shard_map/dynamic_update_slice | solution.py:173
  72.4 9.9 %collective-permute-done.7 = f32[32,32,128]{2,1,0:T(8,128)S(1)} collective-permute-done((f32[32,32,128]{2,1,0:T(8,128)S(1)}, f32[32,32,128]{2,1,0:T(8,128)S(1)}, u32[]{:S(2)}, u32[]{:S(2)}) %collective-permute-start.7) | collective-permute-done | bytes 524320 | tf_op jit(solution)/shard_map/ppermute | solution.py:85
  82.3 0.0 copy-done.4
  82.3 0.0 copy-done.3
  82.3 0.0 copy-start.7
  82.3 6.6 %multiply_reduce_fusion = (f32[8,32,128]{2,1,0:T(8,128)S(1)}, f32[8,32,128]{2,1,0:T(8,128)S(1)}, f32[8,32,128]{2,1,0:T(8,128)S(1)}, f32[8,32,128]{2,1,0:T(8,128)S(1)}) fusion(f32[32,8,32,128]{3,2,1,0:T(8,128)S(1)} %copy-done.1, f32[32,7,32,128]{3,2,1,0:T(8,128)S(1)} %copy-done.4, f32[32,32,128]{2,1,0:T(8,128)S(1)} %collective-permute-done.7, ...), kind=kLoop, calls=%fused_computation | loop fusion | flops 25034752 | bytes 22544648 | tf_op jit(solution)/shard_map/reduce_sum | solution.py:177
  89.0 0.8 broadcast_multiply_fusion
  89.8 0.1 fusion.104
  89.9 0.1 fusion.98
  90.1 3.2 %collective-permute-start.10 = (f32[2,8,1,128]{3,2,1,0:T(1,128)S(1)}, f32[2,8,1,128]{3,2,1,0:T(1,128)S(1)}, u32[]{:S(2)}, u32[]{:S(2)}) collective-permute-start(f32[2,8,1,128]{3,2,1,0:T(1,128)S(1)} %get-tuple-element.37), channel_id=1, source_target_pairs={{1,0},{2,1},{3,2},{5,4},{6,5},{7,6},{9,8},{10,9},{11,10},{13,12},{... | collective-permute-start | bytes 24584 | tf_op jit(solution)/shard_map/ppermute | solution.py:33
  93.3 2.4 %collective-permute-start.9 = (f32[2,8,1,128]{3,2,1,0:T(1,128)S(1)}, f32[2,8,1,128]{3,2,1,0:T(1,128)S(1)}, u32[]{:S(2)}, u32[]{:S(2)}) collective-permute-start(f32[2,8,1,128]{3,2,1,0:T(1,128)S(1)} %get-tuple-element.36), channel_id=1, source_target_pairs={{0,1},{1,2},{2,3},{4,5},{5,6},{6,7},{8,9},{9,10},{10,11},{12,13},{... | collective-permute-start | bytes 24584 | tf_op jit(solution)/shard_map/ppermute | solution.py:33
  95.7 1.9 %collective-permute-start.11 = (f32[2,1,32,128]{3,2,1,0:T(8,128)S(1)}, f32[2,1,32,128]{3,2,1,0:T(8,128)S(1)}, u32[]{:S(2)}, u32[]{:S(2)}) collective-permute-start(f32[2,1,32,128]{3,2,1,0:T(8,128)S(1)} %get-tuple-element.35), channel_id=1, source_target_pairs={{4,0},{8,4},{12,8},{16,12},{20,16},{24,20},{28,24},{5,1},{9,5},{13... | collective-permute-start | bytes 98312 | tf_op jit(solution)/shard_map/ppermute | solution.py:33
  97.6 3.5 %collective-permute-start.8 = (f32[2,1,32,128]{3,2,1,0:T(8,128)S(1)}, f32[2,1,32,128]{3,2,1,0:T(8,128)S(1)}, u32[]{:S(2)}, u32[]{:S(2)}) collective-permute-start(f32[2,1,32,128]{3,2,1,0:T(8,128)S(1)} %get-tuple-element.34), channel_id=1, source_target_pairs={{0,4},{4,8},{8,12},{12,16},{16,20},{20,24},{24,28},{1,5},{5,9},{9,... | collective-permute-start | bytes 98312 | tf_op jit(solution)/shard_map/ppermute | solution.py:33
  101.2 1.2 %fusion.6 = bf16[64,8,32,128]{3,2,1,0:T(8,128)(2,1)S(1)} fusion(bf16[64,8,32,128]{3,2,1,0:T(8,128)(2,1)S(1)} %fusion.7, s32[]{:T(128)S(6)} %select_n.38, f32[32,7,32,128]{3,2,1,0:T(8,128)S(1)} %copy-done.4, f32[32,32,128]{2,1,0:T(8,128)S(1)} %collective-permute-done.7, f32[32,32,128]{2,1,0:T(8,128)S(1)} %get-tuple-element.26), kind=kLoop, calls=%fused_computation.16 | loop fusion | flops 4194304 | bytes 6815748 | tf_op jit(solution)/shard_map/dynamic_update_slice | solution.py:173
  102.3 0.0 copy-start.6
  102.3 0.0 collective-permute-done.10
  102.4 0.0 collective-permute-done.9
  102.4 0.0 collective-permute-done.11
  102.4 0.8 collective-permute-done.8
  103.2 0.5 power_multiply_fusion
  103.8 0.7 fusion.17
  104.4 0.9 fusion.87
  (14 shorter events, 0.1 us)
Async XLA Ops:
  3.2 5.4 %copy-start.9 = (f32[8,32,128]{2,1,0:T(8,128)S(1)}, f32[8,32,128]{2,1,0:T(8,128)}, u32[]{:S(2)}) copy-start(f32[8,32,128]{2,1,0:T(8,128)} %param.8) | copy-start | bytes 393220
  7.2 23.0 %copy-start = (f32[32,8,32,128]{3,2,1,0:T(8,128)}, f32[32,8,32,128]{3,2,1,0:T(8,128)S(1)}, u32[]{:S(2)}) copy-start(f32[32,8,32,128]{3,2,1,0:T(8,128)S(1)} %get-tuple-element.19) | copy-start | bytes 12582916
  7.3 23.0 %copy-start.2 = (f32[32,8,32,128]{3,2,1,0:T(8,128)}, f32[32,8,32,128]{3,2,1,0:T(8,128)S(1)}, u32[]{:S(2)}) copy-start(f32[32,8,32,128]{3,2,1,0:T(8,128)S(1)} %get-tuple-element.21) | copy-start | bytes 12582916
  7.3 17.4 %collective-permute-start = (f32[32,32,128]{2,1,0:T(8,128)S(1)}, f32[32,32,128]{2,1,0:T(8,128)S(1)}, u32[]{:S(2)}, u32[]{:S(2)}) collective-permute-start(f32[32,32,128]{2,1,0:T(8,128)S(1)} %get-tuple-element.18), channel_id=1, source_target_pairs={{0,4},{4,0},{8,12},{12,8},{16,20},{20,16},{24,28},{28,24},{1,5},{5... | collective-permute-start | bytes 1572872 | tf_op jit(solution)/shard_map/ppermute | solution.py:81
  8.6 15.7 %collective-permute-start.1 = (f32[2,1,32,128]{3,2,1,0:T(8,128)S(1)}, f32[2,1,32,128]{3,2,1,0:T(8,128)S(1)}, u32[]{:S(2)}, u32[]{:S(2)}) collective-permute-start(f32[2,1,32,128]{3,2,1,0:T(8,128)S(1)} %get-tuple-element.38), channel_id=1, source_target_pairs={{0,4},{4,8},{8,12},{12,16},{16,20},{20,24},{24,28},{1,5},{5,9},{9,... | collective-permute-start | bytes 98312 | tf_op jit(solution)/shard_map/ppermute | solution.py:33
  10.8 13.6 %collective-permute-start.4 = (f32[2,1,32,128]{3,2,1,0:T(8,128)S(1)}, f32[2,1,32,128]{3,2,1,0:T(8,128)S(1)}, u32[]{:S(2)}, u32[]{:S(2)}) collective-permute-start(f32[2,1,32,128]{3,2,1,0:T(8,128)S(1)} %get-tuple-element.39), channel_id=1, source_target_pairs={{4,0},{8,4},{12,8},{16,12},{20,16},{24,20},{28,24},{5,1},{9,5},{13... | collective-permute-start | bytes 98312 | tf_op jit(solution)/shard_map/ppermute | solution.py:33
  14.8 6.5 %collective-permute-start.2 = (f32[2,8,1,128]{3,2,1,0:T(1,128)S(1)}, f32[2,8,1,128]{3,2,1,0:T(1,128)S(1)}, u32[]{:S(2)}, u32[]{:S(2)}) collective-permute-start(f32[2,8,1,128]{3,2,1,0:T(1,128)S(1)} %get-tuple-element.40), channel_id=1, source_target_pairs={{0,1},{1,2},{2,3},{4,5},{5,6},{6,7},{8,9},{9,10},{10,11},{12,13},{... | collective-permute-start | bytes 24584 | tf_op jit(solution)/shard_map/ppermute | solution.py:33
  19.4 5.0 %collective-permute-start.3 = (f32[2,8,1,128]{3,2,1,0:T(1,128)S(1)}, f32[2,8,1,128]{3,2,1,0:T(1,128)S(1)}, u32[]{:S(2)}, u32[]{:S(2)}) collective-permute-start(f32[2,8,1,128]{3,2,1,0:T(1,128)S(1)} %get-tuple-element.41), channel_id=1, source_target_pairs={{1,0},{2,1},{3,2},{5,4},{6,5},{7,6},{9,8},{10,9},{11,10},{13,12},{... | collective-permute-start | bytes 24584 | tf_op jit(solution)/shard_map/ppermute | solution.py:33
  24.8 14.7 %collective-permute-start.5 = (f32[32,32,128]{2,1,0:T(8,128)S(1)}, f32[32,32,128]{2,1,0:T(8,128)S(1)}, u32[]{:S(2)}, u32[]{:S(2)}) collective-permute-start(f32[32,32,128]{2,1,0:T(8,128)S(1)} %add.228), channel_id=1, source_target_pairs={{0,8},{4,12},{8,16},{12,20},{16,24},{20,28},{1,9},{5,13},{9,17},{1... | collective-permute-start | bytes 1572872 | tf_op jit(solution)/shard_map/ppermute | solution.py:33
  30.3 15.1 %copy-start.8 = (f32[64,32,128]{2,1,0:T(8,128)S(1)}, f32[64,32,128]{2,1,0:T(8,128)}, u32[]{:S(2)}) copy-start(f32[64,32,128]{2,1,0:T(8,128)} %param.12) | copy-start | bytes 3145732
  30.3 15.2 %copy-start.10 = (f32[32,128]{1,0:T(8,128)S(1)}, f32[32,128]{1,0:T(8,128)}, u32[]{:S(2)}) copy-start(f32[32,128]{1,0:T(8,128)} %param.14) | copy-start | bytes 49156
  40.4 27.3 %collective-permute-start.6 = (f32[32,32,128]{2,1,0:T(8,128)}, f32[32,32,128]{2,1,0:T(8,128)}, u32[]{:S(2)}, u32[]{:S(2)}) collective-permute-start(f32[32,32,128]{2,1,0:T(8,128)} %add.229), channel_id=1, source_target_pairs={{0,16},{4,20},{8,24},{12,28},{1,17},{5,21},{9,25},{13,29},{2,18},{... | collective-permute-start | bytes 1572872 | tf_op jit(solution)/shard_map/ppermute | solution.py:33
  67.7 3.5 %copy-start.5 = (f32[32,7,32,128]{3,2,1,0:T(8,128)S(1)}, f32[32,7,32,128]{3,2,1,0:T(8,128)}, u32[]{:S(2)}) copy-start(f32[32,7,32,128]{3,2,1,0:T(8,128)} %fusion.2) | copy-start | bytes 11010052
  69.2 13.1 %collective-permute-start.7 = (f32[32,32,128]{2,1,0:T(8,128)S(1)}, f32[32,32,128]{2,1,0:T(8,128)S(1)}, u32[]{:S(2)}, u32[]{:S(2)}) collective-permute-start(f32[32,32,128]{2,1,0:T(8,128)S(1)} %get-tuple-element.28), channel_id=1, source_target_pairs={{0,4},{4,0},{8,12},{12,8},{16,20},{20,16},{24,28},{28,24},{1,5},{5... | collective-permute-start | bytes 1572872 | tf_op jit(solution)/shard_map/ppermute | solution.py:85
  69.2 13.1 %copy-start.4 = (f32[32,7,32,128]{3,2,1,0:T(8,128)S(1)}, f32[32,7,32,128]{3,2,1,0:T(8,128)}, u32[]{:S(2)}) copy-start(f32[32,7,32,128]{3,2,1,0:T(8,128)} %fusion) | copy-start | bytes 11010052
  70.2 12.1 %copy-start.3 = (f32[32,8,32,128]{3,2,1,0:T(8,128)S(1)}, f32[32,8,32,128]{3,2,1,0:T(8,128)}, u32[]{:S(2)}) copy-start(f32[32,8,32,128]{3,2,1,0:T(8,128)} %copy-done.2) | copy-start | bytes 12582916
  71.2 11.1 %copy-start.1 = (f32[32,8,32,128]{3,2,1,0:T(8,128)S(1)}, f32[32,8,32,128]{3,2,1,0:T(8,128)}, u32[]{:S(2)}) copy-start(f32[32,8,32,128]{3,2,1,0:T(8,128)} %copy-done) | copy-start | bytes 12582916
  82.3 6.7 %copy-start.7 = (f32[8,32,128]{2,1,0:T(8,128)S(1)}, f32[8,32,128]{2,1,0:T(8,128)}, u32[]{:S(2)}) copy-start(f32[8,32,128]{2,1,0:T(8,128)} %param.9) | copy-start | bytes 393220
  90.1 12.3 %collective-permute-start.10 = (f32[2,8,1,128]{3,2,1,0:T(1,128)S(1)}, f32[2,8,1,128]{3,2,1,0:T(1,128)S(1)}, u32[]{:S(2)}, u32[]{:S(2)}) collective-permute-start(f32[2,8,1,128]{3,2,1,0:T(1,128)S(1)} %get-tuple-element.37), channel_id=1, source_target_pairs={{1,0},{2,1},{3,2},{5,4},{6,5},{7,6},{9,8},{10,9},{11,10},{13,12},{... | collective-permute-start | bytes 24584 | tf_op jit(solution)/shard_map/ppermute | solution.py:33
  93.3 9.1 %collective-permute-start.9 = (f32[2,8,1,128]{3,2,1,0:T(1,128)S(1)}, f32[2,8,1,128]{3,2,1,0:T(1,128)S(1)}, u32[]{:S(2)}, u32[]{:S(2)}) collective-permute-start(f32[2,8,1,128]{3,2,1,0:T(1,128)S(1)} %get-tuple-element.36), channel_id=1, source_target_pairs={{0,1},{1,2},{2,3},{4,5},{5,6},{6,7},{8,9},{9,10},{10,11},{12,13},{... | collective-permute-start | bytes 24584 | tf_op jit(solution)/shard_map/ppermute | solution.py:33
  95.7 6.7 %collective-permute-start.11 = (f32[2,1,32,128]{3,2,1,0:T(8,128)S(1)}, f32[2,1,32,128]{3,2,1,0:T(8,128)S(1)}, u32[]{:S(2)}, u32[]{:S(2)}) collective-permute-start(f32[2,1,32,128]{3,2,1,0:T(8,128)S(1)} %get-tuple-element.35), channel_id=1, source_target_pairs={{4,0},{8,4},{12,8},{16,12},{20,16},{24,20},{28,24},{5,1},{9,5},{13... | collective-permute-start | bytes 98312 | tf_op jit(solution)/shard_map/ppermute | solution.py:33
  97.6 5.6 %collective-permute-start.8 = (f32[2,1,32,128]{3,2,1,0:T(8,128)S(1)}, f32[2,1,32,128]{3,2,1,0:T(8,128)S(1)}, u32[]{:S(2)}, u32[]{:S(2)}) collective-permute-start(f32[2,1,32,128]{3,2,1,0:T(8,128)S(1)} %get-tuple-element.34), channel_id=1, source_target_pairs={{0,4},{4,8},{8,12},{12,16},{16,20},{20,24},{24,28},{1,5},{5,9},{9,... | collective-permute-start | bytes 98312 | tf_op jit(solution)/shard_map/ppermute | solution.py:33
  102.3 3.0 %copy-start.6 = (bf16[64,8,32,128]{3,2,1,0:T(8,128)(2,1)}, bf16[64,8,32,128]{3,2,1,0:T(8,128)(2,1)S(1)}, u32[]{:S(2)}) copy-start(bf16[64,8,32,128]{3,2,1,0:T(8,128)(2,1)S(1)} %fusion.6) | copy-start | bytes 12582916

commit v6 on v4

--- a/solution.py
+++ b/solution.py
@@ -63,23 +63,60 @@
     return before
 
 
-def paired_scan(totals, axis, rider):
+def paired_steps(totals, axis):
     count = lax.axis_size(axis)
     half = totals.shape[0] // 2
-    if count % 2 or totals.shape[0] % 2 or count == 2:
-        return exclusive_scan(totals, axis), rider(None)
     is_low = lax.axis_index(axis) % 2 == 0
     first, second = totals[:half], totals[half:]
     mine = jnp.where(is_low, first, second)
     swap = [(i, i ^ 1) for i in range(count)]
-    given = jnp.where(is_low, second, first)
-    got = lax.ppermute(given, axis, swap)
-    got, carried = lax.optimization_barrier((got, rider(given)))
-    before = exclusive_scan(mine + got, axis, stride=2)
-    back = lax.ppermute(jnp.where(is_low, before + mine, before), axis, swap)
-    low_result = jnp.concatenate([before, back])
-    high_result = jnp.concatenate([back, before + got])
-    return jnp.where(is_low, low_result, high_result), carried
+    got = yield jnp.where(is_low, second, first), swap
+    pair_total = mine + got
+    pairs = count // 2
+    before = yield pair_total, shift_pairs(count, 2)
+    through = pair_total + before
+    step = 2
+    while step < pairs:
+        arrived = yield through, shift_pairs(count, 2 * step)
+        before = before + arrived
+        step *= 2
+        if step < pairs:
+            through = through + arrived
+    back = yield jnp.where(is_low, before + mine, before), swap
+    return jnp.where(
+        is_low, jnp.concatenate([before, back]), jnp.concatenate([back, before + got])
+    )
+
+
+def shift_pairs(count, shift):
+    return [(i, i + shift) for i in range(count - shift)]
+
+
+def pipelined_scan(totals, axis, rider, groups=2):
+    count = lax.axis_size(axis)
+    lines = totals.shape[0]
+    if count % 2 or count <= 2 or lines % (2 * groups):
+        return exclusive_scan(totals, axis), rider(None)
+    size = lines // groups
+    steps = [paired_steps(totals[g * size : (g + 1) * size], axis) for g in range(groups)]
+    live, done, carried, stage = {}, {}, None, 0
+    while stage < groups or live:
+        if stage < groups:
+            live[stage] = next(steps[stage])
+        arrived = {g: lax.ppermute(payload, axis, pairs) for g, (payload, pairs) in live.items()}
+        if stage == 0:
+            arrived, carried = lax.optimization_barrier((arrived, rider(live[0][0])))
+        else:
+            arrived = lax.optimization_barrier(arrived)
+        following = {}
+        for g, value in arrived.items():
+            try:
+                following[g] = steps[g].send(value)
+            except StopIteration as finished:
+                done[g] = finished.value
+        live = following
+        stage += 1
+    return jnp.concatenate([done[g] for g in range(groups)]), carried
 
 
 def window(source, step_beam, step_cross, step_depth):
@@ -153,7 +190,7 @@
             fields, _ = lax.optimization_barrier((fields, after))
         return bordered_fields(fields)
 
-    prefix, first_bordered = paired_scan(totals, "beam", first_border)
+    prefix, first_bordered = pipelined_scan(totals, "beam", first_border)
     column = prefix[:, None] + local_column
     radiance = entry_spectral_power[:, None] * jnp.exp(-column)
     spectral_power = radiance.astype(jnp.bfloat16)

time: 106 us -> 104 us (0.981)
  waiting for transfers between devices: 42.1 us -> 33.2 us
  starting transfers between devices: 33.4 us -> 37.4 us
  other arithmetic: 27 us -> 30.2 us
    ppermute x10 -> x8, waiting for transfers between devices: 30.5 us -> 1.9 us  [shifted(): return lax.ppermute(block, axis, pairs)]
    ppermute x2 -> x8, waiting for transfers between devices: 11.6 us -> 31.3 us  [pipelined_scan(): lax.ppermute(payload, axis, pairs)]
    ppermute x2 -> x8, starting transfers between devices: 1.38 us -> 13.3 us  [pipelined_scan(): lax.ppermute(payload, axis, pairs)]
    ppermute x10 -> x8, starting transfers between devices: 32 us -> 24.1 us  [shifted(): return lax.ppermute(block, axis, pairs)]
    add x3 -> x5, other arithmetic: 2.65 us -> 4.88 us  [the longest x2 2.25 us: paired_steps(): before + got]
    select_n x3 -> x6, other arithmetic: 1.59 us -> 2.46 us  [the longest x2 2.18 us: paired_steps(): back = (yield (jnp.where(is_low, before + mine, before), swap))]
  transfers between devices with their start and end apart: 12 -> 16, of which waited for: 6 -> 9; matrix products, arithmetic and copies ran while one was open for 6% -> 8% of each run, Pallas kernels for 0% -> 0%
where the time goes in v6:
time: 104 us; the launch traced here: 103 us
  starting transfers between devices  37.4 us (36%)
  waiting for transfers between devices  33.2 us (32%)
  other arithmetic  30.2 us (29%)
  between operations  1.05 us (1%)
    ppermute x8, waiting for transfers between devices, pipelined_scan(): lax.ppermute(payload, axis, pairs)  31.3 us
    ppermute x8, starting transfers between devices, shifted(): return lax.ppermute(block, axis, pairs)  24.1 us
    ppermute x8, starting transfers between devices, pipelined_scan(): lax.ppermute(payload, axis, pairs)  13.3 us
    reduce_sum x1, other arithmetic, local(): heating = jnp.sum(radiance * (1.0 - jnp.exp(-optical_depth)), axis=0)  6.82 us
    reduce_sum x1, other arithmetic, local(): totals = jnp.sum(optical_depth, axis=1)  6.1 us
    another operation x1, other arithmetic, local(): jnp.cumsum(optical_depth[:, :rows - 1], axis=1)  4.16 us
    add x2, other arithmetic, paired_steps(): before + got  2.25 us
    select_n x2, other arithmetic, paired_steps(): back = (yield (jnp.where(is_low, before + mine, before), swap))  2.18 us
  transfers between devices with their start and end apart: 16, of which 9 were waited for; matrix products, arithmetic and copies ran while one was open for 8% of the time, Pallas kernels for 0%

profile of v6, /device:TPU:9, one launch (start us, length us, event | category | flops | bytes accessed | tf_op | source)
XLA Modules:
  0.0 102.7 jit_solution(8030020712578086032)
XLA Ops:
  0.6 0.7 convert_subtract_fusion
  1.4 1.1 %add_bitcast_fusion = (f32[1,8,32,128]{3,2,1,0:T(8,128)S(1)}, f32[8,32,128]{2,1,0:T(8,128)S(1)}) fusion(f32[8,32,128]{2,1,0:T(8,128)} %param.9, f32[8,32,128]{2,1,0:T(8,128)} %param.10, f32[8,32]{1,0:T(8,128)S(1)} %get-tuple-element.50), kind=kLoop, calls=%fused_computation.185 | loop fusion | flops 262144 | bytes 525312 | tf_op jit(solution)/shard_map/stack | solution.py:169
  2.4 6.1 %fusion.102 = (f32[64,32,128]{2,1,0:T(8,128)S(1)}, f32[64,8,32,128]{3,2,1,0:T(8,128)}) fusion(f32[8,32]{1,0:T(8,128)S(1)} %get-tuple-element.51, bf16[64,8,32,128]{3,2,1,0:T(8,128)(2,1)} %param.11, f32[64]{0:T(128)} %param.13, f32[8,32,128]{2,1,0:T(8,128)S(1)} %get-tuple-element.49), kind=kLoop, calls=%fused_computation.199 | loop fusion | flops 12320768 | bytes 13763840 | tf_op jit(solution)/shard_map/reduce_sum | solution.py:183
  8.6 1.3 %collective-permute-start = (f32[16,32,128]{2,1,0:T(8,128)S(1)}, f32[16,32,128]{2,1,0:T(8,128)S(1)}, u32[]{:S(2)}, u32[]{:S(2)}) collective-permute-start(f32[16,32,128]{2,1,0:T(8,128)S(1)} %slice_select_fusion.2), channel_id=1, source_target_pairs={{0,4},{4,0},{8,12},{12,8},{16,20},{20,16},{24,28},{28,24},{1,5},{5... | collective-permute-start | bytes 786440 | tf_op jit(solution)/shard_map/ppermute | solution.py:106
  9.9 1.9 %collective-permute-start.4 = (f32[2,1,32,128]{3,2,1,0:T(8,128)S(1)}, f32[2,1,32,128]{3,2,1,0:T(8,128)S(1)}, u32[]{:S(2)}, u32[]{:S(2)}) collective-permute-start(f32[2,1,32,128]{3,2,1,0:T(8,128)S(1)} %get-tuple-element.45), channel_id=1, source_target_pairs={{4,0},{8,4},{12,8},{16,12},{20,16},{24,20},{28,24},{5,1},{9,5},{13... | collective-permute-start | bytes 98312 | tf_op jit(solution)/shard_map/ppermute | solution.py:33
  11.9 3.4 %collective-permute-start.1 = (f32[2,1,32,128]{3,2,1,0:T(8,128)S(1)}, f32[2,1,32,128]{3,2,1,0:T(8,128)S(1)}, u32[]{:S(2)}, u32[]{:S(2)}) collective-permute-start(f32[2,1,32,128]{3,2,1,0:T(8,128)S(1)} %get-tuple-element.44), channel_id=1, source_target_pairs={{0,4},{4,8},{8,12},{12,16},{16,20},{20,24},{24,28},{1,5},{5,9},{9,... | collective-permute-start | bytes 98312 | tf_op jit(solution)/shard_map/ppermute | solution.py:33
  15.2 3.4 %collective-permute-start.3 = (f32[2,8,1,128]{3,2,1,0:T(1,128)S(1)}, f32[2,8,1,128]{3,2,1,0:T(1,128)S(1)}, u32[]{:S(2)}, u32[]{:S(2)}) collective-permute-start(f32[2,8,1,128]{3,2,1,0:T(1,128)S(1)} %get-tuple-element.47), channel_id=1, source_target_pairs={{1,0},{2,1},{3,2},{5,4},{6,5},{7,6},{9,8},{10,9},{11,10},{13,12},{... | collective-permute-start | bytes 24584 | tf_op jit(solution)/shard_map/ppermute | solution.py:33
  18.7 3.0 %collective-permute-start.2 = (f32[2,8,1,128]{3,2,1,0:T(1,128)S(1)}, f32[2,8,1,128]{3,2,1,0:T(1,128)S(1)}, u32[]{:S(2)}, u32[]{:S(2)}) collective-permute-start(f32[2,8,1,128]{3,2,1,0:T(1,128)S(1)} %get-tuple-element.46), channel_id=1, source_target_pairs={{0,1},{1,2},{2,3},{4,5},{5,6},{6,7},{8,9},{9,10},{10,11},{12,13},{... | collective-permute-start | bytes 24584 | tf_op jit(solution)/shard_map/ppermute | solution.py:33
  21.7 0.0 collective-permute-done.3
  21.7 0.8 collective-permute-done.2
  22.5 0.0 collective-permute-done.4
  22.5 0.0 collective-permute-done.1
  22.5 0.6 copy-done.9
  23.1 0.3 pad.11
  23.4 0.0 collective-permute-done
  23.4 0.1 slice_select_fusion.1
  23.5 3.2 %collective-permute-start.5 = (f32[16,32,128]{2,1,0:T(8,128)S(1)}, f32[16,32,128]{2,1,0:T(8,128)S(1)}, u32[]{:S(2)}, u32[]{:S(2)}) collective-permute-start(f32[16,32,128]{2,1,0:T(8,128)S(1)} %get-tuple-element.34), channel_id=1, source_target_pairs={{0,8},{4,12},{8,16},{12,20},{16,24},{20,28},{1,9},{5,13},{9,17},{1... | collective-permute-start | bytes 786440 | tf_op jit(solution)/shard_map/ppermute | solution.py:106
  26.7 1.2 %collective-permute-start.6 = (f32[16,32,128]{2,1,0:T(8,128)S(1)}, f32[16,32,128]{2,1,0:T(8,128)S(1)}, u32[]{:S(2)}, u32[]{:S(2)}) collective-permute-start(f32[16,32,128]{2,1,0:T(8,128)S(1)} %get-tuple-element.33), channel_id=1, source_target_pairs={{0,4},{4,0},{8,12},{12,8},{16,20},{20,16},{24,28},{28,24},{1,5},{5... | collective-permute-start | bytes 786440 | tf_op jit(solution)/shard_map/ppermute | solution.py:106
  27.9 5.7 %collective-permute-done.5 = f32[16,32,128]{2,1,0:T(8,128)S(1)} collective-permute-done((f32[16,32,128]{2,1,0:T(8,128)S(1)}, f32[16,32,128]{2,1,0:T(8,128)S(1)}, u32[]{:S(2)}, u32[]{:S(2)}) %collective-permute-start.5) | collective-permute-done | bytes 262176 | tf_op jit(solution)/shard_map/ppermute | solution.py:106
  33.6 1.3 %collective-permute-done.6 = f32[16,32,128]{2,1,0:T(8,128)S(1)} collective-permute-done((f32[16,32,128]{2,1,0:T(8,128)S(1)}, f32[16,32,128]{2,1,0:T(8,128)S(1)}, u32[]{:S(2)}, u32[]{:S(2)}) %collective-permute-start.6) | collective-permute-done | bytes 262176 | tf_op jit(solution)/shard_map/ppermute | solution.py:106
  35.0 0.8 add.182
  35.8 4.2 %collective-permute-start.7 = (f32[16,32,128]{2,1,0:T(8,128)}, f32[16,32,128]{2,1,0:T(8,128)}, u32[]{:S(2)}, u32[]{:S(2)}) collective-permute-start(f32[16,32,128]{2,1,0:T(8,128)} %add.182), channel_id=1, source_target_pairs={{0,16},{4,20},{8,24},{12,28},{1,17},{5,21},{9,25},{13,29},{2,18},{... | collective-permute-start | bytes 786440 | tf_op jit(solution)/shard_map/ppermute | solution.py:106
  40.0 0.8 fusion.96
  40.7 1.9 %collective-permute-start.8 = (f32[16,32,128]{2,1,0:T(8,128)}, f32[16,32,128]{2,1,0:T(8,128)}, u32[]{:S(2)}, u32[]{:S(2)}) collective-permute-start(f32[16,32,128]{2,1,0:T(8,128)} %fusion.96), channel_id=1, source_target_pairs={{0,8},{4,12},{8,16},{12,20},{16,24},{20,28},{1,9},{5,13},{9,17},{1... | collective-permute-start | bytes 786440 | tf_op jit(solution)/shard_map/ppermute | solution.py:106
  42.7 0.0 copy-start.8
  42.7 4.2 %fusion = f32[64,7,32,128]{3,2,1,0:T(8,128)S(1)} fusion(f32[64,8,32,128]{3,2,1,0:T(8,128)} %get-tuple-element.30), kind=kOutput, calls=%fused_computation.5 | output fusion | flops 11010048 | bytes 14680064 | tf_op jit(solution)/shard_map/jit(cumsum)/reduce_window_sum | solution.py:185
  46.9 0.0 copy-start
  46.9 0.0 copy-start.3
  46.9 0.0 copy-start.11
  46.9 3.8 %collective-permute-done.7 = f32[16,32,128]{2,1,0:T(8,128)} collective-permute-done((f32[16,32,128]{2,1,0:T(8,128)}, f32[16,32,128]{2,1,0:T(8,128)}, u32[]{:S(2)}, u32[]{:S(2)}) %collective-permute-start.7) | collective-permute-done | bytes 262176 | tf_op jit(solution)/shard_map/ppermute | solution.py:106
  50.7 5.6 %collective-permute-done.8 = f32[16,32,128]{2,1,0:T(8,128)} collective-permute-done((f32[16,32,128]{2,1,0:T(8,128)}, f32[16,32,128]{2,1,0:T(8,128)}, u32[]{:S(2)}, u32[]{:S(2)}) %collective-permute-start.8) | collective-permute-done | bytes 262176 | tf_op jit(solution)/shard_map/ppermute | solution.py:106
  56.3 1.2 %fusion.103 = (f32[16,32,128]{2,1,0:T(8,128)S(1)}, f32[16,32,128]{2,1,0:T(8,128)S(1)}) fusion(f32[16,32,128]{2,1,0:T(8,128)} %copy-done.5, f32[16,32,128]{2,1,0:T(8,128)} %copy-done.4, f32[16,32,128]{2,1,0:T(8,128)} %collective-permute-done.7), kind=kLoop, calls=%fused_computation.200 | loop fusion | flops 131072 | bytes 1310720 | tf_op jit(solution)/shard_map/add | solution.py:87
  57.5 1.1 %add_select_fusion.1 = f32[16,32,128]{2,1,0:T(8,128)S(1)} fusion(f32[16,32,128]{2,1,0:T(8,128)S(1)} %get-tuple-element.25, pred[]{:T(512)S(6)} %eq.7, f32[64,32,128]{2,1,0:T(8,128)} %copy-done.1), kind=kLoop, calls=%fused_computation.66 | loop fusion | flops 196608 | bytes 1048577 | tf_op jit(solution)/shard_map/jit(_where)/select_n | solution.py:85
  58.6 0.1 collective-permute-start.9
  58.6 1.1 %add.186 = f32[16,32,128]{2,1,0:T(8,128)S(1)} add(f32[16,32,128]{2,1,0:T(8,128)} %fusion.96, f32[16,32,128]{2,1,0:T(8,128)} %collective-permute-done.8) | non-fusion elementwise | flops 65536 | bytes 786432 | tf_op jit(solution)/shard_map/add | solution.py:77
  59.7 1.3 %collective-permute-start.10 = (f32[16,32,128]{2,1,0:T(8,128)S(1)}, f32[16,32,128]{2,1,0:T(8,128)S(1)}, u32[]{:S(2)}, u32[]{:S(2)}) collective-permute-start(f32[16,32,128]{2,1,0:T(8,128)S(1)} %add.186), channel_id=1, source_target_pairs={{0,16},{4,20},{8,24},{12,28},{1,17},{5,21},{9,25},{13,29},{2,18},{... | collective-permute-start | bytes 786440 | tf_op jit(solution)/shard_map/ppermute | solution.py:106
  61.0 0.4 power_multiply_fusion.2
  61.5 3.9 %collective-permute-done.9 = f32[16,32,128]{2,1,0:T(8,128)S(1)} collective-permute-done((f32[16,32,128]{2,1,0:T(8,128)S(1)}, f32[16,32,128]{2,1,0:T(8,128)S(1)}, u32[]{:S(2)}, u32[]{:S(2)}) %collective-permute-start.9) | collective-permute-done | bytes 262176 | tf_op jit(solution)/shard_map/ppermute | solution.py:106
  65.3 5.9 %collective-permute-done.10 = f32[16,32,128]{2,1,0:T(8,128)S(1)} collective-permute-done((f32[16,32,128]{2,1,0:T(8,128)S(1)}, f32[16,32,128]{2,1,0:T(8,128)S(1)}, u32[]{:S(2)}, u32[]{:S(2)}) %collective-permute-start.10) | collective-permute-done | bytes 262176 | tf_op jit(solution)/shard_map/ppermute | solution.py:106
  71.3 1.1 %fusion.104 = (f32[16,32,128]{2,1,0:T(8,128)S(1)}, f32[16,32,128]{2,1,0:T(8,128)S(1)}) fusion(f32[16,32,128]{2,1,0:T(8,128)} %copy-done.6, f32[16,32,128]{2,1,0:T(8,128)} %collective-permute-done.8, f32[16,32,128]{2,1,0:T(8,128)S(1)} %collective-permute-done.10), kind=kLoop, calls=%fused_computation.201 | loop fusion | flops 131072 | bytes 1310720 | tf_op jit(solution)/shard_map/add | solution.py:87
  72.4 1.1 %add_select_fusion = f32[16,32,128]{2,1,0:T(8,128)S(1)} fusion(f32[16,32,128]{2,1,0:T(8,128)S(1)} %get-tuple-element.27, pred[]{:T(512)S(6)} %eq.7, f32[64,32,128]{2,1,0:T(8,128)} %copy-done.1), kind=kLoop, calls=%fused_computation.65 | loop fusion | flops 196608 | bytes 1048577 | tf_op jit(solution)/shard_map/jit(_where)/select_n | solution.py:85
  73.5 0.1 collective-permute-start.11
  73.6 0.9 fusion.44
  74.5 0.1 maximum_select_fusion
  74.5 5.0 %collective-permute-done.11 = f32[16,32,128]{2,1,0:T(8,128)S(1)} collective-permute-done((f32[16,32,128]{2,1,0:T(8,128)S(1)}, f32[16,32,128]{2,1,0:T(8,128)S(1)}, u32[]{:S(2)}, u32[]{:S(2)}) %collective-permute-start.11) | collective-permute-done | bytes 262176 | tf_op jit(solution)/shard_map/ppermute | solution.py:106
  79.5 0.1 maximum_select_fusion.1
  79.6 0.1 pad_maximum_fusion
  79.7 0.0 copy-start.2
  79.7 0.0 copy-start.10
  79.7 6.8 %multiply_reduce_fusion = (f32[8,32,128]{2,1,0:T(8,128)S(1)}, f32[8,32,128]{2,1,0:T(8,128)S(1)}, bf16[64,8,32,128]{3,2,1,0:T(8,128)(2,1)}) fusion(f32[64,7,32,128]{3,2,1,0:T(8,128)S(1)} %fusion, f32[64,32,128]{2,1,0:T(8,128)S(1)} %pad_maximum_fusion, f32[64,32,128]{2,1,0:T(8,128)S(1)} %copy-done.3, f32[8,32]{1,0:T(8,128)S(1)} %get-tuple-element.51, ...), kind=kLoop, calls=%fused_computation | loop fusion | flops 31391744 | bytes 18220288 | tf_op jit(solution)/shard_map/reduce_sum | solution.py:198
  86.5 0.2 fusion.101
  86.7 0.1 fusion.93
  86.9 1.9 %collective-permute-start.15 = (f32[2,1,32,128]{3,2,1,0:T(8,128)S(1)}, f32[2,1,32,128]{3,2,1,0:T(8,128)S(1)}, u32[]{:S(2)}, u32[]{:S(2)}) collective-permute-start(f32[2,1,32,128]{3,2,1,0:T(8,128)S(1)} %get-tuple-element.41), channel_id=1, source_target_pairs={{4,0},{8,4},{12,8},{16,12},{20,16},{24,20},{28,24},{5,1},{9,5},{13... | collective-permute-start | bytes 98312 | tf_op jit(solution)/shard_map/ppermute | solution.py:33
  88.8 3.4 %collective-permute-start.12 = (f32[2,1,32,128]{3,2,1,0:T(8,128)S(1)}, f32[2,1,32,128]{3,2,1,0:T(8,128)S(1)}, u32[]{:S(2)}, u32[]{:S(2)}) collective-permute-start(f32[2,1,32,128]{3,2,1,0:T(8,128)S(1)} %get-tuple-element.40), channel_id=1, source_target_pairs={{0,4},{4,8},{8,12},{12,16},{16,20},{20,24},{24,28},{1,5},{5,9},{9,... | collective-permute-start | bytes 98312 | tf_op jit(solution)/shard_map/ppermute | solution.py:33
  92.2 5.2 %collective-permute-start.14 = (f32[2,8,1,128]{3,2,1,0:T(1,128)S(1)}, f32[2,8,1,128]{3,2,1,0:T(1,128)S(1)}, u32[]{:S(2)}, u32[]{:S(2)}) collective-permute-start(f32[2,8,1,128]{3,2,1,0:T(1,128)S(1)} %get-tuple-element.43), channel_id=1, source_target_pairs={{1,0},{2,1},{3,2},{5,4},{6,5},{7,6},{9,8},{10,9},{11,10},{13,12},{... | collective-permute-start | bytes 24584 | tf_op jit(solution)/shard_map/ppermute | solution.py:33
  97.4 1.9 %collective-permute-start.13 = (f32[2,8,1,128]{3,2,1,0:T(1,128)S(1)}, f32[2,8,1,128]{3,2,1,0:T(1,128)S(1)}, u32[]{:S(2)}, u32[]{:S(2)}) collective-permute-start(f32[2,8,1,128]{3,2,1,0:T(1,128)S(1)} %get-tuple-element.42), channel_id=1, source_target_pairs={{0,1},{1,2},{2,3},{4,5},{5,6},{6,7},{8,9},{9,10},{10,11},{12,13},{... | collective-permute-start | bytes 24584 | tf_op jit(solution)/shard_map/ppermute | solution.py:33
  99.3 0.0 collective-permute-done.14
  99.3 1.1 %collective-permute-done.13 = f32[2,8,1,128]{3,2,1,0:T(1,128)S(1)} collective-permute-done((f32[2,8,1,128]{3,2,1,0:T(1,128)S(1)}, f32[2,8,1,128]{3,2,1,0:T(1,128)S(1)}, u32[]{:S(2)}, u32[]{:S(2)}) %collective-permute-start.13) | collective-permute-done | bytes 8224 | tf_op jit(solution)/shard_map/ppermute | solution.py:33
  100.5 0.0 collective-permute-done.15
  100.5 0.0 collective-permute-done.12
  100.5 0.1 fusion.6
  100.5 0.5 power_multiply_fusion
  101.1 0.7 fusion.12
  101.8 1.0 fusion.82
  (26 shorter events, 0.2 us)
Async XLA Ops:
  0.6 9.3 %copy-start.7 = (f32[8,32,128]{2,1,0:T(8,128)S(1)}, f32[8,32,128]{2,1,0:T(8,128)}, u32[]{:S(2)}) copy-start(f32[8,32,128]{2,1,0:T(8,128)} %param.8) | copy-start | bytes 393220
  8.5 34.1 %copy-start.1 = (f32[64,32,128]{2,1,0:T(8,128)}, f32[64,32,128]{2,1,0:T(8,128)S(1)}, u32[]{:S(2)}) copy-start(f32[64,32,128]{2,1,0:T(8,128)S(1)} %get-tuple-element.29) | copy-start | bytes 3145732
  8.6 14.8 %collective-permute-start = (f32[16,32,128]{2,1,0:T(8,128)S(1)}, f32[16,32,128]{2,1,0:T(8,128)S(1)}, u32[]{:S(2)}, u32[]{:S(2)}) collective-permute-start(f32[16,32,128]{2,1,0:T(8,128)S(1)} %slice_select_fusion.2), channel_id=1, source_target_pairs={{0,4},{4,0},{8,12},{12,8},{16,20},{20,16},{24,28},{28,24},{1,5},{5... | collective-permute-start | bytes 786440 | tf_op jit(solution)/shard_map/ppermute | solution.py:106
  9.9 12.6 %collective-permute-start.4 = (f32[2,1,32,128]{3,2,1,0:T(8,128)S(1)}, f32[2,1,32,128]{3,2,1,0:T(8,128)S(1)}, u32[]{:S(2)}, u32[]{:S(2)}) collective-permute-start(f32[2,1,32,128]{3,2,1,0:T(8,128)S(1)} %get-tuple-element.45), channel_id=1, source_target_pairs={{4,0},{8,4},{12,8},{16,12},{20,16},{24,20},{28,24},{5,1},{9,5},{13... | collective-permute-start | bytes 98312 | tf_op jit(solution)/shard_map/ppermute | solution.py:33
  11.9 10.6 %collective-permute-start.1 = (f32[2,1,32,128]{3,2,1,0:T(8,128)S(1)}, f32[2,1,32,128]{3,2,1,0:T(8,128)S(1)}, u32[]{:S(2)}, u32[]{:S(2)}) collective-permute-start(f32[2,1,32,128]{3,2,1,0:T(8,128)S(1)} %get-tuple-element.44), channel_id=1, source_target_pairs={{0,4},{4,8},{8,12},{12,16},{16,20},{20,24},{24,28},{1,5},{5,9},{9,... | collective-permute-start | bytes 98312 | tf_op jit(solution)/shard_map/ppermute | solution.py:33
  15.2 6.5 %collective-permute-start.3 = (f32[2,8,1,128]{3,2,1,0:T(1,128)S(1)}, f32[2,8,1,128]{3,2,1,0:T(1,128)S(1)}, u32[]{:S(2)}, u32[]{:S(2)}) collective-permute-start(f32[2,8,1,128]{3,2,1,0:T(1,128)S(1)} %get-tuple-element.47), channel_id=1, source_target_pairs={{1,0},{2,1},{3,2},{5,4},{6,5},{7,6},{9,8},{10,9},{11,10},{13,12},{... | collective-permute-start | bytes 24584 | tf_op jit(solution)/shard_map/ppermute | solution.py:33
  18.7 3.8 %collective-permute-start.2 = (f32[2,8,1,128]{3,2,1,0:T(1,128)S(1)}, f32[2,8,1,128]{3,2,1,0:T(1,128)S(1)}, u32[]{:S(2)}, u32[]{:S(2)}) collective-permute-start(f32[2,8,1,128]{3,2,1,0:T(1,128)S(1)} %get-tuple-element.46), channel_id=1, source_target_pairs={{0,1},{1,2},{2,3},{4,5},{5,6},{6,7},{8,9},{9,10},{10,11},{12,13},{... | collective-permute-start | bytes 24584 | tf_op jit(solution)/shard_map/ppermute | solution.py:33
  22.5 0.6 copy-start.9
  23.4 19.3 %copy-start.5 = (f32[16,32,128]{2,1,0:T(8,128)}, f32[16,32,128]{2,1,0:T(8,128)S(1)}, u32[]{:S(2)}) copy-start(f32[16,32,128]{2,1,0:T(8,128)S(1)} %collective-permute-done) | copy-start | bytes 786436
  23.5 10.1 %collective-permute-start.5 = (f32[16,32,128]{2,1,0:T(8,128)S(1)}, f32[16,32,128]{2,1,0:T(8,128)S(1)}, u32[]{:S(2)}, u32[]{:S(2)}) collective-permute-start(f32[16,32,128]{2,1,0:T(8,128)S(1)} %get-tuple-element.34), channel_id=1, source_target_pairs={{0,8},{4,12},{8,16},{12,20},{16,24},{20,28},{1,9},{5,13},{9,17},{1... | collective-permute-start | bytes 786440 | tf_op jit(solution)/shard_map/ppermute | solution.py:106
  26.7 8.2 %collective-permute-start.6 = (f32[16,32,128]{2,1,0:T(8,128)S(1)}, f32[16,32,128]{2,1,0:T(8,128)S(1)}, u32[]{:S(2)}, u32[]{:S(2)}) collective-permute-start(f32[16,32,128]{2,1,0:T(8,128)S(1)} %get-tuple-element.33), channel_id=1, source_target_pairs={{0,4},{4,0},{8,12},{12,8},{16,20},{20,16},{24,28},{28,24},{1,5},{5... | collective-permute-start | bytes 786440 | tf_op jit(solution)/shard_map/ppermute | solution.py:106
  33.6 1.3 %copy-start.4 = (f32[16,32,128]{2,1,0:T(8,128)}, f32[16,32,128]{2,1,0:T(8,128)S(1)}, u32[]{:S(2)}) copy-start(f32[16,32,128]{2,1,0:T(8,128)S(1)} %collective-permute-done.5) | copy-start | bytes 786436
  35.0 7.7 %copy-start.6 = (f32[16,32,128]{2,1,0:T(8,128)}, f32[16,32,128]{2,1,0:T(8,128)S(1)}, u32[]{:S(2)}) copy-start(f32[16,32,128]{2,1,0:T(8,128)S(1)} %collective-permute-done.6) | copy-start | bytes 786436
  35.8 14.9 %collective-permute-start.7 = (f32[16,32,128]{2,1,0:T(8,128)}, f32[16,32,128]{2,1,0:T(8,128)}, u32[]{:S(2)}, u32[]{:S(2)}) collective-permute-start(f32[16,32,128]{2,1,0:T(8,128)} %add.182), channel_id=1, source_target_pairs={{0,16},{4,20},{8,24},{12,28},{1,17},{5,21},{9,25},{13,29},{2,18},{... | collective-permute-start | bytes 786440 | tf_op jit(solution)/shard_map/ppermute | solution.py:106
  40.7 15.6 %collective-permute-start.8 = (f32[16,32,128]{2,1,0:T(8,128)}, f32[16,32,128]{2,1,0:T(8,128)}, u32[]{:S(2)}, u32[]{:S(2)}) collective-permute-start(f32[16,32,128]{2,1,0:T(8,128)} %fusion.96), channel_id=1, source_target_pairs={{0,8},{4,12},{8,16},{12,20},{16,24},{20,28},{1,9},{5,13},{9,17},{1... | collective-permute-start | bytes 786440 | tf_op jit(solution)/shard_map/ppermute | solution.py:106
  42.7 18.3 %copy-start.8 = (f32[32,128]{1,0:T(8,128)S(1)}, f32[32,128]{1,0:T(8,128)}, u32[]{:S(2)}) copy-start(f32[32,128]{1,0:T(8,128)} %param.14) | copy-start | bytes 49156
  46.9 32.8 %copy-start = (bf16[64,8,32,128]{3,2,1,0:T(8,128)(2,1)S(1)}, bf16[64,8,32,128]{3,2,1,0:T(8,128)(2,1)}, u32[]{:S(2)}) copy-start(bf16[64,8,32,128]{3,2,1,0:T(8,128)(2,1)} %param.11) | copy-start | bytes 12582916
  46.9 32.8 %copy-start.3 = (f32[64,32,128]{2,1,0:T(8,128)S(1)}, f32[64,32,128]{2,1,0:T(8,128)}, u32[]{:S(2)}) copy-start(f32[64,32,128]{2,1,0:T(8,128)} %param.12) | copy-start | bytes 3145732
  46.9 32.8 %copy-start.11 = (f32[64]{0:T(128)S(1)}, f32[64]{0:T(128)}, u32[]{:S(2)}) copy-start(f32[64]{0:T(128)} %param.13) | copy-start | bytes 772
  58.6 6.8 %collective-permute-start.9 = (f32[16,32,128]{2,1,0:T(8,128)S(1)}, f32[16,32,128]{2,1,0:T(8,128)S(1)}, u32[]{:S(2)}, u32[]{:S(2)}) collective-permute-start(f32[16,32,128]{2,1,0:T(8,128)S(1)} %add_select_fusion.1), channel_id=1, source_target_pairs={{0,4},{4,0},{8,12},{12,8},{16,20},{20,16},{24,28},{28,24},{1,5},{5... | collective-permute-start | bytes 786440 | tf_op jit(solution)/shard_map/ppermute | solution.py:106
  59.7 11.6 %collective-permute-start.10 = (f32[16,32,128]{2,1,0:T(8,128)S(1)}, f32[16,32,128]{2,1,0:T(8,128)S(1)}, u32[]{:S(2)}, u32[]{:S(2)}) collective-permute-start(f32[16,32,128]{2,1,0:T(8,128)S(1)} %add.186), channel_id=1, source_target_pairs={{0,16},{4,20},{8,24},{12,28},{1,17},{5,21},{9,25},{13,29},{2,18},{... | collective-permute-start | bytes 786440 | tf_op jit(solution)/shard_map/ppermute | solution.py:106
  73.5 6.0 %collective-permute-start.11 = (f32[16,32,128]{2,1,0:T(8,128)S(1)}, f32[16,32,128]{2,1,0:T(8,128)S(1)}, u32[]{:S(2)}, u32[]{:S(2)}) collective-permute-start(f32[16,32,128]{2,1,0:T(8,128)S(1)} %add_select_fusion), channel_id=1, source_target_pairs={{0,4},{4,0},{8,12},{12,8},{16,20},{20,16},{24,28},{28,24},{1,5},{5... | collective-permute-start | bytes 786440 | tf_op jit(solution)/shard_map/ppermute | solution.py:106
  79.7 6.8 %copy-start.2 = (f32[8,32,128]{2,1,0:T(8,128)S(1)}, f32[8,32,128]{2,1,0:T(8,128)}, u32[]{:S(2)}) copy-start(f32[8,32,128]{2,1,0:T(8,128)} %param.9) | copy-start | bytes 393220
  79.7 20.8 %copy-start.10 = (f32[2,1,1,128]{3,2,1,0:T(1,128)S(1)}, f32[2,1,1,128]{3,2,1,0:T(1,128)}, u32[]{:S(2)}) copy-start(f32[2,1,1,128]{3,2,1,0:T(1,128)} %copy-done.9) | copy-start | bytes 3076
  86.9 13.6 %collective-permute-start.15 = (f32[2,1,32,128]{3,2,1,0:T(8,128)S(1)}, f32[2,1,32,128]{3,2,1,0:T(8,128)S(1)}, u32[]{:S(2)}, u32[]{:S(2)}) collective-permute-start(f32[2,1,32,128]{3,2,1,0:T(8,128)S(1)} %get-tuple-element.41), channel_id=1, source_target_pairs={{4,0},{8,4},{12,8},{16,12},{20,16},{24,20},{28,24},{5,1},{9,5},{13... | collective-permute-start | bytes 98312 | tf_op jit(solution)/shard_map/ppermute | solution.py:33
  88.8 11.7 %collective-permute-start.12 = (f32[2,1,32,128]{3,2,1,0:T(8,128)S(1)}, f32[2,1,32,128]{3,2,1,0:T(8,128)S(1)}, u32[]{:S(2)}, u32[]{:S(2)}) collective-permute-start(f32[2,1,32,128]{3,2,1,0:T(8,128)S(1)} %get-tuple-element.40), channel_id=1, source_target_pairs={{0,4},{4,8},{8,12},{12,16},{16,20},{20,24},{24,28},{1,5},{5,9},{9,... | collective-permute-start | bytes 98312 | tf_op jit(solution)/shard_map/ppermute | solution.py:33
  92.2 7.2 %collective-permute-start.14 = (f32[2,8,1,128]{3,2,1,0:T(1,128)S(1)}, f32[2,8,1,128]{3,2,1,0:T(1,128)S(1)}, u32[]{:S(2)}, u32[]{:S(2)}) collective-permute-start(f32[2,8,1,128]{3,2,1,0:T(1,128)S(1)} %get-tuple-element.43), channel_id=1, source_target_pairs={{1,0},{2,1},{3,2},{5,4},{6,5},{7,6},{9,8},{10,9},{11,10},{13,12},{... | collective-permute-start | bytes 24584 | tf_op jit(solution)/shard_map/ppermute | solution.py:33
  97.4 3.1 %collective-permute-start.13 = (f32[2,8,1,128]{3,2,1,0:T(1,128)S(1)}, f32[2,8,1,128]{3,2,1,0:T(1,128)S(1)}, u32[]{:S(2)}, u32[]{:S(2)}) collective-permute-start(f32[2,8,1,128]{3,2,1,0:T(1,128)S(1)} %get-tuple-element.42), channel_id=1, source_target_pairs={{0,1},{1,2},{2,3},{4,5},{5,6},{6,7},{8,9},{9,10},{10,11},{12,13},{... | collective-permute-start | bytes 24584 | tf_op jit(solution)/shard_map/ppermute | solution.py:33

commit v7 on v6

--- a/solution.py
+++ b/solution.py
@@ -104,7 +104,7 @@
         if stage < groups:
             live[stage] = next(steps[stage])
         arrived = {g: lax.ppermute(payload, axis, pairs) for g, (payload, pairs) in live.items()}
-        if stage == 0:
+        if stage == 2:
             arrived, carried = lax.optimization_barrier((arrived, rider(live[0][0])))
         else:
             arrived = lax.optimization_barrier(arrived)

time: 104 us -> 104 us (level)
  waiting for transfers between devices: 33.2 us -> 28.9 us
  starting transfers between devices: 37.4 us -> 39.6 us
    ppermute x8, waiting for transfers between devices: 31.3 us -> 27.7 us  [pipelined_scan(): lax.ppermute(payload, axis, pairs)]
    ppermute x8, starting transfers between devices: 24.1 us -> 25.8 us  [shifted(): return lax.ppermute(block, axis, pairs)]
  transfers between devices with their start and end apart: 16 -> 16, of which waited for: 9 -> 7; matrix products, arithmetic and copies ran while one was open for 8% -> 10% of each run, Pallas kernels for 0% -> 0%
where the time goes in v7:
time: 104 us; the launch traced here: 102 us
  starting transfers between devices  39.6 us (38%)
  other arithmetic  31.2 us (30%)
  waiting for transfers between devices  28.9 us (28%)
  local copies, waits for them, and re-layouts  1.57 us (2%)
    ppermute x8, waiting for transfers between devices, pipelined_scan(): lax.ppermute(payload, axis, pairs)  27.7 us
    ppermute x8, starting transfers between devices, shifted(): return lax.ppermute(block, axis, pairs)  25.8 us
    ppermute x8, starting transfers between devices, pipelined_scan(): lax.ppermute(payload, axis, pairs)  13.9 us
    reduce_sum x1, other arithmetic, local(): heating = jnp.sum(radiance * (1.0 - jnp.exp(-optical_depth)), axis=0)  6.82 us
    reduce_sum x1, other arithmetic, local(): totals = jnp.sum(optical_depth, axis=1)  6.11 us
    another operation x1, other arithmetic, local(): jnp.cumsum(optical_depth[:, :rows - 1], axis=1)  4.16 us
    add x2, other arithmetic, paired_steps(): before + got  2.35 us
    select_n x2, other arithmetic, paired_steps(): back = (yield (jnp.where(is_low, before + mine, before), swap))  2.18 us
  transfers between devices with their start and end apart: 16, of which 7 were waited for; matrix products, arithmetic and copies ran while one was open for 10% of the time, Pallas kernels for 0%

profile of v7, /device:TPU:9, one launch (start us, length us, event | category | flops | bytes accessed | tf_op | source)
XLA Modules:
  0.0 102.3 jit_solution(6649264531021259400)
XLA Ops:
  0.6 0.7 convert_subtract_fusion
  1.3 1.1 %add_bitcast_fusion = (f32[1,8,32,128]{3,2,1,0:T(8,128)S(1)}, f32[8,32,128]{2,1,0:T(8,128)S(1)}) fusion(f32[8,32,128]{2,1,0:T(8,128)} %param.9, f32[8,32,128]{2,1,0:T(8,128)} %param.10, f32[8,32]{1,0:T(8,128)S(1)} %get-tuple-element.48), kind=kLoop, calls=%fused_computation.185 | loop fusion | flops 262144 | bytes 525312 | tf_op jit(solution)/shard_map/stack | solution.py:169
  2.4 6.1 %fusion.102 = (f32[64,32,128]{2,1,0:T(8,128)S(1)}, f32[64,8,32,128]{3,2,1,0:T(8,128)}) fusion(f32[8,32]{1,0:T(8,128)S(1)} %get-tuple-element.49, bf16[64,8,32,128]{3,2,1,0:T(8,128)(2,1)} %param.11, f32[64]{0:T(128)} %param.13, f32[8,32,128]{2,1,0:T(8,128)S(1)} %get-tuple-element.47), kind=kLoop, calls=%fused_computation.199 | loop fusion | flops 12320768 | bytes 13763840 | tf_op jit(solution)/shard_map/reduce_sum | solution.py:183
  8.6 1.3 %collective-permute-start = (f32[16,32,128]{2,1,0:T(8,128)S(1)}, f32[16,32,128]{2,1,0:T(8,128)S(1)}, u32[]{:S(2)}, u32[]{:S(2)}) collective-permute-start(f32[16,32,128]{2,1,0:T(8,128)S(1)} %slice_select_fusion.2), channel_id=1, source_target_pairs={{0,4},{4,0},{8,12},{12,8},{16,20},{20,16},{24,28},{28,24},{1,5},{5... | collective-permute-start | bytes 786440 | tf_op jit(solution)/shard_map/ppermute | solution.py:106
  9.9 5.9 %collective-permute-done = f32[16,32,128]{2,1,0:T(8,128)S(1)} collective-permute-done((f32[16,32,128]{2,1,0:T(8,128)S(1)}, f32[16,32,128]{2,1,0:T(8,128)S(1)}, u32[]{:S(2)}, u32[]{:S(2)}) %collective-permute-start) | collective-permute-done | bytes 262176 | tf_op jit(solution)/shard_map/ppermute | solution.py:106
  15.8 0.1 slice_select_fusion.1
  16.0 3.2 %collective-permute-start.1 = (f32[16,32,128]{2,1,0:T(8,128)S(1)}, f32[16,32,128]{2,1,0:T(8,128)S(1)}, u32[]{:S(2)}, u32[]{:S(2)}) collective-permute-start(f32[16,32,128]{2,1,0:T(8,128)S(1)} %get-tuple-element.32), channel_id=1, source_target_pairs={{0,8},{4,12},{8,16},{12,20},{16,24},{20,28},{1,9},{5,13},{9,17},{1... | collective-permute-start | bytes 786440 | tf_op jit(solution)/shard_map/ppermute | solution.py:106
  19.2 1.3 %collective-permute-start.2 = (f32[16,32,128]{2,1,0:T(8,128)S(1)}, f32[16,32,128]{2,1,0:T(8,128)S(1)}, u32[]{:S(2)}, u32[]{:S(2)}) collective-permute-start(f32[16,32,128]{2,1,0:T(8,128)S(1)} %get-tuple-element.31), channel_id=1, source_target_pairs={{0,4},{4,0},{8,12},{12,8},{16,20},{20,16},{24,28},{28,24},{1,5},{5... | collective-permute-start | bytes 786440 | tf_op jit(solution)/shard_map/ppermute | solution.py:106
  20.5 3.6 %collective-permute-done.1 = f32[16,32,128]{2,1,0:T(8,128)S(1)} collective-permute-done((f32[16,32,128]{2,1,0:T(8,128)S(1)}, f32[16,32,128]{2,1,0:T(8,128)S(1)}, u32[]{:S(2)}, u32[]{:S(2)}) %collective-permute-start.1) | collective-permute-done | bytes 262176 | tf_op jit(solution)/shard_map/ppermute | solution.py:106
  24.1 1.1 %collective-permute-done.2 = f32[16,32,128]{2,1,0:T(8,128)S(1)} collective-permute-done((f32[16,32,128]{2,1,0:T(8,128)S(1)}, f32[16,32,128]{2,1,0:T(8,128)S(1)}, u32[]{:S(2)}, u32[]{:S(2)}) %collective-permute-start.2) | collective-permute-done | bytes 262176 | tf_op jit(solution)/shard_map/ppermute | solution.py:106
  25.2 0.8 add.182
  26.0 3.8 %collective-permute-start.3 = (f32[16,32,128]{2,1,0:T(8,128)}, f32[16,32,128]{2,1,0:T(8,128)}, u32[]{:S(2)}, u32[]{:S(2)}) collective-permute-start(f32[16,32,128]{2,1,0:T(8,128)} %add.182), channel_id=1, source_target_pairs={{0,16},{4,20},{8,24},{12,28},{1,17},{5,21},{9,25},{13,29},{2,18},{... | collective-permute-start | bytes 786440 | tf_op jit(solution)/shard_map/ppermute | solution.py:106
  29.8 0.8 fusion.96
  30.6 0.6 fusion.106
  31.2 4.6 %collective-permute-start.7 = (f32[2,8,1,128]{3,2,1,0:T(1,128)S(1)}, f32[2,8,1,128]{3,2,1,0:T(1,128)S(1)}, u32[]{:S(2)}, u32[]{:S(2)}) collective-permute-start(f32[2,8,1,128]{3,2,1,0:T(1,128)S(1)} %get-tuple-element.45), channel_id=1, source_target_pairs={{1,0},{2,1},{3,2},{5,4},{6,5},{7,6},{9,8},{10,9},{11,10},{13,12},{... | collective-permute-start | bytes 24584 | tf_op jit(solution)/shard_map/ppermute | solution.py:33
  35.9 0.6 fusion.105
  36.5 1.9 %collective-permute-start.4 = (f32[16,32,128]{2,1,0:T(8,128)}, f32[16,32,128]{2,1,0:T(8,128)S(1)}, u32[]{:S(2)}, u32[]{:S(2)}) collective-permute-start(f32[16,32,128]{2,1,0:T(8,128)} %fusion.96), channel_id=1, source_target_pairs={{0,8},{4,12},{8,16},{12,20},{16,24},{20,28},{1,9},{5,13},{9,17},{1... | collective-permute-start | bytes 786440 | tf_op jit(solution)/shard_map/ppermute | solution.py:106
  38.4 4.3 %collective-permute-start.8 = (f32[2,1,32,128]{3,2,1,0:T(8,128)}, f32[2,1,32,128]{3,2,1,0:T(8,128)S(1)}, u32[]{:S(2)}, u32[]{:S(2)}) collective-permute-start(f32[2,1,32,128]{3,2,1,0:T(8,128)} %get-tuple-element.43), channel_id=1, source_target_pairs={{4,0},{8,4},{12,8},{16,12},{20,16},{24,20},{28,24},{5,1},{9,5},{13... | collective-permute-start | bytes 98312 | tf_op jit(solution)/shard_map/ppermute | solution.py:33
  42.8 3.6 %collective-permute-start.6 = (f32[2,8,1,128]{3,2,1,0:T(1,128)}, f32[2,8,1,128]{3,2,1,0:T(1,128)}, u32[]{:S(2)}, u32[]{:S(2)}) collective-permute-start(f32[2,8,1,128]{3,2,1,0:T(1,128)} %get-tuple-element.44), channel_id=1, source_target_pairs={{0,1},{1,2},{2,3},{4,5},{5,6},{6,7},{8,9},{9,10},{10,11},{12,13},{... | collective-permute-start | bytes 24584 | tf_op jit(solution)/shard_map/ppermute | solution.py:33
  46.4 0.0 collective-permute-done.7
  46.4 1.9 %collective-permute-start.5 = (f32[2,1,32,128]{3,2,1,0:T(8,128)}, f32[2,1,32,128]{3,2,1,0:T(8,128)}, u32[]{:S(2)}, u32[]{:S(2)}) collective-permute-start(f32[2,1,32,128]{3,2,1,0:T(8,128)} %get-tuple-element.42), channel_id=1, source_target_pairs={{0,4},{4,8},{8,12},{12,16},{16,20},{20,24},{24,28},{1,5},{5,9},{9,... | collective-permute-start | bytes 98312 | tf_op jit(solution)/shard_map/ppermute | solution.py:33
  48.4 0.0 copy-start.7
  48.4 4.2 %fusion = f32[64,7,32,128]{3,2,1,0:T(8,128)S(1)} fusion(f32[64,8,32,128]{3,2,1,0:T(8,128)} %get-tuple-element.28), kind=kOutput, calls=%fused_computation.5 | output fusion | flops 11010048 | bytes 14680064 | tf_op jit(solution)/shard_map/jit(cumsum)/reduce_window_sum | solution.py:185
  52.5 0.0 copy-start
  52.5 0.0 copy-start.3
  52.6 0.0 copy-start.9
  52.6 0.0 collective-permute-done.6
  52.6 0.0 collective-permute-done.8
  52.6 0.0 collective-permute-done.5
  52.6 1.0 fusion.4
  53.6 0.3 pad.11
  53.9 0.0 collective-permute-done.3
  53.9 0.0 collective-permute-done.4
  53.9 1.3 %fusion.103 = (f32[16,32,128]{2,1,0:T(8,128)S(1)}, f32[16,32,128]{2,1,0:T(8,128)S(1)}) fusion(f32[16,32,128]{2,1,0:T(8,128)} %copy-done.5, f32[16,32,128]{2,1,0:T(8,128)S(1)} %collective-permute-done.1, f32[16,32,128]{2,1,0:T(8,128)} %collective-permute-done.3), kind=kLoop, calls=%fused_computation.200 | loop fusion | flops 131072 | bytes 1310720 | tf_op jit(solution)/shard_map/add | solution.py:87
  55.3 1.1 %add_select_fusion.1 = f32[16,32,128]{2,1,0:T(8,128)S(1)} fusion(f32[16,32,128]{2,1,0:T(8,128)S(1)} %get-tuple-element.23, pred[]{:T(512)S(6)} %eq.7, f32[64,32,128]{2,1,0:T(8,128)} %copy-done.1), kind=kLoop, calls=%fused_computation.66 | loop fusion | flops 196608 | bytes 1048577 | tf_op jit(solution)/shard_map/jit(_where)/select_n | solution.py:85
  56.4 1.0 collective-permute-start.9
  57.3 1.0 add.186
  58.3 1.3 %collective-permute-start.10 = (f32[16,32,128]{2,1,0:T(8,128)S(1)}, f32[16,32,128]{2,1,0:T(8,128)S(1)}, u32[]{:S(2)}, u32[]{:S(2)}) collective-permute-start(f32[16,32,128]{2,1,0:T(8,128)S(1)} %add.186), channel_id=1, source_target_pairs={{0,16},{4,20},{8,24},{12,28},{1,17},{5,21},{9,25},{13,29},{2,18},{... | collective-permute-start | bytes 786440 | tf_op jit(solution)/shard_map/ppermute | solution.py:106
  59.6 0.4 power_multiply_fusion.2
  60.1 3.7 %collective-permute-done.9 = f32[16,32,128]{2,1,0:T(8,128)S(1)} collective-permute-done((f32[16,32,128]{2,1,0:T(8,128)S(1)}, f32[16,32,128]{2,1,0:T(8,128)S(1)}, u32[]{:S(2)}, u32[]{:S(2)}) %collective-permute-start.9) | collective-permute-done | bytes 262176 | tf_op jit(solution)/shard_map/ppermute | solution.py:106
  63.8 7.2 %collective-permute-done.10 = f32[16,32,128]{2,1,0:T(8,128)S(1)} collective-permute-done((f32[16,32,128]{2,1,0:T(8,128)S(1)}, f32[16,32,128]{2,1,0:T(8,128)S(1)}, u32[]{:S(2)}, u32[]{:S(2)}) %collective-permute-start.10) | collective-permute-done | bytes 262176 | tf_op jit(solution)/shard_map/ppermute | solution.py:106
  71.0 1.0 fusion.104
  72.0 1.1 %add_select_fusion = f32[16,32,128]{2,1,0:T(8,128)S(1)} fusion(f32[16,32,128]{2,1,0:T(8,128)S(1)} %get-tuple-element.25, pred[]{:T(512)S(6)} %eq.7, f32[64,32,128]{2,1,0:T(8,128)} %copy-done.1), kind=kLoop, calls=%fused_computation.65 | loop fusion | flops 196608 | bytes 1048577 | tf_op jit(solution)/shard_map/jit(_where)/select_n | solution.py:85
  73.1 0.1 collective-permute-start.11
  73.2 0.9 fusion.44
  74.1 0.1 maximum_select_fusion
  74.2 6.1 %collective-permute-done.11 = f32[16,32,128]{2,1,0:T(8,128)S(1)} collective-permute-done((f32[16,32,128]{2,1,0:T(8,128)S(1)}, f32[16,32,128]{2,1,0:T(8,128)S(1)}, u32[]{:S(2)}, u32[]{:S(2)}) %collective-permute-start.11) | collective-permute-done | bytes 262176 | tf_op jit(solution)/shard_map/ppermute | solution.py:106
  80.3 0.1 maximum_select_fusion.1
  80.3 0.1 pad_maximum_fusion
  80.4 0.0 copy-start.2
  80.5 6.8 %multiply_reduce_fusion = (f32[8,32,128]{2,1,0:T(8,128)S(1)}, f32[8,32,128]{2,1,0:T(8,128)S(1)}, bf16[64,8,32,128]{3,2,1,0:T(8,128)(2,1)}) fusion(f32[64,7,32,128]{3,2,1,0:T(8,128)S(1)} %fusion, f32[64,32,128]{2,1,0:T(8,128)S(1)} %pad_maximum_fusion, f32[64,32,128]{2,1,0:T(8,128)S(1)} %copy-done.3, f32[8,32]{1,0:T(8,128)S(1)} %get-tuple-element.49, ...), kind=kLoop, calls=%fused_computation | loop fusion | flops 31391744 | bytes 18220288 | tf_op jit(solution)/shard_map/reduce_sum | solution.py:198
  87.3 0.1 fusion.101
  87.4 0.1 fusion.93
  87.6 1.9 %collective-permute-start.15 = (f32[2,1,32,128]{3,2,1,0:T(8,128)S(1)}, f32[2,1,32,128]{3,2,1,0:T(8,128)S(1)}, u32[]{:S(2)}, u32[]{:S(2)}) collective-permute-start(f32[2,1,32,128]{3,2,1,0:T(8,128)S(1)} %get-tuple-element.39), channel_id=1, source_target_pairs={{4,0},{8,4},{12,8},{16,12},{20,16},{24,20},{28,24},{5,1},{9,5},{13... | collective-permute-start | bytes 98312 | tf_op jit(solution)/shard_map/ppermute | solution.py:33
  89.5 3.4 %collective-permute-start.12 = (f32[2,1,32,128]{3,2,1,0:T(8,128)S(1)}, f32[2,1,32,128]{3,2,1,0:T(8,128)S(1)}, u32[]{:S(2)}, u32[]{:S(2)}) collective-permute-start(f32[2,1,32,128]{3,2,1,0:T(8,128)S(1)} %get-tuple-element.38), channel_id=1, source_target_pairs={{0,4},{4,8},{8,12},{12,16},{16,20},{20,24},{24,28},{1,5},{5,9},{9,... | collective-permute-start | bytes 98312 | tf_op jit(solution)/shard_map/ppermute | solution.py:33
  92.9 4.1 %collective-permute-start.14 = (f32[2,8,1,128]{3,2,1,0:T(1,128)S(1)}, f32[2,8,1,128]{3,2,1,0:T(1,128)S(1)}, u32[]{:S(2)}, u32[]{:S(2)}) collective-permute-start(f32[2,8,1,128]{3,2,1,0:T(1,128)S(1)} %get-tuple-element.41), channel_id=1, source_target_pairs={{1,0},{2,1},{3,2},{5,4},{6,5},{7,6},{9,8},{10,9},{11,10},{13,12},{... | collective-permute-start | bytes 24584 | tf_op jit(solution)/shard_map/ppermute | solution.py:33
  97.0 1.9 %collective-permute-start.13 = (f32[2,8,1,128]{3,2,1,0:T(1,128)S(1)}, f32[2,8,1,128]{3,2,1,0:T(1,128)S(1)}, u32[]{:S(2)}, u32[]{:S(2)}) collective-permute-start(f32[2,8,1,128]{3,2,1,0:T(1,128)S(1)} %get-tuple-element.40), channel_id=1, source_target_pairs={{0,1},{1,2},{2,3},{4,5},{5,6},{6,7},{8,9},{9,10},{10,11},{12,13},{... | collective-permute-start | bytes 24584 | tf_op jit(solution)/shard_map/ppermute | solution.py:33
  98.9 0.0 collective-permute-done.14
  98.9 1.1 %collective-permute-done.13 = f32[2,8,1,128]{3,2,1,0:T(1,128)S(1)} collective-permute-done((f32[2,8,1,128]{3,2,1,0:T(1,128)S(1)}, f32[2,8,1,128]{3,2,1,0:T(1,128)S(1)}, u32[]{:S(2)}, u32[]{:S(2)}) %collective-permute-start.13) | collective-permute-done | bytes 8224 | tf_op jit(solution)/shard_map/ppermute | solution.py:33
  100.1 0.0 collective-permute-done.15
  100.1 0.0 collective-permute-done.12
  100.1 0.5 power_multiply_fusion
  100.7 0.7 fusion.12
  101.3 1.0 fusion.82
  (22 shorter events, 0.2 us)
Async XLA Ops:
  1.3 19.1 %copy-start.6 = (f32[8,32,128]{2,1,0:T(8,128)S(1)}, f32[8,32,128]{2,1,0:T(8,128)}, u32[]{:S(2)}) copy-start(f32[8,32,128]{2,1,0:T(8,128)} %param.8) | copy-start | bytes 393220
  8.5 39.8 %copy-start.1 = (f32[64,32,128]{2,1,0:T(8,128)}, f32[64,32,128]{2,1,0:T(8,128)S(1)}, u32[]{:S(2)}) copy-start(f32[64,32,128]{2,1,0:T(8,128)S(1)} %get-tuple-element.27) | copy-start | bytes 3145732
  8.6 7.2 %collective-permute-start = (f32[16,32,128]{2,1,0:T(8,128)S(1)}, f32[16,32,128]{2,1,0:T(8,128)S(1)}, u32[]{:S(2)}, u32[]{:S(2)}) collective-permute-start(f32[16,32,128]{2,1,0:T(8,128)S(1)} %slice_select_fusion.2), channel_id=1, source_target_pairs={{0,4},{4,0},{8,12},{12,8},{16,20},{20,16},{24,28},{28,24},{1,5},{5... | collective-permute-start | bytes 786440 | tf_op jit(solution)/shard_map/ppermute | solution.py:106
  15.8 32.5 %copy-start.5 = (f32[16,32,128]{2,1,0:T(8,128)}, f32[16,32,128]{2,1,0:T(8,128)S(1)}, u32[]{:S(2)}) copy-start(f32[16,32,128]{2,1,0:T(8,128)S(1)} %collective-permute-done) | copy-start | bytes 786436
  16.0 8.1 %collective-permute-start.1 = (f32[16,32,128]{2,1,0:T(8,128)S(1)}, f32[16,32,128]{2,1,0:T(8,128)S(1)}, u32[]{:S(2)}, u32[]{:S(2)}) collective-permute-start(f32[16,32,128]{2,1,0:T(8,128)S(1)} %get-tuple-element.32), channel_id=1, source_target_pairs={{0,8},{4,12},{8,16},{12,20},{16,24},{20,28},{1,9},{5,13},{9,17},{1... | collective-permute-start | bytes 786440 | tf_op jit(solution)/shard_map/ppermute | solution.py:106
  19.2 6.0 %collective-permute-start.2 = (f32[16,32,128]{2,1,0:T(8,128)S(1)}, f32[16,32,128]{2,1,0:T(8,128)S(1)}, u32[]{:S(2)}, u32[]{:S(2)}) collective-permute-start(f32[16,32,128]{2,1,0:T(8,128)S(1)} %get-tuple-element.31), channel_id=1, source_target_pairs={{0,4},{4,0},{8,12},{12,8},{16,20},{20,16},{24,28},{28,24},{1,5},{5... | collective-permute-start | bytes 786440 | tf_op jit(solution)/shard_map/ppermute | solution.py:106
  25.2 23.1 %copy-start.4 = (f32[16,32,128]{2,1,0:T(8,128)}, f32[16,32,128]{2,1,0:T(8,128)S(1)}, u32[]{:S(2)}) copy-start(f32[16,32,128]{2,1,0:T(8,128)S(1)} %collective-permute-done.2) | copy-start | bytes 786436
  26.0 27.9 %collective-permute-start.3 = (f32[16,32,128]{2,1,0:T(8,128)}, f32[16,32,128]{2,1,0:T(8,128)}, u32[]{:S(2)}, u32[]{:S(2)}) collective-permute-start(f32[16,32,128]{2,1,0:T(8,128)} %add.182), channel_id=1, source_target_pairs={{0,16},{4,20},{8,24},{12,28},{1,17},{5,21},{9,25},{13,29},{2,18},{... | collective-permute-start | bytes 786440 | tf_op jit(solution)/shard_map/ppermute | solution.py:106
  31.2 15.1 %collective-permute-start.7 = (f32[2,8,1,128]{3,2,1,0:T(1,128)S(1)}, f32[2,8,1,128]{3,2,1,0:T(1,128)S(1)}, u32[]{:S(2)}, u32[]{:S(2)}) collective-permute-start(f32[2,8,1,128]{3,2,1,0:T(1,128)S(1)} %get-tuple-element.45), channel_id=1, source_target_pairs={{1,0},{2,1},{3,2},{5,4},{6,5},{7,6},{9,8},{10,9},{11,10},{13,12},{... | collective-permute-start | bytes 24584 | tf_op jit(solution)/shard_map/ppermute | solution.py:33
  36.5 17.4 %collective-permute-start.4 = (f32[16,32,128]{2,1,0:T(8,128)}, f32[16,32,128]{2,1,0:T(8,128)S(1)}, u32[]{:S(2)}, u32[]{:S(2)}) collective-permute-start(f32[16,32,128]{2,1,0:T(8,128)} %fusion.96), channel_id=1, source_target_pairs={{0,8},{4,12},{8,16},{12,20},{16,24},{20,28},{1,9},{5,13},{9,17},{1... | collective-permute-start | bytes 786440 | tf_op jit(solution)/shard_map/ppermute | solution.py:106
  38.4 14.1 %collective-permute-start.8 = (f32[2,1,32,128]{3,2,1,0:T(8,128)}, f32[2,1,32,128]{3,2,1,0:T(8,128)S(1)}, u32[]{:S(2)}, u32[]{:S(2)}) collective-permute-start(f32[2,1,32,128]{3,2,1,0:T(8,128)} %get-tuple-element.43), channel_id=1, source_target_pairs={{4,0},{8,4},{12,8},{16,12},{20,16},{24,20},{28,24},{5,1},{9,5},{13... | collective-permute-start | bytes 98312 | tf_op jit(solution)/shard_map/ppermute | solution.py:33
  42.8 9.8 %collective-permute-start.6 = (f32[2,8,1,128]{3,2,1,0:T(1,128)}, f32[2,8,1,128]{3,2,1,0:T(1,128)}, u32[]{:S(2)}, u32[]{:S(2)}) collective-permute-start(f32[2,8,1,128]{3,2,1,0:T(1,128)} %get-tuple-element.44), channel_id=1, source_target_pairs={{0,1},{1,2},{2,3},{4,5},{5,6},{6,7},{8,9},{9,10},{10,11},{12,13},{... | collective-permute-start | bytes 24584 | tf_op jit(solution)/shard_map/ppermute | solution.py:33
  46.4 2.0 %copy-start.8 = (f32[2,8,1,128]{3,2,1,0:T(1,128)}, f32[2,8,1,128]{3,2,1,0:T(1,128)S(1)}, u32[]{:S(2)}) copy-start(f32[2,8,1,128]{3,2,1,0:T(1,128)S(1)} %collective-permute-done.7) | copy-start | bytes 24580
  46.4 6.2 %collective-permute-start.5 = (f32[2,1,32,128]{3,2,1,0:T(8,128)}, f32[2,1,32,128]{3,2,1,0:T(8,128)}, u32[]{:S(2)}, u32[]{:S(2)}) collective-permute-start(f32[2,1,32,128]{3,2,1,0:T(8,128)} %get-tuple-element.42), channel_id=1, source_target_pairs={{0,4},{4,8},{8,12},{12,16},{16,20},{20,24},{24,28},{1,5},{5,9},{9,... | collective-permute-start | bytes 98312 | tf_op jit(solution)/shard_map/ppermute | solution.py:33
  48.4 11.3 %copy-start.7 = (f32[32,128]{1,0:T(8,128)S(1)}, f32[32,128]{1,0:T(8,128)}, u32[]{:S(2)}) copy-start(f32[32,128]{1,0:T(8,128)} %param.14) | copy-start | bytes 49156
  52.5 27.9 %copy-start = (bf16[64,8,32,128]{3,2,1,0:T(8,128)(2,1)S(1)}, bf16[64,8,32,128]{3,2,1,0:T(8,128)(2,1)}, u32[]{:S(2)}) copy-start(bf16[64,8,32,128]{3,2,1,0:T(8,128)(2,1)} %param.11) | copy-start | bytes 12582916
  52.5 27.9 %copy-start.3 = (f32[64,32,128]{2,1,0:T(8,128)S(1)}, f32[64,32,128]{2,1,0:T(8,128)}, u32[]{:S(2)}) copy-start(f32[64,32,128]{2,1,0:T(8,128)} %param.12) | copy-start | bytes 3145732
  52.6 27.9 %copy-start.9 = (f32[64]{0:T(128)S(1)}, f32[64]{0:T(128)}, u32[]{:S(2)}) copy-start(f32[64]{0:T(128)} %param.13) | copy-start | bytes 772
  56.4 7.4 %collective-permute-start.9 = (f32[16,32,128]{2,1,0:T(8,128)S(1)}, f32[16,32,128]{2,1,0:T(8,128)S(1)}, u32[]{:S(2)}, u32[]{:S(2)}) collective-permute-start(f32[16,32,128]{2,1,0:T(8,128)S(1)} %add_select_fusion.1), channel_id=1, source_target_pairs={{0,4},{4,0},{8,12},{12,8},{16,20},{20,16},{24,28},{28,24},{1,5},{5... | collective-permute-start | bytes 786440 | tf_op jit(solution)/shard_map/ppermute | solution.py:106
  58.3 12.7 %collective-permute-start.10 = (f32[16,32,128]{2,1,0:T(8,128)S(1)}, f32[16,32,128]{2,1,0:T(8,128)S(1)}, u32[]{:S(2)}, u32[]{:S(2)}) collective-permute-start(f32[16,32,128]{2,1,0:T(8,128)S(1)} %add.186), channel_id=1, source_target_pairs={{0,16},{4,20},{8,24},{12,28},{1,17},{5,21},{9,25},{13,29},{2,18},{... | collective-permute-start | bytes 786440 | tf_op jit(solution)/shard_map/ppermute | solution.py:106
  73.1 7.2 %collective-permute-start.11 = (f32[16,32,128]{2,1,0:T(8,128)S(1)}, f32[16,32,128]{2,1,0:T(8,128)S(1)}, u32[]{:S(2)}, u32[]{:S(2)}) collective-permute-start(f32[16,32,128]{2,1,0:T(8,128)S(1)} %add_select_fusion), channel_id=1, source_target_pairs={{0,4},{4,0},{8,12},{12,8},{16,20},{20,16},{24,28},{28,24},{1,5},{5... | collective-permute-start | bytes 786440 | tf_op jit(solution)/shard_map/ppermute | solution.py:106
  80.4 6.8 %copy-start.2 = (f32[8,32,128]{2,1,0:T(8,128)S(1)}, f32[8,32,128]{2,1,0:T(8,128)}, u32[]{:S(2)}) copy-start(f32[8,32,128]{2,1,0:T(8,128)} %param.9) | copy-start | bytes 393220
  87.6 12.5 %collective-permute-start.15 = (f32[2,1,32,128]{3,2,1,0:T(8,128)S(1)}, f32[2,1,32,128]{3,2,1,0:T(8,128)S(1)}, u32[]{:S(2)}, u32[]{:S(2)}) collective-permute-start(f32[2,1,32,128]{3,2,1,0:T(8,128)S(1)} %get-tuple-element.39), channel_id=1, source_target_pairs={{4,0},{8,4},{12,8},{16,12},{20,16},{24,20},{28,24},{5,1},{9,5},{13... | collective-permute-start | bytes 98312 | tf_op jit(solution)/shard_map/ppermute | solution.py:33
  89.5 10.5 %collective-permute-start.12 = (f32[2,1,32,128]{3,2,1,0:T(8,128)S(1)}, f32[2,1,32,128]{3,2,1,0:T(8,128)S(1)}, u32[]{:S(2)}, u32[]{:S(2)}) collective-permute-start(f32[2,1,32,128]{3,2,1,0:T(8,128)S(1)} %get-tuple-element.38), channel_id=1, source_target_pairs={{0,4},{4,8},{8,12},{12,16},{16,20},{20,24},{24,28},{1,5},{5,9},{9,... | collective-permute-start | bytes 98312 | tf_op jit(solution)/shard_map/ppermute | solution.py:33
  92.9 6.0 %collective-permute-start.14 = (f32[2,8,1,128]{3,2,1,0:T(1,128)S(1)}, f32[2,8,1,128]{3,2,1,0:T(1,128)S(1)}, u32[]{:S(2)}, u32[]{:S(2)}) collective-permute-start(f32[2,8,1,128]{3,2,1,0:T(1,128)S(1)} %get-tuple-element.41), channel_id=1, source_target_pairs={{1,0},{2,1},{3,2},{5,4},{6,5},{7,6},{9,8},{10,9},{11,10},{13,12},{... | collective-permute-start | bytes 24584 | tf_op jit(solution)/shard_map/ppermute | solution.py:33
  97.0 3.1 %collective-permute-start.13 = (f32[2,8,1,128]{3,2,1,0:T(1,128)S(1)}, f32[2,8,1,128]{3,2,1,0:T(1,128)S(1)}, u32[]{:S(2)}, u32[]{:S(2)}) collective-permute-start(f32[2,8,1,128]{3,2,1,0:T(1,128)S(1)} %get-tuple-element.40), channel_id=1, source_target_pairs={{0,1},{1,2},{2,3},{4,5},{5,6},{6,7},{8,9},{9,10},{10,11},{12,13},{... | collective-permute-start | bytes 24584 | tf_op jit(solution)/shard_map/ppermute | solution.py:33

commit v8 on v7

--- a/solution.py
+++ b/solution.py
@@ -92,31 +92,37 @@
     return [(i, i + shift) for i in range(count - shift)]
 
 
-def pipelined_scan(totals, axis, rider, groups=2):
+def pipelined_scan(totals_of, emit, lines, axis, rider, groups=2):
     count = lax.axis_size(axis)
-    lines = totals.shape[0]
     if count % 2 or count <= 2 or lines % (2 * groups):
-        return exclusive_scan(totals, axis), rider(None)
+        earlier = exclusive_scan(totals_of(0, lines, None), axis)
+        return [emit(0, lines, earlier)], rider(None)
     size = lines // groups
-    steps = [paired_steps(totals[g * size : (g + 1) * size], axis) for g in range(groups)]
-    live, done, carried, stage = {}, {}, None, 0
+    steps = [None] * groups
+    steps[0] = paired_steps(totals_of(0, size, None), axis)
+    live, made, carried, stage = {}, [], None, 0
     while stage < groups or live:
         if stage < groups:
             live[stage] = next(steps[stage])
         arrived = {g: lax.ppermute(payload, axis, pairs) for g, (payload, pairs) in live.items()}
+        if stage == 0:
+            for g in range(1, groups):
+                steps[g] = paired_steps(totals_of(g * size, size, live[0][0]), axis)
+        tied = (arrived, made)
         if stage == 2:
-            arrived, carried = lax.optimization_barrier((arrived, rider(live[0][0])))
+            tied, carried = lax.optimization_barrier((tied, rider(live[0][0])))
         else:
-            arrived = lax.optimization_barrier(arrived)
+            tied = lax.optimization_barrier(tied)
+        arrived, made = tied
         following = {}
         for g, value in arrived.items():
             try:
                 following[g] = steps[g].send(value)
             except StopIteration as finished:
-                done[g] = finished.value
+                made = made + [emit(g * size, size, finished.value)]
         live = following
         stage += 1
-    return jnp.concatenate([done[g] for g in range(groups)]), carried
+    return made, carried
 
 
 def window(source, step_beam, step_cross, step_depth):
@@ -176,26 +182,51 @@
         absorb_scale / total_rows * rubidium_number_amount * (1.0 - rubidium_polarization_old)
     )
     glass_term = glass_depth * glass_cells
-    weight = spectral_attenuation_section[:, None, None, None] / (
-        1.0 + earlier_spectral_power.astype(jnp.float32) / saturation
-    )
-    optical_depth = absorber[None] * weight + glass_term[None]
-    totals = jnp.sum(optical_depth, axis=1)
-    local_column = jnp.pad(
-        jnp.cumsum(optical_depth[:, : rows - 1], axis=1), ((0, 0), (1, 0), (0, 0), (0, 0))
-    )
+
+    def depth_of(start, size):
+        weight = spectral_attenuation_section[start : start + size, None, None, None] / (
+            1.0 + earlier_spectral_power[start : start + size].astype(jnp.float32) / saturation
+        )
+        return absorber[None] * weight + glass_term[None], weight
+
+    def totals_of(start, size, after):
+        optical_depth, _ = depth_of(start, size)
+        if after is not None:
+            optical_depth, _ = lax.optimization_barrier((optical_depth, after))
+        return jnp.sum(optical_depth, axis=1)
+
+    def emit(start, size, earlier):
+        optical_depth, weight = depth_of(start, size)
+        local_column = jnp.pad(
+            jnp.cumsum(optical_depth[:, : rows - 1], axis=1), ((0, 0), (1, 0), (0, 0), (0, 0))
+        )
+        column = earlier[:, None] + local_column
+        radiance = entry_spectral_power[start : start + size, None] * jnp.exp(-column)
+        return (
+            radiance.astype(jnp.bfloat16),
+            jnp.sum(weight * radiance, axis=0),
+            jnp.sum(radiance * (1.0 - jnp.exp(-optical_depth)), axis=0),
+        )
+
     def first_border(after):
         fields = physical_quantities
         if after is not None:
             fields, _ = lax.optimization_barrier((fields, after))
         return bordered_fields(fields)
 
-    prefix, first_bordered = pipelined_scan(totals, "beam", first_border)
-    column = prefix[:, None] + local_column
-    radiance = entry_spectral_power[:, None] * jnp.exp(-column)
-    spectral_power = radiance.astype(jnp.bfloat16)
-    pumping = pump_scale * jnp.sum(weight * radiance, axis=0)
-    heating = jnp.sum(radiance * (1.0 - jnp.exp(-optical_depth)), axis=0)
+    lines = earlier_spectral_power.shape[0]
+    made, first_bordered = pipelined_scan(totals_of, emit, lines, "beam", first_border)
+    spectral_power = jnp.zeros(earlier_spectral_power.shape, jnp.bfloat16)
+    start = 0
+    for part, _, _ in made:
+        spectral_power = lax.dynamic_update_slice_in_dim(spectral_power, part, start, axis=0)
+        start += part.shape[0]
+    pumping = made[0][1]
+    heating = made[0][2]
+    for _, part_pumping, part_heating in made[1:]:
+        pumping = pumping + part_pumping
+        heating = heating + part_heating
+    pumping = pump_scale * pumping
     spin_ratio = pumping / (pumping + spin_decay * (1.0 + rubidium_number_amount))
     rubidium_polarization_new = fluid_occupied_sites * spin_ratio
     drift_speed = flow_scale * flow_rate_forward

time: 104 us -> 92 us (0.88)
  waiting for transfers between devices: 28.9 us -> 19.8 us
  other arithmetic: 31.2 us -> 26.8 us
  starting transfers between devices: 39.6 us -> 41.3 us
    ppermute x8, waiting for transfers between devices: 27.7 us -> 16.2 us  [pipelined_scan(): lax.ppermute(payload, axis, pairs)]
    ppermute x8, waiting for transfers between devices: 1.17 us -> 3.61 us  [shifted(): return lax.ppermute(block, axis, pairs)]
    dynamic_update_slice x0 -> x1, other arithmetic: none -> 2.38 us  [local(): lax.dynamic_update_slice_in_dim(spectral_power, part, start, axis=0)]
    add x2, other arithmetic: 2.35 us -> 0.12 us  [paired_steps(): before + got]
    select_n x2, other arithmetic: 2.18 us -> 0.13 us  [paired_steps(): back = (yield (jnp.where(is_low, before + mine, before), swap))]
    ppermute x8, starting transfers between devices: 25.8 us -> 27.8 us  [shifted(): return lax.ppermute(block, axis, pairs)]
    add x2, other arithmetic: 1.81 us -> 0.08 us  [paired_steps(): through = pair_total + before]
    reduce_sum x2 -> x4, other arithmetic: 12.9 us -> 13.7 us  [the longest x2 8.66 us: totals_of(): return jnp.sum(optical_depth, axis=1)]
  transfers between devices with their start and end apart: 16 -> 16, of which waited for: 7 -> 6; matrix products, arithmetic and copies ran while one was open for 10% -> 15% of each run, Pallas kernels for 0% -> 0%
where the time goes in v8:
time: 92 us; the launch traced here: 90.2 us
  starting transfers between devices  41.3 us (45%)
  other arithmetic  26.8 us (29%)
  waiting for transfers between devices  19.8 us (22%)
  local copies, waits for them, and re-layouts  1.14 us (1%)
  between operations  1.08 us (1%)
    ppermute x8, starting transfers between devices, shifted(): return lax.ppermute(block, axis, pairs)  27.8 us
    ppermute x8, waiting for transfers between devices, pipelined_scan(): lax.ppermute(payload, axis, pairs)  16.2 us
    ppermute x8, starting transfers between devices, pipelined_scan(): lax.ppermute(payload, axis, pairs)  13.5 us
    reduce_sum x2, other arithmetic, totals_of(): return jnp.sum(optical_depth, axis=1)  8.66 us
    reduce_sum x2, other arithmetic, emit(): jnp.sum(radiance * (1.0 - jnp.exp(-optical_depth)), axis=0)  5.04 us
    another operation x2, other arithmetic, emit(): jnp.cumsum(optical_depth[:, :rows - 1], axis=1)  3.69 us
    ppermute x8, waiting for transfers between devices, shifted(): return lax.ppermute(block, axis, pairs)  3.61 us
    dynamic_update_slice x1, other arithmetic, local(): lax.dynamic_update_slice_in_dim(spectral_power, part, start, axis=0)  2.38 us
  transfers between devices with their start and end apart: 16, of which 6 were waited for; matrix products, arithmetic and copies ran while one was open for 15% of the time, Pallas kernels for 0%

profile of v8, /device:TPU:9, one launch (start us, length us, event | category | flops | bytes accessed | tf_op | source)
XLA Modules:
  0.0 90.2 jit_solution(6159431450041724962)
XLA Ops:
  0.6 0.7 convert_subtract_fusion
  1.3 0.8 fusion.113
  2.1 1.1 %add_bitcast_fusion = (f32[1,8,32,128]{3,2,1,0:T(8,128)S(1)}, f32[8,32,128]{2,1,0:T(8,128)S(1)}) fusion(f32[8,32,128]{2,1,0:T(8,128)} %param.9, f32[8,32,128]{2,1,0:T(8,128)} %param.10, f32[8,32]{1,0:T(8,128)S(1)} %get-tuple-element.65), kind=kLoop, calls=%fused_computation.192 | loop fusion | flops 262144 | bytes 525312 | tf_op jit(solution)/shard_map/stack | solution.py:175
  3.2 5.9 %fusion.109 = (f32[32,32,128]{2,1,0:T(8,128)S(1)}, f32[32,8,32,128]{3,2,1,0:T(8,128)}, f32[32,8,32,128]{3,2,1,0:T(8,128)}) fusion(f32[8,32]{1,0:T(8,128)S(1)} %get-tuple-element.66, bf16[64,8,32,128]{3,2,1,0:T(8,128)(2,1)} %param.11, f32[32]{0:T(128)S(1)} %get-tuple-element.67, f32[8,32,128]{2,1,0:T(8,128)S(1)} %get-tuple-element.64, ...), kind=kLoop, calls=%fused_computation.209 | loop fusion | flops 11403264 | bytes 13239552 | tf_op jit(solution)/shard_map/reduce_sum | solution.py:196
  9.2 1.3 %collective-permute-start = (f32[16,32,128]{2,1,0:T(8,128)S(1)}, f32[16,32,128]{2,1,0:T(8,128)S(1)}, u32[]{:S(2)}, u32[]{:S(2)}) collective-permute-start(f32[16,32,128]{2,1,0:T(8,128)S(1)} %slice_select_fusion.2), channel_id=1, source_target_pairs={{0,4},{4,0},{8,12},{12,8},{16,20},{20,16},{24,28},{28,24},{1,5},{5... | collective-permute-start | bytes 786440 | tf_op jit(solution)/shard_map/ppermute | solution.py:107
  10.5 2.7 %reduce_sum.55 = f32[32,32,128]{2,1,0:T(8,128)S(1)} reduce(f32[32,8,32,128]{3,2,1,0:T(8,128)} %get-tuple-element.17, f32[]{:T(128)} %constant.18.clone.1), dimensions={1}, to_apply=%region_1.2 | reduce | flops 917504 | bytes 4718596 | tf_op jit(solution)/shard_map/reduce_sum | solution.py:196
  13.3 0.0 copy-start
  13.3 0.3 collective-permute-start.2
  13.6 2.8 %fusion = f32[32,7,32,128]{3,2,1,0:T(8,128)S(1)} fusion(f32[32,8,32,128]{3,2,1,0:T(8,128)} %get-tuple-element.17), kind=kOutput, calls=%fused_computation.11 | output fusion | flops 5505024 | bytes 7340032 | tf_op jit(solution)/shard_map/jit(cumsum)/reduce_window_sum | solution.py:201
  16.4 0.0 copy-start.4
  16.4 0.0 collective-permute-done
  16.4 0.1 fusion.99
  16.5 3.2 %collective-permute-start.1 = (f32[16,32,128]{2,1,0:T(8,128)S(1)}, f32[16,32,128]{2,1,0:T(8,128)S(1)}, u32[]{:S(2)}, u32[]{:S(2)}) collective-permute-start(f32[16,32,128]{2,1,0:T(8,128)S(1)} %fusion.99), channel_id=1, source_target_pairs={{0,8},{4,12},{8,16},{12,20},{16,24},{20,28},{1,9},{5,13},{9,17},{1... | collective-permute-start | bytes 786440 | tf_op jit(solution)/shard_map/ppermute | solution.py:107
  19.7 0.0 copy-start.5
  19.7 0.9 fusion.2
  20.6 1.4 %collective-permute-done.2 = f32[16,32,128]{2,1,0:T(8,128)S(1)} collective-permute-done((f32[16,32,128]{2,1,0:T(8,128)S(1)}, f32[16,32,128]{2,1,0:T(8,128)S(1)}, u32[]{:S(2)}, u32[]{:S(2)}) %collective-permute-start.2) | collective-permute-done | bytes 262176 | tf_op jit(solution)/shard_map/ppermute | solution.py:107
  22.0 1.6 %collective-permute-done.1 = f32[16,32,128]{2,1,0:T(8,128)S(1)} collective-permute-done((f32[16,32,128]{2,1,0:T(8,128)S(1)}, f32[16,32,128]{2,1,0:T(8,128)S(1)}, u32[]{:S(2)}, u32[]{:S(2)}) %collective-permute-start.1) | collective-permute-done | bytes 262176 | tf_op jit(solution)/shard_map/ppermute | solution.py:107
  23.7 4.2 %collective-permute-start.3 = (f32[16,32,128]{2,1,0:T(8,128)S(1)}, f32[16,32,128]{2,1,0:T(8,128)S(1)}, u32[]{:S(2)}, u32[]{:S(2)}) collective-permute-start(f32[16,32,128]{2,1,0:T(8,128)S(1)} %add.215), channel_id=1, source_target_pairs={{0,16},{4,20},{8,24},{12,28},{1,17},{5,21},{9,25},{13,29},{2,18},{... | collective-permute-start | bytes 786440 | tf_op jit(solution)/shard_map/ppermute | solution.py:107
  27.9 0.1 fusion.100
  28.0 6.0 %collective-permute-start.7 = (f32[2,8,1,128]{3,2,1,0:T(1,128)S(1)}, f32[2,8,1,128]{3,2,1,0:T(1,128)S(1)}, u32[]{:S(2)}, u32[]{:S(2)}) collective-permute-start(f32[2,8,1,128]{3,2,1,0:T(1,128)S(1)} %get-tuple-element.62), channel_id=1, source_target_pairs={{1,0},{2,1},{3,2},{5,4},{6,5},{7,6},{9,8},{10,9},{11,10},{13,12},{... | collective-permute-start | bytes 24584 | tf_op jit(solution)/shard_map/ppermute | solution.py:33
  34.0 1.9 %collective-permute-start.4 = (f32[16,32,128]{2,1,0:T(8,128)S(1)}, f32[16,32,128]{2,1,0:T(8,128)S(1)}, u32[]{:S(2)}, u32[]{:S(2)}) collective-permute-start(f32[16,32,128]{2,1,0:T(8,128)S(1)} %fusion.100), channel_id=1, source_target_pairs={{0,8},{4,12},{8,16},{12,20},{16,24},{20,28},{1,9},{5,13},{9,17},{1... | collective-permute-start | bytes 786440 | tf_op jit(solution)/shard_map/ppermute | solution.py:107
  35.9 4.3 %collective-permute-start.8 = (f32[2,1,32,128]{3,2,1,0:T(8,128)S(1)}, f32[2,1,32,128]{3,2,1,0:T(8,128)S(1)}, u32[]{:S(2)}, u32[]{:S(2)}) collective-permute-start(f32[2,1,32,128]{3,2,1,0:T(8,128)S(1)} %get-tuple-element.60), channel_id=1, source_target_pairs={{4,0},{8,4},{12,8},{16,12},{20,16},{24,20},{28,24},{5,1},{9,5},{13... | collective-permute-start | bytes 98312 | tf_op jit(solution)/shard_map/ppermute | solution.py:33
  40.3 3.6 %collective-permute-start.6 = (f32[2,8,1,128]{3,2,1,0:T(1,128)S(1)}, f32[2,8,1,128]{3,2,1,0:T(1,128)S(1)}, u32[]{:S(2)}, u32[]{:S(2)}) collective-permute-start(f32[2,8,1,128]{3,2,1,0:T(1,128)S(1)} %get-tuple-element.61), channel_id=1, source_target_pairs={{0,1},{1,2},{2,3},{4,5},{5,6},{6,7},{8,9},{9,10},{10,11},{12,13},{... | collective-permute-start | bytes 24584 | tf_op jit(solution)/shard_map/ppermute | solution.py:33
  43.8 0.0 collective-permute-done.7
  43.9 1.9 %collective-permute-start.5 = (f32[2,1,32,128]{3,2,1,0:T(8,128)S(1)}, f32[2,1,32,128]{3,2,1,0:T(8,128)S(1)}, u32[]{:S(2)}, u32[]{:S(2)}) collective-permute-start(f32[2,1,32,128]{3,2,1,0:T(8,128)S(1)} %get-tuple-element.59), channel_id=1, source_target_pairs={{0,4},{4,8},{8,12},{12,16},{16,20},{20,24},{24,28},{1,5},{5,9},{9,... | collective-permute-start | bytes 98312 | tf_op jit(solution)/shard_map/ppermute | solution.py:33
  45.8 0.0 collective-permute-done.6
  45.8 0.0 collective-permute-done.8
  45.8 3.6 %collective-permute-done.5 = f32[2,1,32,128]{3,2,1,0:T(8,128)S(1)} collective-permute-done((f32[2,1,32,128]{3,2,1,0:T(8,128)S(1)}, f32[2,1,32,128]{3,2,1,0:T(8,128)S(1)}, u32[]{:S(2)}, u32[]{:S(2)}) %collective-permute-start.5) | collective-permute-done | bytes 32800 | tf_op jit(solution)/shard_map/ppermute | solution.py:33
  49.4 0.1 fusion.7
  49.5 0.3 pad.15
  49.7 0.0 collective-permute-done.3
  49.8 0.0 collective-permute-done.4
  49.8 0.1 fusion.108
  49.8 0.0 copy-start.3
  49.8 0.1 add_select_fusion.1
  49.9 0.1 collective-permute-start.9
  50.0 1.4 %collective-permute-start.10 = (f32[16,32,128]{2,1,0:T(8,128)S(1)}, f32[16,32,128]{2,1,0:T(8,128)S(1)}, u32[]{:S(2)}, u32[]{:S(2)}) collective-permute-start(f32[16,32,128]{2,1,0:T(8,128)S(1)} %add.219), channel_id=1, source_target_pairs={{0,16},{4,20},{8,24},{12,28},{1,17},{5,21},{9,25},{13,29},{2,18},{... | collective-permute-start | bytes 786440 | tf_op jit(solution)/shard_map/ppermute | solution.py:107
  51.5 0.4 power_multiply_fusion.2
  51.9 0.0 copy-start.1
  51.9 0.9 fusion.47
  52.8 5.1 %collective-permute-done.9 = f32[16,32,128]{2,1,0:T(8,128)S(1)} collective-permute-done((f32[16,32,128]{2,1,0:T(8,128)S(1)}, f32[16,32,128]{2,1,0:T(8,128)S(1)}, u32[]{:S(2)}, u32[]{:S(2)}) %collective-permute-start.9) | collective-permute-done | bytes 262176 | tf_op jit(solution)/shard_map/ppermute | solution.py:107
  57.9 4.8 %collective-permute-done.10 = f32[16,32,128]{2,1,0:T(8,128)S(1)} collective-permute-done((f32[16,32,128]{2,1,0:T(8,128)S(1)}, f32[16,32,128]{2,1,0:T(8,128)S(1)}, u32[]{:S(2)}, u32[]{:S(2)}) %collective-permute-start.10) | collective-permute-done | bytes 262176 | tf_op jit(solution)/shard_map/ppermute | solution.py:107
  62.7 0.1 fusion.107
  62.8 0.1 add_select_fusion
  62.9 1.1 %collective-permute-start.11 = (f32[16,32,128]{2,1,0:T(8,128)S(1)}, f32[16,32,128]{2,1,0:T(8,128)S(1)}, u32[]{:S(2)}, u32[]{:S(2)}) collective-permute-start(f32[16,32,128]{2,1,0:T(8,128)S(1)} %add_select_fusion), channel_id=1, source_target_pairs={{0,4},{4,0},{8,12},{12,8},{16,20},{20,16},{24,28},{28,24},{1,5},{5... | collective-permute-start | bytes 786440 | tf_op jit(solution)/shard_map/ppermute | solution.py:107
  63.9 0.2 fusion.110
  64.2 2.4 %multiply_reduce_fusion.2 = (f32[8,32,128]{2,1,0:T(8,128)S(1)}, f32[8,32,128]{2,1,0:T(8,128)S(1)}, bf16[32,8,32,128]{3,2,1,0:T(8,128)(2,1)S(1)}) fusion(f32[32,8,32,128]{3,2,1,0:T(8,128)S(1)} %copy-done, f32[32,7,32,128]{3,2,1,0:T(8,128)S(1)} %fusion.2, f32[32,32,128]{2,1,0:T(8,128)S(1)} %get-tuple-element.69, f32[32,32,128]{2,1,0:T(8,128)S(1)} %get-tuple-element.50, ...), kind=kLoop, calls=%fused_computation.4 | loop fusion | flops 13565952 | bytes 13369472 | tf_op jit(solution)/shard_map/reduce_sum | solution.py:208
  66.5 3.3 %collective-permute-done.11 = f32[16,32,128]{2,1,0:T(8,128)S(1)} collective-permute-done((f32[16,32,128]{2,1,0:T(8,128)S(1)}, f32[16,32,128]{2,1,0:T(8,128)S(1)}, u32[]{:S(2)}, u32[]{:S(2)}) %collective-permute-start.11) | collective-permute-done | bytes 262176 | tf_op jit(solution)/shard_map/ppermute | solution.py:107
  69.9 0.1 maximum_select_fusion.1
  69.9 0.0 copy-start.2
  70.0 2.7 %multiply_reduce_fusion = (f32[8,32,128]{2,1,0:T(8,128)S(1)}, f32[8,32,128]{2,1,0:T(8,128)S(1)}, bf16[32,8,32,128]{3,2,1,0:T(8,128)(2,1)S(1)}) fusion(f32[32,7,32,128]{3,2,1,0:T(8,128)S(1)} %fusion, f32[32,32,128]{2,1,0:T(8,128)S(1)} %maximum_select_fusion.1, f32[32,32,128]{2,1,0:T(8,128)S(1)} %get-tuple-element.49, f32[8,32]{1,0:T(8,128)S(1)} %get-tuple-element.66, ...), kind=kLoop, calls=%fused_computation.1 | loop fusion | flops 15663104 | bytes 9307264 | tf_op jit(solution)/shard_map/reduce_sum | solution.py:208
  72.6 0.8 broadcast_multiply_fusion
  73.4 0.2 fusion.105
  73.6 1.9 %collective-permute-start.15 = (f32[2,1,32,128]{3,2,1,0:T(8,128)S(1)}, f32[2,1,32,128]{3,2,1,0:T(8,128)S(1)}, u32[]{:S(2)}, u32[]{:S(2)}) collective-permute-start(f32[2,1,32,128]{3,2,1,0:T(8,128)S(1)} %get-tuple-element.56), channel_id=1, source_target_pairs={{4,0},{8,4},{12,8},{16,12},{20,16},{24,20},{28,24},{5,1},{9,5},{13... | collective-permute-start | bytes 98312 | tf_op jit(solution)/shard_map/ppermute | solution.py:33
  75.5 3.7 %collective-permute-start.14 = (f32[2,8,1,128]{3,2,1,0:T(1,128)S(1)}, f32[2,8,1,128]{3,2,1,0:T(1,128)S(1)}, u32[]{:S(2)}, u32[]{:S(2)}) collective-permute-start(f32[2,8,1,128]{3,2,1,0:T(1,128)S(1)} %get-tuple-element.58), channel_id=1, source_target_pairs={{1,0},{2,1},{3,2},{5,4},{6,5},{7,6},{9,8},{10,9},{11,10},{13,12},{... | collective-permute-start | bytes 24584 | tf_op jit(solution)/shard_map/ppermute | solution.py:33
  79.2 2.7 %collective-permute-start.13 = (f32[2,8,1,128]{3,2,1,0:T(1,128)S(1)}, f32[2,8,1,128]{3,2,1,0:T(1,128)S(1)}, u32[]{:S(2)}, u32[]{:S(2)}) collective-permute-start(f32[2,8,1,128]{3,2,1,0:T(1,128)S(1)} %get-tuple-element.57), channel_id=1, source_target_pairs={{0,1},{1,2},{2,3},{4,5},{5,6},{6,7},{8,9},{9,10},{10,11},{12,13},{... | collective-permute-start | bytes 24584 | tf_op jit(solution)/shard_map/ppermute | solution.py:33
  82.0 3.6 %collective-permute-start.12 = (f32[2,1,32,128]{3,2,1,0:T(8,128)S(1)}, f32[2,1,32,128]{3,2,1,0:T(8,128)S(1)}, u32[]{:S(2)}, u32[]{:S(2)}) collective-permute-start(f32[2,1,32,128]{3,2,1,0:T(8,128)S(1)} %get-tuple-element.55), channel_id=1, source_target_pairs={{0,4},{4,8},{8,12},{12,16},{16,20},{20,24},{24,28},{1,5},{5,9},{9,... | collective-permute-start | bytes 98312 | tf_op jit(solution)/shard_map/ppermute | solution.py:33
  85.6 2.4 %pad_maximum_fusion = bf16[64,8,32,128]{3,2,1,0:T(8,128)(2,1)} fusion(bf16[32,8,32,128]{3,2,1,0:T(8,128)(2,1)S(1)} %get-tuple-element.42, bf16[32,8,32,128]{3,2,1,0:T(8,128)(2,1)S(1)} %get-tuple-element.25), kind=kLoop, calls=%fused_computation | loop fusion | flops 2097152 | bytes 8388608 | tf_op jit(solution)/shard_map/dynamic_update_slice | solution.py:222
  88.0 0.0 collective-permute-done.14
  88.0 0.0 collective-permute-done.15
  88.0 0.0 collective-permute-done.12
  88.1 0.5 power_multiply_fusion
  88.6 0.6 fusion.15
  89.3 0.9 fusion.85
  (19 shorter events, 0.3 us)
Async XLA Ops:
  9.2 7.3 %collective-permute-start = (f32[16,32,128]{2,1,0:T(8,128)S(1)}, f32[16,32,128]{2,1,0:T(8,128)S(1)}, u32[]{:S(2)}, u32[]{:S(2)}) collective-permute-start(f32[16,32,128]{2,1,0:T(8,128)S(1)} %slice_select_fusion.2), channel_id=1, source_target_pairs={{0,4},{4,0},{8,12},{12,8},{16,20},{20,16},{24,28},{28,24},{1,5},{5... | collective-permute-start | bytes 786440 | tf_op jit(solution)/shard_map/ppermute | solution.py:107
  13.3 6.4 %copy-start = (f32[32,8,32,128]{3,2,1,0:T(8,128)S(1)}, f32[32,8,32,128]{3,2,1,0:T(8,128)}, u32[]{:S(2)}) copy-start(f32[32,8,32,128]{3,2,1,0:T(8,128)} %get-tuple-element.41) | copy-start | bytes 12582916
  13.3 8.7 %collective-permute-start.2 = (f32[16,32,128]{2,1,0:T(8,128)S(1)}, f32[16,32,128]{2,1,0:T(8,128)S(1)}, u32[]{:S(2)}, u32[]{:S(2)}) collective-permute-start(f32[16,32,128]{2,1,0:T(8,128)S(1)} %slice_select_fusion.1), channel_id=1, source_target_pairs={{0,4},{4,0},{8,12},{12,8},{16,20},{20,16},{24,28},{28,24},{1,5},{5... | collective-permute-start | bytes 786440 | tf_op jit(solution)/shard_map/ppermute | solution.py:107
  16.4 4.2 %copy-start.4 = (f32[8,32,128]{2,1,0:T(8,128)S(1)}, f32[8,32,128]{2,1,0:T(8,128)}, u32[]{:S(2)}) copy-start(f32[8,32,128]{2,1,0:T(8,128)} %param.8) | copy-start | bytes 393220
  16.5 7.1 %collective-permute-start.1 = (f32[16,32,128]{2,1,0:T(8,128)S(1)}, f32[16,32,128]{2,1,0:T(8,128)S(1)}, u32[]{:S(2)}, u32[]{:S(2)}) collective-permute-start(f32[16,32,128]{2,1,0:T(8,128)S(1)} %fusion.99), channel_id=1, source_target_pairs={{0,8},{4,12},{8,16},{12,20},{16,24},{20,28},{1,9},{5,13},{9,17},{1... | collective-permute-start | bytes 786440 | tf_op jit(solution)/shard_map/ppermute | solution.py:107
  19.7 26.1 %copy-start.5 = (f32[32,128]{1,0:T(8,128)S(1)}, f32[32,128]{1,0:T(8,128)}, u32[]{:S(2)}) copy-start(f32[32,128]{1,0:T(8,128)} %param.14) | copy-start | bytes 49156
  23.7 26.1 %collective-permute-start.3 = (f32[16,32,128]{2,1,0:T(8,128)S(1)}, f32[16,32,128]{2,1,0:T(8,128)S(1)}, u32[]{:S(2)}, u32[]{:S(2)}) collective-permute-start(f32[16,32,128]{2,1,0:T(8,128)S(1)} %add.215), channel_id=1, source_target_pairs={{0,16},{4,20},{8,24},{12,28},{1,17},{5,21},{9,25},{13,29},{2,18},{... | collective-permute-start | bytes 786440 | tf_op jit(solution)/shard_map/ppermute | solution.py:107
  28.0 15.9 %collective-permute-start.7 = (f32[2,8,1,128]{3,2,1,0:T(1,128)S(1)}, f32[2,8,1,128]{3,2,1,0:T(1,128)S(1)}, u32[]{:S(2)}, u32[]{:S(2)}) collective-permute-start(f32[2,8,1,128]{3,2,1,0:T(1,128)S(1)} %get-tuple-element.62), channel_id=1, source_target_pairs={{1,0},{2,1},{3,2},{5,4},{6,5},{7,6},{9,8},{10,9},{11,10},{13,12},{... | collective-permute-start | bytes 24584 | tf_op jit(solution)/shard_map/ppermute | solution.py:33
  34.0 15.8 %collective-permute-start.4 = (f32[16,32,128]{2,1,0:T(8,128)S(1)}, f32[16,32,128]{2,1,0:T(8,128)S(1)}, u32[]{:S(2)}, u32[]{:S(2)}) collective-permute-start(f32[16,32,128]{2,1,0:T(8,128)S(1)} %fusion.100), channel_id=1, source_target_pairs={{0,8},{4,12},{8,16},{12,20},{16,24},{20,28},{1,9},{5,13},{9,17},{1... | collective-permute-start | bytes 786440 | tf_op jit(solution)/shard_map/ppermute | solution.py:107
  35.9 9.9 %collective-permute-start.8 = (f32[2,1,32,128]{3,2,1,0:T(8,128)S(1)}, f32[2,1,32,128]{3,2,1,0:T(8,128)S(1)}, u32[]{:S(2)}, u32[]{:S(2)}) collective-permute-start(f32[2,1,32,128]{3,2,1,0:T(8,128)S(1)} %get-tuple-element.60), channel_id=1, source_target_pairs={{4,0},{8,4},{12,8},{16,12},{20,16},{24,20},{28,24},{5,1},{9,5},{13... | collective-permute-start | bytes 98312 | tf_op jit(solution)/shard_map/ppermute | solution.py:33
  40.3 5.5 %collective-permute-start.6 = (f32[2,8,1,128]{3,2,1,0:T(1,128)S(1)}, f32[2,8,1,128]{3,2,1,0:T(1,128)S(1)}, u32[]{:S(2)}, u32[]{:S(2)}) collective-permute-start(f32[2,8,1,128]{3,2,1,0:T(1,128)S(1)} %get-tuple-element.61), channel_id=1, source_target_pairs={{0,1},{1,2},{2,3},{4,5},{5,6},{6,7},{8,9},{9,10},{10,11},{12,13},{... | collective-permute-start | bytes 24584 | tf_op jit(solution)/shard_map/ppermute | solution.py:33
  43.9 5.6 %collective-permute-start.5 = (f32[2,1,32,128]{3,2,1,0:T(8,128)S(1)}, f32[2,1,32,128]{3,2,1,0:T(8,128)S(1)}, u32[]{:S(2)}, u32[]{:S(2)}) collective-permute-start(f32[2,1,32,128]{3,2,1,0:T(8,128)S(1)} %get-tuple-element.59), channel_id=1, source_target_pairs={{0,4},{4,8},{8,12},{12,16},{16,20},{20,24},{24,28},{1,5},{5,9},{9,... | collective-permute-start | bytes 98312 | tf_op jit(solution)/shard_map/ppermute | solution.py:33
  49.8 14.1 %copy-start.3 = (f32[64,32,128]{2,1,0:T(8,128)S(1)}, f32[64,32,128]{2,1,0:T(8,128)}, u32[]{:S(2)}) copy-start(f32[64,32,128]{2,1,0:T(8,128)} %param.12) | copy-start | bytes 3145732
  49.9 8.0 %collective-permute-start.9 = (f32[16,32,128]{2,1,0:T(8,128)S(1)}, f32[16,32,128]{2,1,0:T(8,128)S(1)}, u32[]{:S(2)}, u32[]{:S(2)}) collective-permute-start(f32[16,32,128]{2,1,0:T(8,128)S(1)} %add_select_fusion.1), channel_id=1, source_target_pairs={{0,4},{4,0},{8,12},{12,8},{16,20},{20,16},{24,28},{28,24},{1,5},{5... | collective-permute-start | bytes 786440 | tf_op jit(solution)/shard_map/ppermute | solution.py:107
  50.0 12.7 %collective-permute-start.10 = (f32[16,32,128]{2,1,0:T(8,128)S(1)}, f32[16,32,128]{2,1,0:T(8,128)S(1)}, u32[]{:S(2)}, u32[]{:S(2)}) collective-permute-start(f32[16,32,128]{2,1,0:T(8,128)S(1)} %add.219), channel_id=1, source_target_pairs={{0,16},{4,20},{8,24},{12,28},{1,17},{5,21},{9,25},{13,29},{2,18},{... | collective-permute-start | bytes 786440 | tf_op jit(solution)/shard_map/ppermute | solution.py:107
  51.9 12.3 %copy-start.1 = (bf16[64,8,32,128]{3,2,1,0:T(8,128)(2,1)S(1)}, bf16[64,8,32,128]{3,2,1,0:T(8,128)(2,1)}, u32[]{:S(2)}) copy-start(bf16[64,8,32,128]{3,2,1,0:T(8,128)(2,1)} %param.11) | copy-start | bytes 12582916
  62.9 7.0 %collective-permute-start.11 = (f32[16,32,128]{2,1,0:T(8,128)S(1)}, f32[16,32,128]{2,1,0:T(8,128)S(1)}, u32[]{:S(2)}, u32[]{:S(2)}) collective-permute-start(f32[16,32,128]{2,1,0:T(8,128)S(1)} %add_select_fusion), channel_id=1, source_target_pairs={{0,4},{4,0},{8,12},{12,8},{16,20},{20,16},{24,28},{28,24},{1,5},{5... | collective-permute-start | bytes 786440 | tf_op jit(solution)/shard_map/ppermute | solution.py:107
  69.9 2.7 %copy-start.2 = (f32[8,32,128]{2,1,0:T(8,128)S(1)}, f32[8,32,128]{2,1,0:T(8,128)}, u32[]{:S(2)}) copy-start(f32[8,32,128]{2,1,0:T(8,128)} %param.9) | copy-start | bytes 393220
  73.6 14.4 %collective-permute-start.15 = (f32[2,1,32,128]{3,2,1,0:T(8,128)S(1)}, f32[2,1,32,128]{3,2,1,0:T(8,128)S(1)}, u32[]{:S(2)}, u32[]{:S(2)}) collective-permute-start(f32[2,1,32,128]{3,2,1,0:T(8,128)S(1)} %get-tuple-element.56), channel_id=1, source_target_pairs={{4,0},{8,4},{12,8},{16,12},{20,16},{24,20},{28,24},{5,1},{9,5},{13... | collective-permute-start | bytes 98312 | tf_op jit(solution)/shard_map/ppermute | solution.py:33
  75.5 12.4 %collective-permute-start.14 = (f32[2,8,1,128]{3,2,1,0:T(1,128)S(1)}, f32[2,8,1,128]{3,2,1,0:T(1,128)S(1)}, u32[]{:S(2)}, u32[]{:S(2)}) collective-permute-start(f32[2,8,1,128]{3,2,1,0:T(1,128)S(1)} %get-tuple-element.58), channel_id=1, source_target_pairs={{1,0},{2,1},{3,2},{5,4},{6,5},{7,6},{9,8},{10,9},{11,10},{13,12},{... | collective-permute-start | bytes 24584 | tf_op jit(solution)/shard_map/ppermute | solution.py:33
  79.2 8.8 %collective-permute-start.13 = (f32[2,8,1,128]{3,2,1,0:T(1,128)S(1)}, f32[2,8,1,128]{3,2,1,0:T(1,128)S(1)}, u32[]{:S(2)}, u32[]{:S(2)}) collective-permute-start(f32[2,8,1,128]{3,2,1,0:T(1,128)S(1)} %get-tuple-element.57), channel_id=1, source_target_pairs={{0,1},{1,2},{2,3},{4,5},{5,6},{6,7},{8,9},{9,10},{10,11},{12,13},{... | collective-permute-start | bytes 24584 | tf_op jit(solution)/shard_map/ppermute | solution.py:33
  82.0 6.0 %collective-permute-start.12 = (f32[2,1,32,128]{3,2,1,0:T(8,128)S(1)}, f32[2,1,32,128]{3,2,1,0:T(8,128)S(1)}, u32[]{:S(2)}, u32[]{:S(2)}) collective-permute-start(f32[2,1,32,128]{3,2,1,0:T(8,128)S(1)} %get-tuple-element.55), channel_id=1, source_target_pairs={{0,4},{4,8},{8,12},{12,16},{16,20},{20,24},{24,28},{1,5},{5,9},{9,... | collective-permute-start | bytes 98312 | tf_op jit(solution)/shard_map/ppermute | solution.py:33

commit v9 on v8

--- a/solution.py
+++ b/solution.py
@@ -190,9 +190,16 @@
         return absorber[None] * weight + glass_term[None], weight
 
     def totals_of(start, size, after):
+        if after is None:
+            earlier, absorbed = lax.optimization_barrier(
+                (earlier_spectral_power[start : start + size], absorber)
+            )
+            weight = spectral_attenuation_section[start : start + size, None, None, None] / (
+                1.0 + earlier.astype(jnp.float32) / saturation
+            )
+            return jnp.sum(absorbed[None] * weight + glass_term[None], axis=1)
         optical_depth, _ = depth_of(start, size)
-        if after is not None:
-            optical_depth, _ = lax.optimization_barrier((optical_depth, after))
+        optical_depth, _ = lax.optimization_barrier((optical_depth, after))
         return jnp.sum(optical_depth, axis=1)
 
     def emit(start, size, earlier):

time: 92 us -> 93.4 us (1.015)
  the two profiles are of different devices: /device:TPU:9 before, /device:TPU:22 now
where the time goes in v9:
time: 93.4 us; the launch traced here: 93 us
  starting transfers between devices  43 us (46%)
  other arithmetic  26.3 us (28%)
  waiting for transfers between devices  21.4 us (23%)
  local copies, waits for them, and re-layouts  1.25 us (1%)
  between operations  1.07 us (1%)
    ppermute x8, starting transfers between devices, shifted(): return lax.ppermute(block, axis, pairs)  28.1 us
    ppermute x8, waiting for transfers between devices, pipelined_scan(): lax.ppermute(payload, axis, pairs)  18.3 us
    ppermute x8, starting transfers between devices, pipelined_scan(): lax.ppermute(payload, axis, pairs)  14.9 us
    add x1, other arithmetic, depth_of(): return (absorber[None] * weight + glass_term[None], weight)  6.25 us
    reduce_sum x2, other arithmetic, emit(): jnp.sum(radiance * (1.0 - jnp.exp(-optical_depth)), axis=0)  5.33 us
    another operation x2, other arithmetic, emit(): jnp.cumsum(optical_depth[:, :rows - 1], axis=1)  3.54 us
    ppermute x8, waiting for transfers between devices, shifted(): return lax.ppermute(block, axis, pairs)  3.09 us
    reduce_sum x1, other arithmetic, totals_of(): return jnp.sum(optical_depth, axis=1)  2.75 us
  transfers between devices with their start and end apart: 16, of which 7 were waited for; matrix products, arithmetic and copies ran while one was open for 14% of the time, Pallas kernels for 0%

profile of v9, /device:TPU:22, one launch (start us, length us, event | category | flops | bytes accessed | tf_op | source)
XLA Modules:
  0.0 93.0 jit_solution(15519749278667438590)
XLA Ops:
  0.6 0.0 slice-start
  0.7 0.9 fusion.112
  1.6 0.7 convert_multiply_fusion
  2.3 0.1 add_bitcast_fusion
  2.4 0.0 slice-done
  2.4 6.2 %multiply_add_fusion = (f32[32,8,32,128]{3,2,1,0:T(8,128)}, f32[32,8,32,128]{3,2,1,0:T(8,128)}, f32[32,32,128]{2,1,0:T(8,128)S(1)}) fusion(f32[8,32,128]{2,1,0:T(8,128)S(1)} %get-tuple-element.19, f32[8,32]{1,0:T(8,128)S(1)} %get-tuple-element.69, f32[32]{0:T(128)S(1)} %get-tuple-element.71, bf16[64,8,32,128]{3,2,1,0:T(8,128)(2,1)} %param.11, ...), kind=kLoop, calls=%fused_computation.7 | loop fusion | flops 16646144 | bytes 15471616 | tf_op jit(solution)/shard_map/add | solution.py:190
  8.7 0.6 collective-permute-start
  9.2 2.7 %reduce_sum.55 = f32[32,32,128]{2,1,0:T(8,128)S(1)} reduce(f32[32,8,32,128]{3,2,1,0:T(8,128)} %get-tuple-element.21, f32[]{:T(128)} %constant.18.clone.1), dimensions={1}, to_apply=%region_1.2 | reduce | flops 917504 | bytes 4718596 | tf_op jit(solution)/shard_map/reduce_sum | solution.py:203
  12.0 0.0 copy-start.1
  12.1 1.6 %collective-permute-start.2 = (f32[16,32,128]{2,1,0:T(8,128)S(1)}, f32[16,32,128]{2,1,0:T(8,128)S(1)}, u32[]{:S(2)}, u32[]{:S(2)}) collective-permute-start(f32[16,32,128]{2,1,0:T(8,128)S(1)} %slice_select_fusion.1), channel_id=1, source_target_pairs={{0,4},{4,0},{8,12},{12,8},{16,20},{20,16},{24,28},{28,24},{1,5},{5... | collective-permute-start | bytes 786440 | tf_op jit(solution)/shard_map/ppermute | solution.py:107
  13.6 2.7 %fusion = f32[32,7,32,128]{3,2,1,0:T(8,128)S(1)} fusion(f32[32,8,32,128]{3,2,1,0:T(8,128)} %get-tuple-element.21), kind=kOutput, calls=%fused_computation.12 | output fusion | flops 5505024 | bytes 7340032 | tf_op jit(solution)/shard_map/jit(cumsum)/reduce_window_sum | solution.py:208
  16.3 0.0 copy-start.5
  16.3 1.6 %collective-permute-done = f32[16,32,128]{2,1,0:T(8,128)S(1)} collective-permute-done((f32[16,32,128]{2,1,0:T(8,128)S(1)}, f32[16,32,128]{2,1,0:T(8,128)S(1)}, u32[]{:S(2)}, u32[]{:S(2)}) %collective-permute-start) | collective-permute-done | bytes 262176 | tf_op jit(solution)/shard_map/ppermute | solution.py:107
  17.9 0.1 fusion.99
  18.0 3.5 %collective-permute-start.1 = (f32[16,32,128]{2,1,0:T(8,128)S(1)}, f32[16,32,128]{2,1,0:T(8,128)S(1)}, u32[]{:S(2)}, u32[]{:S(2)}) collective-permute-start(f32[16,32,128]{2,1,0:T(8,128)S(1)} %fusion.99), channel_id=1, source_target_pairs={{0,8},{4,12},{8,16},{12,20},{16,24},{20,28},{1,9},{5,13},{9,17},{1... | collective-permute-start | bytes 786440 | tf_op jit(solution)/shard_map/ppermute | solution.py:107
  21.5 0.0 copy-start.6
  21.5 0.9 fusion.2
  22.4 0.0 collective-permute-done.2
  22.4 3.8 %collective-permute-done.1 = f32[16,32,128]{2,1,0:T(8,128)S(1)} collective-permute-done((f32[16,32,128]{2,1,0:T(8,128)S(1)}, f32[16,32,128]{2,1,0:T(8,128)S(1)}, u32[]{:S(2)}, u32[]{:S(2)}) %collective-permute-start.1) | collective-permute-done | bytes 262176 | tf_op jit(solution)/shard_map/ppermute | solution.py:107
  26.3 1.3 %collective-permute-start.3 = (f32[16,32,128]{2,1,0:T(8,128)S(1)}, f32[16,32,128]{2,1,0:T(8,128)S(1)}, u32[]{:S(2)}, u32[]{:S(2)}) collective-permute-start(f32[16,32,128]{2,1,0:T(8,128)S(1)} %add.219), channel_id=1, source_target_pairs={{0,16},{4,20},{8,24},{12,28},{1,17},{5,21},{9,25},{13,29},{2,18},{... | collective-permute-start | bytes 786440 | tf_op jit(solution)/shard_map/ppermute | solution.py:107
  27.6 1.9 %collective-permute-start.6 = (f32[2,8,1,128]{3,2,1,0:T(1,128)S(1)}, f32[2,8,1,128]{3,2,1,0:T(1,128)S(1)}, u32[]{:S(2)}, u32[]{:S(2)}) collective-permute-start(f32[2,8,1,128]{3,2,1,0:T(1,128)S(1)} %get-tuple-element.64), channel_id=1, source_target_pairs={{0,1},{1,2},{2,3},{4,5},{5,6},{6,7},{8,9},{9,10},{10,11},{12,13},{... | collective-permute-start | bytes 24584 | tf_op jit(solution)/shard_map/ppermute | solution.py:33
  29.6 3.6 %collective-permute-start.7 = (f32[2,8,1,128]{3,2,1,0:T(1,128)S(1)}, f32[2,8,1,128]{3,2,1,0:T(1,128)S(1)}, u32[]{:S(2)}, u32[]{:S(2)}) collective-permute-start(f32[2,8,1,128]{3,2,1,0:T(1,128)S(1)} %get-tuple-element.65), channel_id=1, source_target_pairs={{1,0},{2,1},{3,2},{5,4},{6,5},{7,6},{9,8},{10,9},{11,10},{13,12},{... | collective-permute-start | bytes 24584 | tf_op jit(solution)/shard_map/ppermute | solution.py:33
  33.2 3.4 %collective-permute-start.5 = (f32[2,1,32,128]{3,2,1,0:T(8,128)S(1)}, f32[2,1,32,128]{3,2,1,0:T(8,128)S(1)}, u32[]{:S(2)}, u32[]{:S(2)}) collective-permute-start(f32[2,1,32,128]{3,2,1,0:T(8,128)S(1)} %get-tuple-element.62), channel_id=1, source_target_pairs={{0,4},{4,8},{8,12},{12,16},{16,20},{20,24},{24,28},{1,5},{5,9},{9,... | collective-permute-start | bytes 98312 | tf_op jit(solution)/shard_map/ppermute | solution.py:33
  36.6 2.4 %collective-permute-start.8 = (f32[2,1,32,128]{3,2,1,0:T(8,128)S(1)}, f32[2,1,32,128]{3,2,1,0:T(8,128)S(1)}, u32[]{:S(2)}, u32[]{:S(2)}) collective-permute-start(f32[2,1,32,128]{3,2,1,0:T(8,128)S(1)} %get-tuple-element.63), channel_id=1, source_target_pairs={{4,0},{8,4},{12,8},{16,12},{20,16},{24,20},{28,24},{5,1},{9,5},{13... | collective-permute-start | bytes 98312 | tf_op jit(solution)/shard_map/ppermute | solution.py:33
  39.1 0.1 fusion.100
  39.1 0.0 collective-permute-done.6
  39.1 3.5 %collective-permute-start.4 = (f32[16,32,128]{2,1,0:T(8,128)S(1)}, f32[16,32,128]{2,1,0:T(8,128)S(1)}, u32[]{:S(2)}, u32[]{:S(2)}) collective-permute-start(f32[16,32,128]{2,1,0:T(8,128)S(1)} %fusion.100), channel_id=1, source_target_pairs={{0,8},{4,12},{8,16},{12,20},{16,24},{20,28},{1,9},{5,13},{9,17},{1... | collective-permute-start | bytes 786440 | tf_op jit(solution)/shard_map/ppermute | solution.py:107
  42.7 0.0 collective-permute-done.5
  42.7 0.7 collective-permute-done.8
  43.4 0.1 fusion.7
  43.4 0.3 pad.15
  43.7 5.7 %collective-permute-done.4 = f32[16,32,128]{2,1,0:T(8,128)S(1)} collective-permute-done((f32[16,32,128]{2,1,0:T(8,128)S(1)}, f32[16,32,128]{2,1,0:T(8,128)S(1)}, u32[]{:S(2)}, u32[]{:S(2)}) %collective-permute-start.4) | collective-permute-done | bytes 262176 | tf_op jit(solution)/shard_map/ppermute | solution.py:107
  49.4 0.0 collective-permute-done.3
  49.4 0.1 fusion.108
  49.5 0.0 copy-start.3
  49.5 0.1 add_select_fusion.1
  49.6 1.4 %collective-permute-start.10 = (f32[16,32,128]{2,1,0:T(8,128)S(1)}, f32[16,32,128]{2,1,0:T(8,128)S(1)}, u32[]{:S(2)}, u32[]{:S(2)}) collective-permute-start(f32[16,32,128]{2,1,0:T(8,128)S(1)} %add.223), channel_id=1, source_target_pairs={{0,16},{4,20},{8,24},{12,28},{1,17},{5,21},{9,25},{13,29},{2,18},{... | collective-permute-start | bytes 786440 | tf_op jit(solution)/shard_map/ppermute | solution.py:107
  51.0 1.5 %collective-permute-start.9 = (f32[16,32,128]{2,1,0:T(8,128)S(1)}, f32[16,32,128]{2,1,0:T(8,128)S(1)}, u32[]{:S(2)}, u32[]{:S(2)}) collective-permute-start(f32[16,32,128]{2,1,0:T(8,128)S(1)} %add_select_fusion.1), channel_id=1, source_target_pairs={{0,4},{4,0},{8,12},{12,8},{16,20},{20,16},{24,28},{28,24},{1,5},{5... | collective-permute-start | bytes 786440 | tf_op jit(solution)/shard_map/ppermute | solution.py:107
  52.5 0.4 power_multiply_fusion.2
  53.0 0.0 copy-start
  53.0 0.9 fusion.47
  53.9 5.1 %collective-permute-done.10 = f32[16,32,128]{2,1,0:T(8,128)S(1)} collective-permute-done((f32[16,32,128]{2,1,0:T(8,128)S(1)}, f32[16,32,128]{2,1,0:T(8,128)S(1)}, u32[]{:S(2)}, u32[]{:S(2)}) %collective-permute-start.10) | collective-permute-done | bytes 262176 | tf_op jit(solution)/shard_map/ppermute | solution.py:107
  59.0 0.1 fusion.107
  59.0 0.1 add_select_fusion
  59.1 1.5 %collective-permute-start.11 = (f32[16,32,128]{2,1,0:T(8,128)S(1)}, f32[16,32,128]{2,1,0:T(8,128)S(1)}, u32[]{:S(2)}, u32[]{:S(2)}) collective-permute-start(f32[16,32,128]{2,1,0:T(8,128)S(1)} %add_select_fusion), channel_id=1, source_target_pairs={{0,4},{4,0},{8,12},{12,8},{16,20},{20,16},{24,28},{28,24},{1,5},{5... | collective-permute-start | bytes 786440 | tf_op jit(solution)/shard_map/ppermute | solution.py:107
  60.6 0.2 fusion.109
  60.8 2.7 %multiply_reduce_fusion.2 = (f32[8,32,128]{2,1,0:T(8,128)S(1)}, f32[8,32,128]{2,1,0:T(8,128)S(1)}, bf16[32,8,32,128]{3,2,1,0:T(8,128)(2,1)S(1)}) fusion(f32[32,7,32,128]{3,2,1,0:T(8,128)S(1)} %fusion.2, f32[32,32,128]{2,1,0:T(8,128)S(1)} %get-tuple-element.73, f32[32,32,128]{2,1,0:T(8,128)S(1)} %get-tuple-element.53, f32[8,32]{1,0:T(8,128)S(1)} %get-tuple-element.69, ...), kind=kLoop, calls=%fused_computation.4 | loop fusion | flops 15663104 | bytes 9307264 | tf_op jit(solution)/shard_map/reduce_sum | solution.py:215
  63.5 2.0 %collective-permute-done.11 = f32[16,32,128]{2,1,0:T(8,128)S(1)} collective-permute-done((f32[16,32,128]{2,1,0:T(8,128)S(1)}, f32[16,32,128]{2,1,0:T(8,128)S(1)}, u32[]{:S(2)}, u32[]{:S(2)}) %collective-permute-start.11) | collective-permute-done | bytes 262176 | tf_op jit(solution)/shard_map/ppermute | solution.py:107
  65.6 0.1 maximum_select_fusion.1
  65.6 2.7 %multiply_reduce_fusion = (f32[8,32,128]{2,1,0:T(8,128)S(1)}, f32[8,32,128]{2,1,0:T(8,128)S(1)}, bf16[32,8,32,128]{3,2,1,0:T(8,128)(2,1)S(1)}) fusion(f32[32,7,32,128]{3,2,1,0:T(8,128)S(1)} %fusion, f32[32,32,128]{2,1,0:T(8,128)S(1)} %maximum_select_fusion.1, f32[32,32,128]{2,1,0:T(8,128)S(1)} %get-tuple-element.52, f32[8,32]{1,0:T(8,128)S(1)} %get-tuple-element.69, ...), kind=kLoop, calls=%fused_computation.1 | loop fusion | flops 15663104 | bytes 9307264 | tf_op jit(solution)/shard_map/reduce_sum | solution.py:215
  68.3 0.8 broadcast_multiply_fusion
  69.1 0.2 fusion.105
  69.3 1.9 %collective-permute-start.13 = (f32[2,8,1,128]{3,2,1,0:T(1,128)S(1)}, f32[2,8,1,128]{3,2,1,0:T(1,128)S(1)}, u32[]{:S(2)}, u32[]{:S(2)}) collective-permute-start(f32[2,8,1,128]{3,2,1,0:T(1,128)S(1)} %get-tuple-element.60), channel_id=1, source_target_pairs={{0,1},{1,2},{2,3},{4,5},{5,6},{6,7},{8,9},{9,10},{10,11},{12,13},{... | collective-permute-start | bytes 24584 | tf_op jit(solution)/shard_map/ppermute | solution.py:33
  71.2 3.8 %collective-permute-start.14 = (f32[2,8,1,128]{3,2,1,0:T(1,128)S(1)}, f32[2,8,1,128]{3,2,1,0:T(1,128)S(1)}, u32[]{:S(2)}, u32[]{:S(2)}) collective-permute-start(f32[2,8,1,128]{3,2,1,0:T(1,128)S(1)} %get-tuple-element.61), channel_id=1, source_target_pairs={{1,0},{2,1},{3,2},{5,4},{6,5},{7,6},{9,8},{10,9},{11,10},{13,12},{... | collective-permute-start | bytes 24584 | tf_op jit(solution)/shard_map/ppermute | solution.py:33
  75.0 9.0 %collective-permute-start.12 = (f32[2,1,32,128]{3,2,1,0:T(8,128)S(1)}, f32[2,1,32,128]{3,2,1,0:T(8,128)S(1)}, u32[]{:S(2)}, u32[]{:S(2)}) collective-permute-start(f32[2,1,32,128]{3,2,1,0:T(8,128)S(1)} %get-tuple-element.58), channel_id=1, source_target_pairs={{0,4},{4,8},{8,12},{12,16},{16,20},{20,24},{24,28},{1,5},{5,9},{9,... | collective-permute-start | bytes 98312 | tf_op jit(solution)/shard_map/ppermute | solution.py:33
  84.1 1.9 %collective-permute-start.15 = (f32[2,1,32,128]{3,2,1,0:T(8,128)S(1)}, f32[2,1,32,128]{3,2,1,0:T(8,128)S(1)}, u32[]{:S(2)}, u32[]{:S(2)}) collective-permute-start(f32[2,1,32,128]{3,2,1,0:T(8,128)S(1)} %get-tuple-element.59), channel_id=1, source_target_pairs={{4,0},{8,4},{12,8},{16,12},{20,16},{24,20},{28,24},{5,1},{9,5},{13... | collective-permute-start | bytes 98312 | tf_op jit(solution)/shard_map/ppermute | solution.py:33
  86.0 2.4 %pad_maximum_fusion = bf16[64,8,32,128]{3,2,1,0:T(8,128)(2,1)} fusion(bf16[32,8,32,128]{3,2,1,0:T(8,128)(2,1)S(1)} %get-tuple-element.44, bf16[32,8,32,128]{3,2,1,0:T(8,128)(2,1)S(1)} %get-tuple-element.29), kind=kLoop, calls=%fused_computation | loop fusion | flops 2097152 | bytes 8388608 | tf_op jit(solution)/shard_map/dynamic_update_slice | solution.py:229
  88.4 0.0 collective-permute-done.13
  88.4 0.0 collective-permute-done.14
  88.4 0.0 collective-permute-done.12
  88.4 2.4 %collective-permute-done.15 = f32[2,1,32,128]{3,2,1,0:T(8,128)S(1)} collective-permute-done((f32[2,1,32,128]{3,2,1,0:T(8,128)S(1)}, f32[2,1,32,128]{3,2,1,0:T(8,128)S(1)}, u32[]{:S(2)}, u32[]{:S(2)}) %collective-permute-start.15) | collective-permute-done | bytes 32800 | tf_op jit(solution)/shard_map/ppermute | solution.py:33
  90.8 0.5 power_multiply_fusion
  91.4 0.7 fusion.15
  92.1 0.9 fusion.85
  (23 shorter events, 0.3 us)
Async XLA Ops:
  0.6 1.8 %slice-start = ((bf16[64,8,32,128]{3,2,1,0:T(8,128)(2,1)}), bf16[32,8,32,128]{3,2,1,0:T(8,128)(2,1)S(1)}, s32[]{:S(2)}) async-start(bf16[64,8,32,128]{3,2,1,0:T(8,128)(2,1)} %param.11), calls=%async_computation | async-start | bytes 4194304 | tf_op jit(solution)/shard_map/slice | solution.py:195
  0.6 1.6 %copy-start.2 = (f32[8,32,128]{2,1,0:T(8,128)S(1)}, f32[8,32,128]{2,1,0:T(8,128)}, u32[]{:S(2)}) copy-start(f32[8,32,128]{2,1,0:T(8,128)} %param.9) | copy-start | bytes 393220
  0.7 1.6 %copy-start.4 = (f32[8,32,128]{2,1,0:T(8,128)S(1)}, f32[8,32,128]{2,1,0:T(8,128)}, u32[]{:S(2)}) copy-start(f32[8,32,128]{2,1,0:T(8,128)} %param.10) | copy-start | bytes 393220
  8.7 9.3 %collective-permute-start = (f32[16,32,128]{2,1,0:T(8,128)S(1)}, f32[16,32,128]{2,1,0:T(8,128)S(1)}, u32[]{:S(2)}, u32[]{:S(2)}) collective-permute-start(f32[16,32,128]{2,1,0:T(8,128)S(1)} %slice_select_fusion.2), channel_id=1, source_target_pairs={{0,4},{4,0},{8,12},{12,8},{16,20},{20,16},{24,28},{28,24},{1,5},{5... | collective-permute-start | bytes 786440 | tf_op jit(solution)/shard_map/ppermute | solution.py:107
  12.0 9.4 %copy-start.1 = (f32[32,8,32,128]{3,2,1,0:T(8,128)S(1)}, f32[32,8,32,128]{3,2,1,0:T(8,128)}, u32[]{:S(2)}) copy-start(f32[32,8,32,128]{3,2,1,0:T(8,128)} %get-tuple-element.46) | copy-start | bytes 12582916
  12.1 10.3 %collective-permute-start.2 = (f32[16,32,128]{2,1,0:T(8,128)S(1)}, f32[16,32,128]{2,1,0:T(8,128)S(1)}, u32[]{:S(2)}, u32[]{:S(2)}) collective-permute-start(f32[16,32,128]{2,1,0:T(8,128)S(1)} %slice_select_fusion.1), channel_id=1, source_target_pairs={{0,4},{4,0},{8,12},{12,8},{16,20},{20,16},{24,28},{28,24},{1,5},{5... | collective-permute-start | bytes 786440 | tf_op jit(solution)/shard_map/ppermute | solution.py:107
  16.3 6.0 %copy-start.5 = (f32[8,32,128]{2,1,0:T(8,128)S(1)}, f32[8,32,128]{2,1,0:T(8,128)}, u32[]{:S(2)}) copy-start(f32[8,32,128]{2,1,0:T(8,128)} %param.8) | copy-start | bytes 393220
  18.0 8.3 %collective-permute-start.1 = (f32[16,32,128]{2,1,0:T(8,128)S(1)}, f32[16,32,128]{2,1,0:T(8,128)S(1)}, u32[]{:S(2)}, u32[]{:S(2)}) collective-permute-start(f32[16,32,128]{2,1,0:T(8,128)S(1)} %fusion.99), channel_id=1, source_target_pairs={{0,8},{4,12},{8,16},{12,20},{16,24},{20,28},{1,9},{5,13},{9,17},{1... | collective-permute-start | bytes 786440 | tf_op jit(solution)/shard_map/ppermute | solution.py:107
  21.5 21.1 %copy-start.6 = (f32[32,128]{1,0:T(8,128)S(1)}, f32[32,128]{1,0:T(8,128)}, u32[]{:S(2)}) copy-start(f32[32,128]{1,0:T(8,128)} %param.14) | copy-start | bytes 49156
  26.3 23.1 %collective-permute-start.3 = (f32[16,32,128]{2,1,0:T(8,128)S(1)}, f32[16,32,128]{2,1,0:T(8,128)S(1)}, u32[]{:S(2)}, u32[]{:S(2)}) collective-permute-start(f32[16,32,128]{2,1,0:T(8,128)S(1)} %add.219), channel_id=1, source_target_pairs={{0,16},{4,20},{8,24},{12,28},{1,17},{5,21},{9,25},{13,29},{2,18},{... | collective-permute-start | bytes 786440 | tf_op jit(solution)/shard_map/ppermute | solution.py:107
  27.6 11.5 %collective-permute-start.6 = (f32[2,8,1,128]{3,2,1,0:T(1,128)S(1)}, f32[2,8,1,128]{3,2,1,0:T(1,128)S(1)}, u32[]{:S(2)}, u32[]{:S(2)}) collective-permute-start(f32[2,8,1,128]{3,2,1,0:T(1,128)S(1)} %get-tuple-element.64), channel_id=1, source_target_pairs={{0,1},{1,2},{2,3},{4,5},{5,6},{6,7},{8,9},{9,10},{10,11},{12,13},{... | collective-permute-start | bytes 24584 | tf_op jit(solution)/shard_map/ppermute | solution.py:33
  29.6 13.1 %collective-permute-start.7 = (f32[2,8,1,128]{3,2,1,0:T(1,128)S(1)}, f32[2,8,1,128]{3,2,1,0:T(1,128)S(1)}, u32[]{:S(2)}, u32[]{:S(2)}) collective-permute-start(f32[2,8,1,128]{3,2,1,0:T(1,128)S(1)} %get-tuple-element.65), channel_id=1, source_target_pairs={{1,0},{2,1},{3,2},{5,4},{6,5},{7,6},{9,8},{10,9},{11,10},{13,12},{... | collective-permute-start | bytes 24584 | tf_op jit(solution)/shard_map/ppermute | solution.py:33
  33.2 9.5 %collective-permute-start.5 = (f32[2,1,32,128]{3,2,1,0:T(8,128)S(1)}, f32[2,1,32,128]{3,2,1,0:T(8,128)S(1)}, u32[]{:S(2)}, u32[]{:S(2)}) collective-permute-start(f32[2,1,32,128]{3,2,1,0:T(8,128)S(1)} %get-tuple-element.62), channel_id=1, source_target_pairs={{0,4},{4,8},{8,12},{12,16},{16,20},{20,24},{24,28},{1,5},{5,9},{9,... | collective-permute-start | bytes 98312 | tf_op jit(solution)/shard_map/ppermute | solution.py:33
  36.6 6.7 %collective-permute-start.8 = (f32[2,1,32,128]{3,2,1,0:T(8,128)S(1)}, f32[2,1,32,128]{3,2,1,0:T(8,128)S(1)}, u32[]{:S(2)}, u32[]{:S(2)}) collective-permute-start(f32[2,1,32,128]{3,2,1,0:T(8,128)S(1)} %get-tuple-element.63), channel_id=1, source_target_pairs={{4,0},{8,4},{12,8},{16,12},{20,16},{24,20},{28,24},{5,1},{9,5},{13... | collective-permute-start | bytes 98312 | tf_op jit(solution)/shard_map/ppermute | solution.py:33
  39.1 10.2 %collective-permute-start.4 = (f32[16,32,128]{2,1,0:T(8,128)S(1)}, f32[16,32,128]{2,1,0:T(8,128)S(1)}, u32[]{:S(2)}, u32[]{:S(2)}) collective-permute-start(f32[16,32,128]{2,1,0:T(8,128)S(1)} %fusion.100), channel_id=1, source_target_pairs={{0,8},{4,12},{8,16},{12,20},{16,24},{20,28},{1,9},{5,13},{9,17},{1... | collective-permute-start | bytes 786440 | tf_op jit(solution)/shard_map/ppermute | solution.py:107
  49.5 11.2 %copy-start.3 = (f32[64,32,128]{2,1,0:T(8,128)S(1)}, f32[64,32,128]{2,1,0:T(8,128)}, u32[]{:S(2)}) copy-start(f32[64,32,128]{2,1,0:T(8,128)} %param.12) | copy-start | bytes 3145732
  49.6 9.4 %collective-permute-start.10 = (f32[16,32,128]{2,1,0:T(8,128)S(1)}, f32[16,32,128]{2,1,0:T(8,128)S(1)}, u32[]{:S(2)}, u32[]{:S(2)}) collective-permute-start(f32[16,32,128]{2,1,0:T(8,128)S(1)} %add.223), channel_id=1, source_target_pairs={{0,16},{4,20},{8,24},{12,28},{1,17},{5,21},{9,25},{13,29},{2,18},{... | collective-permute-start | bytes 786440 | tf_op jit(solution)/shard_map/ppermute | solution.py:107
  51.0 8.0 %collective-permute-start.9 = (f32[16,32,128]{2,1,0:T(8,128)S(1)}, f32[16,32,128]{2,1,0:T(8,128)S(1)}, u32[]{:S(2)}, u32[]{:S(2)}) collective-permute-start(f32[16,32,128]{2,1,0:T(8,128)S(1)} %add_select_fusion.1), channel_id=1, source_target_pairs={{0,4},{4,0},{8,12},{12,8},{16,20},{20,16},{24,28},{28,24},{1,5},{5... | collective-permute-start | bytes 786440 | tf_op jit(solution)/shard_map/ppermute | solution.py:107
  53.0 7.9 %copy-start = (bf16[64,8,32,128]{3,2,1,0:T(8,128)(2,1)S(1)}, bf16[64,8,32,128]{3,2,1,0:T(8,128)(2,1)}, u32[]{:S(2)}) copy-start(bf16[64,8,32,128]{3,2,1,0:T(8,128)(2,1)} %param.11) | copy-start | bytes 12582916
  59.1 6.4 %collective-permute-start.11 = (f32[16,32,128]{2,1,0:T(8,128)S(1)}, f32[16,32,128]{2,1,0:T(8,128)S(1)}, u32[]{:S(2)}, u32[]{:S(2)}) collective-permute-start(f32[16,32,128]{2,1,0:T(8,128)S(1)} %add_select_fusion), channel_id=1, source_target_pairs={{0,4},{4,0},{8,12},{12,8},{16,20},{20,16},{24,28},{28,24},{1,5},{5... | collective-permute-start | bytes 786440 | tf_op jit(solution)/shard_map/ppermute | solution.py:107
  69.3 19.1 %collective-permute-start.13 = (f32[2,8,1,128]{3,2,1,0:T(1,128)S(1)}, f32[2,8,1,128]{3,2,1,0:T(1,128)S(1)}, u32[]{:S(2)}, u32[]{:S(2)}) collective-permute-start(f32[2,8,1,128]{3,2,1,0:T(1,128)S(1)} %get-tuple-element.60), channel_id=1, source_target_pairs={{0,1},{1,2},{2,3},{4,5},{5,6},{6,7},{8,9},{9,10},{10,11},{12,13},{... | collective-permute-start | bytes 24584 | tf_op jit(solution)/shard_map/ppermute | solution.py:33
  71.2 17.2 %collective-permute-start.14 = (f32[2,8,1,128]{3,2,1,0:T(1,128)S(1)}, f32[2,8,1,128]{3,2,1,0:T(1,128)S(1)}, u32[]{:S(2)}, u32[]{:S(2)}) collective-permute-start(f32[2,8,1,128]{3,2,1,0:T(1,128)S(1)} %get-tuple-element.61), channel_id=1, source_target_pairs={{1,0},{2,1},{3,2},{5,4},{6,5},{7,6},{9,8},{10,9},{11,10},{13,12},{... | collective-permute-start | bytes 24584 | tf_op jit(solution)/shard_map/ppermute | solution.py:33
  75.0 13.4 %collective-permute-start.12 = (f32[2,1,32,128]{3,2,1,0:T(8,128)S(1)}, f32[2,1,32,128]{3,2,1,0:T(8,128)S(1)}, u32[]{:S(2)}, u32[]{:S(2)}) collective-permute-start(f32[2,1,32,128]{3,2,1,0:T(8,128)S(1)} %get-tuple-element.58), channel_id=1, source_target_pairs={{0,4},{4,8},{8,12},{12,16},{16,20},{20,24},{24,28},{1,5},{5,9},{9,... | collective-permute-start | bytes 98312 | tf_op jit(solution)/shard_map/ppermute | solution.py:33
  84.1 6.7 %collective-permute-start.15 = (f32[2,1,32,128]{3,2,1,0:T(8,128)S(1)}, f32[2,1,32,128]{3,2,1,0:T(8,128)S(1)}, u32[]{:S(2)}, u32[]{:S(2)}) collective-permute-start(f32[2,1,32,128]{3,2,1,0:T(8,128)S(1)} %get-tuple-element.59), channel_id=1, source_target_pairs={{4,0},{8,4},{12,8},{16,12},{20,16},{24,20},{28,24},{5,1},{9,5},{13... | collective-permute-start | bytes 98312 | tf_op jit(solution)/shard_map/ppermute | solution.py:33

commit v10 on v8

--- a/solution.py
+++ b/solution.py
@@ -33,12 +33,19 @@
     return lax.ppermute(block, axis, pairs)
 
 
-def bordered_fields(block):
-    _, rows, columns, _ = block.shape
-    low_beam = shifted(block[:, rows - 1 :], "beam", 1)
-    high_beam = shifted(block[:, :1], "beam", -1)
-    low_cross = shifted(block[:, :, columns - 1 :], "cross", 1)
-    high_cross = shifted(block[:, :, :1], "cross", -1)
+def beam_faces(block):
+    rows = block.shape[1]
+    return shifted(block[:, rows - 1 :], "beam", 1), shifted(block[:, :1], "beam", -1)
+
+
+def cross_faces(block):
+    columns = block.shape[2]
+    return shifted(block[:, :, columns - 1 :], "cross", 1), shifted(block[:, :, :1], "cross", -1)
+
+
+def bordered_fields(block, beam=None, cross=None):
+    low_beam, high_beam = beam_faces(block) if beam is None else beam
+    low_cross, high_cross = cross_faces(block) if cross is None else cross
     middle = jnp.concatenate([low_cross, block, high_cross], axis=2)
     zeros = jnp.zeros_like(low_beam[:, :, :1])
     low_beam = jnp.concatenate([zeros, low_beam, zeros], axis=2)
@@ -92,15 +99,15 @@
     return [(i, i + shift) for i in range(count - shift)]
 
 
-def pipelined_scan(totals_of, emit, lines, axis, rider, groups=2):
+def pipelined_scan(totals_of, emit, lines, axis, riders, groups=2):
     count = lax.axis_size(axis)
     if count % 2 or count <= 2 or lines % (2 * groups):
         earlier = exclusive_scan(totals_of(0, lines, None), axis)
-        return [emit(0, lines, earlier)], rider(None)
+        return [emit(0, lines, earlier)], {stage: rider(None) for stage, rider in riders.items()}
     size = lines // groups
     steps = [None] * groups
     steps[0] = paired_steps(totals_of(0, size, None), axis)
-    live, made, carried, stage = {}, [], None, 0
+    live, made, carried, stage = {}, [], {}, 0
     while stage < groups or live:
         if stage < groups:
             live[stage] = next(steps[stage])
@@ -109,8 +116,8 @@
             for g in range(1, groups):
                 steps[g] = paired_steps(totals_of(g * size, size, live[0][0]), axis)
         tied = (arrived, made)
-        if stage == 2:
-            tied, carried = lax.optimization_barrier((tied, rider(live[0][0])))
+        if stage in riders:
+            tied, carried[stage] = lax.optimization_barrier((tied, riders[stage](live[0][0])))
         else:
             tied = lax.optimization_barrier(tied)
         arrived, made = tied
@@ -208,14 +215,20 @@
             jnp.sum(radiance * (1.0 - jnp.exp(-optical_depth)), axis=0),
         )
 
-    def first_border(after):
-        fields = physical_quantities
-        if after is not None:
-            fields, _ = lax.optimization_barrier((fields, after))
-        return bordered_fields(fields)
+    def tied_faces(faces):
+        def exchange(after):
+            fields = physical_quantities
+            if after is not None:
+                fields, _ = lax.optimization_barrier((fields, after))
+            return faces(fields)
+
+        return exchange
 
     lines = earlier_spectral_power.shape[0]
-    made, first_bordered = pipelined_scan(totals_of, emit, lines, "beam", first_border)
+    made, first_faces = pipelined_scan(
+        totals_of, emit, lines, "beam", {2: tied_faces(beam_faces), 3: tied_faces(cross_faces)}
+    )
+    first_bordered = bordered_fields(physical_quantities, first_faces[2], first_faces[3])
     spectral_power = jnp.zeros(earlier_spectral_power.shape, jnp.bfloat16)
     start = 0
     for part, _, _ in made:

time: 92 us -> 89 us (0.967); the launches traced: 90.2 us -> 88.5 us
  waiting for transfers between devices: 19.8 us -> 17 us
  starting transfers between devices: 41.3 us -> 43.2 us
    ppermute x8, waiting for transfers between devices: 16.2 us -> 11.2 us  [pipelined_scan(): lax.ppermute(payload, axis, pairs)]
    ppermute x8, waiting for transfers between devices: 3.61 us -> 5.73 us  [shifted(): return lax.ppermute(block, axis, pairs)]
    ppermute x8, starting transfers between devices: 13.5 us -> 14.6 us  [pipelined_scan(): lax.ppermute(payload, axis, pairs)]
  transfers between devices with their start and end apart: 16 -> 16, of which waited for: 6 -> 7; matrix products, arithmetic and copies ran while one was open for 15% -> 14% of each run, Pallas kernels for 0% -> 0%
where the time goes in v10:
time: 89 us; the launch traced here: 88.5 us
  starting transfers between devices  43.2 us (49%)
  other arithmetic  26.4 us (30%)
  waiting for transfers between devices  17 us (19%)
  between operations  1.05 us (1%)
    ppermute x8, starting transfers between devices, shifted(): return lax.ppermute(block, axis, pairs)  28.6 us
    ppermute x8, starting transfers between devices, pipelined_scan(): lax.ppermute(payload, axis, pairs)  14.6 us
    ppermute x8, waiting for transfers between devices, pipelined_scan(): lax.ppermute(payload, axis, pairs)  11.2 us
    reduce_sum x2, other arithmetic, totals_of(): return jnp.sum(optical_depth, axis=1)  8.66 us
    ppermute x8, waiting for transfers between devices, shifted(): return lax.ppermute(block, axis, pairs)  5.73 us
    reduce_sum x2, other arithmetic, emit(): jnp.sum(radiance * (1.0 - jnp.exp(-optical_depth)), axis=0)  5.06 us
    another operation x2, other arithmetic, emit(): jnp.cumsum(optical_depth[:, :rows - 1], axis=1)  3.4 us
    dynamic_update_slice x1, other arithmetic, local(): lax.dynamic_update_slice_in_dim(spectral_power, part, start, axis=0)  2.38 us
  transfers between devices with their start and end apart: 16, of which 7 were waited for; matrix products, arithmetic and copies ran while one was open for 14% of the time, Pallas kernels for 0%

profile of v10, /device:TPU:9, one launch (start us, length us, event | category | flops | bytes accessed | tf_op | source)
XLA Modules:
  0.0 88.5 jit_solution(16764184371169225356)
XLA Ops:
  0.6 0.7 convert_subtract_fusion
  1.3 0.8 fusion.120
  2.1 1.1 %add_bitcast_fusion = (f32[1,8,32,128]{3,2,1,0:T(8,128)S(1)}, f32[8,32,128]{2,1,0:T(8,128)S(1)}) fusion(f32[8,32,128]{2,1,0:T(8,128)} %param.9, f32[8,32,128]{2,1,0:T(8,128)} %param.10, f32[8,32]{1,0:T(8,128)S(1)} %get-tuple-element.73), kind=kLoop, calls=%fused_computation.215 | loop fusion | flops 262144 | bytes 525312 | tf_op jit(solution)/shard_map/stack | solution.py:182
  3.2 5.9 %fusion.116 = (f32[32,32,128]{2,1,0:T(8,128)S(1)}, f32[32,8,32,128]{3,2,1,0:T(8,128)}, f32[32,8,32,128]{3,2,1,0:T(8,128)}) fusion(f32[8,32]{1,0:T(8,128)S(1)} %get-tuple-element.74, bf16[64,8,32,128]{3,2,1,0:T(8,128)(2,1)} %param.11, f32[32]{0:T(128)S(1)} %get-tuple-element.75, f32[8,32,128]{2,1,0:T(8,128)S(1)} %get-tuple-element.72, ...), kind=kLoop, calls=%fused_computation.230 | loop fusion | flops 11403264 | bytes 13239552 | tf_op jit(solution)/shard_map/reduce_sum | solution.py:203
  9.2 1.3 %collective-permute-start = (f32[16,32,128]{2,1,0:T(8,128)S(1)}, f32[16,32,128]{2,1,0:T(8,128)S(1)}, u32[]{:S(2)}, u32[]{:S(2)}) collective-permute-start(f32[16,32,128]{2,1,0:T(8,128)S(1)} %slice_select_fusion.2), channel_id=1, source_target_pairs={{0,4},{4,0},{8,12},{12,8},{16,20},{20,16},{24,28},{28,24},{1,5},{5... | collective-permute-start | bytes 786440 | tf_op jit(solution)/shard_map/ppermute | solution.py:114
  10.5 2.7 %reduce_sum.55 = f32[32,32,128]{2,1,0:T(8,128)S(1)} reduce(f32[32,8,32,128]{3,2,1,0:T(8,128)} %get-tuple-element.21, f32[]{:T(128)} %constant.18.clone.1), dimensions={1}, to_apply=%region_1.2 | reduce | flops 917504 | bytes 4718596 | tf_op jit(solution)/shard_map/reduce_sum | solution.py:203
  13.3 0.0 copy-start.2
  13.3 0.3 collective-permute-start.2
  13.6 2.8 %collective-permute-done = f32[16,32,128]{2,1,0:T(8,128)S(1)} collective-permute-done((f32[16,32,128]{2,1,0:T(8,128)S(1)}, f32[16,32,128]{2,1,0:T(8,128)S(1)}, u32[]{:S(2)}, u32[]{:S(2)}) %collective-permute-start) | collective-permute-done | bytes 262176 | tf_op jit(solution)/shard_map/ppermute | solution.py:114
  16.4 0.1 fusion.106
  16.5 0.0 copy-start
  16.5 3.5 %collective-permute-start.1 = (f32[16,32,128]{2,1,0:T(8,128)S(1)}, f32[16,32,128]{2,1,0:T(8,128)S(1)}, u32[]{:S(2)}, u32[]{:S(2)}) collective-permute-start(f32[16,32,128]{2,1,0:T(8,128)S(1)} %fusion.106), channel_id=1, source_target_pairs={{0,8},{4,12},{8,16},{12,20},{16,24},{20,28},{1,9},{5,13},{9,17},{1... | collective-permute-start | bytes 786440 | tf_op jit(solution)/shard_map/ppermute | solution.py:114
  19.9 2.5 %fusion = f32[32,7,32,128]{3,2,1,0:T(8,128)S(1)} fusion(f32[32,8,32,128]{3,2,1,0:T(8,128)} %get-tuple-element.21), kind=kOutput, calls=%fused_computation.11 | output fusion | flops 5505024 | bytes 7340032 | tf_op jit(solution)/shard_map/jit(cumsum)/reduce_window_sum | solution.py:208
  22.5 0.0 collective-permute-done.2
  22.6 1.3 %collective-permute-done.1 = f32[16,32,128]{2,1,0:T(8,128)S(1)} collective-permute-done((f32[16,32,128]{2,1,0:T(8,128)S(1)}, f32[16,32,128]{2,1,0:T(8,128)S(1)}, u32[]{:S(2)}, u32[]{:S(2)}) %collective-permute-start.1) | collective-permute-done | bytes 262176 | tf_op jit(solution)/shard_map/ppermute | solution.py:114
  23.9 4.2 %collective-permute-start.3 = (f32[16,32,128]{2,1,0:T(8,128)S(1)}, f32[16,32,128]{2,1,0:T(8,128)S(1)}, u32[]{:S(2)}, u32[]{:S(2)}) collective-permute-start(f32[16,32,128]{2,1,0:T(8,128)S(1)} %add.212), channel_id=1, source_target_pairs={{0,16},{4,20},{8,24},{12,28},{1,17},{5,21},{9,25},{13,29},{2,18},{... | collective-permute-start | bytes 786440 | tf_op jit(solution)/shard_map/ppermute | solution.py:114
  28.1 0.1 fusion.107
  28.2 1.9 %collective-permute-start.4 = (f32[16,32,128]{2,1,0:T(8,128)S(1)}, f32[16,32,128]{2,1,0:T(8,128)S(1)}, u32[]{:S(2)}, u32[]{:S(2)}) collective-permute-start(f32[16,32,128]{2,1,0:T(8,128)S(1)} %fusion.107), channel_id=1, source_target_pairs={{0,8},{4,12},{8,16},{12,20},{16,24},{20,28},{1,9},{5,13},{9,17},{1... | collective-permute-start | bytes 786440 | tf_op jit(solution)/shard_map/ppermute | solution.py:114
  30.1 3.1 %collective-permute-start.5 = (f32[2,1,32,128]{3,2,1,0:T(8,128)S(1)}, f32[2,1,32,128]{3,2,1,0:T(8,128)S(1)}, u32[]{:S(2)}, u32[]{:S(2)}) collective-permute-start(f32[2,1,32,128]{3,2,1,0:T(8,128)S(1)} %get-tuple-element.70), channel_id=1, source_target_pairs={{0,4},{4,8},{8,12},{12,16},{16,20},{20,24},{24,28},{1,5},{5,9},{9,... | collective-permute-start | bytes 98312 | tf_op jit(solution)/shard_map/ppermute | solution.py:33
  33.3 3.1 %collective-permute-start.6 = (f32[2,1,32,128]{3,2,1,0:T(8,128)S(1)}, f32[2,1,32,128]{3,2,1,0:T(8,128)S(1)}, u32[]{:S(2)}, u32[]{:S(2)}) collective-permute-start(f32[2,1,32,128]{3,2,1,0:T(8,128)S(1)} %get-tuple-element.69), channel_id=1, source_target_pairs={{4,0},{8,4},{12,8},{16,12},{20,16},{24,20},{28,24},{5,1},{9,5},{13... | collective-permute-start | bytes 98312 | tf_op jit(solution)/shard_map/ppermute | solution.py:33
  36.4 0.0 copy-start.5
  36.4 0.9 fusion.2
  37.3 0.0 copy-start.4
  37.3 1.5 %collective-permute-done.5 = f32[2,1,32,128]{3,2,1,0:T(8,128)S(1)} collective-permute-done((f32[2,1,32,128]{3,2,1,0:T(8,128)S(1)}, f32[2,1,32,128]{3,2,1,0:T(8,128)S(1)}, u32[]{:S(2)}, u32[]{:S(2)}) %collective-permute-start.5) | collective-permute-done | bytes 32800 | tf_op jit(solution)/shard_map/ppermute | solution.py:33
  38.8 0.0 collective-permute-done.6
  38.8 0.0 collective-permute-done.3
  38.8 5.0 %collective-permute-done.4 = f32[16,32,128]{2,1,0:T(8,128)S(1)} collective-permute-done((f32[16,32,128]{2,1,0:T(8,128)S(1)}, f32[16,32,128]{2,1,0:T(8,128)S(1)}, u32[]{:S(2)}, u32[]{:S(2)}) %collective-permute-start.4) | collective-permute-done | bytes 262176 | tf_op jit(solution)/shard_map/ppermute | solution.py:114
  43.8 0.1 fusion.115
  43.9 0.1 add_select_fusion.1
  43.9 0.0 copy-start.1
  44.0 2.0 %collective-permute-start.7 = (f32[16,32,128]{2,1,0:T(8,128)S(1)}, f32[16,32,128]{2,1,0:T(8,128)S(1)}, u32[]{:S(2)}, u32[]{:S(2)}) collective-permute-start(f32[16,32,128]{2,1,0:T(8,128)S(1)} %add_select_fusion.1), channel_id=1, source_target_pairs={{0,4},{4,0},{8,12},{12,8},{16,20},{20,16},{24,28},{28,24},{1,5},{5... | collective-permute-start | bytes 786440 | tf_op jit(solution)/shard_map/ppermute | solution.py:114
  46.0 1.3 %collective-permute-start.8 = (f32[16,32,128]{2,1,0:T(8,128)S(1)}, f32[16,32,128]{2,1,0:T(8,128)S(1)}, u32[]{:S(2)}, u32[]{:S(2)}) collective-permute-start(f32[16,32,128]{2,1,0:T(8,128)S(1)} %add.216), channel_id=1, source_target_pairs={{0,16},{4,20},{8,24},{12,28},{1,17},{5,21},{9,25},{13,29},{2,18},{... | collective-permute-start | bytes 786440 | tf_op jit(solution)/shard_map/ppermute | solution.py:114
  47.4 5.3 %collective-permute-start.9 = (f32[2,8,1,128]{3,2,1,0:T(1,128)S(1)}, f32[2,8,1,128]{3,2,1,0:T(1,128)S(1)}, u32[]{:S(2)}, u32[]{:S(2)}) collective-permute-start(f32[2,8,1,128]{3,2,1,0:T(1,128)S(1)} %get-tuple-element.68), channel_id=1, source_target_pairs={{0,1},{1,2},{2,3},{4,5},{5,6},{6,7},{8,9},{9,10},{10,11},{12,13},{... | collective-permute-start | bytes 24584 | tf_op jit(solution)/shard_map/ppermute | solution.py:33
  52.6 1.9 %collective-permute-start.10 = (f32[2,8,1,128]{3,2,1,0:T(1,128)S(1)}, f32[2,8,1,128]{3,2,1,0:T(1,128)S(1)}, u32[]{:S(2)}, u32[]{:S(2)}) collective-permute-start(f32[2,8,1,128]{3,2,1,0:T(1,128)S(1)} %get-tuple-element.67), channel_id=1, source_target_pairs={{1,0},{2,1},{3,2},{5,4},{6,5},{7,6},{9,8},{10,9},{11,10},{13,12},{... | collective-permute-start | bytes 24584 | tf_op jit(solution)/shard_map/ppermute | solution.py:33
  54.6 0.0 collective-permute-done.9
  54.6 3.0 %collective-permute-done.10 = f32[2,8,1,128]{3,2,1,0:T(1,128)S(1)} collective-permute-done((f32[2,8,1,128]{3,2,1,0:T(1,128)S(1)}, f32[2,8,1,128]{3,2,1,0:T(1,128)S(1)}, u32[]{:S(2)}, u32[]{:S(2)}) %collective-permute-start.10) | collective-permute-done | bytes 8224 | tf_op jit(solution)/shard_map/ppermute | solution.py:33
  57.6 0.0 collective-permute-done.7
  57.6 0.0 collective-permute-done.8
  57.6 0.1 fusion.114
  57.7 0.1 add_select_fusion
  57.7 0.1 collective-permute-start.11
  57.8 0.1 fusion.7
  57.9 0.5 power_multiply_fusion.2
  58.4 0.2 fusion.117
  58.6 2.4 %multiply_reduce_fusion.2 = (f32[8,32,128]{2,1,0:T(8,128)S(1)}, f32[8,32,128]{2,1,0:T(8,128)S(1)}, bf16[32,8,32,128]{3,2,1,0:T(8,128)(2,1)S(1)}) fusion(f32[32,8,32,128]{3,2,1,0:T(8,128)S(1)} %copy-done, f32[32,7,32,128]{3,2,1,0:T(8,128)S(1)} %fusion.2, f32[32,32,128]{2,1,0:T(8,128)S(1)} %get-tuple-element.77, f32[32,32,128]{2,1,0:T(8,128)S(1)} %get-tuple-element.54, ...), kind=kLoop, calls=%fused_computation.4 | loop fusion | flops 13565952 | bytes 13369472 | tf_op jit(solution)/shard_map/reduce_sum | solution.py:215
  61.1 0.6 fusion.20
  61.7 2.0 %collective-permute-done.11 = f32[16,32,128]{2,1,0:T(8,128)S(1)} collective-permute-done((f32[16,32,128]{2,1,0:T(8,128)S(1)}, f32[16,32,128]{2,1,0:T(8,128)S(1)}, u32[]{:S(2)}, u32[]{:S(2)}) %collective-permute-start.11) | collective-permute-done | bytes 262176 | tf_op jit(solution)/shard_map/ppermute | solution.py:114
  63.7 0.1 maximum_select_fusion.1
  63.8 0.0 copy-start.3
  63.8 2.7 %multiply_reduce_fusion = (f32[8,32,128]{2,1,0:T(8,128)S(1)}, f32[8,32,128]{2,1,0:T(8,128)S(1)}, bf16[32,8,32,128]{3,2,1,0:T(8,128)(2,1)S(1)}) fusion(f32[32,7,32,128]{3,2,1,0:T(8,128)S(1)} %fusion, f32[32,32,128]{2,1,0:T(8,128)S(1)} %maximum_select_fusion.1, f32[32,32,128]{2,1,0:T(8,128)S(1)} %get-tuple-element.53, f32[8,32]{1,0:T(8,128)S(1)} %get-tuple-element.74, ...), kind=kLoop, calls=%fused_computation.1 | loop fusion | flops 15663104 | bytes 9307264 | tf_op jit(solution)/shard_map/reduce_sum | solution.py:215
  66.5 0.8 broadcast_multiply_fusion
  67.3 0.1 fusion.113
  67.5 7.7 %collective-permute-start.15 = (f32[2,1,32,128]{3,2,1,0:T(8,128)S(1)}, f32[2,1,32,128]{3,2,1,0:T(8,128)S(1)}, u32[]{:S(2)}, u32[]{:S(2)}) collective-permute-start(f32[2,1,32,128]{3,2,1,0:T(8,128)S(1)} %get-tuple-element.64), channel_id=1, source_target_pairs={{4,0},{8,4},{12,8},{16,12},{20,16},{24,20},{28,24},{5,1},{9,5},{13... | collective-permute-start | bytes 98312 | tf_op jit(solution)/shard_map/ppermute | solution.py:33
  75.2 1.9 %collective-permute-start.14 = (f32[2,8,1,128]{3,2,1,0:T(1,128)S(1)}, f32[2,8,1,128]{3,2,1,0:T(1,128)S(1)}, u32[]{:S(2)}, u32[]{:S(2)}) collective-permute-start(f32[2,8,1,128]{3,2,1,0:T(1,128)S(1)} %get-tuple-element.66), channel_id=1, source_target_pairs={{1,0},{2,1},{3,2},{5,4},{6,5},{7,6},{9,8},{10,9},{11,10},{13,12},{... | collective-permute-start | bytes 24584 | tf_op jit(solution)/shard_map/ppermute | solution.py:33
  77.1 3.6 %collective-permute-start.13 = (f32[2,8,1,128]{3,2,1,0:T(1,128)S(1)}, f32[2,8,1,128]{3,2,1,0:T(1,128)S(1)}, u32[]{:S(2)}, u32[]{:S(2)}) collective-permute-start(f32[2,8,1,128]{3,2,1,0:T(1,128)S(1)} %get-tuple-element.65), channel_id=1, source_target_pairs={{0,1},{1,2},{2,3},{4,5},{5,6},{6,7},{8,9},{9,10},{10,11},{12,13},{... | collective-permute-start | bytes 24584 | tf_op jit(solution)/shard_map/ppermute | solution.py:33
  80.8 1.9 %collective-permute-start.12 = (f32[2,1,32,128]{3,2,1,0:T(8,128)S(1)}, f32[2,1,32,128]{3,2,1,0:T(8,128)S(1)}, u32[]{:S(2)}, u32[]{:S(2)}) collective-permute-start(f32[2,1,32,128]{3,2,1,0:T(8,128)S(1)} %get-tuple-element.63), channel_id=1, source_target_pairs={{0,4},{4,8},{8,12},{12,16},{16,20},{20,24},{24,28},{1,5},{5,9},{9,... | collective-permute-start | bytes 98312 | tf_op jit(solution)/shard_map/ppermute | solution.py:33
  82.7 2.4 %pad_maximum_fusion = bf16[64,8,32,128]{3,2,1,0:T(8,128)(2,1)} fusion(bf16[32,8,32,128]{3,2,1,0:T(8,128)(2,1)S(1)} %get-tuple-element.50, bf16[32,8,32,128]{3,2,1,0:T(8,128)(2,1)S(1)} %get-tuple-element.30), kind=kLoop, calls=%fused_computation | loop fusion | flops 2097152 | bytes 8388608 | tf_op jit(solution)/shard_map/dynamic_update_slice | solution.py:235
  85.1 0.0 collective-permute-done.14
  85.1 0.0 collective-permute-done.13
  85.1 0.0 collective-permute-done.15
  85.1 1.2 %collective-permute-done.12 = f32[2,1,32,128]{3,2,1,0:T(8,128)S(1)} collective-permute-done((f32[2,1,32,128]{3,2,1,0:T(8,128)S(1)}, f32[2,1,32,128]{3,2,1,0:T(8,128)S(1)}, u32[]{:S(2)}, u32[]{:S(2)}) %collective-permute-start.12) | collective-permute-done | bytes 32800 | tf_op jit(solution)/shard_map/ppermute | solution.py:33
  86.4 0.5 power_multiply_fusion
  87.0 0.7 fusion.29
  87.6 0.9 %fusion.93 = (f32[8,32,128]{2,1,0:T(8,128)}, f32[8,32,128]{2,1,0:T(8,128)}) fusion(f32[2,8,32,128]{3,2,1,0:T(8,128)S(1)} %fusion.29, f32[8,32]{1,0:T(8,128)S(1)} %get-tuple-element.73, f32[8,32,128]{2,1,0:T(8,128)S(1)} %get-tuple-element.37, f32[8,32,128]{2,1,0:T(8,128)S(1)} %get-tuple-element.38, f32[2,8,32,128]{3,2,1,0:T(8,128)S(1)} %fusion.20, ...), kind=kLoop, calls=%fused_computation.196 | loop fusion | flops 1081344 | bytes 1442816 | tf_op jit(solution)/shard_map/add | solution.py:254
  (18 shorter events, 0.3 us)
Async XLA Ops:
  9.2 7.2 %collective-permute-start = (f32[16,32,128]{2,1,0:T(8,128)S(1)}, f32[16,32,128]{2,1,0:T(8,128)S(1)}, u32[]{:S(2)}, u32[]{:S(2)}) collective-permute-start(f32[16,32,128]{2,1,0:T(8,128)S(1)} %slice_select_fusion.2), channel_id=1, source_target_pairs={{0,4},{4,0},{8,12},{12,8},{16,20},{20,16},{24,28},{28,24},{1,5},{5... | collective-permute-start | bytes 786440 | tf_op jit(solution)/shard_map/ppermute | solution.py:114
  13.3 9.2 %copy-start.2 = (f32[8,32,128]{2,1,0:T(8,128)S(1)}, f32[8,32,128]{2,1,0:T(8,128)}, u32[]{:S(2)}) copy-start(f32[8,32,128]{2,1,0:T(8,128)} %param.8) | copy-start | bytes 393220
  13.3 9.3 %collective-permute-start.2 = (f32[16,32,128]{2,1,0:T(8,128)S(1)}, f32[16,32,128]{2,1,0:T(8,128)S(1)}, u32[]{:S(2)}, u32[]{:S(2)}) collective-permute-start(f32[16,32,128]{2,1,0:T(8,128)S(1)} %slice_select_fusion.1), channel_id=1, source_target_pairs={{0,4},{4,0},{8,12},{12,8},{16,20},{20,16},{24,28},{28,24},{1,5},{5... | collective-permute-start | bytes 786440 | tf_op jit(solution)/shard_map/ppermute | solution.py:114
  16.5 19.9 %copy-start = (f32[32,8,32,128]{3,2,1,0:T(8,128)S(1)}, f32[32,8,32,128]{3,2,1,0:T(8,128)}, u32[]{:S(2)}) copy-start(f32[32,8,32,128]{3,2,1,0:T(8,128)} %get-tuple-element.49) | copy-start | bytes 12582916
  16.5 7.4 %collective-permute-start.1 = (f32[16,32,128]{2,1,0:T(8,128)S(1)}, f32[16,32,128]{2,1,0:T(8,128)S(1)}, u32[]{:S(2)}, u32[]{:S(2)}) collective-permute-start(f32[16,32,128]{2,1,0:T(8,128)S(1)} %fusion.106), channel_id=1, source_target_pairs={{0,8},{4,12},{8,16},{12,20},{16,24},{20,28},{1,9},{5,13},{9,17},{1... | collective-permute-start | bytes 786440 | tf_op jit(solution)/shard_map/ppermute | solution.py:114
  23.9 14.9 %collective-permute-start.3 = (f32[16,32,128]{2,1,0:T(8,128)S(1)}, f32[16,32,128]{2,1,0:T(8,128)S(1)}, u32[]{:S(2)}, u32[]{:S(2)}) collective-permute-start(f32[16,32,128]{2,1,0:T(8,128)S(1)} %add.212), channel_id=1, source_target_pairs={{0,16},{4,20},{8,24},{12,28},{1,17},{5,21},{9,25},{13,29},{2,18},{... | collective-permute-start | bytes 786440 | tf_op jit(solution)/shard_map/ppermute | solution.py:114
  28.2 15.6 %collective-permute-start.4 = (f32[16,32,128]{2,1,0:T(8,128)S(1)}, f32[16,32,128]{2,1,0:T(8,128)S(1)}, u32[]{:S(2)}, u32[]{:S(2)}) collective-permute-start(f32[16,32,128]{2,1,0:T(8,128)S(1)} %fusion.107), channel_id=1, source_target_pairs={{0,8},{4,12},{8,16},{12,20},{16,24},{20,28},{1,9},{5,13},{9,17},{1... | collective-permute-start | bytes 786440 | tf_op jit(solution)/shard_map/ppermute | solution.py:114
  30.1 8.6 %collective-permute-start.5 = (f32[2,1,32,128]{3,2,1,0:T(8,128)S(1)}, f32[2,1,32,128]{3,2,1,0:T(8,128)S(1)}, u32[]{:S(2)}, u32[]{:S(2)}) collective-permute-start(f32[2,1,32,128]{3,2,1,0:T(8,128)S(1)} %get-tuple-element.70), channel_id=1, source_target_pairs={{0,4},{4,8},{8,12},{12,16},{16,20},{20,24},{24,28},{1,5},{5,9},{9,... | collective-permute-start | bytes 98312 | tf_op jit(solution)/shard_map/ppermute | solution.py:33
  33.3 5.5 %collective-permute-start.6 = (f32[2,1,32,128]{3,2,1,0:T(8,128)S(1)}, f32[2,1,32,128]{3,2,1,0:T(8,128)S(1)}, u32[]{:S(2)}, u32[]{:S(2)}) collective-permute-start(f32[2,1,32,128]{3,2,1,0:T(8,128)S(1)} %get-tuple-element.69), channel_id=1, source_target_pairs={{4,0},{8,4},{12,8},{16,12},{20,16},{24,20},{28,24},{5,1},{9,5},{13... | collective-permute-start | bytes 98312 | tf_op jit(solution)/shard_map/ppermute | solution.py:33
  36.4 18.1 %copy-start.5 = (f32[32,128]{1,0:T(8,128)S(1)}, f32[32,128]{1,0:T(8,128)}, u32[]{:S(2)}) copy-start(f32[32,128]{1,0:T(8,128)} %param.14) | copy-start | bytes 49156
  37.3 21.1 %copy-start.4 = (f32[64,32,128]{2,1,0:T(8,128)S(1)}, f32[64,32,128]{2,1,0:T(8,128)}, u32[]{:S(2)}) copy-start(f32[64,32,128]{2,1,0:T(8,128)} %param.12) | copy-start | bytes 3145732
  43.9 14.7 %copy-start.1 = (bf16[64,8,32,128]{3,2,1,0:T(8,128)(2,1)S(1)}, bf16[64,8,32,128]{3,2,1,0:T(8,128)(2,1)}, u32[]{:S(2)}) copy-start(bf16[64,8,32,128]{3,2,1,0:T(8,128)(2,1)} %param.11) | copy-start | bytes 12582916
  44.0 13.6 %collective-permute-start.7 = (f32[16,32,128]{2,1,0:T(8,128)S(1)}, f32[16,32,128]{2,1,0:T(8,128)S(1)}, u32[]{:S(2)}, u32[]{:S(2)}) collective-permute-start(f32[16,32,128]{2,1,0:T(8,128)S(1)} %add_select_fusion.1), channel_id=1, source_target_pairs={{0,4},{4,0},{8,12},{12,8},{16,20},{20,16},{24,28},{28,24},{1,5},{5... | collective-permute-start | bytes 786440 | tf_op jit(solution)/shard_map/ppermute | solution.py:114
  46.0 11.6 %collective-permute-start.8 = (f32[16,32,128]{2,1,0:T(8,128)S(1)}, f32[16,32,128]{2,1,0:T(8,128)S(1)}, u32[]{:S(2)}, u32[]{:S(2)}) collective-permute-start(f32[16,32,128]{2,1,0:T(8,128)S(1)} %add.216), channel_id=1, source_target_pairs={{0,16},{4,20},{8,24},{12,28},{1,17},{5,21},{9,25},{13,29},{2,18},{... | collective-permute-start | bytes 786440 | tf_op jit(solution)/shard_map/ppermute | solution.py:114
  47.4 7.2 %collective-permute-start.9 = (f32[2,8,1,128]{3,2,1,0:T(1,128)S(1)}, f32[2,8,1,128]{3,2,1,0:T(1,128)S(1)}, u32[]{:S(2)}, u32[]{:S(2)}) collective-permute-start(f32[2,8,1,128]{3,2,1,0:T(1,128)S(1)} %get-tuple-element.68), channel_id=1, source_target_pairs={{0,1},{1,2},{2,3},{4,5},{5,6},{6,7},{8,9},{9,10},{10,11},{12,13},{... | collective-permute-start | bytes 24584 | tf_op jit(solution)/shard_map/ppermute | solution.py:33
  52.6 5.0 %collective-permute-start.10 = (f32[2,8,1,128]{3,2,1,0:T(1,128)S(1)}, f32[2,8,1,128]{3,2,1,0:T(1,128)S(1)}, u32[]{:S(2)}, u32[]{:S(2)}) collective-permute-start(f32[2,8,1,128]{3,2,1,0:T(1,128)S(1)} %get-tuple-element.67), channel_id=1, source_target_pairs={{1,0},{2,1},{3,2},{5,4},{6,5},{7,6},{9,8},{10,9},{11,10},{13,12},{... | collective-permute-start | bytes 24584 | tf_op jit(solution)/shard_map/ppermute | solution.py:33
  57.7 6.0 %collective-permute-start.11 = (f32[16,32,128]{2,1,0:T(8,128)S(1)}, f32[16,32,128]{2,1,0:T(8,128)S(1)}, u32[]{:S(2)}, u32[]{:S(2)}) collective-permute-start(f32[16,32,128]{2,1,0:T(8,128)S(1)} %add_select_fusion), channel_id=1, source_target_pairs={{0,4},{4,0},{8,12},{12,8},{16,20},{20,16},{24,28},{28,24},{1,5},{5... | collective-permute-start | bytes 786440 | tf_op jit(solution)/shard_map/ppermute | solution.py:114
  63.8 2.7 %copy-start.3 = (f32[8,32,128]{2,1,0:T(8,128)S(1)}, f32[8,32,128]{2,1,0:T(8,128)}, u32[]{:S(2)}) copy-start(f32[8,32,128]{2,1,0:T(8,128)} %param.9) | copy-start | bytes 393220
  67.5 17.6 %collective-permute-start.15 = (f32[2,1,32,128]{3,2,1,0:T(8,128)S(1)}, f32[2,1,32,128]{3,2,1,0:T(8,128)S(1)}, u32[]{:S(2)}, u32[]{:S(2)}) collective-permute-start(f32[2,1,32,128]{3,2,1,0:T(8,128)S(1)} %get-tuple-element.64), channel_id=1, source_target_pairs={{4,0},{8,4},{12,8},{16,12},{20,16},{24,20},{28,24},{5,1},{9,5},{13... | collective-permute-start | bytes 98312 | tf_op jit(solution)/shard_map/ppermute | solution.py:33
  75.2 9.9 %collective-permute-start.14 = (f32[2,8,1,128]{3,2,1,0:T(1,128)S(1)}, f32[2,8,1,128]{3,2,1,0:T(1,128)S(1)}, u32[]{:S(2)}, u32[]{:S(2)}) collective-permute-start(f32[2,8,1,128]{3,2,1,0:T(1,128)S(1)} %get-tuple-element.66), channel_id=1, source_target_pairs={{1,0},{2,1},{3,2},{5,4},{6,5},{7,6},{9,8},{10,9},{11,10},{13,12},{... | collective-permute-start | bytes 24584 | tf_op jit(solution)/shard_map/ppermute | solution.py:33
  77.1 8.0 %collective-permute-start.13 = (f32[2,8,1,128]{3,2,1,0:T(1,128)S(1)}, f32[2,8,1,128]{3,2,1,0:T(1,128)S(1)}, u32[]{:S(2)}, u32[]{:S(2)}) collective-permute-start(f32[2,8,1,128]{3,2,1,0:T(1,128)S(1)} %get-tuple-element.65), channel_id=1, source_target_pairs={{0,1},{1,2},{2,3},{4,5},{5,6},{6,7},{8,9},{9,10},{10,11},{12,13},{... | collective-permute-start | bytes 24584 | tf_op jit(solution)/shard_map/ppermute | solution.py:33
  80.8 5.6 %collective-permute-start.12 = (f32[2,1,32,128]{3,2,1,0:T(8,128)S(1)}, f32[2,1,32,128]{3,2,1,0:T(8,128)S(1)}, u32[]{:S(2)}, u32[]{:S(2)}) collective-permute-start(f32[2,1,32,128]{3,2,1,0:T(8,128)S(1)} %get-tuple-element.63), channel_id=1, source_target_pairs={{0,4},{4,8},{8,12},{12,16},{16,20},{20,24},{24,28},{1,5},{5,9},{9,... | collective-permute-start | bytes 98312 | tf_op jit(solution)/shard_map/ppermute | solution.py:33

commit v11 on v10

--- a/solution.py
+++ b/solution.py
@@ -112,15 +112,15 @@
         if stage < groups:
             live[stage] = next(steps[stage])
         arrived = {g: lax.ppermute(payload, axis, pairs) for g, (payload, pairs) in live.items()}
-        if stage == 0:
-            for g in range(1, groups):
-                steps[g] = paired_steps(totals_of(g * size, size, live[0][0]), axis)
         tied = (arrived, made)
         if stage in riders:
             tied, carried[stage] = lax.optimization_barrier((tied, riders[stage](live[0][0])))
         else:
             tied = lax.optimization_barrier(tied)
         arrived, made = tied
+        if stage == 0:
+            for g in range(1, groups):
+                steps[g] = paired_steps(totals_of(g * size, size, arrived[0]), axis)
         following = {}
         for g, value in arrived.items():
             try:
@@ -196,14 +196,27 @@
         )
         return absorber[None] * weight + glass_term[None], weight
 
+    computed = {}
+
     def totals_of(start, size, after):
-        optical_depth, _ = depth_of(start, size)
-        if after is not None:
-            optical_depth, _ = lax.optimization_barrier((optical_depth, after))
+        if after is None:
+            earlier, absorbed = lax.optimization_barrier(
+                (earlier_spectral_power[start : start + size], absorber)
+            )
+            weight = spectral_attenuation_section[start : start + size, None, None, None] / (
+                1.0 + earlier.astype(jnp.float32) / saturation
+            )
+            return jnp.sum(absorbed[None] * weight + glass_term[None], axis=1)
+        earlier, absorbed, _ = lax.optimization_barrier((earlier_spectral_power, absorber, after))
+        weight = spectral_attenuation_section[start : start + size, None, None, None] / (
+            1.0 + earlier[start : start + size].astype(jnp.float32) / saturation
+        )
+        optical_depth = absorbed[None] * weight + glass_term[None]
+        computed[start] = optical_depth, weight
         return jnp.sum(optical_depth, axis=1)
 
     def emit(start, size, earlier):
-        optical_depth, weight = depth_of(start, size)
+        optical_depth, weight = computed[start] if start in computed else depth_of(start, size)
         local_column = jnp.pad(
             jnp.cumsum(optical_depth[:, : rows - 1], axis=1), ((0, 0), (1, 0), (0, 0), (0, 0))
         )

time: 89 us -> 92.3 us (1.037); the launches traced: 88.5 us -> 90.7 us
  waiting for transfers between devices: 17 us -> 31.3 us
  other arithmetic: 26.4 us -> 19.6 us
  starting transfers between devices: 43.2 us -> 37.8 us
    ppermute x8, waiting for transfers between devices: 11.2 us -> 27.2 us  [pipelined_scan(): lax.ppermute(payload, axis, pairs)]
    reduce_sum x2 -> x1, other arithmetic: 8.66 us -> 1.14 us  [totals_of(): return jnp.sum(optical_depth, axis=1)]
    ppermute x8, starting transfers between devices: 28.6 us -> 24 us  [shifted(): return lax.ppermute(block, axis, pairs)]
    add x0 -> x1, other arithmetic: none -> 3.42 us  [depth_of(): return (absorber[None] * weight + glass_term[None], weight)]
    another operation x2, other arithmetic: 3.4 us -> 1.63 us  [emit(): jnp.cumsum(optical_depth[:, :rows - 1], axis=1)]
    ppermute x8, waiting for transfers between devices: 5.73 us -> 4.14 us  [shifted(): return lax.ppermute(block, axis, pairs)]
    another operation x2, other arithmetic: 1.09 us -> 0.12 us  [local(): jnp.stack([xenon_spin_polarization, heat_ratio - boundary_kelvin])]
  transfers between devices with their start and end apart: 16 -> 16, of which waited for: 7 -> 7; matrix products, arithmetic and copies ran while one was open for 14% -> 10% of each run, Pallas kernels for 0% -> 0%
where the time goes in v11:
time: 92.3 us; the launch traced here: 90.7 us
  starting transfers between devices  37.8 us (41%)
  waiting for transfers between devices  31.3 us (34%)
  other arithmetic  19.6 us (21%)
  between operations  1.09 us (1%)
  local copies, waits for them, and re-layouts  0.96 us (1%)
    ppermute x8, waiting for transfers between devices, pipelined_scan(): lax.ppermute(payload, axis, pairs)  27.2 us
    ppermute x8, starting transfers between devices, shifted(): return lax.ppermute(block, axis, pairs)  24 us
    ppermute x8, starting transfers between devices, pipelined_scan(): lax.ppermute(payload, axis, pairs)  13.7 us
    reduce_sum x2, other arithmetic, emit(): jnp.sum(radiance * (1.0 - jnp.exp(-optical_depth)), axis=0)  5.06 us
    ppermute x8, waiting for transfers between devices, shifted(): return lax.ppermute(block, axis, pairs)  4.14 us
    add x1, other arithmetic, depth_of(): return (absorber[None] * weight + glass_term[None], weight)  3.42 us
    dynamic_update_slice x1, other arithmetic, local(): lax.dynamic_update_slice_in_dim(spectral_power, part, start, axis=0)  2.38 us
  transfers between devices with their start and end apart: 16, of which 7 were waited for; matrix products, arithmetic and copies ran while one was open for 10% of the time, Pallas kernels for 0%

profile of v11, /device:TPU:9, one launch (start us, length us, event | category | flops | bytes accessed | tf_op | source)
XLA Modules:
  0.0 90.7 jit_solution(7833535430276414335)
XLA Ops:
  0.6 0.0 slice-start
  0.7 0.9 fusion.120
  1.6 0.7 convert_subtract_fusion
  2.3 0.1 add_bitcast_fusion
  2.4 0.0 slice-done
  2.4 0.0 copy-start
  2.4 3.4 %multiply_add_fusion = (f32[32,8,32,128]{3,2,1,0:T(8,128)S(1)}, f32[32,32,128]{2,1,0:T(8,128)S(1)}) fusion(f32[8,32,128]{2,1,0:T(8,128)S(1)} %get-tuple-element.26, f32[8,32]{1,0:T(8,128)S(1)} %get-tuple-element.81, f32[32]{0:T(128)S(1)} %get-tuple-element.83, bf16[64,8,32,128]{3,2,1,0:T(8,128)(2,1)} %param.11, bf16[32,8,32,128]{3,2,1,0:T(8,128)(2,1)S(1)} %slice-done), kind=kLoop, calls=%fused_computation.7 | loop fusion | flops 11403264 | bytes 9179648 | tf_op jit(solution)/shard_map/add | solution.py:197
  5.9 1.3 %collective-permute-start = (f32[16,32,128]{2,1,0:T(8,128)S(1)}, f32[16,32,128]{2,1,0:T(8,128)S(1)}, u32[]{:S(2)}, u32[]{:S(2)}) collective-permute-start(f32[16,32,128]{2,1,0:T(8,128)S(1)} %slice_select_fusion.2), channel_id=1, source_target_pairs={{0,4},{4,0},{8,12},{12,8},{16,20},{20,16},{24,28},{28,24},{1,5},{5... | collective-permute-start | bytes 786440 | tf_op jit(solution)/shard_map/ppermute | solution.py:114
  7.2 5.9 %collective-permute-done = f32[16,32,128]{2,1,0:T(8,128)S(1)} collective-permute-done((f32[16,32,128]{2,1,0:T(8,128)S(1)}, f32[16,32,128]{2,1,0:T(8,128)S(1)}, u32[]{:S(2)}, u32[]{:S(2)}) %collective-permute-start) | collective-permute-done | bytes 262176 | tf_op jit(solution)/shard_map/ppermute | solution.py:114
  13.1 0.1 fusion.106
  13.2 3.2 %collective-permute-start.1 = (f32[16,32,128]{2,1,0:T(8,128)S(1)}, f32[16,32,128]{2,1,0:T(8,128)S(1)}, u32[]{:S(2)}, u32[]{:S(2)}) collective-permute-start(f32[16,32,128]{2,1,0:T(8,128)S(1)} %fusion.106), channel_id=1, source_target_pairs={{0,8},{4,12},{8,16},{12,20},{16,24},{20,28},{1,9},{5,13},{9,17},{1... | collective-permute-start | bytes 786440 | tf_op jit(solution)/shard_map/ppermute | solution.py:114
  16.4 1.1 %fusion.116 = (f32[32,32,128]{2,1,0:T(8,128)S(1)}, f32[32,8,32,128]{3,2,1,0:T(8,128)S(1)}) fusion(f32[8,32]{1,0:T(8,128)S(1)} %get-tuple-element.81, bf16[64,8,32,128]{3,2,1,0:T(8,128)(2,1)S(1)} %copy-done, f32[32]{0:T(128)S(1)} %get-tuple-element.82, f32[8,32,128]{2,1,0:T(8,128)S(1)} %get-tuple-element.26), kind=kLoop, calls=%fused_computation.231 | loop fusion | flops 6160384 | bytes 6947968 | tf_op jit(solution)/shard_map/reduce_sum | solution.py:216
  17.5 0.0 copy-start.1
  17.6 1.3 %collective-permute-start.2 = (f32[16,32,128]{2,1,0:T(8,128)S(1)}, f32[16,32,128]{2,1,0:T(8,128)S(1)}, u32[]{:S(2)}, u32[]{:S(2)}) collective-permute-start(f32[16,32,128]{2,1,0:T(8,128)S(1)} %slice_select_fusion.1), channel_id=1, source_target_pairs={{0,4},{4,0},{8,12},{12,8},{16,20},{20,16},{24,28},{28,24},{1,5},{5... | collective-permute-start | bytes 786440 | tf_op jit(solution)/shard_map/ppermute | solution.py:114
  18.9 0.8 fusion.2
  19.7 1.6 %collective-permute-done.1 = f32[16,32,128]{2,1,0:T(8,128)S(1)} collective-permute-done((f32[16,32,128]{2,1,0:T(8,128)S(1)}, f32[16,32,128]{2,1,0:T(8,128)S(1)}, u32[]{:S(2)}, u32[]{:S(2)}) %collective-permute-start.1) | collective-permute-done | bytes 262176 | tf_op jit(solution)/shard_map/ppermute | solution.py:114
  21.3 2.3 %collective-permute-done.2 = f32[16,32,128]{2,1,0:T(8,128)S(1)} collective-permute-done((f32[16,32,128]{2,1,0:T(8,128)S(1)}, f32[16,32,128]{2,1,0:T(8,128)S(1)}, u32[]{:S(2)}, u32[]{:S(2)}) %collective-permute-start.2) | collective-permute-done | bytes 262176 | tf_op jit(solution)/shard_map/ppermute | solution.py:114
  23.7 2.6 %collective-permute-start.3 = (f32[16,32,128]{2,1,0:T(8,128)S(1)}, f32[16,32,128]{2,1,0:T(8,128)S(1)}, u32[]{:S(2)}, u32[]{:S(2)}) collective-permute-start(f32[16,32,128]{2,1,0:T(8,128)S(1)} %add.211), channel_id=1, source_target_pairs={{0,16},{4,20},{8,24},{12,28},{1,17},{5,21},{9,25},{13,29},{2,18},{... | collective-permute-start | bytes 786440 | tf_op jit(solution)/shard_map/ppermute | solution.py:114
  26.3 0.1 fusion.107
  26.3 1.9 %collective-permute-start.4 = (f32[16,32,128]{2,1,0:T(8,128)S(1)}, f32[16,32,128]{2,1,0:T(8,128)S(1)}, u32[]{:S(2)}, u32[]{:S(2)}) collective-permute-start(f32[16,32,128]{2,1,0:T(8,128)S(1)} %fusion.107), channel_id=1, source_target_pairs={{0,8},{4,12},{8,16},{12,20},{16,24},{20,28},{1,9},{5,13},{9,17},{1... | collective-permute-start | bytes 786440 | tf_op jit(solution)/shard_map/ppermute | solution.py:114
  28.3 4.3 %collective-permute-start.6 = (f32[2,1,32,128]{3,2,1,0:T(8,128)S(1)}, f32[2,1,32,128]{3,2,1,0:T(8,128)S(1)}, u32[]{:S(2)}, u32[]{:S(2)}) collective-permute-start(f32[2,1,32,128]{3,2,1,0:T(8,128)S(1)} %get-tuple-element.74), channel_id=1, source_target_pairs={{4,0},{8,4},{12,8},{16,12},{20,16},{24,20},{28,24},{5,1},{9,5},{13... | collective-permute-start | bytes 98312 | tf_op jit(solution)/shard_map/ppermute | solution.py:33
  32.6 1.9 %collective-permute-start.5 = (f32[2,1,32,128]{3,2,1,0:T(8,128)S(1)}, f32[2,1,32,128]{3,2,1,0:T(8,128)S(1)}, u32[]{:S(2)}, u32[]{:S(2)}) collective-permute-start(f32[2,1,32,128]{3,2,1,0:T(8,128)S(1)} %get-tuple-element.75), channel_id=1, source_target_pairs={{0,4},{4,8},{8,12},{12,16},{16,20},{20,24},{24,28},{1,5},{5,9},{9,... | collective-permute-start | bytes 98312 | tf_op jit(solution)/shard_map/ppermute | solution.py:33
  34.6 0.0 collective-permute-done.6
  34.6 4.1 %collective-permute-done.5 = f32[2,1,32,128]{3,2,1,0:T(8,128)S(1)} collective-permute-done((f32[2,1,32,128]{3,2,1,0:T(8,128)S(1)}, f32[2,1,32,128]{3,2,1,0:T(8,128)S(1)}, u32[]{:S(2)}, u32[]{:S(2)}) %collective-permute-start.5) | collective-permute-done | bytes 32800 | tf_op jit(solution)/shard_map/ppermute | solution.py:33
  38.7 3.2 %collective-permute-done.4 = f32[16,32,128]{2,1,0:T(8,128)S(1)} collective-permute-done((f32[16,32,128]{2,1,0:T(8,128)S(1)}, f32[16,32,128]{2,1,0:T(8,128)S(1)}, u32[]{:S(2)}, u32[]{:S(2)}) %collective-permute-start.4) | collective-permute-done | bytes 262176 | tf_op jit(solution)/shard_map/ppermute | solution.py:114
  41.9 0.0 collective-permute-done.3
  41.9 0.1 fusion.115
  42.0 0.1 add_select_fusion.1
  42.1 2.0 %collective-permute-start.7 = (f32[16,32,128]{2,1,0:T(8,128)S(1)}, f32[16,32,128]{2,1,0:T(8,128)S(1)}, u32[]{:S(2)}, u32[]{:S(2)}) collective-permute-start(f32[16,32,128]{2,1,0:T(8,128)S(1)} %add_select_fusion.1), channel_id=1, source_target_pairs={{0,4},{4,0},{8,12},{12,8},{16,20},{20,16},{24,28},{28,24},{1,5},{5... | collective-permute-start | bytes 786440 | tf_op jit(solution)/shard_map/ppermute | solution.py:114
  44.1 4.3 %collective-permute-start.10 = (f32[2,8,1,128]{3,2,1,0:T(1,128)S(1)}, f32[2,8,1,128]{3,2,1,0:T(1,128)S(1)}, u32[]{:S(2)}, u32[]{:S(2)}) collective-permute-start(f32[2,8,1,128]{3,2,1,0:T(1,128)S(1)} %get-tuple-element.72), channel_id=1, source_target_pairs={{1,0},{2,1},{3,2},{5,4},{6,5},{7,6},{9,8},{10,9},{11,10},{13,12},{... | collective-permute-start | bytes 24584 | tf_op jit(solution)/shard_map/ppermute | solution.py:33
  48.4 3.0 %collective-permute-start.9 = (f32[2,8,1,128]{3,2,1,0:T(1,128)S(1)}, f32[2,8,1,128]{3,2,1,0:T(1,128)S(1)}, u32[]{:S(2)}, u32[]{:S(2)}) collective-permute-start(f32[2,8,1,128]{3,2,1,0:T(1,128)S(1)} %get-tuple-element.73), channel_id=1, source_target_pairs={{0,1},{1,2},{2,3},{4,5},{5,6},{6,7},{8,9},{9,10},{10,11},{12,13},{... | collective-permute-start | bytes 24584 | tf_op jit(solution)/shard_map/ppermute | solution.py:33
  51.4 1.3 %collective-permute-start.8 = (f32[16,32,128]{2,1,0:T(8,128)S(1)}, f32[16,32,128]{2,1,0:T(8,128)S(1)}, u32[]{:S(2)}, u32[]{:S(2)}) collective-permute-start(f32[16,32,128]{2,1,0:T(8,128)S(1)} %add.215), channel_id=1, source_target_pairs={{0,16},{4,20},{8,24},{12,28},{1,17},{5,21},{9,25},{13,29},{2,18},{... | collective-permute-start | bytes 786440 | tf_op jit(solution)/shard_map/ppermute | solution.py:114
  52.7 0.0 copy-start.3
  52.7 0.9 fusion
  53.6 0.0 collective-permute-done.10
  53.6 0.0 collective-permute-done.9
  53.6 10.4 %collective-permute-done.8 = f32[16,32,128]{2,1,0:T(8,128)S(1)} collective-permute-done((f32[16,32,128]{2,1,0:T(8,128)S(1)}, f32[16,32,128]{2,1,0:T(8,128)S(1)}, u32[]{:S(2)}, u32[]{:S(2)}) %collective-permute-start.8) | collective-permute-done | bytes 262176 | tf_op jit(solution)/shard_map/ppermute | solution.py:114
  64.0 0.0 collective-permute-done.7
  64.0 0.1 fusion.114
  64.1 0.1 add_select_fusion
  64.2 0.1 collective-permute-start.11
  64.2 0.1 fusion.7
  64.3 0.5 power_multiply_fusion.2
  64.9 0.2 fusion.117
  65.0 2.7 %multiply_reduce_fusion.2 = (f32[8,32,128]{2,1,0:T(8,128)S(1)}, f32[8,32,128]{2,1,0:T(8,128)S(1)}, bf16[32,8,32,128]{3,2,1,0:T(8,128)(2,1)S(1)}) fusion(f32[32,7,32,128]{3,2,1,0:T(8,128)S(1)} %fusion.2, f32[32,32,128]{2,1,0:T(8,128)S(1)} %get-tuple-element.84, f32[32,32,128]{2,1,0:T(8,128)S(1)} %get-tuple-element.59, f32[8,32]{1,0:T(8,128)S(1)} %get-tuple-element.81, ...), kind=kLoop, calls=%fused_computation.4 | loop fusion | flops 15663104 | bytes 9307264 | tf_op jit(solution)/shard_map/reduce_sum | solution.py:228
  67.7 0.7 fusion.20
  68.4 3.7 %collective-permute-done.11 = f32[16,32,128]{2,1,0:T(8,128)S(1)} collective-permute-done((f32[16,32,128]{2,1,0:T(8,128)S(1)}, f32[16,32,128]{2,1,0:T(8,128)S(1)}, u32[]{:S(2)}, u32[]{:S(2)}) %collective-permute-start.11) | collective-permute-done | bytes 262176 | tf_op jit(solution)/shard_map/ppermute | solution.py:114
  72.1 0.1 maximum_select_fusion.1
  72.2 2.4 %multiply_reduce_fusion = (f32[8,32,128]{2,1,0:T(8,128)S(1)}, f32[8,32,128]{2,1,0:T(8,128)S(1)}, bf16[32,8,32,128]{3,2,1,0:T(8,128)(2,1)S(1)}) fusion(f32[32,8,32,128]{3,2,1,0:T(8,128)S(1)} %get-tuple-element.55, f32[32,7,32,128]{3,2,1,0:T(8,128)S(1)} %fusion, f32[32,32,128]{2,1,0:T(8,128)S(1)} %maximum_select_fusion.1, ...), kind=kLoop, calls=%fused_computation.1 | loop fusion | flops 13565952 | bytes 13369472 | tf_op jit(solution)/shard_map/reduce_sum | solution.py:228
  74.6 0.8 broadcast_multiply_fusion
  75.4 0.1 fusion.113
  75.5 1.9 %collective-permute-start.13 = (f32[2,8,1,128]{3,2,1,0:T(1,128)S(1)}, f32[2,8,1,128]{3,2,1,0:T(1,128)S(1)}, u32[]{:S(2)}, u32[]{:S(2)}) collective-permute-start(f32[2,8,1,128]{3,2,1,0:T(1,128)S(1)} %get-tuple-element.70), channel_id=1, source_target_pairs={{0,1},{1,2},{2,3},{4,5},{5,6},{6,7},{8,9},{9,10},{10,11},{12,13},{... | collective-permute-start | bytes 24584 | tf_op jit(solution)/shard_map/ppermute | solution.py:33
  77.5 2.4 %collective-permute-start.14 = (f32[2,8,1,128]{3,2,1,0:T(1,128)S(1)}, f32[2,8,1,128]{3,2,1,0:T(1,128)S(1)}, u32[]{:S(2)}, u32[]{:S(2)}) collective-permute-start(f32[2,8,1,128]{3,2,1,0:T(1,128)S(1)} %get-tuple-element.71), channel_id=1, source_target_pairs={{1,0},{2,1},{3,2},{5,4},{6,5},{7,6},{9,8},{10,9},{11,10},{13,12},{... | collective-permute-start | bytes 24584 | tf_op jit(solution)/shard_map/ppermute | solution.py:33
  79.9 2.1 %collective-permute-start.12 = (f32[2,1,32,128]{3,2,1,0:T(8,128)S(1)}, f32[2,1,32,128]{3,2,1,0:T(8,128)S(1)}, u32[]{:S(2)}, u32[]{:S(2)}) collective-permute-start(f32[2,1,32,128]{3,2,1,0:T(8,128)S(1)} %get-tuple-element.68), channel_id=1, source_target_pairs={{0,4},{4,8},{8,12},{12,16},{16,20},{20,24},{24,28},{1,5},{5,9},{9,... | collective-permute-start | bytes 98312 | tf_op jit(solution)/shard_map/ppermute | solution.py:33
  82.0 4.1 %collective-permute-start.15 = (f32[2,1,32,128]{3,2,1,0:T(8,128)S(1)}, f32[2,1,32,128]{3,2,1,0:T(8,128)S(1)}, u32[]{:S(2)}, u32[]{:S(2)}) collective-permute-start(f32[2,1,32,128]{3,2,1,0:T(8,128)S(1)} %get-tuple-element.69), channel_id=1, source_target_pairs={{4,0},{8,4},{12,8},{16,12},{20,16},{24,20},{28,24},{5,1},{9,5},{13... | collective-permute-start | bytes 98312 | tf_op jit(solution)/shard_map/ppermute | solution.py:33
  86.1 2.4 %pad_maximum_fusion = bf16[64,8,32,128]{3,2,1,0:T(8,128)(2,1)} fusion(bf16[32,8,32,128]{3,2,1,0:T(8,128)(2,1)S(1)} %get-tuple-element.56, bf16[32,8,32,128]{3,2,1,0:T(8,128)(2,1)S(1)} %get-tuple-element.36), kind=kLoop, calls=%fused_computation | loop fusion | flops 2097152 | bytes 8388608 | tf_op jit(solution)/shard_map/dynamic_update_slice | solution.py:248
  88.5 0.0 collective-permute-done.13
  88.5 0.0 collective-permute-done.14
  88.5 0.0 collective-permute-done.12
  88.5 0.0 collective-permute-done.15
  88.5 0.1 fusion.9
  88.5 0.5 power_multiply_fusion
  89.1 0.7 fusion.29
  89.8 0.9 fusion.93
  (20 shorter events, 0.2 us)
Async XLA Ops:
  0.6 1.8 %slice-start = ((bf16[64,8,32,128]{3,2,1,0:T(8,128)(2,1)}), bf16[32,8,32,128]{3,2,1,0:T(8,128)(2,1)S(1)}, s32[]{:S(2)}) async-start(bf16[64,8,32,128]{3,2,1,0:T(8,128)(2,1)} %param.11), calls=%async_computation | async-start | bytes 4194304 | tf_op jit(solution)/shard_map/slice | solution.py:204
  0.6 1.6 %copy-start.2 = (f32[8,32,128]{2,1,0:T(8,128)S(1)}, f32[8,32,128]{2,1,0:T(8,128)}, u32[]{:S(2)}) copy-start(f32[8,32,128]{2,1,0:T(8,128)} %param.9) | copy-start | bytes 393220
  0.7 1.6 %copy-start.4 = (f32[8,32,128]{2,1,0:T(8,128)S(1)}, f32[8,32,128]{2,1,0:T(8,128)}, u32[]{:S(2)}) copy-start(f32[8,32,128]{2,1,0:T(8,128)} %param.10) | copy-start | bytes 393220
  2.4 14.0 %copy-start = (bf16[64,8,32,128]{3,2,1,0:T(8,128)(2,1)S(1)}, bf16[64,8,32,128]{3,2,1,0:T(8,128)(2,1)}, u32[]{:S(2)}) copy-start(bf16[64,8,32,128]{3,2,1,0:T(8,128)(2,1)} %param.11) | copy-start | bytes 12582916
  5.9 7.2 %collective-permute-start = (f32[16,32,128]{2,1,0:T(8,128)S(1)}, f32[16,32,128]{2,1,0:T(8,128)S(1)}, u32[]{:S(2)}, u32[]{:S(2)}) collective-permute-start(f32[16,32,128]{2,1,0:T(8,128)S(1)} %slice_select_fusion.2), channel_id=1, source_target_pairs={{0,4},{4,0},{8,12},{12,8},{16,20},{20,16},{24,28},{28,24},{1,5},{5... | collective-permute-start | bytes 786440 | tf_op jit(solution)/shard_map/ppermute | solution.py:114
  13.2 8.1 %collective-permute-start.1 = (f32[16,32,128]{2,1,0:T(8,128)S(1)}, f32[16,32,128]{2,1,0:T(8,128)S(1)}, u32[]{:S(2)}, u32[]{:S(2)}) collective-permute-start(f32[16,32,128]{2,1,0:T(8,128)S(1)} %fusion.106), channel_id=1, source_target_pairs={{0,8},{4,12},{8,16},{12,20},{16,24},{20,28},{1,9},{5,13},{9,17},{1... | collective-permute-start | bytes 786440 | tf_op jit(solution)/shard_map/ppermute | solution.py:114
  17.5 2.2 %copy-start.1 = (f32[8,32,128]{2,1,0:T(8,128)S(1)}, f32[8,32,128]{2,1,0:T(8,128)}, u32[]{:S(2)}) copy-start(f32[8,32,128]{2,1,0:T(8,128)} %param.8) | copy-start | bytes 393220
  17.6 6.0 %collective-permute-start.2 = (f32[16,32,128]{2,1,0:T(8,128)S(1)}, f32[16,32,128]{2,1,0:T(8,128)S(1)}, u32[]{:S(2)}, u32[]{:S(2)}) collective-permute-start(f32[16,32,128]{2,1,0:T(8,128)S(1)} %slice_select_fusion.1), channel_id=1, source_target_pairs={{0,4},{4,0},{8,12},{12,8},{16,20},{20,16},{24,28},{28,24},{1,5},{5... | collective-permute-start | bytes 786440 | tf_op jit(solution)/shard_map/ppermute | solution.py:114
  18.9 15.6 %copy-start.5 = (f32[32,128]{1,0:T(8,128)S(1)}, f32[32,128]{1,0:T(8,128)}, u32[]{:S(2)}) copy-start(f32[32,128]{1,0:T(8,128)} %param.14) | copy-start | bytes 49156
  23.7 18.3 %collective-permute-start.3 = (f32[16,32,128]{2,1,0:T(8,128)S(1)}, f32[16,32,128]{2,1,0:T(8,128)S(1)}, u32[]{:S(2)}, u32[]{:S(2)}) collective-permute-start(f32[16,32,128]{2,1,0:T(8,128)S(1)} %add.211), channel_id=1, source_target_pairs={{0,16},{4,20},{8,24},{12,28},{1,17},{5,21},{9,25},{13,29},{2,18},{... | collective-permute-start | bytes 786440 | tf_op jit(solution)/shard_map/ppermute | solution.py:114
  26.3 15.6 %collective-permute-start.4 = (f32[16,32,128]{2,1,0:T(8,128)S(1)}, f32[16,32,128]{2,1,0:T(8,128)S(1)}, u32[]{:S(2)}, u32[]{:S(2)}) collective-permute-start(f32[16,32,128]{2,1,0:T(8,128)S(1)} %fusion.107), channel_id=1, source_target_pairs={{0,8},{4,12},{8,16},{12,20},{16,24},{20,28},{1,9},{5,13},{9,17},{1... | collective-permute-start | bytes 786440 | tf_op jit(solution)/shard_map/ppermute | solution.py:114
  28.3 6.3 %collective-permute-start.6 = (f32[2,1,32,128]{3,2,1,0:T(8,128)S(1)}, f32[2,1,32,128]{3,2,1,0:T(8,128)S(1)}, u32[]{:S(2)}, u32[]{:S(2)}) collective-permute-start(f32[2,1,32,128]{3,2,1,0:T(8,128)S(1)} %get-tuple-element.74), channel_id=1, source_target_pairs={{4,0},{8,4},{12,8},{16,12},{20,16},{24,20},{28,24},{5,1},{9,5},{13... | collective-permute-start | bytes 98312 | tf_op jit(solution)/shard_map/ppermute | solution.py:33
  32.6 6.1 %collective-permute-start.5 = (f32[2,1,32,128]{3,2,1,0:T(8,128)S(1)}, f32[2,1,32,128]{3,2,1,0:T(8,128)S(1)}, u32[]{:S(2)}, u32[]{:S(2)}) collective-permute-start(f32[2,1,32,128]{3,2,1,0:T(8,128)S(1)} %get-tuple-element.75), channel_id=1, source_target_pairs={{0,4},{4,8},{8,12},{12,16},{16,20},{20,24},{24,28},{1,5},{5,9},{9,... | collective-permute-start | bytes 98312 | tf_op jit(solution)/shard_map/ppermute | solution.py:33
  42.1 22.0 %collective-permute-start.7 = (f32[16,32,128]{2,1,0:T(8,128)S(1)}, f32[16,32,128]{2,1,0:T(8,128)S(1)}, u32[]{:S(2)}, u32[]{:S(2)}) collective-permute-start(f32[16,32,128]{2,1,0:T(8,128)S(1)} %add_select_fusion.1), channel_id=1, source_target_pairs={{0,4},{4,0},{8,12},{12,8},{16,20},{20,16},{24,28},{28,24},{1,5},{5... | collective-permute-start | bytes 786440 | tf_op jit(solution)/shard_map/ppermute | solution.py:114
  44.1 9.5 %collective-permute-start.10 = (f32[2,8,1,128]{3,2,1,0:T(1,128)S(1)}, f32[2,8,1,128]{3,2,1,0:T(1,128)S(1)}, u32[]{:S(2)}, u32[]{:S(2)}) collective-permute-start(f32[2,8,1,128]{3,2,1,0:T(1,128)S(1)} %get-tuple-element.72), channel_id=1, source_target_pairs={{1,0},{2,1},{3,2},{5,4},{6,5},{7,6},{9,8},{10,9},{11,10},{13,12},{... | collective-permute-start | bytes 24584 | tf_op jit(solution)/shard_map/ppermute | solution.py:33
  48.4 5.2 %collective-permute-start.9 = (f32[2,8,1,128]{3,2,1,0:T(1,128)S(1)}, f32[2,8,1,128]{3,2,1,0:T(1,128)S(1)}, u32[]{:S(2)}, u32[]{:S(2)}) collective-permute-start(f32[2,8,1,128]{3,2,1,0:T(1,128)S(1)} %get-tuple-element.73), channel_id=1, source_target_pairs={{0,1},{1,2},{2,3},{4,5},{5,6},{6,7},{8,9},{9,10},{10,11},{12,13},{... | collective-permute-start | bytes 24584 | tf_op jit(solution)/shard_map/ppermute | solution.py:33
  51.4 12.6 %collective-permute-start.8 = (f32[16,32,128]{2,1,0:T(8,128)S(1)}, f32[16,32,128]{2,1,0:T(8,128)S(1)}, u32[]{:S(2)}, u32[]{:S(2)}) collective-permute-start(f32[16,32,128]{2,1,0:T(8,128)S(1)} %add.215), channel_id=1, source_target_pairs={{0,16},{4,20},{8,24},{12,28},{1,17},{5,21},{9,25},{13,29},{2,18},{... | collective-permute-start | bytes 786440 | tf_op jit(solution)/shard_map/ppermute | solution.py:114
  52.7 12.1 %copy-start.3 = (f32[64,32,128]{2,1,0:T(8,128)S(1)}, f32[64,32,128]{2,1,0:T(8,128)}, u32[]{:S(2)}) copy-start(f32[64,32,128]{2,1,0:T(8,128)} %param.12) | copy-start | bytes 3145732
  64.2 8.0 %collective-permute-start.11 = (f32[16,32,128]{2,1,0:T(8,128)S(1)}, f32[16,32,128]{2,1,0:T(8,128)S(1)}, u32[]{:S(2)}, u32[]{:S(2)}) collective-permute-start(f32[16,32,128]{2,1,0:T(8,128)S(1)} %add_select_fusion), channel_id=1, source_target_pairs={{0,4},{4,0},{8,12},{12,8},{16,20},{20,16},{24,28},{28,24},{1,5},{5... | collective-permute-start | bytes 786440 | tf_op jit(solution)/shard_map/ppermute | solution.py:114
  75.5 12.9 %collective-permute-start.13 = (f32[2,8,1,128]{3,2,1,0:T(1,128)S(1)}, f32[2,8,1,128]{3,2,1,0:T(1,128)S(1)}, u32[]{:S(2)}, u32[]{:S(2)}) collective-permute-start(f32[2,8,1,128]{3,2,1,0:T(1,128)S(1)} %get-tuple-element.70), channel_id=1, source_target_pairs={{0,1},{1,2},{2,3},{4,5},{5,6},{6,7},{8,9},{9,10},{10,11},{12,13},{... | collective-permute-start | bytes 24584 | tf_op jit(solution)/shard_map/ppermute | solution.py:33
  77.5 11.0 %collective-permute-start.14 = (f32[2,8,1,128]{3,2,1,0:T(1,128)S(1)}, f32[2,8,1,128]{3,2,1,0:T(1,128)S(1)}, u32[]{:S(2)}, u32[]{:S(2)}) collective-permute-start(f32[2,8,1,128]{3,2,1,0:T(1,128)S(1)} %get-tuple-element.71), channel_id=1, source_target_pairs={{1,0},{2,1},{3,2},{5,4},{6,5},{7,6},{9,8},{10,9},{11,10},{13,12},{... | collective-permute-start | bytes 24584 | tf_op jit(solution)/shard_map/ppermute | solution.py:33
  79.9 8.6 %collective-permute-start.12 = (f32[2,1,32,128]{3,2,1,0:T(8,128)S(1)}, f32[2,1,32,128]{3,2,1,0:T(8,128)S(1)}, u32[]{:S(2)}, u32[]{:S(2)}) collective-permute-start(f32[2,1,32,128]{3,2,1,0:T(8,128)S(1)} %get-tuple-element.68), channel_id=1, source_target_pairs={{0,4},{4,8},{8,12},{12,16},{16,20},{20,24},{24,28},{1,5},{5,9},{9,... | collective-permute-start | bytes 98312 | tf_op jit(solution)/shard_map/ppermute | solution.py:33
  82.0 6.5 %collective-permute-start.15 = (f32[2,1,32,128]{3,2,1,0:T(8,128)S(1)}, f32[2,1,32,128]{3,2,1,0:T(8,128)S(1)}, u32[]{:S(2)}, u32[]{:S(2)}) collective-permute-start(f32[2,1,32,128]{3,2,1,0:T(8,128)S(1)} %get-tuple-element.69), channel_id=1, source_target_pairs={{4,0},{8,4},{12,8},{16,12},{20,16},{24,20},{28,24},{5,1},{9,5},{13... | collective-permute-start | bytes 98312 | tf_op jit(solution)/shard_map/ppermute | solution.py:33

commit v12 on v10

--- a/solution.py
+++ b/solution.py
@@ -99,11 +99,16 @@
     return [(i, i + shift) for i in range(count - shift)]
 
 
-def pipelined_scan(totals_of, emit, lines, axis, riders, groups=2):
+def pipelined(count, lines, groups=2):
+    return count % 2 == 0 and count > 2 and lines % (2 * groups) == 0
+
+
+def pipelined_scan(totals_of, emit, lines, axis, riders, passenger, groups=2):
     count = lax.axis_size(axis)
-    if count % 2 or count <= 2 or lines % (2 * groups):
+    if not pipelined(count, lines, groups):
         earlier = exclusive_scan(totals_of(0, lines, None), axis)
-        return [emit(0, lines, earlier)], {stage: rider(None) for stage, rider in riders.items()}
+        carried = {stage: rider(None) for stage, rider in riders.items()}
+        return [emit(0, lines, earlier)], carried, None
     size = lines // groups
     steps = [None] * groups
     steps[0] = paired_steps(totals_of(0, size, None), axis)
@@ -111,7 +116,16 @@
     while stage < groups or live:
         if stage < groups:
             live[stage] = next(steps[stage])
-        arrived = {g: lax.ppermute(payload, axis, pairs) for g, (payload, pairs) in live.items()}
+        sent = dict(live)
+        if stage == 0:
+            payload, pairs = live[0]
+            rides = passenger.reshape((-1,) + payload.shape[1:])
+            sent[0] = jnp.concatenate([payload, rides]), pairs
+        arrived = {g: lax.ppermute(payload, axis, pairs) for g, (payload, pairs) in sent.items()}
+        if stage == 0:
+            held = live[0][0].shape[0]
+            passenger = arrived[0][held:].reshape(passenger.shape)
+            arrived[0] = arrived[0][:held]
         if stage == 0:
             for g in range(1, groups):
                 steps[g] = paired_steps(totals_of(g * size, size, live[0][0]), axis)
@@ -129,7 +143,7 @@
                 made = made + [emit(g * size, size, finished.value)]
         live = following
         stage += 1
-    return made, carried
+    return made, carried, passenger
 
 
 def window(source, step_beam, step_cross, step_depth):
@@ -225,10 +239,33 @@
         return exchange
 
     lines = earlier_spectral_power.shape[0]
-    made, first_faces = pipelined_scan(
-        totals_of, emit, lines, "beam", {2: tied_faces(beam_faces), 3: tied_faces(cross_faces)}
-    )
-    first_bordered = bordered_fields(physical_quantities, first_faces[2], first_faces[3])
+    count = lax.axis_size("beam")
+    is_low = lax.axis_index("beam") % 2 == 0
+    last, first = physical_quantities[:, rows - 1 :], physical_quantities[:, :1]
+
+    def across_pairs(fields):
+        pairs = [(i, i + 1) for i in range(1, count - 1, 2)]
+        pairs += [(target, source) for source, target in pairs]
+        rows_now = fields.shape[1]
+        sent = jnp.where(is_low, fields[:, :1], fields[:, rows_now - 1 :])
+        return lax.ppermute(sent, "beam", pairs)
+
+    paired = pipelined(count, lines)
+    beam_rider = tied_faces(across_pairs if paired else beam_faces)
+    made, first_faces, partner_face = pipelined_scan(
+        totals_of,
+        emit,
+        lines,
+        "beam",
+        {2: beam_rider, 3: tied_faces(cross_faces)},
+        jnp.where(is_low, last, first),
+    )
+    if paired:
+        across = first_faces[2]
+        beam = (jnp.where(is_low, across, partner_face), jnp.where(is_low, partner_face, across))
+    else:
+        beam = first_faces[2]
+    first_bordered = bordered_fields(physical_quantities, beam, first_faces[3])
     spectral_power = jnp.zeros(earlier_spectral_power.shape, jnp.bfloat16)
     start = 0
     for part, _, _ in made:

time: 89 us -> 89.7 us (level)
  waiting for transfers between devices: 17 us -> 19.4 us
  starting transfers between devices: 43.2 us -> 41.2 us
    ppermute x8 -> x6, starting transfers between devices: 28.6 us -> 22.4 us  [shifted(): return lax.ppermute(block, axis, pairs)]
    ppermute x0 -> x1, starting transfers between devices: none -> 4.33 us  [across_pairs(): return lax.ppermute(sent, 'beam', pairs)]
    ppermute x0 -> x1, waiting for transfers between devices: none -> 4.26 us  [across_pairs(): return lax.ppermute(sent, 'beam', pairs)]
    ppermute x8 -> x6, waiting for transfers between devices: 5.73 us -> 4.27 us  [shifted(): return lax.ppermute(block, axis, pairs)]
  transfers between devices with their start and end apart: 16 -> 15, of which waited for: 7 -> 8; matrix products, arithmetic and copies ran while one was open for 14% -> 14% of each run, Pallas kernels for 0% -> 0%
where the time goes in v12:
time: 89.7 us; the launch traced here: 89.2 us
  starting transfers between devices  41.2 us (46%)
  other arithmetic  26.6 us (30%)
  waiting for transfers between devices  19.4 us (22%)
  between operations  1.07 us (1%)
    ppermute x6, starting transfers between devices, shifted(): return lax.ppermute(block, axis, pairs)  22.4 us
    ppermute x8, starting transfers between devices, pipelined_scan(): lax.ppermute(payload, axis, pairs)  14.5 us
    ppermute x8, waiting for transfers between devices, pipelined_scan(): lax.ppermute(payload, axis, pairs)  10.9 us
    reduce_sum x2, other arithmetic, totals_of(): return jnp.sum(optical_depth, axis=1)  8.68 us
    reduce_sum x2, other arithmetic, emit(): jnp.sum(radiance * (1.0 - jnp.exp(-optical_depth)), axis=0)  5.06 us
    ppermute x1, starting transfers between devices, across_pairs(): return lax.ppermute(sent, 'beam', pairs)  4.33 us
    ppermute x6, waiting for transfers between devices, shifted(): return lax.ppermute(block, axis, pairs)  4.27 us
    ppermute x1, waiting for transfers between devices, across_pairs(): return lax.ppermute(sent, 'beam', pairs)  4.26 us
  transfers between devices with their start and end apart: 15, of which 8 were waited for; matrix products, arithmetic and copies ran while one was open for 14% of the time, Pallas kernels for 0%

profile of v12, /device:TPU:9, one launch (start us, length us, event | category | flops | bytes accessed | tf_op | source)
XLA Modules:
  0.0 89.2 jit_solution(10640736695562385512)
XLA Ops:
  0.6 0.7 convert_subtract_fusion
  1.3 0.8 fusion.125
  2.1 1.1 %add_bitcast_fusion = (f32[1,8,32,128]{3,2,1,0:T(8,128)S(1)}, f32[8,32,128]{2,1,0:T(8,128)S(1)}) fusion(f32[8,32,128]{2,1,0:T(8,128)} %param.9, f32[8,32,128]{2,1,0:T(8,128)} %param.10, f32[8,32]{1,0:T(8,128)S(1)} %get-tuple-element.71), kind=kLoop, calls=%fused_computation.220 | loop fusion | flops 262144 | bytes 525312 | tf_op jit(solution)/shard_map/stack | solution.py:196
  3.2 0.0 copy-start.2
  3.2 5.9 %fusion.122 = (f32[32,32,128]{2,1,0:T(8,128)S(1)}, f32[32,8,32,128]{3,2,1,0:T(8,128)}, f32[32,8,32,128]{3,2,1,0:T(8,128)}) fusion(f32[8,32]{1,0:T(8,128)S(1)} %get-tuple-element.72, bf16[64,8,32,128]{3,2,1,0:T(8,128)(2,1)} %param.11, f32[32]{0:T(128)S(1)} %get-tuple-element.73, f32[8,32,128]{2,1,0:T(8,128)S(1)} %get-tuple-element.70, ...), kind=kLoop, calls=%fused_computation.243 | loop fusion | flops 11403264 | bytes 13239552 | tf_op jit(solution)/shard_map/reduce_sum | solution.py:217
  9.2 0.0 copy-done.2
  9.2 1.3 %collective-permute-start = (f32[18,32,128]{2,1,0:T(8,128)S(1)}, f32[18,32,128]{2,1,0:T(8,128)S(1)}, u32[]{:S(2)}, u32[]{:S(2)}) collective-permute-start(f32[18,32,128]{2,1,0:T(8,128)S(1)} %pad_maximum_fusion.19), channel_id=1, source_target_pairs={{0,4},{4,0},{8,12},{12,8},{16,20},{20,16},{24,28},{28,24},{1,5},{5... | collective-permute-start | bytes 884744 | tf_op jit(solution)/shard_map/ppermute | solution.py:124
  10.6 2.7 %reduce_sum.55 = f32[32,32,128]{2,1,0:T(8,128)S(1)} reduce(f32[32,8,32,128]{3,2,1,0:T(8,128)} %get-tuple-element.20, f32[]{:T(128)} %constant.55.clone.1), dimensions={1}, to_apply=%region_1.2 | reduce | flops 917504 | bytes 4718596 | tf_op jit(solution)/shard_map/reduce_sum | solution.py:217
  13.3 0.0 copy-start
  13.4 0.3 collective-permute-start.2
  13.7 2.7 %fusion = f32[32,7,32,128]{3,2,1,0:T(8,128)S(1)} fusion(f32[32,8,32,128]{3,2,1,0:T(8,128)} %get-tuple-element.20), kind=kOutput, calls=%fused_computation.11 | output fusion | flops 5505024 | bytes 7340032 | tf_op jit(solution)/shard_map/jit(cumsum)/reduce_window_sum | solution.py:222
  16.4 0.8 collective-permute-done
  17.2 0.1 fusion.106
  17.3 3.2 %collective-permute-start.1 = (f32[16,32,128]{2,1,0:T(8,128)S(1)}, f32[16,32,128]{2,1,0:T(8,128)S(1)}, u32[]{:S(2)}, u32[]{:S(2)}) collective-permute-start(f32[16,32,128]{2,1,0:T(8,128)S(1)} %fusion.106), channel_id=1, source_target_pairs={{0,8},{4,12},{8,16},{12,20},{16,24},{20,28},{1,9},{5,13},{9,17},{1... | collective-permute-start | bytes 786440 | tf_op jit(solution)/shard_map/ppermute | solution.py:124
  20.5 0.0 copy-start.5
  20.5 0.9 fusion.2
  21.4 1.4 %collective-permute-done.2 = f32[16,32,128]{2,1,0:T(8,128)S(1)} collective-permute-done((f32[16,32,128]{2,1,0:T(8,128)S(1)}, f32[16,32,128]{2,1,0:T(8,128)S(1)}, u32[]{:S(2)}, u32[]{:S(2)}) %collective-permute-start.2) | collective-permute-done | bytes 262176 | tf_op jit(solution)/shard_map/ppermute | solution.py:124
  22.8 1.6 %collective-permute-done.1 = f32[16,32,128]{2,1,0:T(8,128)S(1)} collective-permute-done((f32[16,32,128]{2,1,0:T(8,128)S(1)}, f32[16,32,128]{2,1,0:T(8,128)S(1)}, u32[]{:S(2)}, u32[]{:S(2)}) %collective-permute-start.1) | collective-permute-done | bytes 262176 | tf_op jit(solution)/shard_map/ppermute | solution.py:124
  24.4 0.0 copy-start.4
  24.4 4.4 %collective-permute-start.3 = (f32[16,32,128]{2,1,0:T(8,128)S(1)}, f32[16,32,128]{2,1,0:T(8,128)S(1)}, u32[]{:S(2)}, u32[]{:S(2)}) collective-permute-start(f32[16,32,128]{2,1,0:T(8,128)S(1)} %add.213), channel_id=1, source_target_pairs={{0,16},{4,20},{8,24},{12,28},{1,17},{5,21},{9,25},{13,29},{2,18},{... | collective-permute-start | bytes 786440 | tf_op jit(solution)/shard_map/ppermute | solution.py:124
  28.8 0.1 fusion.107
  28.9 1.9 %collective-permute-start.4 = (f32[16,32,128]{2,1,0:T(8,128)S(1)}, f32[16,32,128]{2,1,0:T(8,128)S(1)}, u32[]{:S(2)}, u32[]{:S(2)}) collective-permute-start(f32[16,32,128]{2,1,0:T(8,128)S(1)} %fusion.107), channel_id=1, source_target_pairs={{0,8},{4,12},{8,16},{12,20},{16,24},{20,28},{1,9},{5,13},{9,17},{1... | collective-permute-start | bytes 786440 | tf_op jit(solution)/shard_map/ppermute | solution.py:124
  30.8 4.3 %collective-permute-start.5 = (f32[2,1,32,128]{3,2,1,0:T(8,128)S(1)}, f32[2,1,32,128]{3,2,1,0:T(8,128)S(1)}, u32[]{:S(2)}, u32[]{:S(2)}) collective-permute-start(f32[2,1,32,128]{3,2,1,0:T(8,128)S(1)} %slice_select_fusion.4), channel_id=1, source_target_pairs={{4,8},{12,16},{20,24},{8,4},{16,12},{24,20},{5,9},{13,17},{21,25},... | collective-permute-start | bytes 98312 | tf_op jit(solution)/shard_map/ppermute | solution.py:251
  35.2 0.0 copy-done.5
  35.2 4.3 %collective-permute-done.5 = f32[2,1,32,128]{3,2,1,0:T(8,128)S(1)} collective-permute-done((f32[2,1,32,128]{3,2,1,0:T(8,128)S(1)}, f32[2,1,32,128]{3,2,1,0:T(8,128)S(1)}, u32[]{:S(2)}, u32[]{:S(2)}) %collective-permute-start.5) | collective-permute-done | bytes 32800 | tf_op jit(solution)/shard_map/ppermute | solution.py:251
  39.4 0.0 collective-permute-done.3
  39.4 5.0 %collective-permute-done.4 = f32[16,32,128]{2,1,0:T(8,128)S(1)} collective-permute-done((f32[16,32,128]{2,1,0:T(8,128)S(1)}, f32[16,32,128]{2,1,0:T(8,128)S(1)}, u32[]{:S(2)}, u32[]{:S(2)}) %collective-permute-start.4) | collective-permute-done | bytes 262176 | tf_op jit(solution)/shard_map/ppermute | solution.py:124
  44.5 0.1 fusion.121
  44.6 0.1 add_select_fusion.1
  44.6 0.0 copy-start.1
  44.6 2.0 %collective-permute-start.6 = (f32[16,32,128]{2,1,0:T(8,128)S(1)}, f32[16,32,128]{2,1,0:T(8,128)S(1)}, u32[]{:S(2)}, u32[]{:S(2)}) collective-permute-start(f32[16,32,128]{2,1,0:T(8,128)S(1)} %add_select_fusion.1), channel_id=1, source_target_pairs={{0,4},{4,0},{8,12},{12,8},{16,20},{20,16},{24,28},{28,24},{1,5},{5... | collective-permute-start | bytes 786440 | tf_op jit(solution)/shard_map/ppermute | solution.py:124
  46.7 1.3 %collective-permute-start.7 = (f32[16,32,128]{2,1,0:T(8,128)S(1)}, f32[16,32,128]{2,1,0:T(8,128)S(1)}, u32[]{:S(2)}, u32[]{:S(2)}) collective-permute-start(f32[16,32,128]{2,1,0:T(8,128)S(1)} %add.217), channel_id=1, source_target_pairs={{0,16},{4,20},{8,24},{12,28},{1,17},{5,21},{9,25},{13,29},{2,18},{... | collective-permute-start | bytes 786440 | tf_op jit(solution)/shard_map/ppermute | solution.py:124
  48.0 5.3 %collective-permute-start.8 = (f32[2,8,1,128]{3,2,1,0:T(1,128)S(1)}, f32[2,8,1,128]{3,2,1,0:T(1,128)S(1)}, u32[]{:S(2)}, u32[]{:S(2)}) collective-permute-start(f32[2,8,1,128]{3,2,1,0:T(1,128)S(1)} %get-tuple-element.68), channel_id=1, source_target_pairs={{0,1},{1,2},{2,3},{4,5},{5,6},{6,7},{8,9},{9,10},{10,11},{12,13},{... | collective-permute-start | bytes 24584 | tf_op jit(solution)/shard_map/ppermute | solution.py:33
  53.3 1.9 %collective-permute-start.9 = (f32[2,8,1,128]{3,2,1,0:T(1,128)S(1)}, f32[2,8,1,128]{3,2,1,0:T(1,128)S(1)}, u32[]{:S(2)}, u32[]{:S(2)}) collective-permute-start(f32[2,8,1,128]{3,2,1,0:T(1,128)S(1)} %get-tuple-element.67), channel_id=1, source_target_pairs={{1,0},{2,1},{3,2},{5,4},{6,5},{7,6},{9,8},{10,9},{11,10},{13,12},{... | collective-permute-start | bytes 24584 | tf_op jit(solution)/shard_map/ppermute | solution.py:33
  55.2 0.0 collective-permute-done.8
  55.2 3.0 %collective-permute-done.9 = f32[2,8,1,128]{3,2,1,0:T(1,128)S(1)} collective-permute-done((f32[2,8,1,128]{3,2,1,0:T(1,128)S(1)}, f32[2,8,1,128]{3,2,1,0:T(1,128)S(1)}, u32[]{:S(2)}, u32[]{:S(2)}) %collective-permute-start.9) | collective-permute-done | bytes 8224 | tf_op jit(solution)/shard_map/ppermute | solution.py:33
  58.3 0.0 collective-permute-done.6
  58.3 0.0 collective-permute-done.7
  58.3 0.1 fusion.120
  58.3 0.1 add_select_fusion
  58.4 0.1 collective-permute-start.10
  58.5 0.1 fusion.7
  58.6 0.5 power_multiply_fusion.2
  59.1 0.2 fusion.123
  59.3 2.4 %multiply_reduce_fusion.2 = (f32[8,32,128]{2,1,0:T(8,128)S(1)}, f32[8,32,128]{2,1,0:T(8,128)S(1)}, bf16[32,8,32,128]{3,2,1,0:T(8,128)(2,1)S(1)}) fusion(f32[32,8,32,128]{3,2,1,0:T(8,128)S(1)} %copy-done, f32[32,7,32,128]{3,2,1,0:T(8,128)S(1)} %fusion.2, f32[32,32,128]{2,1,0:T(8,128)S(1)} %get-tuple-element.75, f32[32,32,128]{2,1,0:T(8,128)S(1)} %get-tuple-element.52, ...), kind=kLoop, calls=%fused_computation.4 | loop fusion | flops 13565952 | bytes 13369472 | tf_op jit(solution)/shard_map/reduce_sum | solution.py:229
  61.7 0.6 fusion.20
  62.4 2.0 %collective-permute-done.10 = f32[16,32,128]{2,1,0:T(8,128)S(1)} collective-permute-done((f32[16,32,128]{2,1,0:T(8,128)S(1)}, f32[16,32,128]{2,1,0:T(8,128)S(1)}, u32[]{:S(2)}, u32[]{:S(2)}) %collective-permute-start.10) | collective-permute-done | bytes 262176 | tf_op jit(solution)/shard_map/ppermute | solution.py:124
  64.4 0.1 maximum_select_fusion.1
  64.5 0.0 copy-start.3
  64.5 2.7 %multiply_reduce_fusion = (f32[8,32,128]{2,1,0:T(8,128)S(1)}, f32[8,32,128]{2,1,0:T(8,128)S(1)}, bf16[32,8,32,128]{3,2,1,0:T(8,128)(2,1)S(1)}) fusion(f32[32,7,32,128]{3,2,1,0:T(8,128)S(1)} %fusion, f32[32,32,128]{2,1,0:T(8,128)S(1)} %maximum_select_fusion.1, f32[32,32,128]{2,1,0:T(8,128)S(1)} %get-tuple-element.51, f32[8,32]{1,0:T(8,128)S(1)} %get-tuple-element.72, ...), kind=kLoop, calls=%fused_computation.1 | loop fusion | flops 15663104 | bytes 9307264 | tf_op jit(solution)/shard_map/reduce_sum | solution.py:229
  67.2 0.8 broadcast_multiply_fusion
  68.0 0.1 fusion.119
  68.2 7.7 %collective-permute-start.14 = (f32[2,1,32,128]{3,2,1,0:T(8,128)S(1)}, f32[2,1,32,128]{3,2,1,0:T(8,128)S(1)}, u32[]{:S(2)}, u32[]{:S(2)}) collective-permute-start(f32[2,1,32,128]{3,2,1,0:T(8,128)S(1)} %get-tuple-element.64), channel_id=1, source_target_pairs={{4,0},{8,4},{12,8},{16,12},{20,16},{24,20},{28,24},{5,1},{9,5},{13... | collective-permute-start | bytes 98312 | tf_op jit(solution)/shard_map/ppermute | solution.py:33
  75.9 1.9 %collective-permute-start.13 = (f32[2,8,1,128]{3,2,1,0:T(1,128)S(1)}, f32[2,8,1,128]{3,2,1,0:T(1,128)S(1)}, u32[]{:S(2)}, u32[]{:S(2)}) collective-permute-start(f32[2,8,1,128]{3,2,1,0:T(1,128)S(1)} %get-tuple-element.66), channel_id=1, source_target_pairs={{1,0},{2,1},{3,2},{5,4},{6,5},{7,6},{9,8},{10,9},{11,10},{13,12},{... | collective-permute-start | bytes 24584 | tf_op jit(solution)/shard_map/ppermute | solution.py:33
  77.8 3.6 %collective-permute-start.12 = (f32[2,8,1,128]{3,2,1,0:T(1,128)S(1)}, f32[2,8,1,128]{3,2,1,0:T(1,128)S(1)}, u32[]{:S(2)}, u32[]{:S(2)}) collective-permute-start(f32[2,8,1,128]{3,2,1,0:T(1,128)S(1)} %get-tuple-element.65), channel_id=1, source_target_pairs={{0,1},{1,2},{2,3},{4,5},{5,6},{6,7},{8,9},{9,10},{10,11},{12,13},{... | collective-permute-start | bytes 24584 | tf_op jit(solution)/shard_map/ppermute | solution.py:33
  81.5 1.9 %collective-permute-start.11 = (f32[2,1,32,128]{3,2,1,0:T(8,128)S(1)}, f32[2,1,32,128]{3,2,1,0:T(8,128)S(1)}, u32[]{:S(2)}, u32[]{:S(2)}) collective-permute-start(f32[2,1,32,128]{3,2,1,0:T(8,128)S(1)} %get-tuple-element.63), channel_id=1, source_target_pairs={{0,4},{4,8},{8,12},{12,16},{16,20},{20,24},{24,28},{1,5},{5,9},{9,... | collective-permute-start | bytes 98312 | tf_op jit(solution)/shard_map/ppermute | solution.py:33
  83.4 2.4 %pad_maximum_fusion = bf16[64,8,32,128]{3,2,1,0:T(8,128)(2,1)} fusion(bf16[32,8,32,128]{3,2,1,0:T(8,128)(2,1)S(1)} %get-tuple-element.48, bf16[32,8,32,128]{3,2,1,0:T(8,128)(2,1)S(1)} %get-tuple-element.29), kind=kLoop, calls=%fused_computation | loop fusion | flops 2097152 | bytes 8388608 | tf_op jit(solution)/shard_map/dynamic_update_slice | solution.py:272
  85.8 0.0 collective-permute-done.13
  85.8 0.0 collective-permute-done.12
  85.8 0.0 collective-permute-done.14
  85.8 1.2 %collective-permute-done.11 = f32[2,1,32,128]{3,2,1,0:T(8,128)S(1)} collective-permute-done((f32[2,1,32,128]{3,2,1,0:T(8,128)S(1)}, f32[2,1,32,128]{3,2,1,0:T(8,128)S(1)}, u32[]{:S(2)}, u32[]{:S(2)}) %collective-permute-start.11) | collective-permute-done | bytes 32800 | tf_op jit(solution)/shard_map/ppermute | solution.py:33
  87.1 0.5 power_multiply_fusion
  87.6 0.7 fusion.29
  88.3 0.9 %fusion.93 = (f32[8,32,128]{2,1,0:T(8,128)}, f32[8,32,128]{2,1,0:T(8,128)}) fusion(f32[2,8,32,128]{3,2,1,0:T(8,128)S(1)} %fusion.29, f32[8,32]{1,0:T(8,128)S(1)} %get-tuple-element.71, f32[8,32,128]{2,1,0:T(8,128)S(1)} %get-tuple-element.35, f32[8,32,128]{2,1,0:T(8,128)S(1)} %get-tuple-element.36, f32[2,8,32,128]{3,2,1,0:T(8,128)S(1)} %fusion.20, ...), kind=kLoop, calls=%fused_computation.201 | loop fusion | flops 1081344 | bytes 1442816 | tf_op jit(solution)/shard_map/add | solution.py:291
  (20 shorter events, 0.3 us)
Async XLA Ops:
  3.2 6.0 %copy-start.2 = (f32[8,32,128]{2,1,0:T(8,128)S(1)}, f32[8,32,128]{2,1,0:T(8,128)}, u32[]{:S(2)}) copy-start(f32[8,32,128]{2,1,0:T(8,128)} %param.8) | copy-start | bytes 393220
  9.2 7.9 %collective-permute-start = (f32[18,32,128]{2,1,0:T(8,128)S(1)}, f32[18,32,128]{2,1,0:T(8,128)S(1)}, u32[]{:S(2)}, u32[]{:S(2)}) collective-permute-start(f32[18,32,128]{2,1,0:T(8,128)S(1)} %pad_maximum_fusion.19), channel_id=1, source_target_pairs={{0,4},{4,0},{8,12},{12,8},{16,20},{20,16},{24,28},{28,24},{1,5},{5... | collective-permute-start | bytes 884744 | tf_op jit(solution)/shard_map/ppermute | solution.py:124
  13.3 7.1 %copy-start = (f32[32,8,32,128]{3,2,1,0:T(8,128)S(1)}, f32[32,8,32,128]{3,2,1,0:T(8,128)}, u32[]{:S(2)}) copy-start(f32[32,8,32,128]{3,2,1,0:T(8,128)} %get-tuple-element.47) | copy-start | bytes 12582916
  13.4 9.4 %collective-permute-start.2 = (f32[16,32,128]{2,1,0:T(8,128)S(1)}, f32[16,32,128]{2,1,0:T(8,128)S(1)}, u32[]{:S(2)}, u32[]{:S(2)}) collective-permute-start(f32[16,32,128]{2,1,0:T(8,128)S(1)} %slice_select_fusion.1), channel_id=1, source_target_pairs={{0,4},{4,0},{8,12},{12,8},{16,20},{20,16},{24,28},{28,24},{1,5},{5... | collective-permute-start | bytes 786440 | tf_op jit(solution)/shard_map/ppermute | solution.py:124
  17.3 7.1 %collective-permute-start.1 = (f32[16,32,128]{2,1,0:T(8,128)S(1)}, f32[16,32,128]{2,1,0:T(8,128)S(1)}, u32[]{:S(2)}, u32[]{:S(2)}) collective-permute-start(f32[16,32,128]{2,1,0:T(8,128)S(1)} %fusion.106), channel_id=1, source_target_pairs={{0,8},{4,12},{8,16},{12,20},{16,24},{20,28},{1,9},{5,13},{9,17},{1... | collective-permute-start | bytes 786440 | tf_op jit(solution)/shard_map/ppermute | solution.py:124
  20.5 14.7 %copy-start.5 = (f32[32,128]{1,0:T(8,128)S(1)}, f32[32,128]{1,0:T(8,128)}, u32[]{:S(2)}) copy-start(f32[32,128]{1,0:T(8,128)} %param.14) | copy-start | bytes 49156
  24.4 34.7 %copy-start.4 = (f32[64,32,128]{2,1,0:T(8,128)S(1)}, f32[64,32,128]{2,1,0:T(8,128)}, u32[]{:S(2)}) copy-start(f32[64,32,128]{2,1,0:T(8,128)} %param.12) | copy-start | bytes 3145732
  24.4 15.0 %collective-permute-start.3 = (f32[16,32,128]{2,1,0:T(8,128)S(1)}, f32[16,32,128]{2,1,0:T(8,128)S(1)}, u32[]{:S(2)}, u32[]{:S(2)}) collective-permute-start(f32[16,32,128]{2,1,0:T(8,128)S(1)} %add.213), channel_id=1, source_target_pairs={{0,16},{4,20},{8,24},{12,28},{1,17},{5,21},{9,25},{13,29},{2,18},{... | collective-permute-start | bytes 786440 | tf_op jit(solution)/shard_map/ppermute | solution.py:124
  28.9 15.6 %collective-permute-start.4 = (f32[16,32,128]{2,1,0:T(8,128)S(1)}, f32[16,32,128]{2,1,0:T(8,128)S(1)}, u32[]{:S(2)}, u32[]{:S(2)}) collective-permute-start(f32[16,32,128]{2,1,0:T(8,128)S(1)} %fusion.107), channel_id=1, source_target_pairs={{0,8},{4,12},{8,16},{12,20},{16,24},{20,28},{1,9},{5,13},{9,17},{1... | collective-permute-start | bytes 786440 | tf_op jit(solution)/shard_map/ppermute | solution.py:124
  30.8 8.6 %collective-permute-start.5 = (f32[2,1,32,128]{3,2,1,0:T(8,128)S(1)}, f32[2,1,32,128]{3,2,1,0:T(8,128)S(1)}, u32[]{:S(2)}, u32[]{:S(2)}) collective-permute-start(f32[2,1,32,128]{3,2,1,0:T(8,128)S(1)} %slice_select_fusion.4), channel_id=1, source_target_pairs={{4,8},{12,16},{20,24},{8,4},{16,12},{24,20},{5,9},{13,17},{21,25},... | collective-permute-start | bytes 98312 | tf_op jit(solution)/shard_map/ppermute | solution.py:251
  44.6 14.7 %copy-start.1 = (bf16[64,8,32,128]{3,2,1,0:T(8,128)(2,1)S(1)}, bf16[64,8,32,128]{3,2,1,0:T(8,128)(2,1)}, u32[]{:S(2)}) copy-start(bf16[64,8,32,128]{3,2,1,0:T(8,128)(2,1)} %param.11) | copy-start | bytes 12582916
  44.6 13.6 %collective-permute-start.6 = (f32[16,32,128]{2,1,0:T(8,128)S(1)}, f32[16,32,128]{2,1,0:T(8,128)S(1)}, u32[]{:S(2)}, u32[]{:S(2)}) collective-permute-start(f32[16,32,128]{2,1,0:T(8,128)S(1)} %add_select_fusion.1), channel_id=1, source_target_pairs={{0,4},{4,0},{8,12},{12,8},{16,20},{20,16},{24,28},{28,24},{1,5},{5... | collective-permute-start | bytes 786440 | tf_op jit(solution)/shard_map/ppermute | solution.py:124
  46.7 11.6 %collective-permute-start.7 = (f32[16,32,128]{2,1,0:T(8,128)S(1)}, f32[16,32,128]{2,1,0:T(8,128)S(1)}, u32[]{:S(2)}, u32[]{:S(2)}) collective-permute-start(f32[16,32,128]{2,1,0:T(8,128)S(1)} %add.217), channel_id=1, source_target_pairs={{0,16},{4,20},{8,24},{12,28},{1,17},{5,21},{9,25},{13,29},{2,18},{... | collective-permute-start | bytes 786440 | tf_op jit(solution)/shard_map/ppermute | solution.py:124
  48.0 7.2 %collective-permute-start.8 = (f32[2,8,1,128]{3,2,1,0:T(1,128)S(1)}, f32[2,8,1,128]{3,2,1,0:T(1,128)S(1)}, u32[]{:S(2)}, u32[]{:S(2)}) collective-permute-start(f32[2,8,1,128]{3,2,1,0:T(1,128)S(1)} %get-tuple-element.68), channel_id=1, source_target_pairs={{0,1},{1,2},{2,3},{4,5},{5,6},{6,7},{8,9},{9,10},{10,11},{12,13},{... | collective-permute-start | bytes 24584 | tf_op jit(solution)/shard_map/ppermute | solution.py:33
  53.3 5.0 %collective-permute-start.9 = (f32[2,8,1,128]{3,2,1,0:T(1,128)S(1)}, f32[2,8,1,128]{3,2,1,0:T(1,128)S(1)}, u32[]{:S(2)}, u32[]{:S(2)}) collective-permute-start(f32[2,8,1,128]{3,2,1,0:T(1,128)S(1)} %get-tuple-element.67), channel_id=1, source_target_pairs={{1,0},{2,1},{3,2},{5,4},{6,5},{7,6},{9,8},{10,9},{11,10},{13,12},{... | collective-permute-start | bytes 24584 | tf_op jit(solution)/shard_map/ppermute | solution.py:33
  58.4 6.0 %collective-permute-start.10 = (f32[16,32,128]{2,1,0:T(8,128)S(1)}, f32[16,32,128]{2,1,0:T(8,128)S(1)}, u32[]{:S(2)}, u32[]{:S(2)}) collective-permute-start(f32[16,32,128]{2,1,0:T(8,128)S(1)} %add_select_fusion), channel_id=1, source_target_pairs={{0,4},{4,0},{8,12},{12,8},{16,20},{20,16},{24,28},{28,24},{1,5},{5... | collective-permute-start | bytes 786440 | tf_op jit(solution)/shard_map/ppermute | solution.py:124
  64.5 2.7 %copy-start.3 = (f32[8,32,128]{2,1,0:T(8,128)S(1)}, f32[8,32,128]{2,1,0:T(8,128)}, u32[]{:S(2)}) copy-start(f32[8,32,128]{2,1,0:T(8,128)} %param.9) | copy-start | bytes 393220
  68.2 17.6 %collective-permute-start.14 = (f32[2,1,32,128]{3,2,1,0:T(8,128)S(1)}, f32[2,1,32,128]{3,2,1,0:T(8,128)S(1)}, u32[]{:S(2)}, u32[]{:S(2)}) collective-permute-start(f32[2,1,32,128]{3,2,1,0:T(8,128)S(1)} %get-tuple-element.64), channel_id=1, source_target_pairs={{4,0},{8,4},{12,8},{16,12},{20,16},{24,20},{28,24},{5,1},{9,5},{13... | collective-permute-start | bytes 98312 | tf_op jit(solution)/shard_map/ppermute | solution.py:33
  75.9 9.9 %collective-permute-start.13 = (f32[2,8,1,128]{3,2,1,0:T(1,128)S(1)}, f32[2,8,1,128]{3,2,1,0:T(1,128)S(1)}, u32[]{:S(2)}, u32[]{:S(2)}) collective-permute-start(f32[2,8,1,128]{3,2,1,0:T(1,128)S(1)} %get-tuple-element.66), channel_id=1, source_target_pairs={{1,0},{2,1},{3,2},{5,4},{6,5},{7,6},{9,8},{10,9},{11,10},{13,12},{... | collective-permute-start | bytes 24584 | tf_op jit(solution)/shard_map/ppermute | solution.py:33
  77.8 8.0 %collective-permute-start.12 = (f32[2,8,1,128]{3,2,1,0:T(1,128)S(1)}, f32[2,8,1,128]{3,2,1,0:T(1,128)S(1)}, u32[]{:S(2)}, u32[]{:S(2)}) collective-permute-start(f32[2,8,1,128]{3,2,1,0:T(1,128)S(1)} %get-tuple-element.65), channel_id=1, source_target_pairs={{0,1},{1,2},{2,3},{4,5},{5,6},{6,7},{8,9},{9,10},{10,11},{12,13},{... | collective-permute-start | bytes 24584 | tf_op jit(solution)/shard_map/ppermute | solution.py:33
  81.5 5.6 %collective-permute-start.11 = (f32[2,1,32,128]{3,2,1,0:T(8,128)S(1)}, f32[2,1,32,128]{3,2,1,0:T(8,128)S(1)}, u32[]{:S(2)}, u32[]{:S(2)}) collective-permute-start(f32[2,1,32,128]{3,2,1,0:T(8,128)S(1)} %get-tuple-element.63), channel_id=1, source_target_pairs={{0,4},{4,8},{8,12},{12,16},{16,20},{20,24},{24,28},{1,5},{5,9},{9,... | collective-permute-start | bytes 98312 | tf_op jit(solution)/shard_map/ppermute | solution.py:33

commit v13 on v10

--- a/solution.py
+++ b/solution.py
@@ -226,9 +226,9 @@
 
     lines = earlier_spectral_power.shape[0]
     made, first_faces = pipelined_scan(
-        totals_of, emit, lines, "beam", {2: tied_faces(beam_faces), 3: tied_faces(cross_faces)}
-    )
-    first_bordered = bordered_fields(physical_quantities, first_faces[2], first_faces[3])
+        totals_of, emit, lines, "beam", {1: tied_faces(cross_faces), 2: tied_faces(beam_faces)}
+    )
+    first_bordered = bordered_fields(physical_quantities, first_faces[2], first_faces[1])
     spectral_power = jnp.zeros(earlier_spectral_power.shape, jnp.bfloat16)
     start = 0
     for part, _, _ in made:

time: 89 us -> 92.8 us (1.043); the launches traced: 88.5 us -> 91.1 us
  waiting for transfers between devices: 17 us -> 24.3 us
  starting transfers between devices: 43.2 us -> 38.2 us
    ppermute x8, waiting for transfers between devices: 11.2 us -> 16.2 us  [pipelined_scan(): lax.ppermute(payload, axis, pairs)]
    ppermute x8, starting transfers between devices: 28.6 us -> 25.1 us  [shifted(): return lax.ppermute(block, axis, pairs)]
    ppermute x8, waiting for transfers between devices: 5.73 us -> 8.17 us  [shifted(): return lax.ppermute(block, axis, pairs)]
    ppermute x8, starting transfers between devices: 14.6 us -> 13.2 us  [pipelined_scan(): lax.ppermute(payload, axis, pairs)]
where the time goes in v13:
time: 92.8 us; the launch traced here: 91.1 us
  starting transfers between devices  38.2 us (41%)
  other arithmetic  26.6 us (29%)
  waiting for transfers between devices  24.3 us (26%)
  between operations  1.05 us (1%)
    ppermute x8, starting transfers between devices, shifted(): return lax.ppermute(block, axis, pairs)  25.1 us
    ppermute x8, waiting for transfers between devices, pipelined_scan(): lax.ppermute(payload, axis, pairs)  16.2 us
    ppermute x8, starting transfers between devices, pipelined_scan(): lax.ppermute(payload, axis, pairs)  13.2 us
    reduce_sum x2, other arithmetic, totals_of(): return jnp.sum(optical_depth, axis=1)  8.66 us
    ppermute x8, waiting for transfers between devices, shifted(): return lax.ppermute(block, axis, pairs)  8.17 us
    reduce_sum x2, other arithmetic, emit(): jnp.sum(radiance * (1.0 - jnp.exp(-optical_depth)), axis=0)  5.06 us
    another operation x2, other arithmetic, emit(): jnp.cumsum(optical_depth[:, :rows - 1], axis=1)  3.55 us
    dynamic_update_slice x1, other arithmetic, local(): lax.dynamic_update_slice_in_dim(spectral_power, part, start, axis=0)  2.38 us
  transfers between devices with their start and end apart: 16, of which 7 were waited for; matrix products, arithmetic and copies ran while one was open for 14% of the time, Pallas kernels for 0%

profile of v13, /device:TPU:9, one launch (start us, length us, event | category | flops | bytes accessed | tf_op | source)
XLA Modules:
  0.0 91.1 jit_solution(11379180044068039525)
XLA Ops:
  0.6 0.7 convert_subtract_fusion
  1.3 0.8 fusion.120
  2.1 1.1 %add_bitcast_fusion = (f32[1,8,32,128]{3,2,1,0:T(8,128)S(1)}, f32[8,32,128]{2,1,0:T(8,128)S(1)}) fusion(f32[8,32,128]{2,1,0:T(8,128)} %param.9, f32[8,32,128]{2,1,0:T(8,128)} %param.10, f32[8,32]{1,0:T(8,128)S(1)} %get-tuple-element.73), kind=kLoop, calls=%fused_computation.215 | loop fusion | flops 262144 | bytes 525312 | tf_op jit(solution)/shard_map/stack | solution.py:182
  3.2 5.9 %fusion.116 = (f32[32,32,128]{2,1,0:T(8,128)S(1)}, f32[32,8,32,128]{3,2,1,0:T(8,128)}, f32[32,8,32,128]{3,2,1,0:T(8,128)}) fusion(f32[8,32]{1,0:T(8,128)S(1)} %get-tuple-element.74, bf16[64,8,32,128]{3,2,1,0:T(8,128)(2,1)} %param.11, f32[32]{0:T(128)S(1)} %get-tuple-element.75, f32[8,32,128]{2,1,0:T(8,128)S(1)} %get-tuple-element.72, ...), kind=kLoop, calls=%fused_computation.230 | loop fusion | flops 11403264 | bytes 13239552 | tf_op jit(solution)/shard_map/reduce_sum | solution.py:203
  9.2 1.3 %collective-permute-start = (f32[16,32,128]{2,1,0:T(8,128)S(1)}, f32[16,32,128]{2,1,0:T(8,128)S(1)}, u32[]{:S(2)}, u32[]{:S(2)}) collective-permute-start(f32[16,32,128]{2,1,0:T(8,128)S(1)} %slice_select_fusion.2), channel_id=1, source_target_pairs={{0,4},{4,0},{8,12},{12,8},{16,20},{20,16},{24,28},{28,24},{1,5},{5... | collective-permute-start | bytes 786440 | tf_op jit(solution)/shard_map/ppermute | solution.py:114
  10.5 2.7 %reduce_sum.55 = f32[32,32,128]{2,1,0:T(8,128)S(1)} reduce(f32[32,8,32,128]{3,2,1,0:T(8,128)} %get-tuple-element.21, f32[]{:T(128)} %constant.18.clone.1), dimensions={1}, to_apply=%region_1.2 | reduce | flops 917504 | bytes 4718596 | tf_op jit(solution)/shard_map/reduce_sum | solution.py:203
  13.2 0.0 copy-start.2
  13.3 0.0 copy-start
  13.3 0.3 collective-permute-start.2
  13.6 2.7 %fusion = f32[32,7,32,128]{3,2,1,0:T(8,128)S(1)} fusion(f32[32,8,32,128]{3,2,1,0:T(8,128)} %get-tuple-element.21), kind=kOutput, calls=%fused_computation.11 | output fusion | flops 5505024 | bytes 7340032 | tf_op jit(solution)/shard_map/jit(cumsum)/reduce_window_sum | solution.py:208
  16.3 0.1 collective-permute-done
  16.4 0.1 fusion.106
  16.5 3.2 %collective-permute-start.1 = (f32[16,32,128]{2,1,0:T(8,128)S(1)}, f32[16,32,128]{2,1,0:T(8,128)S(1)}, u32[]{:S(2)}, u32[]{:S(2)}) collective-permute-start(f32[16,32,128]{2,1,0:T(8,128)S(1)} %fusion.106), channel_id=1, source_target_pairs={{0,8},{4,12},{8,16},{12,20},{16,24},{20,28},{1,9},{5,13},{9,17},{1... | collective-permute-start | bytes 786440 | tf_op jit(solution)/shard_map/ppermute | solution.py:114
  19.7 6.0 %collective-permute-start.3 = (f32[2,8,1,128]{3,2,1,0:T(1,128)S(1)}, f32[2,8,1,128]{3,2,1,0:T(1,128)S(1)}, u32[]{:S(2)}, u32[]{:S(2)}) collective-permute-start(f32[2,8,1,128]{3,2,1,0:T(1,128)S(1)} %get-tuple-element.70), channel_id=1, source_target_pairs={{0,1},{1,2},{2,3},{4,5},{5,6},{6,7},{8,9},{9,10},{10,11},{12,13},{... | collective-permute-start | bytes 24584 | tf_op jit(solution)/shard_map/ppermute | solution.py:33
  25.7 1.9 %collective-permute-start.4 = (f32[2,8,1,128]{3,2,1,0:T(1,128)S(1)}, f32[2,8,1,128]{3,2,1,0:T(1,128)S(1)}, u32[]{:S(2)}, u32[]{:S(2)}) collective-permute-start(f32[2,8,1,128]{3,2,1,0:T(1,128)S(1)} %get-tuple-element.69), channel_id=1, source_target_pairs={{1,0},{2,1},{3,2},{5,4},{6,5},{7,6},{9,8},{10,9},{11,10},{13,12},{... | collective-permute-start | bytes 24584 | tf_op jit(solution)/shard_map/ppermute | solution.py:33
  27.6 0.0 copy-start.5
  27.6 0.9 fusion.2
  28.5 0.0 collective-permute-done.2
  28.5 0.0 collective-permute-done.3
  28.5 2.1 %collective-permute-done.4 = f32[2,8,1,128]{3,2,1,0:T(1,128)S(1)} collective-permute-done((f32[2,8,1,128]{3,2,1,0:T(1,128)S(1)}, f32[2,8,1,128]{3,2,1,0:T(1,128)S(1)}, u32[]{:S(2)}, u32[]{:S(2)}) %collective-permute-start.4) | collective-permute-done | bytes 8224 | tf_op jit(solution)/shard_map/ppermute | solution.py:33
  30.6 0.0 collective-permute-done.1
  30.7 2.0 %collective-permute-start.5 = (f32[16,32,128]{2,1,0:T(8,128)S(1)}, f32[16,32,128]{2,1,0:T(8,128)S(1)}, u32[]{:S(2)}, u32[]{:S(2)}) collective-permute-start(f32[16,32,128]{2,1,0:T(8,128)S(1)} %add.212), channel_id=1, source_target_pairs={{0,16},{4,20},{8,24},{12,28},{1,17},{5,21},{9,25},{13,29},{2,18},{... | collective-permute-start | bytes 786440 | tf_op jit(solution)/shard_map/ppermute | solution.py:114
  32.7 0.1 fusion.107
  32.8 2.5 %collective-permute-start.6 = (f32[16,32,128]{2,1,0:T(8,128)S(1)}, f32[16,32,128]{2,1,0:T(8,128)S(1)}, u32[]{:S(2)}, u32[]{:S(2)}) collective-permute-start(f32[16,32,128]{2,1,0:T(8,128)S(1)} %fusion.107), channel_id=1, source_target_pairs={{0,8},{4,12},{8,16},{12,20},{16,24},{20,28},{1,9},{5,13},{9,17},{1... | collective-permute-start | bytes 786440 | tf_op jit(solution)/shard_map/ppermute | solution.py:114
  35.3 3.1 %collective-permute-start.7 = (f32[2,1,32,128]{3,2,1,0:T(8,128)S(1)}, f32[2,1,32,128]{3,2,1,0:T(8,128)S(1)}, u32[]{:S(2)}, u32[]{:S(2)}) collective-permute-start(f32[2,1,32,128]{3,2,1,0:T(8,128)S(1)} %get-tuple-element.68), channel_id=1, source_target_pairs={{0,4},{4,8},{8,12},{12,16},{16,20},{20,24},{24,28},{1,5},{5,9},{9,... | collective-permute-start | bytes 98312 | tf_op jit(solution)/shard_map/ppermute | solution.py:33
  38.4 3.0 %collective-permute-start.8 = (f32[2,1,32,128]{3,2,1,0:T(8,128)S(1)}, f32[2,1,32,128]{3,2,1,0:T(8,128)S(1)}, u32[]{:S(2)}, u32[]{:S(2)}) collective-permute-start(f32[2,1,32,128]{3,2,1,0:T(8,128)S(1)} %get-tuple-element.67), channel_id=1, source_target_pairs={{4,0},{8,4},{12,8},{16,12},{20,16},{24,20},{28,24},{5,1},{9,5},{13... | collective-permute-start | bytes 98312 | tf_op jit(solution)/shard_map/ppermute | solution.py:33
  41.5 6.0 %collective-permute-done.7 = f32[2,1,32,128]{3,2,1,0:T(8,128)S(1)} collective-permute-done((f32[2,1,32,128]{3,2,1,0:T(8,128)S(1)}, f32[2,1,32,128]{3,2,1,0:T(8,128)S(1)}, u32[]{:S(2)}, u32[]{:S(2)}) %collective-permute-start.7) | collective-permute-done | bytes 32800 | tf_op jit(solution)/shard_map/ppermute | solution.py:33
  47.5 0.0 collective-permute-done.5
  47.5 2.0 %collective-permute-done.6 = f32[16,32,128]{2,1,0:T(8,128)S(1)} collective-permute-done((f32[16,32,128]{2,1,0:T(8,128)S(1)}, f32[16,32,128]{2,1,0:T(8,128)S(1)}, u32[]{:S(2)}, u32[]{:S(2)}) %collective-permute-start.6) | collective-permute-done | bytes 262176 | tf_op jit(solution)/shard_map/ppermute | solution.py:114
  49.5 0.1 fusion.115
  49.5 0.0 copy-start.4
  49.6 0.1 add_select_fusion.1
  49.6 2.1 %collective-permute-start.9 = (f32[16,32,128]{2,1,0:T(8,128)S(1)}, f32[16,32,128]{2,1,0:T(8,128)S(1)}, u32[]{:S(2)}, u32[]{:S(2)}) collective-permute-start(f32[16,32,128]{2,1,0:T(8,128)S(1)} %add_select_fusion.1), channel_id=1, source_target_pairs={{0,4},{4,0},{8,12},{12,8},{16,20},{20,16},{24,28},{28,24},{1,5},{5... | collective-permute-start | bytes 786440 | tf_op jit(solution)/shard_map/ppermute | solution.py:114
  51.7 1.3 %collective-permute-start.10 = (f32[16,32,128]{2,1,0:T(8,128)S(1)}, f32[16,32,128]{2,1,0:T(8,128)S(1)}, u32[]{:S(2)}, u32[]{:S(2)}) collective-permute-start(f32[16,32,128]{2,1,0:T(8,128)S(1)} %add.216), channel_id=1, source_target_pairs={{0,16},{4,20},{8,24},{12,28},{1,17},{5,21},{9,25},{13,29},{2,18},{... | collective-permute-start | bytes 786440 | tf_op jit(solution)/shard_map/ppermute | solution.py:114
  53.1 0.1 fusion.7
  53.1 0.0 copy-start.1
  53.1 0.5 power_multiply_fusion.2
  53.7 0.7 fusion.20
  54.4 4.2 %collective-permute-done.9 = f32[16,32,128]{2,1,0:T(8,128)S(1)} collective-permute-done((f32[16,32,128]{2,1,0:T(8,128)S(1)}, f32[16,32,128]{2,1,0:T(8,128)S(1)}, u32[]{:S(2)}, u32[]{:S(2)}) %collective-permute-start.9) | collective-permute-done | bytes 262176 | tf_op jit(solution)/shard_map/ppermute | solution.py:114
  58.5 5.9 %collective-permute-done.10 = f32[16,32,128]{2,1,0:T(8,128)S(1)} collective-permute-done((f32[16,32,128]{2,1,0:T(8,128)S(1)}, f32[16,32,128]{2,1,0:T(8,128)S(1)}, u32[]{:S(2)}, u32[]{:S(2)}) %collective-permute-start.10) | collective-permute-done | bytes 262176 | tf_op jit(solution)/shard_map/ppermute | solution.py:114
  64.4 0.1 fusion.114
  64.5 0.1 add_select_fusion
  64.6 0.5 collective-permute-start.11
  65.1 0.2 fusion.117
  65.3 2.4 %multiply_reduce_fusion.2 = (f32[8,32,128]{2,1,0:T(8,128)S(1)}, f32[8,32,128]{2,1,0:T(8,128)S(1)}, bf16[32,8,32,128]{3,2,1,0:T(8,128)(2,1)S(1)}) fusion(f32[32,8,32,128]{3,2,1,0:T(8,128)S(1)} %copy-done, f32[32,7,32,128]{3,2,1,0:T(8,128)S(1)} %fusion.2, f32[32,32,128]{2,1,0:T(8,128)S(1)} %get-tuple-element.77, f32[32,32,128]{2,1,0:T(8,128)S(1)} %get-tuple-element.54, ...), kind=kLoop, calls=%fused_computation.4 | loop fusion | flops 13565952 | bytes 13369472 | tf_op jit(solution)/shard_map/reduce_sum | solution.py:215
  67.7 4.1 %collective-permute-done.11 = f32[16,32,128]{2,1,0:T(8,128)S(1)} collective-permute-done((f32[16,32,128]{2,1,0:T(8,128)S(1)}, f32[16,32,128]{2,1,0:T(8,128)S(1)}, u32[]{:S(2)}, u32[]{:S(2)}) %collective-permute-start.11) | collective-permute-done | bytes 262176 | tf_op jit(solution)/shard_map/ppermute | solution.py:114
  71.7 0.1 maximum_select_fusion.1
  71.8 0.0 copy-start.3
  71.8 2.7 %multiply_reduce_fusion = (f32[8,32,128]{2,1,0:T(8,128)S(1)}, f32[8,32,128]{2,1,0:T(8,128)S(1)}, bf16[32,8,32,128]{3,2,1,0:T(8,128)(2,1)S(1)}) fusion(f32[32,7,32,128]{3,2,1,0:T(8,128)S(1)} %fusion, f32[32,32,128]{2,1,0:T(8,128)S(1)} %maximum_select_fusion.1, f32[32,32,128]{2,1,0:T(8,128)S(1)} %get-tuple-element.53, f32[8,32]{1,0:T(8,128)S(1)} %get-tuple-element.74, ...), kind=kLoop, calls=%fused_computation.1 | loop fusion | flops 15663104 | bytes 9307264 | tf_op jit(solution)/shard_map/reduce_sum | solution.py:215
  74.5 0.8 broadcast_multiply_fusion
  75.3 0.1 fusion.113
  75.5 1.9 %collective-permute-start.15 = (f32[2,1,32,128]{3,2,1,0:T(8,128)S(1)}, f32[2,1,32,128]{3,2,1,0:T(8,128)S(1)}, u32[]{:S(2)}, u32[]{:S(2)}) collective-permute-start(f32[2,1,32,128]{3,2,1,0:T(8,128)S(1)} %get-tuple-element.64), channel_id=1, source_target_pairs={{4,0},{8,4},{12,8},{16,12},{20,16},{24,20},{28,24},{5,1},{9,5},{13... | collective-permute-start | bytes 98312 | tf_op jit(solution)/shard_map/ppermute | solution.py:33
  77.4 3.5 %collective-permute-start.14 = (f32[2,8,1,128]{3,2,1,0:T(1,128)S(1)}, f32[2,8,1,128]{3,2,1,0:T(1,128)S(1)}, u32[]{:S(2)}, u32[]{:S(2)}) collective-permute-start(f32[2,8,1,128]{3,2,1,0:T(1,128)S(1)} %get-tuple-element.66), channel_id=1, source_target_pairs={{1,0},{2,1},{3,2},{5,4},{6,5},{7,6},{9,8},{10,9},{11,10},{13,12},{... | collective-permute-start | bytes 24584 | tf_op jit(solution)/shard_map/ppermute | solution.py:33
  80.9 2.1 %collective-permute-start.13 = (f32[2,8,1,128]{3,2,1,0:T(1,128)S(1)}, f32[2,8,1,128]{3,2,1,0:T(1,128)S(1)}, u32[]{:S(2)}, u32[]{:S(2)}) collective-permute-start(f32[2,8,1,128]{3,2,1,0:T(1,128)S(1)} %get-tuple-element.65), channel_id=1, source_target_pairs={{0,1},{1,2},{2,3},{4,5},{5,6},{6,7},{8,9},{9,10},{10,11},{12,13},{... | collective-permute-start | bytes 24584 | tf_op jit(solution)/shard_map/ppermute | solution.py:33
  83.0 3.5 %collective-permute-start.12 = (f32[2,1,32,128]{3,2,1,0:T(8,128)S(1)}, f32[2,1,32,128]{3,2,1,0:T(8,128)S(1)}, u32[]{:S(2)}, u32[]{:S(2)}) collective-permute-start(f32[2,1,32,128]{3,2,1,0:T(8,128)S(1)} %get-tuple-element.63), channel_id=1, source_target_pairs={{0,4},{4,8},{8,12},{12,16},{16,20},{20,24},{24,28},{1,5},{5,9},{9,... | collective-permute-start | bytes 98312 | tf_op jit(solution)/shard_map/ppermute | solution.py:33
  86.5 2.4 %pad_maximum_fusion = bf16[64,8,32,128]{3,2,1,0:T(8,128)(2,1)} fusion(bf16[32,8,32,128]{3,2,1,0:T(8,128)(2,1)S(1)} %get-tuple-element.50, bf16[32,8,32,128]{3,2,1,0:T(8,128)(2,1)S(1)} %get-tuple-element.30), kind=kLoop, calls=%fused_computation | loop fusion | flops 2097152 | bytes 8388608 | tf_op jit(solution)/shard_map/dynamic_update_slice | solution.py:235
  88.9 0.0 collective-permute-done.14
  88.9 0.0 collective-permute-done.13
  88.9 0.0 collective-permute-done.15
  88.9 0.0 collective-permute-done.12
  88.9 0.1 fusion.9
  88.9 0.5 power_multiply_fusion
  89.5 0.7 fusion.29
  90.2 0.9 fusion.93
  (18 shorter events, 0.2 us)
Async XLA Ops:
  9.2 7.2 %collective-permute-start = (f32[16,32,128]{2,1,0:T(8,128)S(1)}, f32[16,32,128]{2,1,0:T(8,128)S(1)}, u32[]{:S(2)}, u32[]{:S(2)}) collective-permute-start(f32[16,32,128]{2,1,0:T(8,128)S(1)} %slice_select_fusion.2), channel_id=1, source_target_pairs={{0,4},{4,0},{8,12},{12,8},{16,20},{20,16},{24,28},{28,24},{1,5},{5... | collective-permute-start | bytes 786440 | tf_op jit(solution)/shard_map/ppermute | solution.py:114
  13.2 3.1 %copy-start.2 = (f32[8,32,128]{2,1,0:T(8,128)S(1)}, f32[8,32,128]{2,1,0:T(8,128)}, u32[]{:S(2)}) copy-start(f32[8,32,128]{2,1,0:T(8,128)} %param.8) | copy-start | bytes 393220
  13.3 14.3 %copy-start = (f32[32,8,32,128]{3,2,1,0:T(8,128)S(1)}, f32[32,8,32,128]{3,2,1,0:T(8,128)}, u32[]{:S(2)}) copy-start(f32[32,8,32,128]{3,2,1,0:T(8,128)} %get-tuple-element.49) | copy-start | bytes 12582916
  13.3 15.2 %collective-permute-start.2 = (f32[16,32,128]{2,1,0:T(8,128)S(1)}, f32[16,32,128]{2,1,0:T(8,128)S(1)}, u32[]{:S(2)}, u32[]{:S(2)}) collective-permute-start(f32[16,32,128]{2,1,0:T(8,128)S(1)} %slice_select_fusion.1), channel_id=1, source_target_pairs={{0,4},{4,0},{8,12},{12,8},{16,20},{20,16},{24,28},{28,24},{1,5},{5... | collective-permute-start | bytes 786440 | tf_op jit(solution)/shard_map/ppermute | solution.py:114
  16.5 14.2 %collective-permute-start.1 = (f32[16,32,128]{2,1,0:T(8,128)S(1)}, f32[16,32,128]{2,1,0:T(8,128)S(1)}, u32[]{:S(2)}, u32[]{:S(2)}) collective-permute-start(f32[16,32,128]{2,1,0:T(8,128)S(1)} %fusion.106), channel_id=1, source_target_pairs={{0,8},{4,12},{8,16},{12,20},{16,24},{20,28},{1,9},{5,13},{9,17},{1... | collective-permute-start | bytes 786440 | tf_op jit(solution)/shard_map/ppermute | solution.py:114
  19.7 8.8 %collective-permute-start.3 = (f32[2,8,1,128]{3,2,1,0:T(1,128)S(1)}, f32[2,8,1,128]{3,2,1,0:T(1,128)S(1)}, u32[]{:S(2)}, u32[]{:S(2)}) collective-permute-start(f32[2,8,1,128]{3,2,1,0:T(1,128)S(1)} %get-tuple-element.70), channel_id=1, source_target_pairs={{0,1},{1,2},{2,3},{4,5},{5,6},{6,7},{8,9},{9,10},{10,11},{12,13},{... | collective-permute-start | bytes 24584 | tf_op jit(solution)/shard_map/ppermute | solution.py:33
  25.7 5.0 %collective-permute-start.4 = (f32[2,8,1,128]{3,2,1,0:T(1,128)S(1)}, f32[2,8,1,128]{3,2,1,0:T(1,128)S(1)}, u32[]{:S(2)}, u32[]{:S(2)}) collective-permute-start(f32[2,8,1,128]{3,2,1,0:T(1,128)S(1)} %get-tuple-element.69), channel_id=1, source_target_pairs={{1,0},{2,1},{3,2},{5,4},{6,5},{7,6},{9,8},{10,9},{11,10},{13,12},{... | collective-permute-start | bytes 24584 | tf_op jit(solution)/shard_map/ppermute | solution.py:33
  27.6 13.9 %copy-start.5 = (f32[32,128]{1,0:T(8,128)S(1)}, f32[32,128]{1,0:T(8,128)}, u32[]{:S(2)}) copy-start(f32[32,128]{1,0:T(8,128)} %param.14) | copy-start | bytes 49156
  30.7 16.8 %collective-permute-start.5 = (f32[16,32,128]{2,1,0:T(8,128)S(1)}, f32[16,32,128]{2,1,0:T(8,128)S(1)}, u32[]{:S(2)}, u32[]{:S(2)}) collective-permute-start(f32[16,32,128]{2,1,0:T(8,128)S(1)} %add.212), channel_id=1, source_target_pairs={{0,16},{4,20},{8,24},{12,28},{1,17},{5,21},{9,25},{13,29},{2,18},{... | collective-permute-start | bytes 786440 | tf_op jit(solution)/shard_map/ppermute | solution.py:114
  32.8 16.7 %collective-permute-start.6 = (f32[16,32,128]{2,1,0:T(8,128)S(1)}, f32[16,32,128]{2,1,0:T(8,128)S(1)}, u32[]{:S(2)}, u32[]{:S(2)}) collective-permute-start(f32[16,32,128]{2,1,0:T(8,128)S(1)} %fusion.107), channel_id=1, source_target_pairs={{0,8},{4,12},{8,16},{12,20},{16,24},{20,28},{1,9},{5,13},{9,17},{1... | collective-permute-start | bytes 786440 | tf_op jit(solution)/shard_map/ppermute | solution.py:114
  35.3 12.2 %collective-permute-start.7 = (f32[2,1,32,128]{3,2,1,0:T(8,128)S(1)}, f32[2,1,32,128]{3,2,1,0:T(8,128)S(1)}, u32[]{:S(2)}, u32[]{:S(2)}) collective-permute-start(f32[2,1,32,128]{3,2,1,0:T(8,128)S(1)} %get-tuple-element.68), channel_id=1, source_target_pairs={{0,4},{4,8},{8,12},{12,16},{16,20},{20,24},{24,28},{1,5},{5,9},{9,... | collective-permute-start | bytes 98312 | tf_op jit(solution)/shard_map/ppermute | solution.py:33
  38.4 9.1 %collective-permute-start.8 = (f32[2,1,32,128]{3,2,1,0:T(8,128)S(1)}, f32[2,1,32,128]{3,2,1,0:T(8,128)S(1)}, u32[]{:S(2)}, u32[]{:S(2)}) collective-permute-start(f32[2,1,32,128]{3,2,1,0:T(8,128)S(1)} %get-tuple-element.67), channel_id=1, source_target_pairs={{4,0},{8,4},{12,8},{16,12},{20,16},{24,20},{28,24},{5,1},{9,5},{13... | collective-permute-start | bytes 98312 | tf_op jit(solution)/shard_map/ppermute | solution.py:33
  49.5 15.5 %copy-start.4 = (f32[64,32,128]{2,1,0:T(8,128)S(1)}, f32[64,32,128]{2,1,0:T(8,128)}, u32[]{:S(2)}) copy-start(f32[64,32,128]{2,1,0:T(8,128)} %param.12) | copy-start | bytes 3145732
  49.6 8.9 %collective-permute-start.9 = (f32[16,32,128]{2,1,0:T(8,128)S(1)}, f32[16,32,128]{2,1,0:T(8,128)S(1)}, u32[]{:S(2)}, u32[]{:S(2)}) collective-permute-start(f32[16,32,128]{2,1,0:T(8,128)S(1)} %add_select_fusion.1), channel_id=1, source_target_pairs={{0,4},{4,0},{8,12},{12,8},{16,20},{20,16},{24,28},{28,24},{1,5},{5... | collective-permute-start | bytes 786440 | tf_op jit(solution)/shard_map/ppermute | solution.py:114
  51.7 12.7 %collective-permute-start.10 = (f32[16,32,128]{2,1,0:T(8,128)S(1)}, f32[16,32,128]{2,1,0:T(8,128)S(1)}, u32[]{:S(2)}, u32[]{:S(2)}) collective-permute-start(f32[16,32,128]{2,1,0:T(8,128)S(1)} %add.216), channel_id=1, source_target_pairs={{0,16},{4,20},{8,24},{12,28},{1,17},{5,21},{9,25},{13,29},{2,18},{... | collective-permute-start | bytes 786440 | tf_op jit(solution)/shard_map/ppermute | solution.py:114
  53.1 12.1 %copy-start.1 = (bf16[64,8,32,128]{3,2,1,0:T(8,128)(2,1)S(1)}, bf16[64,8,32,128]{3,2,1,0:T(8,128)(2,1)}, u32[]{:S(2)}) copy-start(bf16[64,8,32,128]{3,2,1,0:T(8,128)(2,1)} %param.11) | copy-start | bytes 12582916
  64.6 7.2 %collective-permute-start.11 = (f32[16,32,128]{2,1,0:T(8,128)S(1)}, f32[16,32,128]{2,1,0:T(8,128)S(1)}, u32[]{:S(2)}, u32[]{:S(2)}) collective-permute-start(f32[16,32,128]{2,1,0:T(8,128)S(1)} %add_select_fusion), channel_id=1, source_target_pairs={{0,4},{4,0},{8,12},{12,8},{16,20},{20,16},{24,28},{28,24},{1,5},{5... | collective-permute-start | bytes 786440 | tf_op jit(solution)/shard_map/ppermute | solution.py:114
  71.8 2.7 %copy-start.3 = (f32[8,32,128]{2,1,0:T(8,128)S(1)}, f32[8,32,128]{2,1,0:T(8,128)}, u32[]{:S(2)}) copy-start(f32[8,32,128]{2,1,0:T(8,128)} %param.9) | copy-start | bytes 393220
  75.5 13.4 %collective-permute-start.15 = (f32[2,1,32,128]{3,2,1,0:T(8,128)S(1)}, f32[2,1,32,128]{3,2,1,0:T(8,128)S(1)}, u32[]{:S(2)}, u32[]{:S(2)}) collective-permute-start(f32[2,1,32,128]{3,2,1,0:T(8,128)S(1)} %get-tuple-element.64), channel_id=1, source_target_pairs={{4,0},{8,4},{12,8},{16,12},{20,16},{24,20},{28,24},{5,1},{9,5},{13... | collective-permute-start | bytes 98312 | tf_op jit(solution)/shard_map/ppermute | solution.py:33
  77.4 11.5 %collective-permute-start.14 = (f32[2,8,1,128]{3,2,1,0:T(1,128)S(1)}, f32[2,8,1,128]{3,2,1,0:T(1,128)S(1)}, u32[]{:S(2)}, u32[]{:S(2)}) collective-permute-start(f32[2,8,1,128]{3,2,1,0:T(1,128)S(1)} %get-tuple-element.66), channel_id=1, source_target_pairs={{1,0},{2,1},{3,2},{5,4},{6,5},{7,6},{9,8},{10,9},{11,10},{13,12},{... | collective-permute-start | bytes 24584 | tf_op jit(solution)/shard_map/ppermute | solution.py:33
  80.9 8.0 %collective-permute-start.13 = (f32[2,8,1,128]{3,2,1,0:T(1,128)S(1)}, f32[2,8,1,128]{3,2,1,0:T(1,128)S(1)}, u32[]{:S(2)}, u32[]{:S(2)}) collective-permute-start(f32[2,8,1,128]{3,2,1,0:T(1,128)S(1)} %get-tuple-element.65), channel_id=1, source_target_pairs={{0,1},{1,2},{2,3},{4,5},{5,6},{6,7},{8,9},{9,10},{10,11},{12,13},{... | collective-permute-start | bytes 24584 | tf_op jit(solution)/shard_map/ppermute | solution.py:33
  83.0 5.9 %collective-permute-start.12 = (f32[2,1,32,128]{3,2,1,0:T(8,128)S(1)}, f32[2,1,32,128]{3,2,1,0:T(8,128)S(1)}, u32[]{:S(2)}, u32[]{:S(2)}) collective-permute-start(f32[2,1,32,128]{3,2,1,0:T(8,128)S(1)} %get-tuple-element.63), channel_id=1, source_target_pairs={{0,4},{4,8},{8,12},{12,16},{16,20},{20,24},{24,28},{1,5},{5,9},{9,... | collective-permute-start | bytes 98312 | tf_op jit(solution)/shard_map/ppermute | solution.py:33

commit v14 on v10

--- a/solution.py
+++ b/solution.py
@@ -107,7 +107,7 @@
     size = lines // groups
     steps = [None] * groups
     steps[0] = paired_steps(totals_of(0, size, None), axis)
-    live, made, carried, stage = {}, [], {}, 0
+    live, made, carried, in_flight, stage = {}, [], {}, {}, 0
     while stage < groups or live:
         if stage < groups:
             live[stage] = next(steps[stage])
@@ -115,12 +115,10 @@
         if stage == 0:
             for g in range(1, groups):
                 steps[g] = paired_steps(totals_of(g * size, size, live[0][0]), axis)
-        tied = (arrived, made)
-        if stage in riders:
-            tied, carried[stage] = lax.optimization_barrier((tied, riders[stage](live[0][0])))
-        else:
-            tied = lax.optimization_barrier(tied)
-        arrived, made = tied
+        issued = riders[stage](live[0][0]) if stage in riders else None
+        arrived, made, landed = lax.optimization_barrier((arrived, made, in_flight))
+        carried.update(landed)
+        in_flight = {} if issued is None else {stage: issued}
         following = {}
         for g, value in arrived.items():
             try:
@@ -129,6 +127,7 @@
                 made = made + [emit(g * size, size, finished.value)]
         live = following
         stage += 1
+    carried.update(in_flight)
     return made, carried
 
 

time: 89 us -> 92 us (1.034)
  waiting for transfers between devices: 17 us -> 21.7 us
  starting transfers between devices: 43.2 us -> 41.3 us
    ppermute x8, waiting for transfers between devices: 11.2 us -> 20 us  [pipelined_scan(): lax.ppermute(payload, axis, pairs)]
    ppermute x8, waiting for transfers between devices: 5.73 us -> 1.72 us  [shifted(): return lax.ppermute(block, axis, pairs)]
    ppermute x8, starting transfers between devices: 14.6 us -> 13.6 us  [pipelined_scan(): lax.ppermute(payload, axis, pairs)]
    ppermute x8, starting transfers between devices: 28.6 us -> 27.7 us  [shifted(): return lax.ppermute(block, axis, pairs)]
  transfers between devices with their start and end apart: 16 -> 16, of which waited for: 7 -> 8; matrix products, arithmetic and copies ran while one was open for 14% -> 13% of each run, Pallas kernels for 0% -> 0%
where the time goes in v14:
time: 92 us; the launch traced here: 91.5 us
  starting transfers between devices  41.3 us (45%)
  other arithmetic  26.6 us (29%)
  waiting for transfers between devices  21.7 us (24%)
  between operations  1.07 us (1%)
    ppermute x8, starting transfers between devices, shifted(): return lax.ppermute(block, axis, pairs)  27.7 us
    ppermute x8, waiting for transfers between devices, pipelined_scan(): lax.ppermute(payload, axis, pairs)  20 us
    ppermute x8, starting transfers between devices, pipelined_scan(): lax.ppermute(payload, axis, pairs)  13.6 us
    reduce_sum x2, other arithmetic, totals_of(): return jnp.sum(optical_depth, axis=1)  8.66 us
    reduce_sum x2, other arithmetic, emit(): jnp.sum(radiance * (1.0 - jnp.exp(-optical_depth)), axis=0)  5.06 us
    another operation x2, other arithmetic, emit(): jnp.cumsum(optical_depth[:, :rows - 1], axis=1)  3.55 us
    dynamic_update_slice x1, other arithmetic, local(): lax.dynamic_update_slice_in_dim(spectral_power, part, start, axis=0)  2.38 us
  transfers between devices with their start and end apart: 16, of which 8 were waited for; matrix products, arithmetic and copies ran while one was open for 13% of the time, Pallas kernels for 0%

profile of v14, /device:TPU:9, one launch (start us, length us, event | category | flops | bytes accessed | tf_op | source)
XLA Modules:
  0.0 91.5 jit_solution(2384735454142037819)
XLA Ops:
  0.6 0.7 convert_subtract_fusion
  1.3 0.8 fusion.120
  2.1 1.1 %add_bitcast_fusion = (f32[1,8,32,128]{3,2,1,0:T(8,128)S(1)}, f32[8,32,128]{2,1,0:T(8,128)S(1)}) fusion(f32[8,32,128]{2,1,0:T(8,128)} %param.9, f32[8,32,128]{2,1,0:T(8,128)} %param.10, f32[8,32]{1,0:T(8,128)S(1)} %get-tuple-element.73), kind=kLoop, calls=%fused_computation.215 | loop fusion | flops 262144 | bytes 525312 | tf_op jit(solution)/shard_map/stack | solution.py:181
  3.2 5.9 %fusion.116 = (f32[32,32,128]{2,1,0:T(8,128)S(1)}, f32[32,8,32,128]{3,2,1,0:T(8,128)}, f32[32,8,32,128]{3,2,1,0:T(8,128)}) fusion(f32[8,32]{1,0:T(8,128)S(1)} %get-tuple-element.74, bf16[64,8,32,128]{3,2,1,0:T(8,128)(2,1)} %param.11, f32[32]{0:T(128)S(1)} %get-tuple-element.75, f32[8,32,128]{2,1,0:T(8,128)S(1)} %get-tuple-element.72, ...), kind=kLoop, calls=%fused_computation.230 | loop fusion | flops 11403264 | bytes 13239552 | tf_op jit(solution)/shard_map/reduce_sum | solution.py:202
  9.2 1.3 %collective-permute-start = (f32[16,32,128]{2,1,0:T(8,128)S(1)}, f32[16,32,128]{2,1,0:T(8,128)S(1)}, u32[]{:S(2)}, u32[]{:S(2)}) collective-permute-start(f32[16,32,128]{2,1,0:T(8,128)S(1)} %slice_select_fusion.2), channel_id=1, source_target_pairs={{0,4},{4,0},{8,12},{12,8},{16,20},{20,16},{24,28},{28,24},{1,5},{5... | collective-permute-start | bytes 786440 | tf_op jit(solution)/shard_map/ppermute | solution.py:114
  10.5 2.7 %reduce_sum.55 = f32[32,32,128]{2,1,0:T(8,128)S(1)} reduce(f32[32,8,32,128]{3,2,1,0:T(8,128)} %get-tuple-element.21, f32[]{:T(128)} %constant.18.clone.1), dimensions={1}, to_apply=%region_1.2 | reduce | flops 917504 | bytes 4718596 | tf_op jit(solution)/shard_map/reduce_sum | solution.py:202
  13.3 0.0 copy-start
  13.3 0.3 collective-permute-start.2
  13.6 2.7 %fusion = f32[32,7,32,128]{3,2,1,0:T(8,128)S(1)} fusion(f32[32,8,32,128]{3,2,1,0:T(8,128)} %get-tuple-element.21), kind=kOutput, calls=%fused_computation.11 | output fusion | flops 5505024 | bytes 7340032 | tf_op jit(solution)/shard_map/jit(cumsum)/reduce_window_sum | solution.py:207
  16.3 0.1 collective-permute-done
  16.4 0.1 fusion.106
  16.5 3.2 %collective-permute-start.1 = (f32[16,32,128]{2,1,0:T(8,128)S(1)}, f32[16,32,128]{2,1,0:T(8,128)S(1)}, u32[]{:S(2)}, u32[]{:S(2)}) collective-permute-start(f32[16,32,128]{2,1,0:T(8,128)S(1)} %fusion.106), channel_id=1, source_target_pairs={{0,8},{4,12},{8,16},{12,20},{16,24},{20,28},{1,9},{5,13},{9,17},{1... | collective-permute-start | bytes 786440 | tf_op jit(solution)/shard_map/ppermute | solution.py:114
  19.7 0.0 copy-start.2
  19.7 0.0 copy-start.5
  19.7 0.9 fusion.2
  20.6 0.0 copy-start.4
  20.6 1.4 %collective-permute-done.2 = f32[16,32,128]{2,1,0:T(8,128)S(1)} collective-permute-done((f32[16,32,128]{2,1,0:T(8,128)S(1)}, f32[16,32,128]{2,1,0:T(8,128)S(1)}, u32[]{:S(2)}, u32[]{:S(2)}) %collective-permute-start.2) | collective-permute-done | bytes 262176 | tf_op jit(solution)/shard_map/ppermute | solution.py:114
  22.0 1.6 %collective-permute-done.1 = f32[16,32,128]{2,1,0:T(8,128)S(1)} collective-permute-done((f32[16,32,128]{2,1,0:T(8,128)S(1)}, f32[16,32,128]{2,1,0:T(8,128)S(1)}, u32[]{:S(2)}, u32[]{:S(2)}) %collective-permute-start.1) | collective-permute-done | bytes 262176 | tf_op jit(solution)/shard_map/ppermute | solution.py:114
  23.6 4.2 %collective-permute-start.3 = (f32[16,32,128]{2,1,0:T(8,128)S(1)}, f32[16,32,128]{2,1,0:T(8,128)S(1)}, u32[]{:S(2)}, u32[]{:S(2)}) collective-permute-start(f32[16,32,128]{2,1,0:T(8,128)S(1)} %add.212), channel_id=1, source_target_pairs={{0,16},{4,20},{8,24},{12,28},{1,17},{5,21},{9,25},{13,29},{2,18},{... | collective-permute-start | bytes 786440 | tf_op jit(solution)/shard_map/ppermute | solution.py:114
  27.9 0.1 fusion.107
  27.9 1.9 %collective-permute-start.4 = (f32[16,32,128]{2,1,0:T(8,128)S(1)}, f32[16,32,128]{2,1,0:T(8,128)S(1)}, u32[]{:S(2)}, u32[]{:S(2)}) collective-permute-start(f32[16,32,128]{2,1,0:T(8,128)S(1)} %fusion.107), channel_id=1, source_target_pairs={{0,8},{4,12},{8,16},{12,20},{16,24},{20,28},{1,9},{5,13},{9,17},{1... | collective-permute-start | bytes 786440 | tf_op jit(solution)/shard_map/ppermute | solution.py:114
  29.9 7.9 %collective-permute-done.3 = f32[16,32,128]{2,1,0:T(8,128)S(1)} collective-permute-done((f32[16,32,128]{2,1,0:T(8,128)S(1)}, f32[16,32,128]{2,1,0:T(8,128)S(1)}, u32[]{:S(2)}, u32[]{:S(2)}) %collective-permute-start.3) | collective-permute-done | bytes 262176 | tf_op jit(solution)/shard_map/ppermute | solution.py:114
  37.8 5.8 %collective-permute-done.4 = f32[16,32,128]{2,1,0:T(8,128)S(1)} collective-permute-done((f32[16,32,128]{2,1,0:T(8,128)S(1)}, f32[16,32,128]{2,1,0:T(8,128)S(1)}, u32[]{:S(2)}, u32[]{:S(2)}) %collective-permute-start.4) | collective-permute-done | bytes 262176 | tf_op jit(solution)/shard_map/ppermute | solution.py:114
  43.5 0.1 fusion.115
  43.6 0.0 copy-start.1
  43.6 0.1 add_select_fusion.1
  43.7 1.3 %collective-permute-start.5 = (f32[16,32,128]{2,1,0:T(8,128)S(1)}, f32[16,32,128]{2,1,0:T(8,128)S(1)}, u32[]{:S(2)}, u32[]{:S(2)}) collective-permute-start(f32[16,32,128]{2,1,0:T(8,128)S(1)} %add_select_fusion.1), channel_id=1, source_target_pairs={{0,4},{4,0},{8,12},{12,8},{16,20},{20,16},{24,28},{28,24},{1,5},{5... | collective-permute-start | bytes 786440 | tf_op jit(solution)/shard_map/ppermute | solution.py:114
  45.0 1.3 %collective-permute-start.6 = (f32[16,32,128]{2,1,0:T(8,128)S(1)}, f32[16,32,128]{2,1,0:T(8,128)S(1)}, u32[]{:S(2)}, u32[]{:S(2)}) collective-permute-start(f32[16,32,128]{2,1,0:T(8,128)S(1)} %add.216), channel_id=1, source_target_pairs={{0,16},{4,20},{8,24},{12,28},{1,17},{5,21},{9,25},{13,29},{2,18},{... | collective-permute-start | bytes 786440 | tf_op jit(solution)/shard_map/ppermute | solution.py:114
  46.4 2.4 %collective-permute-start.7 = (f32[2,1,32,128]{3,2,1,0:T(8,128)S(1)}, f32[2,1,32,128]{3,2,1,0:T(8,128)S(1)}, u32[]{:S(2)}, u32[]{:S(2)}) collective-permute-start(f32[2,1,32,128]{3,2,1,0:T(8,128)S(1)} %get-tuple-element.70), channel_id=1, source_target_pairs={{0,4},{4,8},{8,12},{12,16},{16,20},{20,24},{24,28},{1,5},{5,9},{9,... | collective-permute-start | bytes 98312 | tf_op jit(solution)/shard_map/ppermute | solution.py:33
  48.8 5.6 %collective-permute-start.8 = (f32[2,1,32,128]{3,2,1,0:T(8,128)S(1)}, f32[2,1,32,128]{3,2,1,0:T(8,128)S(1)}, u32[]{:S(2)}, u32[]{:S(2)}) collective-permute-start(f32[2,1,32,128]{3,2,1,0:T(8,128)S(1)} %get-tuple-element.69), channel_id=1, source_target_pairs={{4,0},{8,4},{12,8},{16,12},{20,16},{24,20},{28,24},{5,1},{9,5},{13... | collective-permute-start | bytes 98312 | tf_op jit(solution)/shard_map/ppermute | solution.py:33
  54.4 5.7 %collective-permute-start.10 = (f32[2,8,1,128]{3,2,1,0:T(1,128)S(1)}, f32[2,8,1,128]{3,2,1,0:T(1,128)S(1)}, u32[]{:S(2)}, u32[]{:S(2)}) collective-permute-start(f32[2,8,1,128]{3,2,1,0:T(1,128)S(1)} %get-tuple-element.68), channel_id=1, source_target_pairs={{0,1},{1,2},{2,3},{4,5},{5,6},{6,7},{8,9},{9,10},{10,11},{12,13},{... | collective-permute-start | bytes 24584 | tf_op jit(solution)/shard_map/ppermute | solution.py:33
  60.1 0.0 collective-permute-done.7
  60.1 1.9 %collective-permute-start.11 = (f32[2,8,1,128]{3,2,1,0:T(1,128)S(1)}, f32[2,8,1,128]{3,2,1,0:T(1,128)S(1)}, u32[]{:S(2)}, u32[]{:S(2)}) collective-permute-start(f32[2,8,1,128]{3,2,1,0:T(1,128)S(1)} %get-tuple-element.67), channel_id=1, source_target_pairs={{1,0},{2,1},{3,2},{5,4},{6,5},{7,6},{9,8},{10,9},{11,10},{13,12},{... | collective-permute-start | bytes 24584 | tf_op jit(solution)/shard_map/ppermute | solution.py:33
  62.1 0.0 collective-permute-done.8
  62.1 0.0 collective-permute-done.5
  62.1 0.0 collective-permute-done.6
  62.1 0.1 fusion.114
  62.2 0.1 add_select_fusion
  62.2 0.1 collective-permute-start.9
  62.3 0.2 fusion.117
  62.5 2.4 %multiply_reduce_fusion.2 = (f32[8,32,128]{2,1,0:T(8,128)S(1)}, f32[8,32,128]{2,1,0:T(8,128)S(1)}, bf16[32,8,32,128]{3,2,1,0:T(8,128)(2,1)S(1)}) fusion(f32[32,8,32,128]{3,2,1,0:T(8,128)S(1)} %copy-done, f32[32,7,32,128]{3,2,1,0:T(8,128)S(1)} %fusion.2, f32[32,32,128]{2,1,0:T(8,128)S(1)} %get-tuple-element.77, f32[32,32,128]{2,1,0:T(8,128)S(1)} %get-tuple-element.54, ...), kind=kLoop, calls=%fused_computation.4 | loop fusion | flops 13565952 | bytes 13369472 | tf_op jit(solution)/shard_map/reduce_sum | solution.py:214
  64.9 0.0 collective-permute-done.10
  64.9 0.5 collective-permute-done.11
  65.4 3.2 %collective-permute-done.9 = f32[16,32,128]{2,1,0:T(8,128)S(1)} collective-permute-done((f32[16,32,128]{2,1,0:T(8,128)S(1)}, f32[16,32,128]{2,1,0:T(8,128)S(1)}, u32[]{:S(2)}, u32[]{:S(2)}) %collective-permute-start.9) | collective-permute-done | bytes 262176 | tf_op jit(solution)/shard_map/ppermute | solution.py:114
  68.6 0.1 fusion.7
  68.7 0.5 power_multiply_fusion.2
  69.2 0.1 maximum_select_fusion.1
  69.3 0.0 copy-start.3
  69.3 2.7 %multiply_reduce_fusion = (f32[8,32,128]{2,1,0:T(8,128)S(1)}, f32[8,32,128]{2,1,0:T(8,128)S(1)}, bf16[32,8,32,128]{3,2,1,0:T(8,128)(2,1)S(1)}) fusion(f32[32,7,32,128]{3,2,1,0:T(8,128)S(1)} %fusion, f32[32,32,128]{2,1,0:T(8,128)S(1)} %maximum_select_fusion.1, f32[32,32,128]{2,1,0:T(8,128)S(1)} %get-tuple-element.53, f32[8,32]{1,0:T(8,128)S(1)} %get-tuple-element.74, ...), kind=kLoop, calls=%fused_computation.1 | loop fusion | flops 15663104 | bytes 9307264 | tf_op jit(solution)/shard_map/reduce_sum | solution.py:214
  72.0 0.8 broadcast_multiply_fusion
  72.8 0.7 fusion.20
  73.4 0.2 fusion.113
  73.6 3.6 %collective-permute-start.15 = (f32[2,1,32,128]{3,2,1,0:T(8,128)S(1)}, f32[2,1,32,128]{3,2,1,0:T(8,128)S(1)}, u32[]{:S(2)}, u32[]{:S(2)}) collective-permute-start(f32[2,1,32,128]{3,2,1,0:T(8,128)S(1)} %get-tuple-element.64), channel_id=1, source_target_pairs={{4,0},{8,4},{12,8},{16,12},{20,16},{24,20},{28,24},{5,1},{9,5},{13... | collective-permute-start | bytes 98312 | tf_op jit(solution)/shard_map/ppermute | solution.py:33
  77.2 1.9 %collective-permute-start.14 = (f32[2,8,1,128]{3,2,1,0:T(1,128)S(1)}, f32[2,8,1,128]{3,2,1,0:T(1,128)S(1)}, u32[]{:S(2)}, u32[]{:S(2)}) collective-permute-start(f32[2,8,1,128]{3,2,1,0:T(1,128)S(1)} %get-tuple-element.66), channel_id=1, source_target_pairs={{1,0},{2,1},{3,2},{5,4},{6,5},{7,6},{9,8},{10,9},{11,10},{13,12},{... | collective-permute-start | bytes 24584 | tf_op jit(solution)/shard_map/ppermute | solution.py:33
  79.2 4.6 %collective-permute-start.13 = (f32[2,8,1,128]{3,2,1,0:T(1,128)S(1)}, f32[2,8,1,128]{3,2,1,0:T(1,128)S(1)}, u32[]{:S(2)}, u32[]{:S(2)}) collective-permute-start(f32[2,8,1,128]{3,2,1,0:T(1,128)S(1)} %get-tuple-element.65), channel_id=1, source_target_pairs={{0,1},{1,2},{2,3},{4,5},{5,6},{6,7},{8,9},{9,10},{10,11},{12,13},{... | collective-permute-start | bytes 24584 | tf_op jit(solution)/shard_map/ppermute | solution.py:33
  83.8 1.9 %collective-permute-start.12 = (f32[2,1,32,128]{3,2,1,0:T(8,128)S(1)}, f32[2,1,32,128]{3,2,1,0:T(8,128)S(1)}, u32[]{:S(2)}, u32[]{:S(2)}) collective-permute-start(f32[2,1,32,128]{3,2,1,0:T(8,128)S(1)} %get-tuple-element.63), channel_id=1, source_target_pairs={{0,4},{4,8},{8,12},{12,16},{16,20},{20,24},{24,28},{1,5},{5,9},{9,... | collective-permute-start | bytes 98312 | tf_op jit(solution)/shard_map/ppermute | solution.py:33
  85.7 2.4 %pad_maximum_fusion = bf16[64,8,32,128]{3,2,1,0:T(8,128)(2,1)} fusion(bf16[32,8,32,128]{3,2,1,0:T(8,128)(2,1)S(1)} %get-tuple-element.50, bf16[32,8,32,128]{3,2,1,0:T(8,128)(2,1)S(1)} %get-tuple-element.30), kind=kLoop, calls=%fused_computation | loop fusion | flops 2097152 | bytes 8388608 | tf_op jit(solution)/shard_map/dynamic_update_slice | solution.py:234
  88.1 0.0 collective-permute-done.14
  88.1 0.0 collective-permute-done.13
  88.1 0.0 collective-permute-done.15
  88.1 1.2 %collective-permute-done.12 = f32[2,1,32,128]{3,2,1,0:T(8,128)S(1)} collective-permute-done((f32[2,1,32,128]{3,2,1,0:T(8,128)S(1)}, f32[2,1,32,128]{3,2,1,0:T(8,128)S(1)}, u32[]{:S(2)}, u32[]{:S(2)}) %collective-permute-start.12) | collective-permute-done | bytes 32800 | tf_op jit(solution)/shard_map/ppermute | solution.py:33
  89.4 0.5 power_multiply_fusion
  90.0 0.7 fusion.29
  90.6 0.9 fusion.93
  (18 shorter events, 0.3 us)
Async XLA Ops:
  9.2 7.2 %collective-permute-start = (f32[16,32,128]{2,1,0:T(8,128)S(1)}, f32[16,32,128]{2,1,0:T(8,128)S(1)}, u32[]{:S(2)}, u32[]{:S(2)}) collective-permute-start(f32[16,32,128]{2,1,0:T(8,128)S(1)} %slice_select_fusion.2), channel_id=1, source_target_pairs={{0,4},{4,0},{8,12},{12,8},{16,20},{20,16},{24,28},{28,24},{1,5},{5... | collective-permute-start | bytes 786440 | tf_op jit(solution)/shard_map/ppermute | solution.py:114
  13.3 6.4 %copy-start = (f32[32,8,32,128]{3,2,1,0:T(8,128)S(1)}, f32[32,8,32,128]{3,2,1,0:T(8,128)}, u32[]{:S(2)}) copy-start(f32[32,8,32,128]{3,2,1,0:T(8,128)} %get-tuple-element.49) | copy-start | bytes 12582916
  13.3 8.7 %collective-permute-start.2 = (f32[16,32,128]{2,1,0:T(8,128)S(1)}, f32[16,32,128]{2,1,0:T(8,128)S(1)}, u32[]{:S(2)}, u32[]{:S(2)}) collective-permute-start(f32[16,32,128]{2,1,0:T(8,128)S(1)} %slice_select_fusion.1), channel_id=1, source_target_pairs={{0,4},{4,0},{8,12},{12,8},{16,20},{20,16},{24,28},{28,24},{1,5},{5... | collective-permute-start | bytes 786440 | tf_op jit(solution)/shard_map/ppermute | solution.py:114
  16.5 7.1 %collective-permute-start.1 = (f32[16,32,128]{2,1,0:T(8,128)S(1)}, f32[16,32,128]{2,1,0:T(8,128)S(1)}, u32[]{:S(2)}, u32[]{:S(2)}) collective-permute-start(f32[16,32,128]{2,1,0:T(8,128)S(1)} %fusion.106), channel_id=1, source_target_pairs={{0,8},{4,12},{8,16},{12,20},{16,24},{20,28},{1,9},{5,13},{9,17},{1... | collective-permute-start | bytes 786440 | tf_op jit(solution)/shard_map/ppermute | solution.py:114
  19.7 10.2 %copy-start.2 = (f32[8,32,128]{2,1,0:T(8,128)S(1)}, f32[8,32,128]{2,1,0:T(8,128)}, u32[]{:S(2)}) copy-start(f32[8,32,128]{2,1,0:T(8,128)} %param.8) | copy-start | bytes 393220
  19.7 10.2 %copy-start.5 = (f32[32,128]{1,0:T(8,128)S(1)}, f32[32,128]{1,0:T(8,128)}, u32[]{:S(2)}) copy-start(f32[32,128]{1,0:T(8,128)} %param.14) | copy-start | bytes 49156
  20.6 41.7 %copy-start.4 = (f32[64,32,128]{2,1,0:T(8,128)S(1)}, f32[64,32,128]{2,1,0:T(8,128)}, u32[]{:S(2)}) copy-start(f32[64,32,128]{2,1,0:T(8,128)} %param.12) | copy-start | bytes 3145732
  23.6 14.2 %collective-permute-start.3 = (f32[16,32,128]{2,1,0:T(8,128)S(1)}, f32[16,32,128]{2,1,0:T(8,128)S(1)}, u32[]{:S(2)}, u32[]{:S(2)}) collective-permute-start(f32[16,32,128]{2,1,0:T(8,128)S(1)} %add.212), channel_id=1, source_target_pairs={{0,16},{4,20},{8,24},{12,28},{1,17},{5,21},{9,25},{13,29},{2,18},{... | collective-permute-start | bytes 786440 | tf_op jit(solution)/shard_map/ppermute | solution.py:114
  27.9 15.6 %collective-permute-start.4 = (f32[16,32,128]{2,1,0:T(8,128)S(1)}, f32[16,32,128]{2,1,0:T(8,128)S(1)}, u32[]{:S(2)}, u32[]{:S(2)}) collective-permute-start(f32[16,32,128]{2,1,0:T(8,128)S(1)} %fusion.107), channel_id=1, source_target_pairs={{0,8},{4,12},{8,16},{12,20},{16,24},{20,28},{1,9},{5,13},{9,17},{1... | collective-permute-start | bytes 786440 | tf_op jit(solution)/shard_map/ppermute | solution.py:114
  43.6 18.9 %copy-start.1 = (bf16[64,8,32,128]{3,2,1,0:T(8,128)(2,1)S(1)}, bf16[64,8,32,128]{3,2,1,0:T(8,128)(2,1)}, u32[]{:S(2)}) copy-start(bf16[64,8,32,128]{3,2,1,0:T(8,128)(2,1)} %param.11) | copy-start | bytes 12582916
  43.7 18.4 %collective-permute-start.5 = (f32[16,32,128]{2,1,0:T(8,128)S(1)}, f32[16,32,128]{2,1,0:T(8,128)S(1)}, u32[]{:S(2)}, u32[]{:S(2)}) collective-permute-start(f32[16,32,128]{2,1,0:T(8,128)S(1)} %add_select_fusion.1), channel_id=1, source_target_pairs={{0,4},{4,0},{8,12},{12,8},{16,20},{20,16},{24,28},{28,24},{1,5},{5... | collective-permute-start | bytes 786440 | tf_op jit(solution)/shard_map/ppermute | solution.py:114
  45.0 17.1 %collective-permute-start.6 = (f32[16,32,128]{2,1,0:T(8,128)S(1)}, f32[16,32,128]{2,1,0:T(8,128)S(1)}, u32[]{:S(2)}, u32[]{:S(2)}) collective-permute-start(f32[16,32,128]{2,1,0:T(8,128)S(1)} %add.216), channel_id=1, source_target_pairs={{0,16},{4,20},{8,24},{12,28},{1,17},{5,21},{9,25},{13,29},{2,18},{... | collective-permute-start | bytes 786440 | tf_op jit(solution)/shard_map/ppermute | solution.py:114
  46.4 13.8 %collective-permute-start.7 = (f32[2,1,32,128]{3,2,1,0:T(8,128)S(1)}, f32[2,1,32,128]{3,2,1,0:T(8,128)S(1)}, u32[]{:S(2)}, u32[]{:S(2)}) collective-permute-start(f32[2,1,32,128]{3,2,1,0:T(8,128)S(1)} %get-tuple-element.70), channel_id=1, source_target_pairs={{0,4},{4,8},{8,12},{12,16},{16,20},{20,24},{24,28},{1,5},{5,9},{9,... | collective-permute-start | bytes 98312 | tf_op jit(solution)/shard_map/ppermute | solution.py:33
  48.8 13.3 %collective-permute-start.8 = (f32[2,1,32,128]{3,2,1,0:T(8,128)S(1)}, f32[2,1,32,128]{3,2,1,0:T(8,128)S(1)}, u32[]{:S(2)}, u32[]{:S(2)}) collective-permute-start(f32[2,1,32,128]{3,2,1,0:T(8,128)S(1)} %get-tuple-element.69), channel_id=1, source_target_pairs={{4,0},{8,4},{12,8},{16,12},{20,16},{24,20},{28,24},{5,1},{9,5},{13... | collective-permute-start | bytes 98312 | tf_op jit(solution)/shard_map/ppermute | solution.py:33
  54.4 10.5 %collective-permute-start.10 = (f32[2,8,1,128]{3,2,1,0:T(1,128)S(1)}, f32[2,8,1,128]{3,2,1,0:T(1,128)S(1)}, u32[]{:S(2)}, u32[]{:S(2)}) collective-permute-start(f32[2,8,1,128]{3,2,1,0:T(1,128)S(1)} %get-tuple-element.68), channel_id=1, source_target_pairs={{0,1},{1,2},{2,3},{4,5},{5,6},{6,7},{8,9},{9,10},{10,11},{12,13},{... | collective-permute-start | bytes 24584 | tf_op jit(solution)/shard_map/ppermute | solution.py:33
  60.1 5.3 %collective-permute-start.11 = (f32[2,8,1,128]{3,2,1,0:T(1,128)S(1)}, f32[2,8,1,128]{3,2,1,0:T(1,128)S(1)}, u32[]{:S(2)}, u32[]{:S(2)}) collective-permute-start(f32[2,8,1,128]{3,2,1,0:T(1,128)S(1)} %get-tuple-element.67), channel_id=1, source_target_pairs={{1,0},{2,1},{3,2},{5,4},{6,5},{7,6},{9,8},{10,9},{11,10},{13,12},{... | collective-permute-start | bytes 24584 | tf_op jit(solution)/shard_map/ppermute | solution.py:33
  62.2 6.4 %collective-permute-start.9 = (f32[16,32,128]{2,1,0:T(8,128)S(1)}, f32[16,32,128]{2,1,0:T(8,128)S(1)}, u32[]{:S(2)}, u32[]{:S(2)}) collective-permute-start(f32[16,32,128]{2,1,0:T(8,128)S(1)} %add_select_fusion), channel_id=1, source_target_pairs={{0,4},{4,0},{8,12},{12,8},{16,20},{20,16},{24,28},{28,24},{1,5},{5... | collective-permute-start | bytes 786440 | tf_op jit(solution)/shard_map/ppermute | solution.py:114
  69.3 2.7 %copy-start.3 = (f32[8,32,128]{2,1,0:T(8,128)S(1)}, f32[8,32,128]{2,1,0:T(8,128)}, u32[]{:S(2)}) copy-start(f32[8,32,128]{2,1,0:T(8,128)} %param.9) | copy-start | bytes 393220
  73.6 14.5 %collective-permute-start.15 = (f32[2,1,32,128]{3,2,1,0:T(8,128)S(1)}, f32[2,1,32,128]{3,2,1,0:T(8,128)S(1)}, u32[]{:S(2)}, u32[]{:S(2)}) collective-permute-start(f32[2,1,32,128]{3,2,1,0:T(8,128)S(1)} %get-tuple-element.64), channel_id=1, source_target_pairs={{4,0},{8,4},{12,8},{16,12},{20,16},{24,20},{28,24},{5,1},{9,5},{13... | collective-permute-start | bytes 98312 | tf_op jit(solution)/shard_map/ppermute | solution.py:33
  77.2 10.9 %collective-permute-start.14 = (f32[2,8,1,128]{3,2,1,0:T(1,128)S(1)}, f32[2,8,1,128]{3,2,1,0:T(1,128)S(1)}, u32[]{:S(2)}, u32[]{:S(2)}) collective-permute-start(f32[2,8,1,128]{3,2,1,0:T(1,128)S(1)} %get-tuple-element.66), channel_id=1, source_target_pairs={{1,0},{2,1},{3,2},{5,4},{6,5},{7,6},{9,8},{10,9},{11,10},{13,12},{... | collective-permute-start | bytes 24584 | tf_op jit(solution)/shard_map/ppermute | solution.py:33
  79.2 9.0 %collective-permute-start.13 = (f32[2,8,1,128]{3,2,1,0:T(1,128)S(1)}, f32[2,8,1,128]{3,2,1,0:T(1,128)S(1)}, u32[]{:S(2)}, u32[]{:S(2)}) collective-permute-start(f32[2,8,1,128]{3,2,1,0:T(1,128)S(1)} %get-tuple-element.65), channel_id=1, source_target_pairs={{0,1},{1,2},{2,3},{4,5},{5,6},{6,7},{8,9},{9,10},{10,11},{12,13},{... | collective-permute-start | bytes 24584 | tf_op jit(solution)/shard_map/ppermute | solution.py:33
  83.8 5.6 %collective-permute-start.12 = (f32[2,1,32,128]{3,2,1,0:T(8,128)S(1)}, f32[2,1,32,128]{3,2,1,0:T(8,128)S(1)}, u32[]{:S(2)}, u32[]{:S(2)}) collective-permute-start(f32[2,1,32,128]{3,2,1,0:T(8,128)S(1)} %get-tuple-element.63), channel_id=1, source_target_pairs={{0,4},{4,8},{8,12},{12,16},{16,20},{20,24},{24,28},{1,5},{5,9},{9,... | collective-permute-start | bytes 98312 | tf_op jit(solution)/shard_map/ppermute | solution.py:33

commit v15 on v13

--- a/solution.py
+++ b/solution.py
@@ -226,9 +226,9 @@
 
     lines = earlier_spectral_power.shape[0]
     made, first_faces = pipelined_scan(
-        totals_of, emit, lines, "beam", {1: tied_faces(cross_faces), 2: tied_faces(beam_faces)}
-    )
-    first_bordered = bordered_fields(physical_quantities, first_faces[2], first_faces[1])
+        totals_of, emit, lines, "beam", {2: tied_faces(cross_faces), 3: tied_faces(beam_faces)}
+    )
+    first_bordered = bordered_fields(physical_quantities, first_faces[3], first_faces[2])
     spectral_power = jnp.zeros(earlier_spectral_power.shape, jnp.bfloat16)
     start = 0
     for part, _, _ in made:

time: 92.8 us -> 88.4 us (0.953)
  waiting for transfers between devices: 24.3 us -> 10.4 us
  starting transfers between devices: 38.2 us -> 48.7 us
    ppermute x8, waiting for transfers between devices: 16.2 us -> 5.71 us  [pipelined_scan(): lax.ppermute(payload, axis, pairs)]
    ppermute x8, starting transfers between devices: 25.1 us -> 32.8 us  [shifted(): return lax.ppermute(block, axis, pairs)]
    ppermute x8, waiting for transfers between devices: 8.17 us -> 4.73 us  [shifted(): return lax.ppermute(block, axis, pairs)]
    ppermute x8, starting transfers between devices: 13.2 us -> 15.8 us  [pipelined_scan(): lax.ppermute(payload, axis, pairs)]
where the time goes in v15:
time: 88.4 us; the launch traced here: 87.4 us
  starting transfers between devices  48.7 us (55%)
  other arithmetic  26.4 us (30%)
  waiting for transfers between devices  10.4 us (12%)
  between operations  1.04 us (1%)
    ppermute x8, starting transfers between devices, shifted(): return lax.ppermute(block, axis, pairs)  32.8 us
    ppermute x8, starting transfers between devices, pipelined_scan(): lax.ppermute(payload, axis, pairs)  15.8 us
    reduce_sum x2, other arithmetic, totals_of(): return jnp.sum(optical_depth, axis=1)  8.66 us
    ppermute x8, waiting for transfers between devices, pipelined_scan(): lax.ppermute(payload, axis, pairs)  5.71 us
    reduce_sum x2, other arithmetic, emit(): jnp.sum(radiance * (1.0 - jnp.exp(-optical_depth)), axis=0)  5.06 us
    ppermute x8, waiting for transfers between devices, shifted(): return lax.ppermute(block, axis, pairs)  4.73 us
    another operation x2, other arithmetic, emit(): jnp.cumsum(optical_depth[:, :rows - 1], axis=1)  3.4 us
    dynamic_update_slice x1, other arithmetic, local(): lax.dynamic_update_slice_in_dim(spectral_power, part, start, axis=0)  2.38 us
  transfers between devices with their start and end apart: 16, of which 7 were waited for; matrix products, arithmetic and copies ran while one was open for 14% of the time, Pallas kernels for 0%

profile of v15, /device:TPU:9, one launch (start us, length us, event | category | flops | bytes accessed | tf_op | source)
XLA Modules:
  0.0 87.4 jit_solution(13784207516499261159)
XLA Ops:
  0.6 0.7 convert_subtract_fusion
  1.3 0.8 fusion.120
  2.1 1.1 %add_bitcast_fusion = (f32[1,8,32,128]{3,2,1,0:T(8,128)S(1)}, f32[8,32,128]{2,1,0:T(8,128)S(1)}) fusion(f32[8,32,128]{2,1,0:T(8,128)} %param.9, f32[8,32,128]{2,1,0:T(8,128)} %param.10, f32[8,32]{1,0:T(8,128)S(1)} %get-tuple-element.73), kind=kLoop, calls=%fused_computation.215 | loop fusion | flops 262144 | bytes 525312 | tf_op jit(solution)/shard_map/stack | solution.py:182
  3.2 5.9 %fusion.116 = (f32[32,32,128]{2,1,0:T(8,128)S(1)}, f32[32,8,32,128]{3,2,1,0:T(8,128)}, f32[32,8,32,128]{3,2,1,0:T(8,128)}) fusion(f32[8,32]{1,0:T(8,128)S(1)} %get-tuple-element.74, bf16[64,8,32,128]{3,2,1,0:T(8,128)(2,1)} %param.11, f32[32]{0:T(128)S(1)} %get-tuple-element.75, f32[8,32,128]{2,1,0:T(8,128)S(1)} %get-tuple-element.72, ...), kind=kLoop, calls=%fused_computation.230 | loop fusion | flops 11403264 | bytes 13239552 | tf_op jit(solution)/shard_map/reduce_sum | solution.py:203
  9.2 1.3 %collective-permute-start = (f32[16,32,128]{2,1,0:T(8,128)S(1)}, f32[16,32,128]{2,1,0:T(8,128)S(1)}, u32[]{:S(2)}, u32[]{:S(2)}) collective-permute-start(f32[16,32,128]{2,1,0:T(8,128)S(1)} %slice_select_fusion.2), channel_id=1, source_target_pairs={{0,4},{4,0},{8,12},{12,8},{16,20},{20,16},{24,28},{28,24},{1,5},{5... | collective-permute-start | bytes 786440 | tf_op jit(solution)/shard_map/ppermute | solution.py:114
  10.5 2.7 %reduce_sum.55 = f32[32,32,128]{2,1,0:T(8,128)S(1)} reduce(f32[32,8,32,128]{3,2,1,0:T(8,128)} %get-tuple-element.21, f32[]{:T(128)} %constant.18.clone.1), dimensions={1}, to_apply=%region_1.2 | reduce | flops 917504 | bytes 4718596 | tf_op jit(solution)/shard_map/reduce_sum | solution.py:203
  13.3 0.0 copy-start.2
  13.3 0.3 collective-permute-start.2
  13.6 2.8 %collective-permute-done = f32[16,32,128]{2,1,0:T(8,128)S(1)} collective-permute-done((f32[16,32,128]{2,1,0:T(8,128)S(1)}, f32[16,32,128]{2,1,0:T(8,128)S(1)}, u32[]{:S(2)}, u32[]{:S(2)}) %collective-permute-start) | collective-permute-done | bytes 262176 | tf_op jit(solution)/shard_map/ppermute | solution.py:114
  16.4 0.1 fusion.106
  16.5 0.0 copy-start
  16.5 3.5 %collective-permute-start.1 = (f32[16,32,128]{2,1,0:T(8,128)S(1)}, f32[16,32,128]{2,1,0:T(8,128)S(1)}, u32[]{:S(2)}, u32[]{:S(2)}) collective-permute-start(f32[16,32,128]{2,1,0:T(8,128)S(1)} %fusion.106), channel_id=1, source_target_pairs={{0,8},{4,12},{8,16},{12,20},{16,24},{20,28},{1,9},{5,13},{9,17},{1... | collective-permute-start | bytes 786440 | tf_op jit(solution)/shard_map/ppermute | solution.py:114
  19.9 2.5 %fusion = f32[32,7,32,128]{3,2,1,0:T(8,128)S(1)} fusion(f32[32,8,32,128]{3,2,1,0:T(8,128)} %get-tuple-element.21), kind=kOutput, calls=%fused_computation.11 | output fusion | flops 5505024 | bytes 7340032 | tf_op jit(solution)/shard_map/jit(cumsum)/reduce_window_sum | solution.py:208
  22.5 0.0 collective-permute-done.2
  22.6 1.3 %collective-permute-done.1 = f32[16,32,128]{2,1,0:T(8,128)S(1)} collective-permute-done((f32[16,32,128]{2,1,0:T(8,128)S(1)}, f32[16,32,128]{2,1,0:T(8,128)S(1)}, u32[]{:S(2)}, u32[]{:S(2)}) %collective-permute-start.1) | collective-permute-done | bytes 262176 | tf_op jit(solution)/shard_map/ppermute | solution.py:114
  23.9 4.2 %collective-permute-start.3 = (f32[16,32,128]{2,1,0:T(8,128)S(1)}, f32[16,32,128]{2,1,0:T(8,128)S(1)}, u32[]{:S(2)}, u32[]{:S(2)}) collective-permute-start(f32[16,32,128]{2,1,0:T(8,128)S(1)} %add.212), channel_id=1, source_target_pairs={{0,16},{4,20},{8,24},{12,28},{1,17},{5,21},{9,25},{13,29},{2,18},{... | collective-permute-start | bytes 786440 | tf_op jit(solution)/shard_map/ppermute | solution.py:114
  28.1 0.1 fusion.107
  28.2 1.9 %collective-permute-start.4 = (f32[16,32,128]{2,1,0:T(8,128)S(1)}, f32[16,32,128]{2,1,0:T(8,128)S(1)}, u32[]{:S(2)}, u32[]{:S(2)}) collective-permute-start(f32[16,32,128]{2,1,0:T(8,128)S(1)} %fusion.107), channel_id=1, source_target_pairs={{0,8},{4,12},{8,16},{12,20},{16,24},{20,28},{1,9},{5,13},{9,17},{1... | collective-permute-start | bytes 786440 | tf_op jit(solution)/shard_map/ppermute | solution.py:114
  30.1 7.1 %collective-permute-start.5 = (f32[2,8,1,128]{3,2,1,0:T(1,128)S(1)}, f32[2,8,1,128]{3,2,1,0:T(1,128)S(1)}, u32[]{:S(2)}, u32[]{:S(2)}) collective-permute-start(f32[2,8,1,128]{3,2,1,0:T(1,128)S(1)} %get-tuple-element.70), channel_id=1, source_target_pairs={{0,1},{1,2},{2,3},{4,5},{5,6},{6,7},{8,9},{9,10},{10,11},{12,13},{... | collective-permute-start | bytes 24584 | tf_op jit(solution)/shard_map/ppermute | solution.py:33
  37.3 1.9 %collective-permute-start.6 = (f32[2,8,1,128]{3,2,1,0:T(1,128)S(1)}, f32[2,8,1,128]{3,2,1,0:T(1,128)S(1)}, u32[]{:S(2)}, u32[]{:S(2)}) collective-permute-start(f32[2,8,1,128]{3,2,1,0:T(1,128)S(1)} %get-tuple-element.69), channel_id=1, source_target_pairs={{1,0},{2,1},{3,2},{5,4},{6,5},{7,6},{9,8},{10,9},{11,10},{13,12},{... | collective-permute-start | bytes 24584 | tf_op jit(solution)/shard_map/ppermute | solution.py:33
  39.2 0.0 copy-start.5
  39.2 0.9 fusion.2
  40.1 0.0 copy-start.4
  40.1 0.0 collective-permute-done.5
  40.1 2.1 %collective-permute-done.6 = f32[2,8,1,128]{3,2,1,0:T(1,128)S(1)} collective-permute-done((f32[2,8,1,128]{3,2,1,0:T(1,128)S(1)}, f32[2,8,1,128]{3,2,1,0:T(1,128)S(1)}, u32[]{:S(2)}, u32[]{:S(2)}) %collective-permute-start.6) | collective-permute-done | bytes 8224 | tf_op jit(solution)/shard_map/ppermute | solution.py:33
  42.2 0.0 collective-permute-done.3
  42.3 1.6 %collective-permute-done.4 = f32[16,32,128]{2,1,0:T(8,128)S(1)} collective-permute-done((f32[16,32,128]{2,1,0:T(8,128)S(1)}, f32[16,32,128]{2,1,0:T(8,128)S(1)}, u32[]{:S(2)}, u32[]{:S(2)}) %collective-permute-start.4) | collective-permute-done | bytes 262176 | tf_op jit(solution)/shard_map/ppermute | solution.py:114
  43.8 0.1 fusion.115
  43.9 0.1 add_select_fusion.1
  43.9 0.0 copy-start.1
  44.0 1.3 %collective-permute-start.7 = (f32[16,32,128]{2,1,0:T(8,128)S(1)}, f32[16,32,128]{2,1,0:T(8,128)S(1)}, u32[]{:S(2)}, u32[]{:S(2)}) collective-permute-start(f32[16,32,128]{2,1,0:T(8,128)S(1)} %add_select_fusion.1), channel_id=1, source_target_pairs={{0,4},{4,0},{8,12},{12,8},{16,20},{20,16},{24,28},{28,24},{1,5},{5... | collective-permute-start | bytes 786440 | tf_op jit(solution)/shard_map/ppermute | solution.py:114
  45.3 1.3 %collective-permute-start.8 = (f32[16,32,128]{2,1,0:T(8,128)S(1)}, f32[16,32,128]{2,1,0:T(8,128)S(1)}, u32[]{:S(2)}, u32[]{:S(2)}) collective-permute-start(f32[16,32,128]{2,1,0:T(8,128)S(1)} %add.216), channel_id=1, source_target_pairs={{0,16},{4,20},{8,24},{12,28},{1,17},{5,21},{9,25},{13,29},{2,18},{... | collective-permute-start | bytes 786440 | tf_op jit(solution)/shard_map/ppermute | solution.py:114
  46.6 2.4 %collective-permute-start.9 = (f32[2,1,32,128]{3,2,1,0:T(8,128)S(1)}, f32[2,1,32,128]{3,2,1,0:T(8,128)S(1)}, u32[]{:S(2)}, u32[]{:S(2)}) collective-permute-start(f32[2,1,32,128]{3,2,1,0:T(8,128)S(1)} %get-tuple-element.68), channel_id=1, source_target_pairs={{0,4},{4,8},{8,12},{12,16},{16,20},{20,24},{24,28},{1,5},{5,9},{9,... | collective-permute-start | bytes 98312 | tf_op jit(solution)/shard_map/ppermute | solution.py:33
  49.0 5.6 %collective-permute-start.10 = (f32[2,1,32,128]{3,2,1,0:T(8,128)S(1)}, f32[2,1,32,128]{3,2,1,0:T(8,128)S(1)}, u32[]{:S(2)}, u32[]{:S(2)}) collective-permute-start(f32[2,1,32,128]{3,2,1,0:T(8,128)S(1)} %get-tuple-element.67), channel_id=1, source_target_pairs={{4,0},{8,4},{12,8},{16,12},{20,16},{24,20},{28,24},{5,1},{9,5},{13... | collective-permute-start | bytes 98312 | tf_op jit(solution)/shard_map/ppermute | solution.py:33
  54.7 0.8 collective-permute-done.9
  55.5 0.2 collective-permute-done.10
  55.7 0.0 collective-permute-done.7
  55.7 0.0 collective-permute-done.8
  55.7 0.1 fusion.114
  55.7 0.1 add_select_fusion
  55.8 2.0 %collective-permute-start.11 = (f32[16,32,128]{2,1,0:T(8,128)S(1)}, f32[16,32,128]{2,1,0:T(8,128)S(1)}, u32[]{:S(2)}, u32[]{:S(2)}) collective-permute-start(f32[16,32,128]{2,1,0:T(8,128)S(1)} %add_select_fusion), channel_id=1, source_target_pairs={{0,4},{4,0},{8,12},{12,8},{16,20},{20,16},{24,28},{28,24},{1,5},{5... | collective-permute-start | bytes 786440 | tf_op jit(solution)/shard_map/ppermute | solution.py:114
  57.8 0.1 fusion.7
  57.9 0.5 power_multiply_fusion.2
  58.5 0.2 fusion.117
  58.7 2.4 %multiply_reduce_fusion.2 = (f32[8,32,128]{2,1,0:T(8,128)S(1)}, f32[8,32,128]{2,1,0:T(8,128)S(1)}, bf16[32,8,32,128]{3,2,1,0:T(8,128)(2,1)S(1)}) fusion(f32[32,8,32,128]{3,2,1,0:T(8,128)S(1)} %copy-done, f32[32,7,32,128]{3,2,1,0:T(8,128)S(1)} %fusion.2, f32[32,32,128]{2,1,0:T(8,128)S(1)} %get-tuple-element.77, f32[32,32,128]{2,1,0:T(8,128)S(1)} %get-tuple-element.54, ...), kind=kLoop, calls=%fused_computation.4 | loop fusion | flops 13565952 | bytes 13369472 | tf_op jit(solution)/shard_map/reduce_sum | solution.py:215
  61.1 0.6 fusion.20
  61.7 0.0 collective-permute-done.11
  61.7 0.1 maximum_select_fusion.1
  61.8 0.0 copy-start.3
  61.8 2.7 %multiply_reduce_fusion = (f32[8,32,128]{2,1,0:T(8,128)S(1)}, f32[8,32,128]{2,1,0:T(8,128)S(1)}, bf16[32,8,32,128]{3,2,1,0:T(8,128)(2,1)S(1)}) fusion(f32[32,7,32,128]{3,2,1,0:T(8,128)S(1)} %fusion, f32[32,32,128]{2,1,0:T(8,128)S(1)} %maximum_select_fusion.1, f32[32,32,128]{2,1,0:T(8,128)S(1)} %get-tuple-element.53, f32[8,32]{1,0:T(8,128)S(1)} %get-tuple-element.74, ...), kind=kLoop, calls=%fused_computation.1 | loop fusion | flops 15663104 | bytes 9307264 | tf_op jit(solution)/shard_map/reduce_sum | solution.py:215
  64.5 0.8 broadcast_multiply_fusion
  65.3 0.1 fusion.113
  65.5 4.1 %collective-permute-start.15 = (f32[2,1,32,128]{3,2,1,0:T(8,128)S(1)}, f32[2,1,32,128]{3,2,1,0:T(8,128)S(1)}, u32[]{:S(2)}, u32[]{:S(2)}) collective-permute-start(f32[2,1,32,128]{3,2,1,0:T(8,128)S(1)} %get-tuple-element.64), channel_id=1, source_target_pairs={{4,0},{8,4},{12,8},{16,12},{20,16},{24,20},{28,24},{5,1},{9,5},{13... | collective-permute-start | bytes 98312 | tf_op jit(solution)/shard_map/ppermute | solution.py:33
  69.6 6.7 %collective-permute-start.14 = (f32[2,8,1,128]{3,2,1,0:T(1,128)S(1)}, f32[2,8,1,128]{3,2,1,0:T(1,128)S(1)}, u32[]{:S(2)}, u32[]{:S(2)}) collective-permute-start(f32[2,8,1,128]{3,2,1,0:T(1,128)S(1)} %get-tuple-element.66), channel_id=1, source_target_pairs={{1,0},{2,1},{3,2},{5,4},{6,5},{7,6},{9,8},{10,9},{11,10},{13,12},{... | collective-permute-start | bytes 24584 | tf_op jit(solution)/shard_map/ppermute | solution.py:33
  76.3 3.0 %collective-permute-start.13 = (f32[2,8,1,128]{3,2,1,0:T(1,128)S(1)}, f32[2,8,1,128]{3,2,1,0:T(1,128)S(1)}, u32[]{:S(2)}, u32[]{:S(2)}) collective-permute-start(f32[2,8,1,128]{3,2,1,0:T(1,128)S(1)} %get-tuple-element.65), channel_id=1, source_target_pairs={{0,1},{1,2},{2,3},{4,5},{5,6},{6,7},{8,9},{9,10},{10,11},{12,13},{... | collective-permute-start | bytes 24584 | tf_op jit(solution)/shard_map/ppermute | solution.py:33
  79.3 1.9 %collective-permute-start.12 = (f32[2,1,32,128]{3,2,1,0:T(8,128)S(1)}, f32[2,1,32,128]{3,2,1,0:T(8,128)S(1)}, u32[]{:S(2)}, u32[]{:S(2)}) collective-permute-start(f32[2,1,32,128]{3,2,1,0:T(8,128)S(1)} %get-tuple-element.63), channel_id=1, source_target_pairs={{0,4},{4,8},{8,12},{12,16},{16,20},{20,24},{24,28},{1,5},{5,9},{9,... | collective-permute-start | bytes 98312 | tf_op jit(solution)/shard_map/ppermute | solution.py:33
  81.3 2.4 %pad_maximum_fusion = bf16[64,8,32,128]{3,2,1,0:T(8,128)(2,1)} fusion(bf16[32,8,32,128]{3,2,1,0:T(8,128)(2,1)S(1)} %get-tuple-element.50, bf16[32,8,32,128]{3,2,1,0:T(8,128)(2,1)S(1)} %get-tuple-element.30), kind=kLoop, calls=%fused_computation | loop fusion | flops 2097152 | bytes 8388608 | tf_op jit(solution)/shard_map/dynamic_update_slice | solution.py:235
  83.6 0.0 collective-permute-done.14
  83.6 0.0 collective-permute-done.13
  83.6 0.0 collective-permute-done.15
  83.6 1.6 %collective-permute-done.12 = f32[2,1,32,128]{3,2,1,0:T(8,128)S(1)} collective-permute-done((f32[2,1,32,128]{3,2,1,0:T(8,128)S(1)}, f32[2,1,32,128]{3,2,1,0:T(8,128)S(1)}, u32[]{:S(2)}, u32[]{:S(2)}) %collective-permute-start.12) | collective-permute-done | bytes 32800 | tf_op jit(solution)/shard_map/ppermute | solution.py:33
  85.3 0.5 power_multiply_fusion
  85.9 0.7 fusion.29
  86.5 0.9 %fusion.93 = (f32[8,32,128]{2,1,0:T(8,128)}, f32[8,32,128]{2,1,0:T(8,128)}) fusion(f32[2,8,32,128]{3,2,1,0:T(8,128)S(1)} %fusion.29, f32[8,32]{1,0:T(8,128)S(1)} %get-tuple-element.73, f32[8,32,128]{2,1,0:T(8,128)S(1)} %get-tuple-element.37, f32[8,32,128]{2,1,0:T(8,128)S(1)} %get-tuple-element.38, f32[2,8,32,128]{3,2,1,0:T(8,128)S(1)} %fusion.20, ...), kind=kLoop, calls=%fused_computation.196 | loop fusion | flops 1081344 | bytes 1442816 | tf_op jit(solution)/shard_map/add | solution.py:254
  (18 shorter events, 0.3 us)
Async XLA Ops:
  9.2 7.2 %collective-permute-start = (f32[16,32,128]{2,1,0:T(8,128)S(1)}, f32[16,32,128]{2,1,0:T(8,128)S(1)}, u32[]{:S(2)}, u32[]{:S(2)}) collective-permute-start(f32[16,32,128]{2,1,0:T(8,128)S(1)} %slice_select_fusion.2), channel_id=1, source_target_pairs={{0,4},{4,0},{8,12},{12,8},{16,20},{20,16},{24,28},{28,24},{1,5},{5... | collective-permute-start | bytes 786440 | tf_op jit(solution)/shard_map/ppermute | solution.py:114
  13.3 9.2 %copy-start.2 = (f32[8,32,128]{2,1,0:T(8,128)S(1)}, f32[8,32,128]{2,1,0:T(8,128)}, u32[]{:S(2)}) copy-start(f32[8,32,128]{2,1,0:T(8,128)} %param.8) | copy-start | bytes 393220
  13.3 9.3 %collective-permute-start.2 = (f32[16,32,128]{2,1,0:T(8,128)S(1)}, f32[16,32,128]{2,1,0:T(8,128)S(1)}, u32[]{:S(2)}, u32[]{:S(2)}) collective-permute-start(f32[16,32,128]{2,1,0:T(8,128)S(1)} %slice_select_fusion.1), channel_id=1, source_target_pairs={{0,4},{4,0},{8,12},{12,8},{16,20},{20,16},{24,28},{28,24},{1,5},{5... | collective-permute-start | bytes 786440 | tf_op jit(solution)/shard_map/ppermute | solution.py:114
  16.5 22.8 %copy-start = (f32[32,8,32,128]{3,2,1,0:T(8,128)S(1)}, f32[32,8,32,128]{3,2,1,0:T(8,128)}, u32[]{:S(2)}) copy-start(f32[32,8,32,128]{3,2,1,0:T(8,128)} %get-tuple-element.49) | copy-start | bytes 12582916
  16.5 7.4 %collective-permute-start.1 = (f32[16,32,128]{2,1,0:T(8,128)S(1)}, f32[16,32,128]{2,1,0:T(8,128)S(1)}, u32[]{:S(2)}, u32[]{:S(2)}) collective-permute-start(f32[16,32,128]{2,1,0:T(8,128)S(1)} %fusion.106), channel_id=1, source_target_pairs={{0,8},{4,12},{8,16},{12,20},{16,24},{20,28},{1,9},{5,13},{9,17},{1... | collective-permute-start | bytes 786440 | tf_op jit(solution)/shard_map/ppermute | solution.py:114
  23.9 18.4 %collective-permute-start.3 = (f32[16,32,128]{2,1,0:T(8,128)S(1)}, f32[16,32,128]{2,1,0:T(8,128)S(1)}, u32[]{:S(2)}, u32[]{:S(2)}) collective-permute-start(f32[16,32,128]{2,1,0:T(8,128)S(1)} %add.212), channel_id=1, source_target_pairs={{0,16},{4,20},{8,24},{12,28},{1,17},{5,21},{9,25},{13,29},{2,18},{... | collective-permute-start | bytes 786440 | tf_op jit(solution)/shard_map/ppermute | solution.py:114
  28.2 15.6 %collective-permute-start.4 = (f32[16,32,128]{2,1,0:T(8,128)S(1)}, f32[16,32,128]{2,1,0:T(8,128)S(1)}, u32[]{:S(2)}, u32[]{:S(2)}) collective-permute-start(f32[16,32,128]{2,1,0:T(8,128)S(1)} %fusion.107), channel_id=1, source_target_pairs={{0,8},{4,12},{8,16},{12,20},{16,24},{20,28},{1,9},{5,13},{9,17},{1... | collective-permute-start | bytes 786440 | tf_op jit(solution)/shard_map/ppermute | solution.py:114
  30.1 10.0 %collective-permute-start.5 = (f32[2,8,1,128]{3,2,1,0:T(1,128)S(1)}, f32[2,8,1,128]{3,2,1,0:T(1,128)S(1)}, u32[]{:S(2)}, u32[]{:S(2)}) collective-permute-start(f32[2,8,1,128]{3,2,1,0:T(1,128)S(1)} %get-tuple-element.70), channel_id=1, source_target_pairs={{0,1},{1,2},{2,3},{4,5},{5,6},{6,7},{8,9},{9,10},{10,11},{12,13},{... | collective-permute-start | bytes 24584 | tf_op jit(solution)/shard_map/ppermute | solution.py:33
  37.3 5.0 %collective-permute-start.6 = (f32[2,8,1,128]{3,2,1,0:T(1,128)S(1)}, f32[2,8,1,128]{3,2,1,0:T(1,128)S(1)}, u32[]{:S(2)}, u32[]{:S(2)}) collective-permute-start(f32[2,8,1,128]{3,2,1,0:T(1,128)S(1)} %get-tuple-element.69), channel_id=1, source_target_pairs={{1,0},{2,1},{3,2},{5,4},{6,5},{7,6},{9,8},{10,9},{11,10},{13,12},{... | collective-permute-start | bytes 24584 | tf_op jit(solution)/shard_map/ppermute | solution.py:33
  39.2 15.5 %copy-start.5 = (f32[32,128]{1,0:T(8,128)S(1)}, f32[32,128]{1,0:T(8,128)}, u32[]{:S(2)}) copy-start(f32[32,128]{1,0:T(8,128)} %param.14) | copy-start | bytes 49156
  40.1 18.4 %copy-start.4 = (f32[64,32,128]{2,1,0:T(8,128)S(1)}, f32[64,32,128]{2,1,0:T(8,128)}, u32[]{:S(2)}) copy-start(f32[64,32,128]{2,1,0:T(8,128)} %param.12) | copy-start | bytes 3145732
  43.9 14.7 %copy-start.1 = (bf16[64,8,32,128]{3,2,1,0:T(8,128)(2,1)S(1)}, bf16[64,8,32,128]{3,2,1,0:T(8,128)(2,1)}, u32[]{:S(2)}) copy-start(bf16[64,8,32,128]{3,2,1,0:T(8,128)(2,1)} %param.11) | copy-start | bytes 12582916
  44.0 11.7 %collective-permute-start.7 = (f32[16,32,128]{2,1,0:T(8,128)S(1)}, f32[16,32,128]{2,1,0:T(8,128)S(1)}, u32[]{:S(2)}, u32[]{:S(2)}) collective-permute-start(f32[16,32,128]{2,1,0:T(8,128)S(1)} %add_select_fusion.1), channel_id=1, source_target_pairs={{0,4},{4,0},{8,12},{12,8},{16,20},{20,16},{24,28},{28,24},{1,5},{5... | collective-permute-start | bytes 786440 | tf_op jit(solution)/shard_map/ppermute | solution.py:114
  45.3 10.4 %collective-permute-start.8 = (f32[16,32,128]{2,1,0:T(8,128)S(1)}, f32[16,32,128]{2,1,0:T(8,128)S(1)}, u32[]{:S(2)}, u32[]{:S(2)}) collective-permute-start(f32[16,32,128]{2,1,0:T(8,128)S(1)} %add.216), channel_id=1, source_target_pairs={{0,16},{4,20},{8,24},{12,28},{1,17},{5,21},{9,25},{13,29},{2,18},{... | collective-permute-start | bytes 786440 | tf_op jit(solution)/shard_map/ppermute | solution.py:114
  46.6 8.9 %collective-permute-start.9 = (f32[2,1,32,128]{3,2,1,0:T(8,128)S(1)}, f32[2,1,32,128]{3,2,1,0:T(8,128)S(1)}, u32[]{:S(2)}, u32[]{:S(2)}) collective-permute-start(f32[2,1,32,128]{3,2,1,0:T(8,128)S(1)} %get-tuple-element.68), channel_id=1, source_target_pairs={{0,4},{4,8},{8,12},{12,16},{16,20},{20,24},{24,28},{1,5},{5,9},{9,... | collective-permute-start | bytes 98312 | tf_op jit(solution)/shard_map/ppermute | solution.py:33
  49.0 6.6 %collective-permute-start.10 = (f32[2,1,32,128]{3,2,1,0:T(8,128)S(1)}, f32[2,1,32,128]{3,2,1,0:T(8,128)S(1)}, u32[]{:S(2)}, u32[]{:S(2)}) collective-permute-start(f32[2,1,32,128]{3,2,1,0:T(8,128)S(1)} %get-tuple-element.67), channel_id=1, source_target_pairs={{4,0},{8,4},{12,8},{16,12},{20,16},{24,20},{28,24},{5,1},{9,5},{13... | collective-permute-start | bytes 98312 | tf_op jit(solution)/shard_map/ppermute | solution.py:33
  55.8 5.9 %collective-permute-start.11 = (f32[16,32,128]{2,1,0:T(8,128)S(1)}, f32[16,32,128]{2,1,0:T(8,128)S(1)}, u32[]{:S(2)}, u32[]{:S(2)}) collective-permute-start(f32[16,32,128]{2,1,0:T(8,128)S(1)} %add_select_fusion), channel_id=1, source_target_pairs={{0,4},{4,0},{8,12},{12,8},{16,20},{20,16},{24,28},{28,24},{1,5},{5... | collective-permute-start | bytes 786440 | tf_op jit(solution)/shard_map/ppermute | solution.py:114
  61.8 2.7 %copy-start.3 = (f32[8,32,128]{2,1,0:T(8,128)S(1)}, f32[8,32,128]{2,1,0:T(8,128)}, u32[]{:S(2)}) copy-start(f32[8,32,128]{2,1,0:T(8,128)} %param.9) | copy-start | bytes 393220
  65.5 18.2 %collective-permute-start.15 = (f32[2,1,32,128]{3,2,1,0:T(8,128)S(1)}, f32[2,1,32,128]{3,2,1,0:T(8,128)S(1)}, u32[]{:S(2)}, u32[]{:S(2)}) collective-permute-start(f32[2,1,32,128]{3,2,1,0:T(8,128)S(1)} %get-tuple-element.64), channel_id=1, source_target_pairs={{4,0},{8,4},{12,8},{16,12},{20,16},{24,20},{28,24},{5,1},{9,5},{13... | collective-permute-start | bytes 98312 | tf_op jit(solution)/shard_map/ppermute | solution.py:33
  69.6 14.0 %collective-permute-start.14 = (f32[2,8,1,128]{3,2,1,0:T(1,128)S(1)}, f32[2,8,1,128]{3,2,1,0:T(1,128)S(1)}, u32[]{:S(2)}, u32[]{:S(2)}) collective-permute-start(f32[2,8,1,128]{3,2,1,0:T(1,128)S(1)} %get-tuple-element.66), channel_id=1, source_target_pairs={{1,0},{2,1},{3,2},{5,4},{6,5},{7,6},{9,8},{10,9},{11,10},{13,12},{... | collective-permute-start | bytes 24584 | tf_op jit(solution)/shard_map/ppermute | solution.py:33
  76.3 7.3 %collective-permute-start.13 = (f32[2,8,1,128]{3,2,1,0:T(1,128)S(1)}, f32[2,8,1,128]{3,2,1,0:T(1,128)S(1)}, u32[]{:S(2)}, u32[]{:S(2)}) collective-permute-start(f32[2,8,1,128]{3,2,1,0:T(1,128)S(1)} %get-tuple-element.65), channel_id=1, source_target_pairs={{0,1},{1,2},{2,3},{4,5},{5,6},{6,7},{8,9},{9,10},{10,11},{12,13},{... | collective-permute-start | bytes 24584 | tf_op jit(solution)/shard_map/ppermute | solution.py:33
  79.3 5.9 %collective-permute-start.12 = (f32[2,1,32,128]{3,2,1,0:T(8,128)S(1)}, f32[2,1,32,128]{3,2,1,0:T(8,128)S(1)}, u32[]{:S(2)}, u32[]{:S(2)}) collective-permute-start(f32[2,1,32,128]{3,2,1,0:T(8,128)S(1)} %get-tuple-element.63), channel_id=1, source_target_pairs={{0,4},{4,8},{8,12},{12,16},{16,20},{20,24},{24,28},{1,5},{5,9},{9,... | collective-permute-start | bytes 98312 | tf_op jit(solution)/shard_map/ppermute | solution.py:33

commit v16 on v15

--- a/solution.py
+++ b/solution.py
@@ -230,10 +230,10 @@
     )
     first_bordered = bordered_fields(physical_quantities, first_faces[3], first_faces[2])
     spectral_power = jnp.zeros(earlier_spectral_power.shape, jnp.bfloat16)
-    start = 0
+    start = jnp.minimum(lax.axis_index("beam"), 0)
     for part, _, _ in made:
         spectral_power = lax.dynamic_update_slice_in_dim(spectral_power, part, start, axis=0)
-        start += part.shape[0]
+        start = start + part.shape[0]
     pumping = made[0][1]
     heating = made[0][2]
     for _, part_pumping, part_heating in made[1:]:

time: 88.4 us -> 96 us (1.086)
  other arithmetic: 26.4 us -> 34.3 us
  local copies, waits for them, and re-layouts: 0.86 us -> 3.77 us
  waiting for transfers between devices: 10.4 us -> 7.66 us
  starting transfers between devices: 48.7 us -> 47.4 us
    another operation x2, other arithmetic: 3.4 us -> 6.8 us  [emit(): jnp.cumsum(optical_depth[:, :rows - 1], axis=1)]
    ppermute x8, starting transfers between devices: 32.8 us -> 30.6 us  [shifted(): return lax.ppermute(block, axis, pairs)]
    reduce_sum x2, other arithmetic: 5.06 us -> 6.87 us  [emit(): jnp.sum(radiance * (1.0 - jnp.exp(-optical_depth)), axis=0)]
    ppermute x8, waiting for transfers between devices: 4.73 us -> 3.18 us  [shifted(): return lax.ppermute(block, axis, pairs)]
    ppermute x8, waiting for transfers between devices: 5.71 us -> 4.47 us  [pipelined_scan(): lax.ppermute(payload, axis, pairs)]
    dynamic_update_slice x1, other arithmetic: 2.38 us -> 1.17 us  [local(): lax.dynamic_update_slice_in_dim(spectral_power, part, start, axis=0)]
    broadcast_in_dim x0 -> x1, local copies, waits for them, and re-layouts: none -> 1 us  [local(): spectral_power = jnp.zeros(earlier_spectral_power.shape, jnp.bfloat16)]
    ppermute x8, starting transfers between devices: 15.8 us -> 16.8 us  [pipelined_scan(): lax.ppermute(payload, axis, pairs)]
  transfers between devices with their start and end apart: 16 -> 16, of which waited for: 7 -> 4; matrix products, arithmetic and copies ran while one was open for 14% -> 22% of each run, Pallas kernels for 0% -> 0%
where the time goes in v16:
time: 96 us; the launch traced here: 94.4 us
  starting transfers between devices  47.4 us (49%)
  other arithmetic  34.3 us (36%)
  waiting for transfers between devices  7.66 us (8%)
  local copies, waits for them, and re-layouts  3.77 us (4%)
  between operations  1.27 us (1%)
    ppermute x8, starting transfers between devices, shifted(): return lax.ppermute(block, axis, pairs)  30.6 us
    ppermute x8, starting transfers between devices, pipelined_scan(): lax.ppermute(payload, axis, pairs)  16.8 us
    reduce_sum x2, other arithmetic, totals_of(): return jnp.sum(optical_depth, axis=1)  8.67 us
    reduce_sum x2, other arithmetic, emit(): jnp.sum(radiance * (1.0 - jnp.exp(-optical_depth)), axis=0)  6.87 us
    another operation x2, other arithmetic, emit(): jnp.cumsum(optical_depth[:, :rows - 1], axis=1)  6.8 us
    ppermute x8, waiting for transfers between devices, pipelined_scan(): lax.ppermute(payload, axis, pairs)  4.47 us
    ppermute x8, waiting for transfers between devices, shifted(): return lax.ppermute(block, axis, pairs)  3.18 us
    sub x2, other arithmetic, advance(): transport = diffused - drift_speed * (center - upstream)  2.08 us
  transfers between devices with their start and end apart: 16, of which 4 were waited for; matrix products, arithmetic and copies ran while one was open for 22% of the time, Pallas kernels for 0%

profile of v16, /device:TPU:9, one launch (start us, length us, event | category | flops | bytes accessed | tf_op | source)
XLA Modules:
  0.0 94.4 jit_solution(9030709383737977569)
XLA Ops:
  0.6 0.7 convert_subtract_fusion
  1.3 0.8 fusion.121
  2.1 1.1 %add_bitcast_fusion = (f32[1,8,32,128]{3,2,1,0:T(8,128)S(1)}, f32[8,32,128]{2,1,0:T(8,128)S(1)}) fusion(f32[8,32,128]{2,1,0:T(8,128)} %param.9, f32[8,32,128]{2,1,0:T(8,128)} %param.10, f32[8,32]{1,0:T(8,128)S(1)} %get-tuple-element.72), kind=kLoop, calls=%fused_computation.215 | loop fusion | flops 262144 | bytes 525312 | tf_op jit(solution)/shard_map/stack | solution.py:182
  3.2 5.9 %fusion.117 = (f32[32,32,128]{2,1,0:T(8,128)S(1)}, f32[32,8,32,128]{3,2,1,0:T(8,128)}, f32[32,8,32,128]{3,2,1,0:T(8,128)}) fusion(f32[8,32]{1,0:T(8,128)S(1)} %get-tuple-element.73, bf16[64,8,32,128]{3,2,1,0:T(8,128)(2,1)} %param.11, f32[32]{0:T(128)S(1)} %get-tuple-element.75, f32[8,32,128]{2,1,0:T(8,128)S(1)} %get-tuple-element.71, ...), kind=kLoop, calls=%fused_computation.231 | loop fusion | flops 11403264 | bytes 13239552 | tf_op jit(solution)/shard_map/reduce_sum | solution.py:203
  9.2 1.3 %collective-permute-start = (f32[16,32,128]{2,1,0:T(8,128)S(1)}, f32[16,32,128]{2,1,0:T(8,128)S(1)}, u32[]{:S(2)}, u32[]{:S(2)}) collective-permute-start(f32[16,32,128]{2,1,0:T(8,128)S(1)} %slice_select_fusion.2), channel_id=1, source_target_pairs={{0,4},{4,0},{8,12},{12,8},{16,20},{20,16},{24,28},{28,24},{1,5},{5... | collective-permute-start | bytes 786440 | tf_op jit(solution)/shard_map/ppermute | solution.py:114
  10.5 2.7 %reduce_sum.55 = f32[32,32,128]{2,1,0:T(8,128)S(1)} reduce(f32[32,8,32,128]{3,2,1,0:T(8,128)} %get-tuple-element.21, f32[]{:T(128)} %constant.56.clone.1), dimensions={1}, to_apply=%region_1.2 | reduce | flops 917504 | bytes 4718596 | tf_op jit(solution)/shard_map/reduce_sum | solution.py:203
  13.3 0.0 copy-start.5
  13.3 0.3 collective-permute-start.2
  13.6 2.8 %collective-permute-done = f32[16,32,128]{2,1,0:T(8,128)S(1)} collective-permute-done((f32[16,32,128]{2,1,0:T(8,128)S(1)}, f32[16,32,128]{2,1,0:T(8,128)S(1)}, u32[]{:S(2)}, u32[]{:S(2)}) %collective-permute-start) | collective-permute-done | bytes 262176 | tf_op jit(solution)/shard_map/ppermute | solution.py:114
  16.5 0.1 fusion.107
  16.5 0.0 copy-start
  16.5 3.5 %collective-permute-start.1 = (f32[16,32,128]{2,1,0:T(8,128)S(1)}, f32[16,32,128]{2,1,0:T(8,128)S(1)}, u32[]{:S(2)}, u32[]{:S(2)}) collective-permute-start(f32[16,32,128]{2,1,0:T(8,128)S(1)} %fusion.107), channel_id=1, source_target_pairs={{0,8},{4,12},{8,16},{12,20},{16,24},{20,28},{1,9},{5,13},{9,17},{1... | collective-permute-start | bytes 786440 | tf_op jit(solution)/shard_map/ppermute | solution.py:114
  20.0 4.5 %fusion = f32[32,7,32,128]{3,2,1,0:T(8,128)} fusion(f32[32,8,32,128]{3,2,1,0:T(8,128)} %get-tuple-element.21), kind=kOutput, calls=%fused_computation.10 | output fusion | flops 5505024 | bytes 7340032 | tf_op jit(solution)/shard_map/jit(cumsum)/reduce_window_sum | solution.py:208
  24.5 0.0 collective-permute-done.2
  24.6 0.0 collective-permute-done.1
  24.6 0.1 fusion.108
  24.6 3.3 %collective-permute-start.4 = (f32[16,32,128]{2,1,0:T(8,128)S(1)}, f32[16,32,128]{2,1,0:T(8,128)S(1)}, u32[]{:S(2)}, u32[]{:S(2)}) collective-permute-start(f32[16,32,128]{2,1,0:T(8,128)S(1)} %fusion.108), channel_id=1, source_target_pairs={{0,8},{4,12},{8,16},{12,20},{16,24},{20,28},{1,9},{5,13},{9,17},{1... | collective-permute-start | bytes 786440 | tf_op jit(solution)/shard_map/ppermute | solution.py:114
  28.0 1.7 %collective-permute-start.3 = (f32[16,32,128]{2,1,0:T(8,128)S(1)}, f32[16,32,128]{2,1,0:T(8,128)S(1)}, u32[]{:S(2)}, u32[]{:S(2)}) collective-permute-start(f32[16,32,128]{2,1,0:T(8,128)S(1)} %add.223), channel_id=1, source_target_pairs={{0,16},{4,20},{8,24},{12,28},{1,17},{5,21},{9,25},{13,29},{2,18},{... | collective-permute-start | bytes 786440 | tf_op jit(solution)/shard_map/ppermute | solution.py:114
  29.7 7.1 %collective-permute-start.5 = (f32[2,8,1,128]{3,2,1,0:T(1,128)S(1)}, f32[2,8,1,128]{3,2,1,0:T(1,128)S(1)}, u32[]{:S(2)}, u32[]{:S(2)}) collective-permute-start(f32[2,8,1,128]{3,2,1,0:T(1,128)S(1)} %get-tuple-element.69), channel_id=1, source_target_pairs={{0,1},{1,2},{2,3},{4,5},{5,6},{6,7},{8,9},{9,10},{10,11},{12,13},{... | collective-permute-start | bytes 24584 | tf_op jit(solution)/shard_map/ppermute | solution.py:33
  36.8 1.9 %collective-permute-start.6 = (f32[2,8,1,128]{3,2,1,0:T(1,128)S(1)}, f32[2,8,1,128]{3,2,1,0:T(1,128)S(1)}, u32[]{:S(2)}, u32[]{:S(2)}) collective-permute-start(f32[2,8,1,128]{3,2,1,0:T(1,128)S(1)} %get-tuple-element.68), channel_id=1, source_target_pairs={{1,0},{2,1},{3,2},{5,4},{6,5},{7,6},{9,8},{10,9},{11,10},{13,12},{... | collective-permute-start | bytes 24584 | tf_op jit(solution)/shard_map/ppermute | solution.py:33
  38.8 0.0 copy-start.19
  38.8 2.3 %fusion.2 = f32[32,7,32,128]{3,2,1,0:T(8,128)} fusion(f32[32,8,32,128]{3,2,1,0:T(8,128)S(1)} %copy-done), kind=kOutput, calls=%fused_computation.12 | output fusion | flops 5505024 | bytes 7340032 | tf_op jit(solution)/shard_map/jit(cumsum)/reduce_window_sum | solution.py:208
  41.1 0.7 collective-permute-done.6
  41.8 0.0 collective-permute-done.4
  41.8 0.0 collective-permute-done.3
  41.8 0.1 fusion.116
  41.9 0.8 add_select_fusion.1
  42.7 1.2 %collective-permute-start.7 = (f32[16,32,128]{2,1,0:T(8,128)}, f32[16,32,128]{2,1,0:T(8,128)S(1)}, u32[]{:S(2)}, u32[]{:S(2)}) collective-permute-start(f32[16,32,128]{2,1,0:T(8,128)} %add_select_fusion.1), channel_id=1, source_target_pairs={{0,4},{4,0},{8,12},{12,8},{16,20},{20,16},{24,28},{28,24},{1,5},{5... | collective-permute-start | bytes 786440 | tf_op jit(solution)/shard_map/ppermute | solution.py:114
  43.9 0.7 add.227
  44.6 4.5 %collective-permute-start.8 = (f32[16,32,128]{2,1,0:T(8,128)}, f32[16,32,128]{2,1,0:T(8,128)S(1)}, u32[]{:S(2)}, u32[]{:S(2)}) collective-permute-start(f32[16,32,128]{2,1,0:T(8,128)} %add.227), channel_id=1, source_target_pairs={{0,16},{4,20},{8,24},{12,28},{1,17},{5,21},{9,25},{13,29},{2,18},{... | collective-permute-start | bytes 786440 | tf_op jit(solution)/shard_map/ppermute | solution.py:114
  49.2 0.6 fusion.119
  49.8 1.9 %collective-permute-start.10 = (f32[2,1,32,128]{3,2,1,0:T(8,128)}, f32[2,1,32,128]{3,2,1,0:T(8,128)}, u32[]{:S(2)}, u32[]{:S(2)}) collective-permute-start(f32[2,1,32,128]{3,2,1,0:T(8,128)} %get-tuple-element.66), channel_id=1, source_target_pairs={{4,0},{8,4},{12,8},{16,12},{20,16},{24,20},{28,24},{5,1},{9,5},{13... | collective-permute-start | bytes 98312 | tf_op jit(solution)/shard_map/ppermute | solution.py:33
  51.7 3.4 %collective-permute-start.9 = (f32[2,1,32,128]{3,2,1,0:T(8,128)}, f32[2,1,32,128]{3,2,1,0:T(8,128)}, u32[]{:S(2)}, u32[]{:S(2)}) collective-permute-start(f32[2,1,32,128]{3,2,1,0:T(8,128)} %get-tuple-element.67), channel_id=1, source_target_pairs={{0,4},{4,8},{8,12},{12,16},{16,20},{20,24},{24,28},{1,5},{5,9},{9,... | collective-permute-start | bytes 98312 | tf_op jit(solution)/shard_map/ppermute | solution.py:33
  55.1 0.0 copy-start.1
  55.2 2.4 %collective-permute-done.9 = f32[2,1,32,128]{3,2,1,0:T(8,128)} collective-permute-done((f32[2,1,32,128]{3,2,1,0:T(8,128)}, f32[2,1,32,128]{3,2,1,0:T(8,128)}, u32[]{:S(2)}, u32[]{:S(2)}) %collective-permute-start.9) | collective-permute-done | bytes 32800 | tf_op jit(solution)/shard_map/ppermute | solution.py:33
  57.6 1.6 %collective-permute-done.8 = f32[16,32,128]{2,1,0:T(8,128)S(1)} collective-permute-done((f32[16,32,128]{2,1,0:T(8,128)}, f32[16,32,128]{2,1,0:T(8,128)S(1)}, u32[]{:S(2)}, u32[]{:S(2)}) %collective-permute-start.8) | collective-permute-done | bytes 262176 | tf_op jit(solution)/shard_map/ppermute | solution.py:114
  59.2 0.7 copy-done.10
  60.0 1.0 %fusion.115 = (f32[16,32,128]{2,1,0:T(8,128)S(1)}, f32[16,32,128]{2,1,0:T(8,128)S(1)}) fusion(f32[16,32,128]{2,1,0:T(8,128)S(1)} %collective-permute-done.2, f32[16,32,128]{2,1,0:T(8,128)S(1)} %collective-permute-done.4, f32[16,32,128]{2,1,0:T(8,128)} %copy-done.10), kind=kLoop, calls=%fused_computation.229 | loop fusion | flops 131072 | bytes 1310720 | tf_op jit(solution)/shard_map/add | solution.py:94
  61.0 0.1 add_select_fusion
  61.0 1.0 %collective-permute-start.11 = (f32[16,32,128]{2,1,0:T(8,128)S(1)}, f32[16,32,128]{2,1,0:T(8,128)S(1)}, u32[]{:S(2)}, u32[]{:S(2)}) collective-permute-start(f32[16,32,128]{2,1,0:T(8,128)S(1)} %add_select_fusion), channel_id=1, source_target_pairs={{0,4},{4,0},{8,12},{12,8},{16,20},{20,16},{24,28},{28,24},{1,5},{5... | collective-permute-start | bytes 786440 | tf_op jit(solution)/shard_map/ppermute | solution.py:114
  62.0 0.9 fusion.8
  62.9 0.5 power_multiply_fusion.2
  63.5 0.2 fusion.118
  63.7 0.0 copy-start.18
  63.7 0.0 copy-start.3
  63.7 4.3 %multiply_reduce_fusion.2 = (f32[8,32,128]{2,1,0:T(8,128)S(1)}, f32[8,32,128]{2,1,0:T(8,128)S(1)}, bf16[32,8,32,128]{3,2,1,0:T(8,128)(2,1)S(1)}) fusion(f32[32,8,32,128]{3,2,1,0:T(8,128)S(1)} %copy-done.1, f32[32,7,32,128]{3,2,1,0:T(8,128)} %fusion.2, f32[32,32,128]{2,1,0:T(8,128)S(1)} %get-tuple-element.76, f32[32,32,128]{2,1,0:T(8,128)S(1)} %get-tuple-element.53, ...), kind=kLoop, calls=%fused_computation.3 | loop fusion | flops 13565952 | bytes 13369472 | tf_op jit(solution)/shard_map/reduce_sum | solution.py:215
  68.1 1.4 %fusion.21 = f32[2,8,32,128]{3,2,1,0:T(8,128)S(1)} fusion(f32[2,1,1,128]{3,2,1,0:T(1,128)S(1)} %broadcast.79, f32[2,10,34,128]{3,2,1,0:T(8,128)S(1)} %fusion.8, f32[1,10,34,130]{3,2,1,0:T(8,128)S(1)} %get-tuple-element.59, f32[1,10,34,130]{3,2,1,0:T(8,128)S(1)} %get-tuple-element.58, f32[2,8,1,128]{3,2,1,0:T(1,128)S(1)} %copy-done.16, ...), kind=kLoop, calls=%fused_computation.94 | loop fusion | flops 3670016 | bytes 1325376 | tf_op jit(solution)/shard_map/sub | solution.py:159
  69.5 0.0 copy-start.6
  69.6 0.1 maximum_select_fusion.1
  69.7 2.5 %multiply_reduce_fusion = (f32[8,32,128]{2,1,0:T(8,128)S(1)}, f32[8,32,128]{2,1,0:T(8,128)S(1)}) fusion(f32[32,7,32,128]{3,2,1,0:T(8,128)S(1)} %copy-done.2, f32[32,32,128]{2,1,0:T(8,128)S(1)} %maximum_select_fusion.1, f32[32,32,128]{2,1,0:T(8,128)S(1)} %get-tuple-element.52, f32[8,32]{1,0:T(8,128)S(1)} %copy-done.14, ...), kind=kLoop, calls=%fused_computation | loop fusion | flops 14614528 | bytes 7210112 | tf_op jit(solution)/shard_map/reduce_sum | solution.py:215
  72.2 0.8 broadcast_multiply_fusion
  73.0 0.2 fusion.114
  73.2 8.0 %collective-permute-start.13 = (f32[2,8,1,128]{3,2,1,0:T(1,128)S(1)}, f32[2,8,1,128]{3,2,1,0:T(1,128)S(1)}, u32[]{:S(2)}, u32[]{:S(2)}) collective-permute-start(f32[2,8,1,128]{3,2,1,0:T(1,128)S(1)} %get-tuple-element.64), channel_id=1, source_target_pairs={{0,1},{1,2},{2,3},{4,5},{5,6},{6,7},{8,9},{9,10},{10,11},{12,13},{... | collective-permute-start | bytes 24584 | tf_op jit(solution)/shard_map/ppermute | solution.py:33
  81.2 1.9 %collective-permute-start.14 = (f32[2,8,1,128]{3,2,1,0:T(1,128)S(1)}, f32[2,8,1,128]{3,2,1,0:T(1,128)S(1)}, u32[]{:S(2)}, u32[]{:S(2)}) collective-permute-start(f32[2,8,1,128]{3,2,1,0:T(1,128)S(1)} %get-tuple-element.65), channel_id=1, source_target_pairs={{1,0},{2,1},{3,2},{5,4},{6,5},{7,6},{9,8},{10,9},{11,10},{13,12},{... | collective-permute-start | bytes 24584 | tf_op jit(solution)/shard_map/ppermute | solution.py:33
  83.1 2.3 %collective-permute-start.12 = (f32[2,1,32,128]{3,2,1,0:T(8,128)S(1)}, f32[2,1,32,128]{3,2,1,0:T(8,128)S(1)}, u32[]{:S(2)}, u32[]{:S(2)}) collective-permute-start(f32[2,1,32,128]{3,2,1,0:T(8,128)S(1)} %get-tuple-element.62), channel_id=1, source_target_pairs={{0,4},{4,8},{8,12},{12,16},{16,20},{20,24},{24,28},{1,5},{5,9},{9,... | collective-permute-start | bytes 98312 | tf_op jit(solution)/shard_map/ppermute | solution.py:33
  85.4 4.0 %collective-permute-start.15 = (f32[2,1,32,128]{3,2,1,0:T(8,128)S(1)}, f32[2,1,32,128]{3,2,1,0:T(8,128)S(1)}, u32[]{:S(2)}, u32[]{:S(2)}) collective-permute-start(f32[2,1,32,128]{3,2,1,0:T(8,128)S(1)} %get-tuple-element.63), channel_id=1, source_target_pairs={{4,0},{8,4},{12,8},{16,12},{20,16},{24,20},{28,24},{5,1},{9,5},{13... | collective-permute-start | bytes 98312 | tf_op jit(solution)/shard_map/ppermute | solution.py:33
  89.5 1.0 %broadcast_in_dim.2 = bf16[64,8,32,128]{3,2,1,0:T(8,128)(2,1)S(1)} broadcast(bf16[]{:T(256)} %constant.23.clone.1), dimensions={} | broadcast | bytes 4194306 | tf_op jit(solution)/shard_map/broadcast_in_dim | solution.py:232
  90.5 0.5 constant_dynamic-update-slice_fusion
  91.0 1.2 %fusion.6 = bf16[64,8,32,128]{3,2,1,0:T(8,128)(2,1)S(1)} fusion(bf16[64,8,32,128]{3,2,1,0:T(8,128)(2,1)S(1)} %constant_dynamic-update-slice_fusion, s32[]{:T(128)S(6)} %select_n.75, f32[32,7,32,128]{3,2,1,0:T(8,128)S(1)} %copy-done.2, f32[32,32,128]{2,1,0:T(8,128)S(1)} %maximum_select_fusion.1, f32[32,32,128]{2,1,0:T(8,128)S(1)} %get-tuple-element.52), kind=kLoop, calls=%fused_computation.16 | loop fusion | flops 4194304 | bytes 6815748 | tf_op jit(solution)/shard_map/dynamic_update_slice | solution.py:235
  92.2 0.0 copy-start.4
  92.2 0.1 fusion.10
  92.3 0.5 power_multiply_fusion
  92.8 0.7 fusion.30
  93.5 0.9 fusion.94
  (56 shorter events, 0.3 us)
Async XLA Ops:
  1.3 7.8 %copy-start.11 = (f32[8,32]{1,0:T(8,128)}, f32[8,32]{1,0:T(8,128)S(1)}, u32[]{:S(2)}) copy-start(f32[8,32]{1,0:T(8,128)S(1)} %get-tuple-element.72) | copy-start | bytes 3076
  1.3 7.8 %copy-start.13 = (f32[8,32]{1,0:T(8,128)}, f32[8,32]{1,0:T(8,128)S(1)}, u32[]{:S(2)}) copy-start(f32[8,32]{1,0:T(8,128)S(1)} %get-tuple-element.73) | copy-start | bytes 3076
  2.1 7.0 %copy-start.20 = (f32[32]{0:T(128)}, f32[32]{0:T(128)S(1)}, u32[]{:S(2)}) copy-start(f32[32]{0:T(128)S(1)} %get-tuple-element.74) | copy-start | bytes 388
  2.1 7.0 %copy-start.22 = (f32[32]{0:T(128)}, f32[32]{0:T(128)S(1)}, u32[]{:S(2)}) copy-start(f32[32]{0:T(128)S(1)} %get-tuple-element.75) | copy-start | bytes 388
  9.2 7.2 %collective-permute-start = (f32[16,32,128]{2,1,0:T(8,128)S(1)}, f32[16,32,128]{2,1,0:T(8,128)S(1)}, u32[]{:S(2)}, u32[]{:S(2)}) collective-permute-start(f32[16,32,128]{2,1,0:T(8,128)S(1)} %slice_select_fusion.2), channel_id=1, source_target_pairs={{0,4},{4,0},{8,12},{12,8},{16,20},{20,16},{24,28},{28,24},{1,5},{5... | collective-permute-start | bytes 786440 | tf_op jit(solution)/shard_map/ppermute | solution.py:114
  13.3 11.2 %copy-start.5 = (f32[8,32,128]{2,1,0:T(8,128)S(1)}, f32[8,32,128]{2,1,0:T(8,128)}, u32[]{:S(2)}) copy-start(f32[8,32,128]{2,1,0:T(8,128)} %param.8) | copy-start | bytes 393220
  13.3 11.2 %collective-permute-start.2 = (f32[16,32,128]{2,1,0:T(8,128)S(1)}, f32[16,32,128]{2,1,0:T(8,128)S(1)}, u32[]{:S(2)}, u32[]{:S(2)}) collective-permute-start(f32[16,32,128]{2,1,0:T(8,128)S(1)} %slice_select_fusion.1), channel_id=1, source_target_pairs={{0,4},{4,0},{8,12},{12,8},{16,20},{20,16},{24,28},{28,24},{1,5},{5... | collective-permute-start | bytes 786440 | tf_op jit(solution)/shard_map/ppermute | solution.py:114
  16.5 8.1 %copy-start.8 = (f32[16,32,128]{2,1,0:T(8,128)}, f32[16,32,128]{2,1,0:T(8,128)S(1)}, u32[]{:S(2)}) copy-start(f32[16,32,128]{2,1,0:T(8,128)S(1)} %collective-permute-done) | copy-start | bytes 786436
  16.5 22.3 %copy-start = (f32[32,8,32,128]{3,2,1,0:T(8,128)S(1)}, f32[32,8,32,128]{3,2,1,0:T(8,128)}, u32[]{:S(2)}) copy-start(f32[32,8,32,128]{3,2,1,0:T(8,128)} %get-tuple-element.49) | copy-start | bytes 12582916
  16.5 8.0 %collective-permute-start.1 = (f32[16,32,128]{2,1,0:T(8,128)S(1)}, f32[16,32,128]{2,1,0:T(8,128)S(1)}, u32[]{:S(2)}, u32[]{:S(2)}) collective-permute-start(f32[16,32,128]{2,1,0:T(8,128)S(1)} %fusion.107), channel_id=1, source_target_pairs={{0,8},{4,12},{8,16},{12,20},{16,24},{20,28},{1,9},{5,13},{9,17},{1... | collective-permute-start | bytes 786440 | tf_op jit(solution)/shard_map/ppermute | solution.py:114
  24.6 17.2 %copy-start.9 = (f32[16,32,128]{2,1,0:T(8,128)S(1)}, f32[16,32,128]{2,1,0:T(8,128)}, u32[]{:S(2)}) copy-start(f32[16,32,128]{2,1,0:T(8,128)} %copy-done.8) | copy-start | bytes 786436
  24.6 17.2 %collective-permute-start.4 = (f32[16,32,128]{2,1,0:T(8,128)S(1)}, f32[16,32,128]{2,1,0:T(8,128)S(1)}, u32[]{:S(2)}, u32[]{:S(2)}) collective-permute-start(f32[16,32,128]{2,1,0:T(8,128)S(1)} %fusion.108), channel_id=1, source_target_pairs={{0,8},{4,12},{8,16},{12,20},{16,24},{20,28},{1,9},{5,13},{9,17},{1... | collective-permute-start | bytes 786440 | tf_op jit(solution)/shard_map/ppermute | solution.py:114
  28.0 13.8 %collective-permute-start.3 = (f32[16,32,128]{2,1,0:T(8,128)S(1)}, f32[16,32,128]{2,1,0:T(8,128)S(1)}, u32[]{:S(2)}, u32[]{:S(2)}) collective-permute-start(f32[16,32,128]{2,1,0:T(8,128)S(1)} %add.223), channel_id=1, source_target_pairs={{0,16},{4,20},{8,24},{12,28},{1,17},{5,21},{9,25},{13,29},{2,18},{... | collective-permute-start | bytes 786440 | tf_op jit(solution)/shard_map/ppermute | solution.py:114
  29.7 11.4 %collective-permute-start.5 = (f32[2,8,1,128]{3,2,1,0:T(1,128)S(1)}, f32[2,8,1,128]{3,2,1,0:T(1,128)S(1)}, u32[]{:S(2)}, u32[]{:S(2)}) collective-permute-start(f32[2,8,1,128]{3,2,1,0:T(1,128)S(1)} %get-tuple-element.69), channel_id=1, source_target_pairs={{0,1},{1,2},{2,3},{4,5},{5,6},{6,7},{8,9},{9,10},{10,11},{12,13},{... | collective-permute-start | bytes 24584 | tf_op jit(solution)/shard_map/ppermute | solution.py:33
  36.8 5.0 %collective-permute-start.6 = (f32[2,8,1,128]{3,2,1,0:T(1,128)S(1)}, f32[2,8,1,128]{3,2,1,0:T(1,128)S(1)}, u32[]{:S(2)}, u32[]{:S(2)}) collective-permute-start(f32[2,8,1,128]{3,2,1,0:T(1,128)S(1)} %get-tuple-element.68), channel_id=1, source_target_pairs={{1,0},{2,1},{3,2},{5,4},{6,5},{7,6},{9,8},{10,9},{11,10},{13,12},{... | collective-permute-start | bytes 24584 | tf_op jit(solution)/shard_map/ppermute | solution.py:33
  38.8 16.3 %copy-start.19 = (f32[32,128]{1,0:T(8,128)S(1)}, f32[32,128]{1,0:T(8,128)}, u32[]{:S(2)}) copy-start(f32[32,128]{1,0:T(8,128)} %param.14) | copy-start | bytes 49156
  41.1 22.4 %copy-start.7 = (f32[64,32,128]{2,1,0:T(8,128)S(1)}, f32[64,32,128]{2,1,0:T(8,128)}, u32[]{:S(2)}) copy-start(f32[64,32,128]{2,1,0:T(8,128)} %param.12) | copy-start | bytes 3145732
  41.1 10.7 %copy-start.15 = (f32[2,8,1,128]{3,2,1,0:T(1,128)}, f32[2,8,1,128]{3,2,1,0:T(1,128)S(1)}, u32[]{:S(2)}) copy-start(f32[2,8,1,128]{3,2,1,0:T(1,128)S(1)} %collective-permute-done.5) | copy-start | bytes 24580
  41.8 13.3 %copy-start.17 = (f32[2,8,1,128]{3,2,1,0:T(1,128)}, f32[2,8,1,128]{3,2,1,0:T(1,128)S(1)}, u32[]{:S(2)}) copy-start(f32[2,8,1,128]{3,2,1,0:T(1,128)S(1)} %collective-permute-done.6) | copy-start | bytes 24580
  42.7 17.3 %collective-permute-start.7 = (f32[16,32,128]{2,1,0:T(8,128)}, f32[16,32,128]{2,1,0:T(8,128)S(1)}, u32[]{:S(2)}, u32[]{:S(2)}) collective-permute-start(f32[16,32,128]{2,1,0:T(8,128)} %add_select_fusion.1), channel_id=1, source_target_pairs={{0,4},{4,0},{8,12},{12,8},{16,20},{20,16},{24,28},{28,24},{1,5},{5... | collective-permute-start | bytes 786440 | tf_op jit(solution)/shard_map/ppermute | solution.py:114
  44.6 14.6 %collective-permute-start.8 = (f32[16,32,128]{2,1,0:T(8,128)}, f32[16,32,128]{2,1,0:T(8,128)S(1)}, u32[]{:S(2)}, u32[]{:S(2)}) collective-permute-start(f32[16,32,128]{2,1,0:T(8,128)} %add.227), channel_id=1, source_target_pairs={{0,16},{4,20},{8,24},{12,28},{1,17},{5,21},{9,25},{13,29},{2,18},{... | collective-permute-start | bytes 786440 | tf_op jit(solution)/shard_map/ppermute | solution.py:114
  49.8 5.4 %collective-permute-start.10 = (f32[2,1,32,128]{3,2,1,0:T(8,128)}, f32[2,1,32,128]{3,2,1,0:T(8,128)}, u32[]{:S(2)}, u32[]{:S(2)}) collective-permute-start(f32[2,1,32,128]{3,2,1,0:T(8,128)} %get-tuple-element.66), channel_id=1, source_target_pairs={{4,0},{8,4},{12,8},{16,12},{20,16},{24,20},{28,24},{5,1},{9,5},{13... | collective-permute-start | bytes 98312 | tf_op jit(solution)/shard_map/ppermute | solution.py:33
  51.7 5.9 %collective-permute-start.9 = (f32[2,1,32,128]{3,2,1,0:T(8,128)}, f32[2,1,32,128]{3,2,1,0:T(8,128)}, u32[]{:S(2)}, u32[]{:S(2)}) collective-permute-start(f32[2,1,32,128]{3,2,1,0:T(8,128)} %get-tuple-element.67), channel_id=1, source_target_pairs={{0,4},{4,8},{8,12},{12,16},{16,20},{20,24},{24,28},{1,5},{5,9},{9,... | collective-permute-start | bytes 98312 | tf_op jit(solution)/shard_map/ppermute | solution.py:33
  55.1 8.5 %copy-start.1 = (f32[32,8,32,128]{3,2,1,0:T(8,128)S(1)}, f32[32,8,32,128]{3,2,1,0:T(8,128)}, u32[]{:S(2)}) copy-start(f32[32,8,32,128]{3,2,1,0:T(8,128)} %get-tuple-element.49) | copy-start | bytes 12582916
  55.2 8.5 %copy-start.23 = (f32[32]{0:T(128)S(1)}, f32[32]{0:T(128)}, u32[]{:S(2)}) copy-start(f32[32]{0:T(128)} %copy-done.22) | copy-start | bytes 388
  59.2 0.7 copy-start.10
  61.0 8.5 %collective-permute-start.11 = (f32[16,32,128]{2,1,0:T(8,128)S(1)}, f32[16,32,128]{2,1,0:T(8,128)S(1)}, u32[]{:S(2)}, u32[]{:S(2)}) collective-permute-start(f32[16,32,128]{2,1,0:T(8,128)S(1)} %add_select_fusion), channel_id=1, source_target_pairs={{0,4},{4,0},{8,12},{12,8},{16,20},{20,16},{24,28},{28,24},{1,5},{5... | collective-permute-start | bytes 786440 | tf_op jit(solution)/shard_map/ppermute | solution.py:114
  63.7 4.4 %copy-start.16 = (f32[2,8,1,128]{3,2,1,0:T(1,128)S(1)}, f32[2,8,1,128]{3,2,1,0:T(1,128)}, u32[]{:S(2)}) copy-start(f32[2,8,1,128]{3,2,1,0:T(1,128)} %copy-done.15) | copy-start | bytes 24580
  63.7 4.4 %copy-start.18 = (f32[2,8,1,128]{3,2,1,0:T(1,128)S(1)}, f32[2,8,1,128]{3,2,1,0:T(1,128)}, u32[]{:S(2)}) copy-start(f32[2,8,1,128]{3,2,1,0:T(1,128)} %copy-done.17) | copy-start | bytes 24580
  63.7 5.9 %copy-start.2 = (f32[32,7,32,128]{3,2,1,0:T(8,128)S(1)}, f32[32,7,32,128]{3,2,1,0:T(8,128)}, u32[]{:S(2)}) copy-start(f32[32,7,32,128]{3,2,1,0:T(8,128)} %fusion) | copy-start | bytes 11010052
  63.7 5.9 %copy-start.3 = (bf16[64,8,32,128]{3,2,1,0:T(8,128)(2,1)S(1)}, bf16[64,8,32,128]{3,2,1,0:T(8,128)(2,1)}, u32[]{:S(2)}) copy-start(bf16[64,8,32,128]{3,2,1,0:T(8,128)(2,1)} %param.11) | copy-start | bytes 12582916
  63.7 5.9 %copy-start.14 = (f32[8,32]{1,0:T(8,128)S(1)}, f32[8,32]{1,0:T(8,128)}, u32[]{:S(2)}) copy-start(f32[8,32]{1,0:T(8,128)} %copy-done.13) | copy-start | bytes 3076
  63.7 5.9 %copy-start.21 = (f32[32]{0:T(128)S(1)}, f32[32]{0:T(128)}, u32[]{:S(2)}) copy-start(f32[32]{0:T(128)} %copy-done.20) | copy-start | bytes 388
  69.5 2.7 %copy-start.6 = (f32[8,32,128]{2,1,0:T(8,128)S(1)}, f32[8,32,128]{2,1,0:T(8,128)}, u32[]{:S(2)}) copy-start(f32[8,32,128]{2,1,0:T(8,128)} %param.9) | copy-start | bytes 393220
  69.6 2.7 %copy-start.12 = (f32[8,32]{1,0:T(8,128)S(1)}, f32[8,32]{1,0:T(8,128)}, u32[]{:S(2)}) copy-start(f32[8,32]{1,0:T(8,128)} %copy-done.11) | copy-start | bytes 3076
  73.2 19.0 %collective-permute-start.13 = (f32[2,8,1,128]{3,2,1,0:T(1,128)S(1)}, f32[2,8,1,128]{3,2,1,0:T(1,128)S(1)}, u32[]{:S(2)}, u32[]{:S(2)}) collective-permute-start(f32[2,8,1,128]{3,2,1,0:T(1,128)S(1)} %get-tuple-element.64), channel_id=1, source_target_pairs={{0,1},{1,2},{2,3},{4,5},{5,6},{6,7},{8,9},{9,10},{10,11},{12,13},{... | collective-permute-start | bytes 24584 | tf_op jit(solution)/shard_map/ppermute | solution.py:33
  81.2 11.0 %collective-permute-start.14 = (f32[2,8,1,128]{3,2,1,0:T(1,128)S(1)}, f32[2,8,1,128]{3,2,1,0:T(1,128)S(1)}, u32[]{:S(2)}, u32[]{:S(2)}) collective-permute-start(f32[2,8,1,128]{3,2,1,0:T(1,128)S(1)} %get-tuple-element.65), channel_id=1, source_target_pairs={{1,0},{2,1},{3,2},{5,4},{6,5},{7,6},{9,8},{10,9},{11,10},{13,12},{... | collective-permute-start | bytes 24584 | tf_op jit(solution)/shard_map/ppermute | solution.py:33
  83.1 9.1 %collective-permute-start.12 = (f32[2,1,32,128]{3,2,1,0:T(8,128)S(1)}, f32[2,1,32,128]{3,2,1,0:T(8,128)S(1)}, u32[]{:S(2)}, u32[]{:S(2)}) collective-permute-start(f32[2,1,32,128]{3,2,1,0:T(8,128)S(1)} %get-tuple-element.62), channel_id=1, source_target_pairs={{0,4},{4,8},{8,12},{12,16},{16,20},{20,24},{24,28},{1,5},{5,9},{9,... | collective-permute-start | bytes 98312 | tf_op jit(solution)/shard_map/ppermute | solution.py:33
  85.4 6.8 %collective-permute-start.15 = (f32[2,1,32,128]{3,2,1,0:T(8,128)S(1)}, f32[2,1,32,128]{3,2,1,0:T(8,128)S(1)}, u32[]{:S(2)}, u32[]{:S(2)}) collective-permute-start(f32[2,1,32,128]{3,2,1,0:T(8,128)S(1)} %get-tuple-element.63), channel_id=1, source_target_pairs={{4,0},{8,4},{12,8},{16,12},{20,16},{24,20},{28,24},{5,1},{9,5},{13... | collective-permute-start | bytes 98312 | tf_op jit(solution)/shard_map/ppermute | solution.py:33
  92.2 2.2 %copy-start.4 = (bf16[64,8,32,128]{3,2,1,0:T(8,128)(2,1)}, bf16[64,8,32,128]{3,2,1,0:T(8,128)(2,1)S(1)}, u32[]{:S(2)}) copy-start(bf16[64,8,32,128]{3,2,1,0:T(8,128)(2,1)S(1)} %fusion.6) | copy-start | bytes 12582916

commit v17 on v15

--- a/solution.py
+++ b/solution.py
@@ -104,9 +104,12 @@
     if count % 2 or count <= 2 or lines % (2 * groups):
         earlier = exclusive_scan(totals_of(0, lines, None), axis)
         return [emit(0, lines, earlier)], {stage: rider(None) for stage, rider in riders.items()}
-    size = lines // groups
+    first = max(2, lines // (2 * groups) // 2 * 2)
+    sizes = [first] + [(lines - first) // (groups - 1) // 2 * 2] * (groups - 1)
+    sizes[-1] += lines - sum(sizes)
+    starts = [sum(sizes[:g]) for g in range(groups)]
     steps = [None] * groups
-    steps[0] = paired_steps(totals_of(0, size, None), axis)
+    steps[0] = paired_steps(totals_of(0, sizes[0], None), axis)
     live, made, carried, stage = {}, [], {}, 0
     while stage < groups or live:
         if stage < groups:
@@ -114,7 +117,7 @@
         arrived = {g: lax.ppermute(payload, axis, pairs) for g, (payload, pairs) in live.items()}
         if stage == 0:
             for g in range(1, groups):
-                steps[g] = paired_steps(totals_of(g * size, size, live[0][0]), axis)
+                steps[g] = paired_steps(totals_of(starts[g], sizes[g], live[0][0]), axis)
         tied = (arrived, made)
         if stage in riders:
             tied, carried[stage] = lax.optimization_barrier((tied, riders[stage](live[0][0])))
@@ -126,7 +129,7 @@
             try:
                 following[g] = steps[g].send(value)
             except StopIteration as finished:
-                made = made + [emit(g * size, size, finished.value)]
+                made = made + [emit(starts[g], sizes[g], finished.value)]
         live = following
         stage += 1
     return made, carried

time: 88.4 us -> 95.8 us (1.084)
  the two profiles are of different devices: /device:TPU:9 before, /device:TPU:14 now
where the time goes in v17:
time: 95.8 us; the launch traced here: 95.3 us
  starting transfers between devices  44.3 us (46%)
  other arithmetic  28.8 us (30%)
  waiting for transfers between devices  21 us (22%)
  between operations  1.08 us (1%)
    ppermute x8, starting transfers between devices, shifted(): return lax.ppermute(block, axis, pairs)  25.8 us
    ppermute x8, starting transfers between devices, pipelined_scan(): lax.ppermute(payload, axis, pairs)  18.5 us
    ppermute x8, waiting for transfers between devices, pipelined_scan(): lax.ppermute(payload, axis, pairs)  12.7 us
    ppermute x8, waiting for transfers between devices, shifted(): return lax.ppermute(block, axis, pairs)  8.29 us
    reduce_sum x2, other arithmetic, totals_of(): return jnp.sum(optical_depth, axis=1)  5.47 us
    reduce_sum x2, other arithmetic, emit(): jnp.sum(radiance * (1.0 - jnp.exp(-optical_depth)), axis=0)  5.13 us
    add x1, other arithmetic, depth_of(): return (absorber[None] * weight + glass_term[None], weight)  4.03 us
    another operation x2, other arithmetic, emit(): jnp.cumsum(optical_depth[:, :rows - 1], axis=1)  3.85 us
  transfers between devices with their start and end apart: 16, of which 6 were waited for; matrix products, arithmetic and copies ran while one was open for 17% of the time, Pallas kernels for 0%

profile of v17, /device:TPU:14, one launch (start us, length us, event | category | flops | bytes accessed | tf_op | source)
XLA Modules:
  0.0 95.3 jit_solution(13956457237700123816)
XLA Ops:
  0.6 0.0 copy-start.5
  0.7 0.0 copy-start
  0.7 0.8 convert_subtract_fusion
  1.5 1.3 %add_bitcast_fusion = (f32[1,8,32,128]{3,2,1,0:T(8,128)S(1)}, f32[8,32,128]{2,1,0:T(8,128)S(1)}) fusion(f32[8,32,128]{2,1,0:T(8,128)} %param.9, f32[8,32,128]{2,1,0:T(8,128)} %param.10, f32[8,32]{1,0:T(8,128)S(1)} %get-tuple-element.70), kind=kLoop, calls=%fused_computation.216 | loop fusion | flops 262144 | bytes 525312 | tf_op jit(solution)/shard_map/stack | solution.py:185
  2.8 1.8 %fusion.116 = (f32[16,32,128]{2,1,0:T(8,128)S(1)}, f32[16,8,32,128]{3,2,1,0:T(8,128)S(1)}) fusion(f32[8,32]{1,0:T(8,128)S(1)} %get-tuple-element.71, bf16[64,8,32,128]{3,2,1,0:T(8,128)(2,1)} %param.11, f32[16]{0:T(128)} %bitcast.61, f32[8,32,128]{2,1,0:T(8,128)S(1)} %get-tuple-element.69), kind=kLoop, calls=%fused_computation.230 | loop fusion | flops 3080192 | bytes 3540032 | tf_op jit(solution)/shard_map/reduce_sum | solution.py:206
  4.6 0.7 slice_select_fusion.2
  5.3 0.5 collective-permute-start
  5.8 0.1 slice.208
  5.9 4.0 %multiply_add_fusion = f32[48,8,32,128]{3,2,1,0:T(8,128)} fusion(f32[8,32]{1,0:T(8,128)S(1)} %get-tuple-element.71, f32[48]{0:T(128)S(1)} %slice.208, f32[8,32,128]{2,1,0:T(8,128)S(1)} %get-tuple-element.69, bf16[64,8,32,128]{3,2,1,0:T(8,128)(2,1)S(1)} %copy-done), kind=kLoop, calls=%fused_computation.3 | loop fusion | flops 7864320 | bytes 9569472 | tf_op jit(solution)/shard_map/add | solution.py:200
  9.9 3.6 %reduce_sum.55 = f32[48,32,128]{2,1,0:T(8,128)S(1)} reduce(f32[48,8,32,128]{3,2,1,0:T(8,128)} %multiply_add_fusion, f32[]{:T(128)} %constant.29.clone.1), dimensions={1}, to_apply=%region_1.2 | reduce | flops 1376256 | bytes 7077892 | tf_op jit(solution)/shard_map/reduce_sum | solution.py:206
  13.6 0.1 slice_select_fusion.1
  13.6 1.6 %collective-permute-start.2 = (f32[24,32,128]{2,1,0:T(8,128)S(1)}, f32[24,32,128]{2,1,0:T(8,128)S(1)}, u32[]{:S(2)}, u32[]{:S(2)}) collective-permute-start(f32[24,32,128]{2,1,0:T(8,128)S(1)} %slice_select_fusion.1), channel_id=1, source_target_pairs={{0,4},{4,0},{8,12},{12,8},{16,20},{20,16},{24,28},{28,24},{1,5},{5... | collective-permute-start | bytes 1179656 | tf_op jit(solution)/shard_map/ppermute | solution.py:117
  15.2 0.0 collective-permute-done
  15.2 0.0 copy-start.2
  15.2 3.6 %collective-permute-start.1 = (f32[8,32,128]{2,1,0:T(8,128)S(1)}, f32[8,32,128]{2,1,0:T(8,128)S(1)}, u32[]{:S(2)}, u32[]{:S(2)}) collective-permute-start(f32[8,32,128]{2,1,0:T(8,128)S(1)} %fusion.107), channel_id=1, source_target_pairs={{0,8},{4,12},{8,16},{12,20},{16,24},{20,28},{1,9},{5,13},{9,17},{1... | collective-permute-start | bytes 393224 | tf_op jit(solution)/shard_map/ppermute | solution.py:117
  18.9 3.4 %fusion = f32[48,7,32,128]{3,2,1,0:T(8,128)S(1)} fusion(f32[48,8,32,128]{3,2,1,0:T(8,128)} %multiply_add_fusion), kind=kOutput, calls=%fused_computation.5 | output fusion | flops 8257536 | bytes 11010048 | tf_op jit(solution)/shard_map/jit(cumsum)/reduce_window_sum | solution.py:211
  22.3 0.0 copy-start.4
  22.3 2.0 %collective-permute-done.2 = f32[24,32,128]{2,1,0:T(8,128)S(1)} collective-permute-done((f32[24,32,128]{2,1,0:T(8,128)S(1)}, f32[24,32,128]{2,1,0:T(8,128)S(1)}, u32[]{:S(2)}, u32[]{:S(2)}) %collective-permute-start.2) | collective-permute-done | bytes 393248 | tf_op jit(solution)/shard_map/ppermute | solution.py:117
  24.3 0.1 fusion.106
  24.4 3.5 %collective-permute-start.4 = (f32[24,32,128]{2,1,0:T(8,128)S(1)}, f32[24,32,128]{2,1,0:T(8,128)S(1)}, u32[]{:S(2)}, u32[]{:S(2)}) collective-permute-start(f32[24,32,128]{2,1,0:T(8,128)S(1)} %fusion.106), channel_id=1, source_target_pairs={{0,8},{4,12},{8,16},{12,20},{16,24},{20,28},{1,9},{5,13},{9,17},{1... | collective-permute-start | bytes 1179656 | tf_op jit(solution)/shard_map/ppermute | solution.py:117
  27.9 2.3 %collective-permute-start.3 = (f32[8,32,128]{2,1,0:T(8,128)S(1)}, f32[8,32,128]{2,1,0:T(8,128)S(1)}, u32[]{:S(2)}, u32[]{:S(2)}) collective-permute-start(f32[8,32,128]{2,1,0:T(8,128)S(1)} %add.215), channel_id=1, source_target_pairs={{0,16},{4,20},{8,24},{12,28},{1,17},{5,21},{9,25},{13,29},{2,18},{... | collective-permute-start | bytes 393224 | tf_op jit(solution)/shard_map/ppermute | solution.py:117
  30.2 1.9 %collective-permute-start.5 = (f32[2,8,1,128]{3,2,1,0:T(1,128)S(1)}, f32[2,8,1,128]{3,2,1,0:T(1,128)S(1)}, u32[]{:S(2)}, u32[]{:S(2)}) collective-permute-start(f32[2,8,1,128]{3,2,1,0:T(1,128)S(1)} %get-tuple-element.67), channel_id=1, source_target_pairs={{0,1},{1,2},{2,3},{4,5},{5,6},{6,7},{8,9},{9,10},{10,11},{12,13},{... | collective-permute-start | bytes 24584 | tf_op jit(solution)/shard_map/ppermute | solution.py:33
  32.1 3.6 %collective-permute-start.6 = (f32[2,8,1,128]{3,2,1,0:T(1,128)S(1)}, f32[2,8,1,128]{3,2,1,0:T(1,128)S(1)}, u32[]{:S(2)}, u32[]{:S(2)}) collective-permute-start(f32[2,8,1,128]{3,2,1,0:T(1,128)S(1)} %get-tuple-element.66), channel_id=1, source_target_pairs={{1,0},{2,1},{3,2},{5,4},{6,5},{7,6},{9,8},{10,9},{11,10},{13,12},{... | collective-permute-start | bytes 24584 | tf_op jit(solution)/shard_map/ppermute | solution.py:33
  35.8 0.5 fusion.3
  36.3 0.0 collective-permute-done.5
  36.3 0.8 collective-permute-done.6
  37.1 3.5 %collective-permute-done.3 = f32[8,32,128]{2,1,0:T(8,128)S(1)} collective-permute-done((f32[8,32,128]{2,1,0:T(8,128)S(1)}, f32[8,32,128]{2,1,0:T(8,128)S(1)}, u32[]{:S(2)}, u32[]{:S(2)}) %collective-permute-start.3) | collective-permute-done | bytes 131104 | tf_op jit(solution)/shard_map/ppermute | solution.py:117
  40.6 0.0 collective-permute-done.4
  40.7 0.0 copy-start.1
  40.7 0.0 slice-start
  40.7 1.6 %collective-permute-start.7 = (f32[8,32,128]{2,1,0:T(8,128)S(1)}, f32[8,32,128]{2,1,0:T(8,128)S(1)}, u32[]{:S(2)}, u32[]{:S(2)}) collective-permute-start(f32[8,32,128]{2,1,0:T(8,128)S(1)} %add_select_fusion.1), channel_id=1, source_target_pairs={{0,4},{4,0},{8,12},{12,8},{16,20},{20,16},{24,28},{28,24},{1,5},{5... | collective-permute-start | bytes 393224 | tf_op jit(solution)/shard_map/ppermute | solution.py:117
  42.3 0.1 add.219
  42.4 5.3 %collective-permute-start.8 = (f32[24,32,128]{2,1,0:T(8,128)S(1)}, f32[24,32,128]{2,1,0:T(8,128)S(1)}, u32[]{:S(2)}, u32[]{:S(2)}) collective-permute-start(f32[24,32,128]{2,1,0:T(8,128)S(1)} %add.219), channel_id=1, source_target_pairs={{0,16},{4,20},{8,24},{12,28},{1,17},{5,21},{9,25},{13,29},{2,18},{... | collective-permute-start | bytes 1179656 | tf_op jit(solution)/shard_map/ppermute | solution.py:117
  47.7 2.5 %collective-permute-start.10 = (f32[2,1,32,128]{3,2,1,0:T(8,128)S(1)}, f32[2,1,32,128]{3,2,1,0:T(8,128)S(1)}, u32[]{:S(2)}, u32[]{:S(2)}) collective-permute-start(f32[2,1,32,128]{3,2,1,0:T(8,128)S(1)} %get-tuple-element.64), channel_id=1, source_target_pairs={{4,0},{8,4},{12,8},{16,12},{20,16},{24,20},{28,24},{5,1},{9,5},{13... | collective-permute-start | bytes 98312 | tf_op jit(solution)/shard_map/ppermute | solution.py:33
  50.3 4.2 %collective-permute-start.9 = (f32[2,1,32,128]{3,2,1,0:T(8,128)S(1)}, f32[2,1,32,128]{3,2,1,0:T(8,128)S(1)}, u32[]{:S(2)}, u32[]{:S(2)}) collective-permute-start(f32[2,1,32,128]{3,2,1,0:T(8,128)S(1)} %get-tuple-element.65), channel_id=1, source_target_pairs={{0,4},{4,8},{8,12},{12,16},{16,20},{20,24},{24,28},{1,5},{5,9},{9,... | collective-permute-start | bytes 98312 | tf_op jit(solution)/shard_map/ppermute | solution.py:33
  54.5 5.0 %collective-permute-done.9 = f32[2,1,32,128]{3,2,1,0:T(8,128)S(1)} collective-permute-done((f32[2,1,32,128]{3,2,1,0:T(8,128)S(1)}, f32[2,1,32,128]{3,2,1,0:T(8,128)S(1)}, u32[]{:S(2)}, u32[]{:S(2)}) %collective-permute-start.9) | collective-permute-done | bytes 32800 | tf_op jit(solution)/shard_map/ppermute | solution.py:33
  59.5 0.0 collective-permute-done.7
  59.5 0.0 collective-permute-done.8
  59.5 0.1 fusion.114
  59.7 0.1 add_select_fusion
  59.8 0.1 collective-permute-start.11
  60.0 1.1 %multiply_reduce_fusion.2 = (f32[8,32,128]{2,1,0:T(8,128)S(1)}, f32[8,32,128]{2,1,0:T(8,128)S(1)}, bf16[16,8,32,128]{3,2,1,0:T(8,128)(2,1)S(1)}) fusion(f32[16,8,32,128]{3,2,1,0:T(8,128)S(1)} %get-tuple-element.49, f32[16,7,32,128]{3,2,1,0:T(8,128)S(1)} %fusion.3, f32[16,32,128]{2,1,0:T(8,128)S(1)} %maximum_select_fusion.1, f32[16,32,128]{2,1,0:T(8,128)S(1)} %slice-done, ...), kind=kLoop, calls=%fused_computation.9 | loop fusion | flops 6750208 | bytes 6815808 | tf_op jit(solution)/shard_map/reduce_sum | solution.py:218
  61.1 0.0 slice-start.1
  61.1 0.1 fusion.7
  61.2 0.5 power_multiply_fusion.2
  61.8 0.7 fusion.20
  62.4 7.3 %collective-permute-done.11 = f32[24,32,128]{2,1,0:T(8,128)S(1)} collective-permute-done((f32[24,32,128]{2,1,0:T(8,128)S(1)}, f32[24,32,128]{2,1,0:T(8,128)S(1)}, u32[]{:S(2)}, u32[]{:S(2)}) %collective-permute-start.11) | collective-permute-done | bytes 393248 | tf_op jit(solution)/shard_map/ppermute | solution.py:117
  69.7 0.1 maximum_select_fusion
  69.8 0.0 copy-start.3
  69.9 4.0 %multiply_reduce_fusion = (f32[8,32,128]{2,1,0:T(8,128)S(1)}, f32[8,32,128]{2,1,0:T(8,128)S(1)}, bf16[48,8,32,128]{3,2,1,0:T(8,128)(2,1)S(1)}) fusion(f32[48,7,32,128]{3,2,1,0:T(8,128)S(1)} %fusion, f32[48,32,128]{2,1,0:T(8,128)S(1)} %maximum_select_fusion, f32[48,32,128]{2,1,0:T(8,128)S(1)} %slice-done.1, f32[8,32]{1,0:T(8,128)S(1)} %get-tuple-element.71, ...), kind=kLoop, calls=%fused_computation | loop fusion | flops 23527424 | bytes 13763776 | tf_op jit(solution)/shard_map/reduce_sum | solution.py:218
  73.9 0.8 broadcast_multiply_fusion
  74.6 0.2 fusion.113
  74.8 1.9 %collective-permute-start.13 = (f32[2,8,1,128]{3,2,1,0:T(1,128)S(1)}, f32[2,8,1,128]{3,2,1,0:T(1,128)S(1)}, u32[]{:S(2)}, u32[]{:S(2)}) collective-permute-start(f32[2,8,1,128]{3,2,1,0:T(1,128)S(1)} %get-tuple-element.62), channel_id=1, source_target_pairs={{0,1},{1,2},{2,3},{4,5},{5,6},{6,7},{8,9},{9,10},{10,11},{12,13},{... | collective-permute-start | bytes 24584 | tf_op jit(solution)/shard_map/ppermute | solution.py:33
  76.8 4.4 %collective-permute-start.14 = (f32[2,8,1,128]{3,2,1,0:T(1,128)S(1)}, f32[2,8,1,128]{3,2,1,0:T(1,128)S(1)}, u32[]{:S(2)}, u32[]{:S(2)}) collective-permute-start(f32[2,8,1,128]{3,2,1,0:T(1,128)S(1)} %get-tuple-element.63), channel_id=1, source_target_pairs={{1,0},{2,1},{3,2},{5,4},{6,5},{7,6},{9,8},{10,9},{11,10},{13,12},{... | collective-permute-start | bytes 24584 | tf_op jit(solution)/shard_map/ppermute | solution.py:33
  81.1 5.3 %collective-permute-start.12 = (f32[2,1,32,128]{3,2,1,0:T(8,128)S(1)}, f32[2,1,32,128]{3,2,1,0:T(8,128)S(1)}, u32[]{:S(2)}, u32[]{:S(2)}) collective-permute-start(f32[2,1,32,128]{3,2,1,0:T(8,128)S(1)} %get-tuple-element.60), channel_id=1, source_target_pairs={{0,4},{4,8},{8,12},{12,16},{16,20},{20,24},{24,28},{1,5},{5,9},{9,... | collective-permute-start | bytes 98312 | tf_op jit(solution)/shard_map/ppermute | solution.py:33
  86.4 1.9 %collective-permute-start.15 = (f32[2,1,32,128]{3,2,1,0:T(8,128)S(1)}, f32[2,1,32,128]{3,2,1,0:T(8,128)S(1)}, u32[]{:S(2)}, u32[]{:S(2)}) collective-permute-start(f32[2,1,32,128]{3,2,1,0:T(8,128)S(1)} %get-tuple-element.61), channel_id=1, source_target_pairs={{4,0},{8,4},{12,8},{16,12},{20,16},{24,20},{28,24},{5,1},{9,5},{13... | collective-permute-start | bytes 98312 | tf_op jit(solution)/shard_map/ppermute | solution.py:33
  88.3 2.4 %pad_maximum_fusion = bf16[64,8,32,128]{3,2,1,0:T(8,128)(2,1)} fusion(bf16[48,8,32,128]{3,2,1,0:T(8,128)(2,1)S(1)} %get-tuple-element.50, bf16[16,8,32,128]{3,2,1,0:T(8,128)(2,1)S(1)} %get-tuple-element.30), kind=kLoop, calls=%fused_computation.7 | loop fusion | flops 2097152 | bytes 8388608 | tf_op jit(solution)/shard_map/dynamic_update_slice | solution.py:238
  90.7 0.0 collective-permute-done.13
  90.7 0.0 collective-permute-done.14
  90.7 2.4 %collective-permute-done.15 = f32[2,1,32,128]{3,2,1,0:T(8,128)S(1)} collective-permute-done((f32[2,1,32,128]{3,2,1,0:T(8,128)S(1)}, f32[2,1,32,128]{3,2,1,0:T(8,128)S(1)}, u32[]{:S(2)}, u32[]{:S(2)}) %collective-permute-start.15) | collective-permute-done | bytes 32800 | tf_op jit(solution)/shard_map/ppermute | solution.py:33
  93.1 0.1 fusion.9
  93.2 0.5 power_multiply_fusion
  93.7 0.7 fusion.29
  94.4 0.9 fusion.93
  (23 shorter events, 0.2 us)
Async XLA Ops:
  0.6 5.2 %copy-start.5 = (f32[64]{0:T(128)S(1)}, f32[64]{0:T(128)}, u32[]{:S(2)}) copy-start(f32[64]{0:T(128)} %param.13) | copy-start | bytes 772
  0.7 5.2 %copy-start = (bf16[64,8,32,128]{3,2,1,0:T(8,128)(2,1)S(1)}, bf16[64,8,32,128]{3,2,1,0:T(8,128)(2,1)}, u32[]{:S(2)}) copy-start(bf16[64,8,32,128]{3,2,1,0:T(8,128)(2,1)} %param.11) | copy-start | bytes 12582916
  5.3 9.9 %collective-permute-start = (f32[8,32,128]{2,1,0:T(8,128)}, f32[8,32,128]{2,1,0:T(8,128)S(1)}, u32[]{:S(2)}, u32[]{:S(2)}) collective-permute-start(f32[8,32,128]{2,1,0:T(8,128)} %slice_select_fusion.2), channel_id=1, source_target_pairs={{0,4},{4,0},{8,12},{12,8},{16,20},{20,16},{24,28},{28,24},{1,5},{5... | collective-permute-start | bytes 393224 | tf_op jit(solution)/shard_map/ppermute | solution.py:117
  13.6 10.6 %collective-permute-start.2 = (f32[24,32,128]{2,1,0:T(8,128)S(1)}, f32[24,32,128]{2,1,0:T(8,128)S(1)}, u32[]{:S(2)}, u32[]{:S(2)}) collective-permute-start(f32[24,32,128]{2,1,0:T(8,128)S(1)} %slice_select_fusion.1), channel_id=1, source_target_pairs={{0,4},{4,0},{8,12},{12,8},{16,20},{20,16},{24,28},{28,24},{1,5},{5... | collective-permute-start | bytes 1179656 | tf_op jit(solution)/shard_map/ppermute | solution.py:117
  15.2 7.0 %copy-start.2 = (f32[8,32,128]{2,1,0:T(8,128)S(1)}, f32[8,32,128]{2,1,0:T(8,128)}, u32[]{:S(2)}) copy-start(f32[8,32,128]{2,1,0:T(8,128)} %param.8) | copy-start | bytes 393220
  15.2 7.0 %collective-permute-start.1 = (f32[8,32,128]{2,1,0:T(8,128)S(1)}, f32[8,32,128]{2,1,0:T(8,128)S(1)}, u32[]{:S(2)}, u32[]{:S(2)}) collective-permute-start(f32[8,32,128]{2,1,0:T(8,128)S(1)} %fusion.107), channel_id=1, source_target_pairs={{0,8},{4,12},{8,16},{12,20},{16,24},{20,28},{1,9},{5,13},{9,17},{1... | collective-permute-start | bytes 393224 | tf_op jit(solution)/shard_map/ppermute | solution.py:117
  22.3 32.2 %copy-start.4 = (f32[32,128]{1,0:T(8,128)S(1)}, f32[32,128]{1,0:T(8,128)}, u32[]{:S(2)}) copy-start(f32[32,128]{1,0:T(8,128)} %param.14) | copy-start | bytes 49156
  24.4 16.3 %collective-permute-start.4 = (f32[24,32,128]{2,1,0:T(8,128)S(1)}, f32[24,32,128]{2,1,0:T(8,128)S(1)}, u32[]{:S(2)}, u32[]{:S(2)}) collective-permute-start(f32[24,32,128]{2,1,0:T(8,128)S(1)} %fusion.106), channel_id=1, source_target_pairs={{0,8},{4,12},{8,16},{12,20},{16,24},{20,28},{1,9},{5,13},{9,17},{1... | collective-permute-start | bytes 1179656 | tf_op jit(solution)/shard_map/ppermute | solution.py:117
  27.9 12.8 %collective-permute-start.3 = (f32[8,32,128]{2,1,0:T(8,128)S(1)}, f32[8,32,128]{2,1,0:T(8,128)S(1)}, u32[]{:S(2)}, u32[]{:S(2)}) collective-permute-start(f32[8,32,128]{2,1,0:T(8,128)S(1)} %add.215), channel_id=1, source_target_pairs={{0,16},{4,20},{8,24},{12,28},{1,17},{5,21},{9,25},{13,29},{2,18},{... | collective-permute-start | bytes 393224 | tf_op jit(solution)/shard_map/ppermute | solution.py:117
  30.2 6.1 %collective-permute-start.5 = (f32[2,8,1,128]{3,2,1,0:T(1,128)S(1)}, f32[2,8,1,128]{3,2,1,0:T(1,128)S(1)}, u32[]{:S(2)}, u32[]{:S(2)}) collective-permute-start(f32[2,8,1,128]{3,2,1,0:T(1,128)S(1)} %get-tuple-element.67), channel_id=1, source_target_pairs={{0,1},{1,2},{2,3},{4,5},{5,6},{6,7},{8,9},{9,10},{10,11},{12,13},{... | collective-permute-start | bytes 24584 | tf_op jit(solution)/shard_map/ppermute | solution.py:33
  32.1 5.0 %collective-permute-start.6 = (f32[2,8,1,128]{3,2,1,0:T(1,128)S(1)}, f32[2,8,1,128]{3,2,1,0:T(1,128)S(1)}, u32[]{:S(2)}, u32[]{:S(2)}) collective-permute-start(f32[2,8,1,128]{3,2,1,0:T(1,128)S(1)} %get-tuple-element.66), channel_id=1, source_target_pairs={{1,0},{2,1},{3,2},{5,4},{6,5},{7,6},{9,8},{10,9},{11,10},{13,12},{... | collective-permute-start | bytes 24584 | tf_op jit(solution)/shard_map/ppermute | solution.py:33
  40.7 19.3 %copy-start.1 = (bf16[64,8,32,128]{3,2,1,0:T(8,128)(2,1)S(1)}, bf16[64,8,32,128]{3,2,1,0:T(8,128)(2,1)}, u32[]{:S(2)}) copy-start(bf16[64,8,32,128]{3,2,1,0:T(8,128)(2,1)} %param.11) | copy-start | bytes 12582916
  40.7 19.3 %slice-start = ((f32[64,32,128]{2,1,0:T(8,128)}), f32[16,32,128]{2,1,0:T(8,128)S(1)}, s32[]{:S(2)}) async-start(f32[64,32,128]{2,1,0:T(8,128)} %param.12), calls=%async_computation | async-start | bytes 524288 | tf_op jit(solution)/shard_map/slice | solution.py:214
  40.7 18.8 %collective-permute-start.7 = (f32[8,32,128]{2,1,0:T(8,128)S(1)}, f32[8,32,128]{2,1,0:T(8,128)S(1)}, u32[]{:S(2)}, u32[]{:S(2)}) collective-permute-start(f32[8,32,128]{2,1,0:T(8,128)S(1)} %add_select_fusion.1), channel_id=1, source_target_pairs={{0,4},{4,0},{8,12},{12,8},{16,20},{20,16},{24,28},{28,24},{1,5},{5... | collective-permute-start | bytes 393224 | tf_op jit(solution)/shard_map/ppermute | solution.py:117
  42.4 17.2 %collective-permute-start.8 = (f32[24,32,128]{2,1,0:T(8,128)S(1)}, f32[24,32,128]{2,1,0:T(8,128)S(1)}, u32[]{:S(2)}, u32[]{:S(2)}) collective-permute-start(f32[24,32,128]{2,1,0:T(8,128)S(1)} %add.219), channel_id=1, source_target_pairs={{0,16},{4,20},{8,24},{12,28},{1,17},{5,21},{9,25},{13,29},{2,18},{... | collective-permute-start | bytes 1179656 | tf_op jit(solution)/shard_map/ppermute | solution.py:117
  47.7 6.8 %collective-permute-start.10 = (f32[2,1,32,128]{3,2,1,0:T(8,128)S(1)}, f32[2,1,32,128]{3,2,1,0:T(8,128)S(1)}, u32[]{:S(2)}, u32[]{:S(2)}) collective-permute-start(f32[2,1,32,128]{3,2,1,0:T(8,128)S(1)} %get-tuple-element.64), channel_id=1, source_target_pairs={{4,0},{8,4},{12,8},{16,12},{20,16},{24,20},{28,24},{5,1},{9,5},{13... | collective-permute-start | bytes 98312 | tf_op jit(solution)/shard_map/ppermute | solution.py:33
  50.3 9.3 %collective-permute-start.9 = (f32[2,1,32,128]{3,2,1,0:T(8,128)S(1)}, f32[2,1,32,128]{3,2,1,0:T(8,128)S(1)}, u32[]{:S(2)}, u32[]{:S(2)}) collective-permute-start(f32[2,1,32,128]{3,2,1,0:T(8,128)S(1)} %get-tuple-element.65), channel_id=1, source_target_pairs={{0,4},{4,8},{8,12},{12,16},{16,20},{20,24},{24,28},{1,5},{5,9},{9,... | collective-permute-start | bytes 98312 | tf_op jit(solution)/shard_map/ppermute | solution.py:33
  59.8 9.9 %collective-permute-start.11 = (f32[24,32,128]{2,1,0:T(8,128)S(1)}, f32[24,32,128]{2,1,0:T(8,128)S(1)}, u32[]{:S(2)}, u32[]{:S(2)}) collective-permute-start(f32[24,32,128]{2,1,0:T(8,128)S(1)} %add_select_fusion), channel_id=1, source_target_pairs={{0,4},{4,0},{8,12},{12,8},{16,20},{20,16},{24,28},{28,24},{1,5},{5... | collective-permute-start | bytes 1179656 | tf_op jit(solution)/shard_map/ppermute | solution.py:117
  61.1 8.7 %slice-start.1 = ((f32[64,32,128]{2,1,0:T(8,128)}), f32[48,32,128]{2,1,0:T(8,128)S(1)}, s32[]{:S(2)}) async-start(f32[64,32,128]{2,1,0:T(8,128)} %param.12), calls=%async_computation.1 | async-start | bytes 1572864 | tf_op jit(solution)/shard_map/slice | solution.py:214
  69.8 4.0 %copy-start.3 = (f32[8,32,128]{2,1,0:T(8,128)S(1)}, f32[8,32,128]{2,1,0:T(8,128)}, u32[]{:S(2)}) copy-start(f32[8,32,128]{2,1,0:T(8,128)} %param.9) | copy-start | bytes 393220
  74.8 15.9 %collective-permute-start.13 = (f32[2,8,1,128]{3,2,1,0:T(1,128)S(1)}, f32[2,8,1,128]{3,2,1,0:T(1,128)S(1)}, u32[]{:S(2)}, u32[]{:S(2)}) collective-permute-start(f32[2,8,1,128]{3,2,1,0:T(1,128)S(1)} %get-tuple-element.62), channel_id=1, source_target_pairs={{0,1},{1,2},{2,3},{4,5},{5,6},{6,7},{8,9},{9,10},{10,11},{12,13},{... | collective-permute-start | bytes 24584 | tf_op jit(solution)/shard_map/ppermute | solution.py:33
  76.8 14.0 %collective-permute-start.14 = (f32[2,8,1,128]{3,2,1,0:T(1,128)S(1)}, f32[2,8,1,128]{3,2,1,0:T(1,128)S(1)}, u32[]{:S(2)}, u32[]{:S(2)}) collective-permute-start(f32[2,8,1,128]{3,2,1,0:T(1,128)S(1)} %get-tuple-element.63), channel_id=1, source_target_pairs={{1,0},{2,1},{3,2},{5,4},{6,5},{7,6},{9,8},{10,9},{11,10},{13,12},{... | collective-permute-start | bytes 24584 | tf_op jit(solution)/shard_map/ppermute | solution.py:33
  81.1 9.6 %collective-permute-start.12 = (f32[2,1,32,128]{3,2,1,0:T(8,128)S(1)}, f32[2,1,32,128]{3,2,1,0:T(8,128)S(1)}, u32[]{:S(2)}, u32[]{:S(2)}) collective-permute-start(f32[2,1,32,128]{3,2,1,0:T(8,128)S(1)} %get-tuple-element.60), channel_id=1, source_target_pairs={{0,4},{4,8},{8,12},{12,16},{16,20},{20,24},{24,28},{1,5},{5,9},{9,... | collective-permute-start | bytes 98312 | tf_op jit(solution)/shard_map/ppermute | solution.py:33
  86.4 6.7 %collective-permute-start.15 = (f32[2,1,32,128]{3,2,1,0:T(8,128)S(1)}, f32[2,1,32,128]{3,2,1,0:T(8,128)S(1)}, u32[]{:S(2)}, u32[]{:S(2)}) collective-permute-start(f32[2,1,32,128]{3,2,1,0:T(8,128)S(1)} %get-tuple-element.61), channel_id=1, source_target_pairs={{4,0},{8,4},{12,8},{16,12},{20,16},{24,20},{28,24},{5,1},{9,5},{13... | collective-permute-start | bytes 98312 | tf_op jit(solution)/shard_map/ppermute | solution.py:33

commit v18 on v17

--- a/solution.py
+++ b/solution.py
@@ -104,9 +104,9 @@
     if count % 2 or count <= 2 or lines % (2 * groups):
         earlier = exclusive_scan(totals_of(0, lines, None), axis)
         return [emit(0, lines, earlier)], {stage: rider(None) for stage, rider in riders.items()}
-    first = max(2, lines // (2 * groups) // 2 * 2)
-    sizes = [first] + [(lines - first) // (groups - 1) // 2 * 2] * (groups - 1)
-    sizes[-1] += lines - sum(sizes)
+    last = max(2, lines // (2 * groups) // 2 * 2)
+    sizes = [(lines - last) // (groups - 1) // 2 * 2] * (groups - 1) + [last]
+    sizes[0] += lines - sum(sizes)
     starts = [sum(sizes[:g]) for g in range(groups)]
     steps = [None] * groups
     steps[0] = paired_steps(totals_of(0, sizes[0], None), axis)

time: 95.8 us -> 95.9 us (level)
  the two profiles are of different devices: /device:TPU:14 before, /device:TPU:9 now
where the time goes in v18:
time: 95.9 us; the launch traced here: 95.4 us
  starting transfers between devices  44.9 us (47%)
  other arithmetic  27.7 us (29%)
  waiting for transfers between devices  21.5 us (22%)
  between operations  1.11 us (1%)
    ppermute x8, starting transfers between devices, shifted(): return lax.ppermute(block, axis, pairs)  28.9 us
    ppermute x8, starting transfers between devices, pipelined_scan(): lax.ppermute(payload, axis, pairs)  16.1 us
    ppermute x8, waiting for transfers between devices, pipelined_scan(): lax.ppermute(payload, axis, pairs)  15.9 us
    ppermute x8, waiting for transfers between devices, shifted(): return lax.ppermute(block, axis, pairs)  5.57 us
    reduce_sum x2, other arithmetic, totals_of(): return jnp.sum(optical_depth, axis=1)  5.31 us
    reduce_sum x2, other arithmetic, emit(): jnp.sum(radiance * (1.0 - jnp.exp(-optical_depth)), axis=0)  4.87 us
    another operation x2, other arithmetic, emit(): jnp.cumsum(optical_depth[:, :rows - 1], axis=1)  3.88 us
    dynamic_update_slice x1, other arithmetic, local(): lax.dynamic_update_slice_in_dim(spectral_power, part, start, axis=0)  2.38 us
  transfers between devices with their start and end apart: 16, of which 6 were waited for; matrix products, arithmetic and copies ran while one was open for 15% of the time, Pallas kernels for 0%

profile of v18, /device:TPU:9, one launch (start us, length us, event | category | flops | bytes accessed | tf_op | source)
XLA Modules:
  0.0 95.4 jit_solution(7606695140872925708)
XLA Ops:
  0.6 0.7 convert_subtract_fusion
  1.3 1.1 %add_bitcast_fusion = (f32[1,8,32,128]{3,2,1,0:T(8,128)S(1)}, f32[8,32,128]{2,1,0:T(8,128)S(1)}) fusion(f32[8,32,128]{2,1,0:T(8,128)} %param.9, f32[8,32,128]{2,1,0:T(8,128)} %param.10, f32[8,32]{1,0:T(8,128)S(1)} %get-tuple-element.70), kind=kLoop, calls=%fused_computation.216 | loop fusion | flops 262144 | bytes 525312 | tf_op jit(solution)/shard_map/stack | solution.py:185
  2.4 0.0 copy-start.4
  2.4 5.1 %fusion.116 = (f32[48,32,128]{2,1,0:T(8,128)S(1)}, f32[48,8,32,128]{3,2,1,0:T(8,128)}) fusion(f32[8,32]{1,0:T(8,128)S(1)} %get-tuple-element.71, bf16[64,8,32,128]{3,2,1,0:T(8,128)(2,1)} %param.11, f32[48]{0:T(128)} %bitcast.63, f32[8,32,128]{2,1,0:T(8,128)S(1)} %get-tuple-element.69), kind=kLoop, calls=%fused_computation.230 | loop fusion | flops 9240576 | bytes 10355904 | tf_op jit(solution)/shard_map/reduce_sum | solution.py:206
  7.5 0.8 slice_select_fusion
  8.3 1.2 %collective-permute-start = (f32[24,32,128]{2,1,0:T(8,128)}, f32[24,32,128]{2,1,0:T(8,128)}, u32[]{:S(2)}, u32[]{:S(2)}) collective-permute-start(f32[24,32,128]{2,1,0:T(8,128)} %slice_select_fusion), channel_id=1, source_target_pairs={{0,4},{4,0},{8,12},{12,8},{16,20},{20,16},{24,28},{28,24},{1,5},{5... | collective-permute-start | bytes 1179656 | tf_op jit(solution)/shard_map/ppermute | solution.py:117
  9.5 0.1 slice.208
  9.6 1.7 %multiply_add_fusion.1 = f32[16,8,32,128]{3,2,1,0:T(8,128)S(1)} fusion(f32[8,32]{1,0:T(8,128)S(1)} %get-tuple-element.71, f32[16]{0:T(128)S(1)} %slice.208, f32[8,32,128]{2,1,0:T(8,128)S(1)} %get-tuple-element.69, bf16[64,8,32,128]{3,2,1,0:T(8,128)(2,1)} %param.11), kind=kLoop, calls=%fused_computation.12 | loop fusion | flops 2621440 | bytes 3277888 | tf_op jit(solution)/shard_map/add | solution.py:200
  11.3 0.2 reduce_sum.55
  11.6 0.3 collective-permute-start.2
  11.9 6.7 %collective-permute-done = f32[24,32,128]{2,1,0:T(8,128)} collective-permute-done((f32[24,32,128]{2,1,0:T(8,128)}, f32[24,32,128]{2,1,0:T(8,128)}, u32[]{:S(2)}, u32[]{:S(2)}) %collective-permute-start) | collective-permute-done | bytes 393248 | tf_op jit(solution)/shard_map/ppermute | solution.py:117
  18.6 1.1 %fusion.106 = f32[24,32,128]{2,1,0:T(8,128)S(1)} fusion(f32[24,32,128]{2,1,0:T(8,128)} %collective-permute-done, f32[48,32,128]{2,1,0:T(8,128)S(1)} %get-tuple-element.48, pred[]{:T(512)S(6)} %eq.7), kind=kLoop, calls=%fused_computation.213 | loop fusion | flops 196608 | bytes 1572865 | tf_op jit(solution)/shard_map/add | solution.py:81
  19.7 3.2 %collective-permute-start.1 = (f32[24,32,128]{2,1,0:T(8,128)S(1)}, f32[24,32,128]{2,1,0:T(8,128)S(1)}, u32[]{:S(2)}, u32[]{:S(2)}) collective-permute-start(f32[24,32,128]{2,1,0:T(8,128)S(1)} %fusion.106), channel_id=1, source_target_pairs={{0,8},{4,12},{8,16},{12,20},{16,24},{20,28},{1,9},{5,13},{9,17},{1... | collective-permute-start | bytes 1179656 | tf_op jit(solution)/shard_map/ppermute | solution.py:117
  22.9 0.0 copy-start.1
  22.9 3.4 %fusion = f32[48,7,32,128]{3,2,1,0:T(8,128)S(1)} fusion(f32[48,8,32,128]{3,2,1,0:T(8,128)} %get-tuple-element.49), kind=kOutput, calls=%fused_computation.5 | output fusion | flops 8257536 | bytes 11010048 | tf_op jit(solution)/shard_map/jit(cumsum)/reduce_window_sum | solution.py:211
  26.3 0.0 collective-permute-done.2
  26.3 3.1 %collective-permute-done.1 = f32[24,32,128]{2,1,0:T(8,128)S(1)} collective-permute-done((f32[24,32,128]{2,1,0:T(8,128)S(1)}, f32[24,32,128]{2,1,0:T(8,128)S(1)}, u32[]{:S(2)}, u32[]{:S(2)}) %collective-permute-start.1) | collective-permute-done | bytes 393248 | tf_op jit(solution)/shard_map/ppermute | solution.py:117
  29.5 0.1 add.215
  29.5 0.0 copy-start.3
  29.6 4.2 %collective-permute-start.3 = (f32[24,32,128]{2,1,0:T(8,128)S(1)}, f32[24,32,128]{2,1,0:T(8,128)S(1)}, u32[]{:S(2)}, u32[]{:S(2)}) collective-permute-start(f32[24,32,128]{2,1,0:T(8,128)S(1)} %add.215), channel_id=1, source_target_pairs={{0,16},{4,20},{8,24},{12,28},{1,17},{5,21},{9,25},{13,29},{2,18},{... | collective-permute-start | bytes 1179656 | tf_op jit(solution)/shard_map/ppermute | solution.py:117
  33.8 1.9 %collective-permute-start.4 = (f32[8,32,128]{2,1,0:T(8,128)S(1)}, f32[8,32,128]{2,1,0:T(8,128)S(1)}, u32[]{:S(2)}, u32[]{:S(2)}) collective-permute-start(f32[8,32,128]{2,1,0:T(8,128)S(1)} %fusion.107), channel_id=1, source_target_pairs={{0,8},{4,12},{8,16},{12,20},{16,24},{20,28},{1,9},{5,13},{9,17},{1... | collective-permute-start | bytes 393224 | tf_op jit(solution)/shard_map/ppermute | solution.py:117
  35.8 6.9 %collective-permute-start.5 = (f32[2,8,1,128]{3,2,1,0:T(1,128)S(1)}, f32[2,8,1,128]{3,2,1,0:T(1,128)S(1)}, u32[]{:S(2)}, u32[]{:S(2)}) collective-permute-start(f32[2,8,1,128]{3,2,1,0:T(1,128)S(1)} %get-tuple-element.67), channel_id=1, source_target_pairs={{0,1},{1,2},{2,3},{4,5},{5,6},{6,7},{8,9},{9,10},{10,11},{12,13},{... | collective-permute-start | bytes 24584 | tf_op jit(solution)/shard_map/ppermute | solution.py:33
  42.7 1.9 %collective-permute-start.6 = (f32[2,8,1,128]{3,2,1,0:T(1,128)S(1)}, f32[2,8,1,128]{3,2,1,0:T(1,128)S(1)}, u32[]{:S(2)}, u32[]{:S(2)}) collective-permute-start(f32[2,8,1,128]{3,2,1,0:T(1,128)S(1)} %get-tuple-element.66), channel_id=1, source_target_pairs={{1,0},{2,1},{3,2},{5,4},{6,5},{7,6},{9,8},{10,9},{11,10},{13,12},{... | collective-permute-start | bytes 24584 | tf_op jit(solution)/shard_map/ppermute | solution.py:33
  44.6 0.0 slice-start
  44.6 0.5 fusion.3
  45.1 0.0 collective-permute-done.5
  45.1 2.5 %collective-permute-done.6 = f32[2,8,1,128]{3,2,1,0:T(1,128)S(1)} collective-permute-done((f32[2,8,1,128]{3,2,1,0:T(1,128)S(1)}, f32[2,8,1,128]{3,2,1,0:T(1,128)S(1)}, u32[]{:S(2)}, u32[]{:S(2)}) %collective-permute-start.6) | collective-permute-done | bytes 8224 | tf_op jit(solution)/shard_map/ppermute | solution.py:33
  47.7 6.1 %collective-permute-done.4 = f32[8,32,128]{2,1,0:T(8,128)S(1)} collective-permute-done((f32[8,32,128]{2,1,0:T(8,128)S(1)}, f32[8,32,128]{2,1,0:T(8,128)S(1)}, u32[]{:S(2)}, u32[]{:S(2)}) %collective-permute-start.4) | collective-permute-done | bytes 131104 | tf_op jit(solution)/shard_map/ppermute | solution.py:117
  53.7 0.0 collective-permute-done.3
  53.7 1.1 %fusion.115 = (f32[24,32,128]{2,1,0:T(8,128)S(1)}, f32[24,32,128]{2,1,0:T(8,128)S(1)}) fusion(f32[24,32,128]{2,1,0:T(8,128)} %collective-permute-done, f32[24,32,128]{2,1,0:T(8,128)S(1)} %collective-permute-done.1, f32[24,32,128]{2,1,0:T(8,128)S(1)} %collective-permute-done.3), kind=kLoop, calls=%fused_computation.229 | loop fusion | flops 196608 | bytes 1966080 | tf_op jit(solution)/shard_map/add | solution.py:94
  54.8 0.1 add_select_fusion
  54.9 0.0 copy-start
  55.0 0.0 slice-start.2
  55.0 1.3 %collective-permute-start.7 = (f32[24,32,128]{2,1,0:T(8,128)S(1)}, f32[24,32,128]{2,1,0:T(8,128)S(1)}, u32[]{:S(2)}, u32[]{:S(2)}) collective-permute-start(f32[24,32,128]{2,1,0:T(8,128)S(1)} %add_select_fusion), channel_id=1, source_target_pairs={{0,4},{4,0},{8,12},{12,8},{16,20},{20,16},{24,28},{28,24},{1,5},{5... | collective-permute-start | bytes 1179656 | tf_op jit(solution)/shard_map/ppermute | solution.py:117
  56.3 2.3 %collective-permute-start.8 = (f32[8,32,128]{2,1,0:T(8,128)S(1)}, f32[8,32,128]{2,1,0:T(8,128)S(1)}, u32[]{:S(2)}, u32[]{:S(2)}) collective-permute-start(f32[8,32,128]{2,1,0:T(8,128)S(1)} %add.219), channel_id=1, source_target_pairs={{0,16},{4,20},{8,24},{12,28},{1,17},{5,21},{9,25},{13,29},{2,18},{... | collective-permute-start | bytes 393224 | tf_op jit(solution)/shard_map/ppermute | solution.py:117
  58.6 2.3 %collective-permute-start.9 = (f32[2,1,32,128]{3,2,1,0:T(8,128)S(1)}, f32[2,1,32,128]{3,2,1,0:T(8,128)S(1)}, u32[]{:S(2)}, u32[]{:S(2)}) collective-permute-start(f32[2,1,32,128]{3,2,1,0:T(8,128)S(1)} %get-tuple-element.65), channel_id=1, source_target_pairs={{0,4},{4,8},{8,12},{12,16},{16,20},{20,24},{24,28},{1,5},{5,9},{9,... | collective-permute-start | bytes 98312 | tf_op jit(solution)/shard_map/ppermute | solution.py:33
  60.9 4.7 %collective-permute-start.10 = (f32[2,1,32,128]{3,2,1,0:T(8,128)S(1)}, f32[2,1,32,128]{3,2,1,0:T(8,128)S(1)}, u32[]{:S(2)}, u32[]{:S(2)}) collective-permute-start(f32[2,1,32,128]{3,2,1,0:T(8,128)S(1)} %get-tuple-element.64), channel_id=1, source_target_pairs={{4,0},{8,4},{12,8},{16,12},{20,16},{24,20},{28,24},{5,1},{9,5},{13... | collective-permute-start | bytes 98312 | tf_op jit(solution)/shard_map/ppermute | solution.py:33
  65.7 0.0 collective-permute-done.9
  65.7 1.4 %collective-permute-done.10 = f32[2,1,32,128]{3,2,1,0:T(8,128)S(1)} collective-permute-done((f32[2,1,32,128]{3,2,1,0:T(8,128)S(1)}, f32[2,1,32,128]{3,2,1,0:T(8,128)S(1)}, u32[]{:S(2)}, u32[]{:S(2)}) %collective-permute-start.10) | collective-permute-done | bytes 32800 | tf_op jit(solution)/shard_map/ppermute | solution.py:33
  67.1 0.0 collective-permute-done.8
  67.1 0.0 collective-permute-done.7
  67.2 1.5 %collective-permute-start.11 = (f32[8,32,128]{2,1,0:T(8,128)S(1)}, f32[8,32,128]{2,1,0:T(8,128)S(1)}, u32[]{:S(2)}, u32[]{:S(2)}) collective-permute-start(f32[8,32,128]{2,1,0:T(8,128)S(1)} %add_select_fusion.1), channel_id=1, source_target_pairs={{0,4},{4,0},{8,12},{12,8},{16,20},{20,16},{24,28},{28,24},{1,5},{5... | collective-permute-start | bytes 393224 | tf_op jit(solution)/shard_map/ppermute | solution.py:117
  68.7 0.1 fusion.7
  68.8 0.5 power_multiply_fusion.2
  69.4 0.1 maximum_select_fusion
  69.5 0.0 slice-start.3
  69.5 3.6 %multiply_reduce_fusion = (f32[8,32,128]{2,1,0:T(8,128)S(1)}, f32[8,32,128]{2,1,0:T(8,128)S(1)}, bf16[48,8,32,128]{3,2,1,0:T(8,128)(2,1)S(1)}) fusion(f32[48,8,32,128]{3,2,1,0:T(8,128)S(1)} %bitcast.59, f32[48,7,32,128]{3,2,1,0:T(8,128)S(1)} %fusion, f32[48,32,128]{2,1,0:T(8,128)S(1)} %maximum_select_fusion, f32[48,32,128]{2,1,0:T(8,128)S(1)} %slice-done.2, ...), kind=kLoop, calls=%fused_computation | loop fusion | flops 20381696 | bytes 19923136 | tf_op jit(solution)/shard_map/reduce_sum | solution.py:218
  73.1 0.0 copy-start.2
  73.1 0.7 fusion.20
  73.8 0.0 collective-permute-done.11
  73.9 1.3 %multiply_reduce_fusion.2 = (f32[8,32,128]{2,1,0:T(8,128)S(1)}, f32[8,32,128]{2,1,0:T(8,128)S(1)}, bf16[16,8,32,128]{3,2,1,0:T(8,128)(2,1)S(1)}) fusion(f32[16,7,32,128]{3,2,1,0:T(8,128)S(1)} %fusion.3, f32[16,32,128]{2,1,0:T(8,128)S(1)} %maximum_select_fusion.1, f32[16,32,128]{2,1,0:T(8,128)S(1)} %slice-done.3, f32[8,32]{1,0:T(8,128)S(1)} %get-tuple-element.71, ...), kind=kLoop, calls=%fused_computation.9 | loop fusion | flops 7798784 | bytes 4850752 | tf_op jit(solution)/shard_map/reduce_sum | solution.py:218
  75.2 0.8 broadcast_multiply_fusion
  75.9 0.1 fusion.113
  76.1 3.2 %collective-permute-start.15 = (f32[2,1,32,128]{3,2,1,0:T(8,128)S(1)}, f32[2,1,32,128]{3,2,1,0:T(8,128)S(1)}, u32[]{:S(2)}, u32[]{:S(2)}) collective-permute-start(f32[2,1,32,128]{3,2,1,0:T(8,128)S(1)} %get-tuple-element.61), channel_id=1, source_target_pairs={{4,0},{8,4},{12,8},{16,12},{20,16},{24,20},{28,24},{5,1},{9,5},{13... | collective-permute-start | bytes 98312 | tf_op jit(solution)/shard_map/ppermute | solution.py:33
  79.3 5.0 %collective-permute-start.14 = (f32[2,8,1,128]{3,2,1,0:T(1,128)S(1)}, f32[2,8,1,128]{3,2,1,0:T(1,128)S(1)}, u32[]{:S(2)}, u32[]{:S(2)}) collective-permute-start(f32[2,8,1,128]{3,2,1,0:T(1,128)S(1)} %get-tuple-element.63), channel_id=1, source_target_pairs={{1,0},{2,1},{3,2},{5,4},{6,5},{7,6},{9,8},{10,9},{11,10},{13,12},{... | collective-permute-start | bytes 24584 | tf_op jit(solution)/shard_map/ppermute | solution.py:33
  84.2 3.0 %collective-permute-start.13 = (f32[2,8,1,128]{3,2,1,0:T(1,128)S(1)}, f32[2,8,1,128]{3,2,1,0:T(1,128)S(1)}, u32[]{:S(2)}, u32[]{:S(2)}) collective-permute-start(f32[2,8,1,128]{3,2,1,0:T(1,128)S(1)} %get-tuple-element.62), channel_id=1, source_target_pairs={{0,1},{1,2},{2,3},{4,5},{5,6},{6,7},{8,9},{9,10},{10,11},{12,13},{... | collective-permute-start | bytes 24584 | tf_op jit(solution)/shard_map/ppermute | solution.py:33
  87.3 1.9 %collective-permute-start.12 = (f32[2,1,32,128]{3,2,1,0:T(8,128)S(1)}, f32[2,1,32,128]{3,2,1,0:T(8,128)S(1)}, u32[]{:S(2)}, u32[]{:S(2)}) collective-permute-start(f32[2,1,32,128]{3,2,1,0:T(8,128)S(1)} %get-tuple-element.60), channel_id=1, source_target_pairs={{0,4},{4,8},{8,12},{12,16},{16,20},{20,24},{24,28},{1,5},{5,9},{9,... | collective-permute-start | bytes 98312 | tf_op jit(solution)/shard_map/ppermute | solution.py:33
  89.2 2.4 %pad_maximum_fusion = bf16[64,8,32,128]{3,2,1,0:T(8,128)(2,1)} fusion(bf16[16,8,32,128]{3,2,1,0:T(8,128)(2,1)S(1)} %get-tuple-element.51, bf16[48,8,32,128]{3,2,1,0:T(8,128)(2,1)S(1)} %get-tuple-element.30), kind=kLoop, calls=%fused_computation.7 | loop fusion | flops 2097152 | bytes 8388608 | tf_op jit(solution)/shard_map/dynamic_update_slice | solution.py:238
  91.6 0.0 collective-permute-done.14
  91.6 0.0 collective-permute-done.13
  91.6 1.6 %collective-permute-done.12 = f32[2,1,32,128]{3,2,1,0:T(8,128)S(1)} collective-permute-done((f32[2,1,32,128]{3,2,1,0:T(8,128)S(1)}, f32[2,1,32,128]{3,2,1,0:T(8,128)S(1)}, u32[]{:S(2)}, u32[]{:S(2)}) %collective-permute-start.12) | collective-permute-done | bytes 32800 | tf_op jit(solution)/shard_map/ppermute | solution.py:33
  93.2 0.5 power_multiply_fusion
  93.8 0.7 fusion.29
  94.5 0.9 fusion.93
  (26 shorter events, 0.3 us)
Async XLA Ops:
  2.4 7.1 %copy-start.4 = (f32[64]{0:T(128)S(1)}, f32[64]{0:T(128)}, u32[]{:S(2)}) copy-start(f32[64]{0:T(128)} %param.13) | copy-start | bytes 772
  8.3 10.3 %collective-permute-start = (f32[24,32,128]{2,1,0:T(8,128)}, f32[24,32,128]{2,1,0:T(8,128)}, u32[]{:S(2)}, u32[]{:S(2)}) collective-permute-start(f32[24,32,128]{2,1,0:T(8,128)} %slice_select_fusion), channel_id=1, source_target_pairs={{0,4},{4,0},{8,12},{12,8},{16,20},{20,16},{24,28},{28,24},{1,5},{5... | collective-permute-start | bytes 1179656 | tf_op jit(solution)/shard_map/ppermute | solution.py:117
  11.6 14.8 %collective-permute-start.2 = (f32[8,32,128]{2,1,0:T(8,128)S(1)}, f32[8,32,128]{2,1,0:T(8,128)S(1)}, u32[]{:S(2)}, u32[]{:S(2)}) collective-permute-start(f32[8,32,128]{2,1,0:T(8,128)S(1)} %slice_select_fusion.3), channel_id=1, source_target_pairs={{0,4},{4,0},{8,12},{12,8},{16,20},{20,16},{24,28},{28,24},{1,5},{5... | collective-permute-start | bytes 393224 | tf_op jit(solution)/shard_map/ppermute | solution.py:117
  19.7 9.8 %collective-permute-start.1 = (f32[24,32,128]{2,1,0:T(8,128)S(1)}, f32[24,32,128]{2,1,0:T(8,128)S(1)}, u32[]{:S(2)}, u32[]{:S(2)}) collective-permute-start(f32[24,32,128]{2,1,0:T(8,128)S(1)} %fusion.106), channel_id=1, source_target_pairs={{0,8},{4,12},{8,16},{12,20},{16,24},{20,28},{1,9},{5,13},{9,17},{1... | collective-permute-start | bytes 1179656 | tf_op jit(solution)/shard_map/ppermute | solution.py:117
  22.9 3.4 %copy-start.1 = (f32[8,32,128]{2,1,0:T(8,128)S(1)}, f32[8,32,128]{2,1,0:T(8,128)}, u32[]{:S(2)}) copy-start(f32[8,32,128]{2,1,0:T(8,128)} %param.8) | copy-start | bytes 393220
  29.5 36.1 %copy-start.3 = (f32[32,128]{1,0:T(8,128)S(1)}, f32[32,128]{1,0:T(8,128)}, u32[]{:S(2)}) copy-start(f32[32,128]{1,0:T(8,128)} %param.14) | copy-start | bytes 49156
  29.6 24.2 %collective-permute-start.3 = (f32[24,32,128]{2,1,0:T(8,128)S(1)}, f32[24,32,128]{2,1,0:T(8,128)S(1)}, u32[]{:S(2)}, u32[]{:S(2)}) collective-permute-start(f32[24,32,128]{2,1,0:T(8,128)S(1)} %add.215), channel_id=1, source_target_pairs={{0,16},{4,20},{8,24},{12,28},{1,17},{5,21},{9,25},{13,29},{2,18},{... | collective-permute-start | bytes 1179656 | tf_op jit(solution)/shard_map/ppermute | solution.py:117
  33.8 19.9 %collective-permute-start.4 = (f32[8,32,128]{2,1,0:T(8,128)S(1)}, f32[8,32,128]{2,1,0:T(8,128)S(1)}, u32[]{:S(2)}, u32[]{:S(2)}) collective-permute-start(f32[8,32,128]{2,1,0:T(8,128)S(1)} %fusion.107), channel_id=1, source_target_pairs={{0,8},{4,12},{8,16},{12,20},{16,24},{20,28},{1,9},{5,13},{9,17},{1... | collective-permute-start | bytes 393224 | tf_op jit(solution)/shard_map/ppermute | solution.py:117
  35.8 9.3 %collective-permute-start.5 = (f32[2,8,1,128]{3,2,1,0:T(1,128)S(1)}, f32[2,8,1,128]{3,2,1,0:T(1,128)S(1)}, u32[]{:S(2)}, u32[]{:S(2)}) collective-permute-start(f32[2,8,1,128]{3,2,1,0:T(1,128)S(1)} %get-tuple-element.67), channel_id=1, source_target_pairs={{0,1},{1,2},{2,3},{4,5},{5,6},{6,7},{8,9},{9,10},{10,11},{12,13},{... | collective-permute-start | bytes 24584 | tf_op jit(solution)/shard_map/ppermute | solution.py:33
  42.7 5.0 %collective-permute-start.6 = (f32[2,8,1,128]{3,2,1,0:T(1,128)S(1)}, f32[2,8,1,128]{3,2,1,0:T(1,128)S(1)}, u32[]{:S(2)}, u32[]{:S(2)}) collective-permute-start(f32[2,8,1,128]{3,2,1,0:T(1,128)S(1)} %get-tuple-element.66), channel_id=1, source_target_pairs={{1,0},{2,1},{3,2},{5,4},{6,5},{7,6},{9,8},{10,9},{11,10},{13,12},{... | collective-permute-start | bytes 24584 | tf_op jit(solution)/shard_map/ppermute | solution.py:33
  44.6 24.8 %slice-start = ((s8[6291456]{0:T(1024)(128)(4,1)}), s8[4194304]{0:T(1024)(128)(4,1)S(1)}, s32[]{:S(2)}) async-start(s8[6291456]{0:T(1024)(128)(4,1)} %bitcast.58), calls=%async_computation | async-start | bytes 8388608
  54.9 14.5 %slice-start.1 = ((s8[6291456]{0:T(1024)(128)(4,1)}), s8[2097152]{0:T(1024)(128)(4,1)S(1)}, s32[]{:S(2)}) async-start(s8[6291456]{0:T(1024)(128)(4,1)} %bitcast.58), calls=%async_computation.1 | async-start | bytes 4194304
  54.9 14.5 %copy-start = (bf16[64,8,32,128]{3,2,1,0:T(8,128)(2,1)S(1)}, bf16[64,8,32,128]{3,2,1,0:T(8,128)(2,1)}, u32[]{:S(2)}) copy-start(bf16[64,8,32,128]{3,2,1,0:T(8,128)(2,1)} %param.11) | copy-start | bytes 12582916
  55.0 14.5 %slice-start.2 = ((f32[64,32,128]{2,1,0:T(8,128)}), f32[48,32,128]{2,1,0:T(8,128)S(1)}, s32[]{:S(2)}) async-start(f32[64,32,128]{2,1,0:T(8,128)} %param.12), calls=%async_computation.2 | async-start | bytes 1572864 | tf_op jit(solution)/shard_map/slice | solution.py:214
  55.0 12.2 %collective-permute-start.7 = (f32[24,32,128]{2,1,0:T(8,128)S(1)}, f32[24,32,128]{2,1,0:T(8,128)S(1)}, u32[]{:S(2)}, u32[]{:S(2)}) collective-permute-start(f32[24,32,128]{2,1,0:T(8,128)S(1)} %add_select_fusion), channel_id=1, source_target_pairs={{0,4},{4,0},{8,12},{12,8},{16,20},{20,16},{24,28},{28,24},{1,5},{5... | collective-permute-start | bytes 1179656 | tf_op jit(solution)/shard_map/ppermute | solution.py:117
  56.3 10.8 %collective-permute-start.8 = (f32[8,32,128]{2,1,0:T(8,128)S(1)}, f32[8,32,128]{2,1,0:T(8,128)S(1)}, u32[]{:S(2)}, u32[]{:S(2)}) collective-permute-start(f32[8,32,128]{2,1,0:T(8,128)S(1)} %add.219), channel_id=1, source_target_pairs={{0,16},{4,20},{8,24},{12,28},{1,17},{5,21},{9,25},{13,29},{2,18},{... | collective-permute-start | bytes 393224 | tf_op jit(solution)/shard_map/ppermute | solution.py:117
  58.6 7.0 %collective-permute-start.9 = (f32[2,1,32,128]{3,2,1,0:T(8,128)S(1)}, f32[2,1,32,128]{3,2,1,0:T(8,128)S(1)}, u32[]{:S(2)}, u32[]{:S(2)}) collective-permute-start(f32[2,1,32,128]{3,2,1,0:T(8,128)S(1)} %get-tuple-element.65), channel_id=1, source_target_pairs={{0,4},{4,8},{8,12},{12,16},{16,20},{20,24},{24,28},{1,5},{5,9},{9,... | collective-permute-start | bytes 98312 | tf_op jit(solution)/shard_map/ppermute | solution.py:33
  60.9 6.2 %collective-permute-start.10 = (f32[2,1,32,128]{3,2,1,0:T(8,128)S(1)}, f32[2,1,32,128]{3,2,1,0:T(8,128)S(1)}, u32[]{:S(2)}, u32[]{:S(2)}) collective-permute-start(f32[2,1,32,128]{3,2,1,0:T(8,128)S(1)} %get-tuple-element.64), channel_id=1, source_target_pairs={{4,0},{8,4},{12,8},{16,12},{20,16},{24,20},{28,24},{5,1},{9,5},{13... | collective-permute-start | bytes 98312 | tf_op jit(solution)/shard_map/ppermute | solution.py:33
  67.2 6.6 %collective-permute-start.11 = (f32[8,32,128]{2,1,0:T(8,128)S(1)}, f32[8,32,128]{2,1,0:T(8,128)S(1)}, u32[]{:S(2)}, u32[]{:S(2)}) collective-permute-start(f32[8,32,128]{2,1,0:T(8,128)S(1)} %add_select_fusion.1), channel_id=1, source_target_pairs={{0,4},{4,0},{8,12},{12,8},{16,20},{20,16},{24,28},{28,24},{1,5},{5... | collective-permute-start | bytes 393224 | tf_op jit(solution)/shard_map/ppermute | solution.py:117
  69.5 4.3 %slice-start.3 = ((f32[64,32,128]{2,1,0:T(8,128)}), f32[16,32,128]{2,1,0:T(8,128)S(1)}, s32[]{:S(2)}) async-start(f32[64,32,128]{2,1,0:T(8,128)} %param.12), calls=%async_computation.3 | async-start | bytes 524288 | tf_op jit(solution)/shard_map/slice | solution.py:214
  73.1 2.0 %copy-start.2 = (f32[8,32,128]{2,1,0:T(8,128)S(1)}, f32[8,32,128]{2,1,0:T(8,128)}, u32[]{:S(2)}) copy-start(f32[8,32,128]{2,1,0:T(8,128)} %param.9) | copy-start | bytes 393220
  76.1 15.5 %collective-permute-start.15 = (f32[2,1,32,128]{3,2,1,0:T(8,128)S(1)}, f32[2,1,32,128]{3,2,1,0:T(8,128)S(1)}, u32[]{:S(2)}, u32[]{:S(2)}) collective-permute-start(f32[2,1,32,128]{3,2,1,0:T(8,128)S(1)} %get-tuple-element.61), channel_id=1, source_target_pairs={{4,0},{8,4},{12,8},{16,12},{20,16},{24,20},{28,24},{5,1},{9,5},{13... | collective-permute-start | bytes 98312 | tf_op jit(solution)/shard_map/ppermute | solution.py:33
  79.3 12.3 %collective-permute-start.14 = (f32[2,8,1,128]{3,2,1,0:T(1,128)S(1)}, f32[2,8,1,128]{3,2,1,0:T(1,128)S(1)}, u32[]{:S(2)}, u32[]{:S(2)}) collective-permute-start(f32[2,8,1,128]{3,2,1,0:T(1,128)S(1)} %get-tuple-element.63), channel_id=1, source_target_pairs={{1,0},{2,1},{3,2},{5,4},{6,5},{7,6},{9,8},{10,9},{11,10},{13,12},{... | collective-permute-start | bytes 24584 | tf_op jit(solution)/shard_map/ppermute | solution.py:33
  84.2 7.3 %collective-permute-start.13 = (f32[2,8,1,128]{3,2,1,0:T(1,128)S(1)}, f32[2,8,1,128]{3,2,1,0:T(1,128)S(1)}, u32[]{:S(2)}, u32[]{:S(2)}) collective-permute-start(f32[2,8,1,128]{3,2,1,0:T(1,128)S(1)} %get-tuple-element.62), channel_id=1, source_target_pairs={{0,1},{1,2},{2,3},{4,5},{5,6},{6,7},{8,9},{9,10},{10,11},{12,13},{... | collective-permute-start | bytes 24584 | tf_op jit(solution)/shard_map/ppermute | solution.py:33
  87.3 5.9 %collective-permute-start.12 = (f32[2,1,32,128]{3,2,1,0:T(8,128)S(1)}, f32[2,1,32,128]{3,2,1,0:T(8,128)S(1)}, u32[]{:S(2)}, u32[]{:S(2)}) collective-permute-start(f32[2,1,32,128]{3,2,1,0:T(8,128)S(1)} %get-tuple-element.60), channel_id=1, source_target_pairs={{0,4},{4,8},{8,12},{12,16},{16,20},{20,24},{24,28},{1,5},{5,9},{9,... | collective-permute-start | bytes 98312 | tf_op jit(solution)/shard_map/ppermute | solution.py:33

commit v19 on v15

--- a/solution.py
+++ b/solution.py
@@ -33,14 +33,27 @@
     return lax.ppermute(block, axis, pairs)
 
 
+def faces(block, axis, dim):
+    size = block.shape[dim]
+    last = lax.slice_in_dim(block, size - 1, size, axis=dim)
+    first = lax.slice_in_dim(block, 0, 1, axis=dim)
+    count = lax.axis_size(axis)
+    if count % 2:
+        return shifted(last, axis, 1), shifted(first, axis, -1)
+    is_even = lax.axis_index(axis) % 2 == 0
+    within = lax.ppermute(jnp.where(is_even, last, first), axis, [(i, i ^ 1) for i in range(count)])
+    pairs = [(i, i + 1) for i in range(1, count - 1, 2)]
+    pairs += [(target, source) for source, target in pairs]
+    across = lax.ppermute(jnp.where(is_even, first, last), axis, pairs)
+    return jnp.where(is_even, across, within), jnp.where(is_even, within, across)
+
+
 def beam_faces(block):
-    rows = block.shape[1]
-    return shifted(block[:, rows - 1 :], "beam", 1), shifted(block[:, :1], "beam", -1)
+    return faces(block, "beam", 1)
 
 
 def cross_faces(block):
-    columns = block.shape[2]
-    return shifted(block[:, :, columns - 1 :], "cross", 1), shifted(block[:, :, :1], "cross", -1)
+    return faces(block, "cross", 2)
 
 
 def bordered_fields(block, beam=None, cross=None):

time: 88.4 us -> 83.8 us (0.948)
  starting transfers between devices: 48.7 us -> 43.1 us
  other arithmetic: 26.4 us -> 30.1 us
  waiting for transfers between devices: 10.4 us -> 8.29 us
    ppermute x8, starting transfers between devices: 32.8 us -> 27.8 us  [the longest x4 20.6 us: faces(): across = lax.ppermute(jnp.where(is_even, first, last), axis, pairs)]
    another operation x2, other arithmetic: 3.4 us -> 7.1 us  [emit(): jnp.cumsum(optical_depth[:, :rows - 1], axis=1)]
    ppermute x8, waiting for transfers between devices: 4.73 us -> 1.56 us  [the longest x4 1.55 us: faces(): across = lax.ppermute(jnp.where(is_even, first, last), axis, pairs)]
    reduce_sum x2 -> x1, other arithmetic: 5.06 us -> 2.38 us  [emit(): jnp.sum(radiance * (1.0 - jnp.exp(-optical_depth)), axis=0)]
    reduce_sum x0 -> x1, other arithmetic: none -> 2.68 us  [emit(): jnp.sum(weight * radiance, axis=0)]
    ppermute x8, waiting for transfers between devices: 5.71 us -> 6.73 us  [pipelined_scan(): lax.ppermute(payload, axis, pairs)]
  transfers between devices with their start and end apart: 16 -> 16, of which waited for: 7 -> 3; matrix products, arithmetic and copies ran while one was open for 14% -> 20% of each run, Pallas kernels for 0% -> 0%
where the time goes in v19:
time: 83.8 us; the launch traced here: 83.4 us
  starting transfers between devices  43.1 us (51%)
  other arithmetic  30.1 us (36%)
  waiting for transfers between devices  8.29 us (10%)
  between operations  1.12 us (1%)
  local copies, waits for them, and re-layouts  0.84 us (1%)
    ppermute x4, starting transfers between devices, faces(): across = lax.ppermute(jnp.where(is_even, first, last), axis, pairs)  20.6 us
    ppermute x8, starting transfers between devices, pipelined_scan(): lax.ppermute(payload, axis, pairs)  15.3 us
    reduce_sum x2, other arithmetic, totals_of(): return jnp.sum(optical_depth, axis=1)  8.64 us
    ppermute x4, starting transfers between devices, faces(): lax.ppermute(jnp.where(is_even, last, first), axis, [(i, i ^ 1) for i in...  7.16 us
    another operation x2, other arithmetic, emit(): jnp.cumsum(optical_depth[:, :rows - 1], axis=1)  7.1 us
    ppermute x8, waiting for transfers between devices, pipelined_scan(): lax.ppermute(payload, axis, pairs)  6.73 us
    reduce_sum x1, other arithmetic, emit(): jnp.sum(weight * radiance, axis=0)  2.68 us
    reduce_sum x1, other arithmetic, emit(): jnp.sum(radiance * (1.0 - jnp.exp(-optical_depth)), axis=0)  2.38 us
  transfers between devices with their start and end apart: 16, of which 3 were waited for; matrix products, arithmetic and copies ran while one was open for 20% of the time, Pallas kernels for 0%

profile of v19, /device:TPU:9, one launch (start us, length us, event | category | flops | bytes accessed | tf_op | source)
XLA Modules:
  0.0 83.4 jit_solution(15844359373547303519)
XLA Ops:
  0.6 0.7 convert_subtract_fusion
  1.3 0.8 fusion.120
  2.1 1.1 %add_bitcast_fusion = (f32[1,8,32,128]{3,2,1,0:T(8,128)S(1)}, f32[8,32,128]{2,1,0:T(8,128)S(1)}) fusion(f32[8,32,128]{2,1,0:T(8,128)} %param.9, f32[8,32,128]{2,1,0:T(8,128)} %param.10, f32[8,32]{1,0:T(8,128)S(1)} %get-tuple-element.82), kind=kLoop, calls=%fused_computation.215 | loop fusion | flops 262144 | bytes 525312 | tf_op jit(solution)/shard_map/stack | solution.py:195
  3.2 5.9 %fusion.118 = (f32[32,32,128]{2,1,0:T(8,128)S(1)}, f32[32,8,32,128]{3,2,1,0:T(8,128)}, f32[32,8,32,128]{3,2,1,0:T(8,128)}) fusion(f32[8,32]{1,0:T(8,128)S(1)} %get-tuple-element.83, bf16[64,8,32,128]{3,2,1,0:T(8,128)(2,1)} %param.11, f32[32]{0:T(128)S(1)} %get-tuple-element.84, f32[8,32,128]{2,1,0:T(8,128)S(1)} %get-tuple-element.73, ...), kind=kLoop, calls=%fused_computation.246 | loop fusion | flops 11403264 | bytes 13239552 | tf_op jit(solution)/shard_map/reduce_sum | solution.py:216
  9.1 1.3 %collective-permute-start = (f32[16,32,128]{2,1,0:T(8,128)S(1)}, f32[16,32,128]{2,1,0:T(8,128)S(1)}, u32[]{:S(2)}, u32[]{:S(2)}) collective-permute-start(f32[16,32,128]{2,1,0:T(8,128)S(1)} %slice_select_fusion.2), channel_id=1, source_target_pairs={{0,4},{4,0},{8,12},{12,8},{16,20},{20,16},{24,28},{28,24},{1,5},{5... | collective-permute-start | bytes 786440 | tf_op jit(solution)/shard_map/ppermute | solution.py:127
  10.4 2.7 %reduce_sum.55 = f32[32,32,128]{2,1,0:T(8,128)S(1)} reduce(f32[32,8,32,128]{3,2,1,0:T(8,128)} %get-tuple-element.21, f32[]{:T(128)} %constant.65.clone.1), dimensions={1}, to_apply=%region_1.2 | reduce | flops 917504 | bytes 4718596 | tf_op jit(solution)/shard_map/reduce_sum | solution.py:216
  13.2 0.0 copy-start.3
  13.2 0.3 collective-permute-start.2
  13.5 2.8 %collective-permute-done = f32[16,32,128]{2,1,0:T(8,128)S(1)} collective-permute-done((f32[16,32,128]{2,1,0:T(8,128)S(1)}, f32[16,32,128]{2,1,0:T(8,128)S(1)}, u32[]{:S(2)}, u32[]{:S(2)}) %collective-permute-start) | collective-permute-done | bytes 262176 | tf_op jit(solution)/shard_map/ppermute | solution.py:127
  16.4 0.1 fusion.106
  16.4 3.2 %collective-permute-start.1 = (f32[16,32,128]{2,1,0:T(8,128)S(1)}, f32[16,32,128]{2,1,0:T(8,128)S(1)}, u32[]{:S(2)}, u32[]{:S(2)}) collective-permute-start(f32[16,32,128]{2,1,0:T(8,128)S(1)} %fusion.106), channel_id=1, source_target_pairs={{0,8},{4,12},{8,16},{12,20},{16,24},{20,28},{1,9},{5,13},{9,17},{1... | collective-permute-start | bytes 786440 | tf_op jit(solution)/shard_map/ppermute | solution.py:127
  19.6 4.5 %fusion = f32[32,7,32,128]{3,2,1,0:T(8,128)} fusion(f32[32,8,32,128]{3,2,1,0:T(8,128)} %get-tuple-element.21), kind=kOutput, calls=%fused_computation.11 | output fusion | flops 5505024 | bytes 7340032 | tf_op jit(solution)/shard_map/jit(cumsum)/reduce_window_sum | solution.py:221
  24.2 0.0 collective-permute-done.2
  24.2 0.0 collective-permute-done.1
  24.2 3.6 %collective-permute-start.3 = (f32[16,32,128]{2,1,0:T(8,128)S(1)}, f32[16,32,128]{2,1,0:T(8,128)S(1)}, u32[]{:S(2)}, u32[]{:S(2)}) collective-permute-start(f32[16,32,128]{2,1,0:T(8,128)S(1)} %add.218), channel_id=1, source_target_pairs={{0,16},{4,20},{8,24},{12,28},{1,17},{5,21},{9,25},{13,29},{2,18},{... | collective-permute-start | bytes 786440 | tf_op jit(solution)/shard_map/ppermute | solution.py:127
  27.8 0.1 fusion.107
  27.9 1.9 %collective-permute-start.4 = (f32[16,32,128]{2,1,0:T(8,128)S(1)}, f32[16,32,128]{2,1,0:T(8,128)S(1)}, u32[]{:S(2)}, u32[]{:S(2)}) collective-permute-start(f32[16,32,128]{2,1,0:T(8,128)S(1)} %fusion.107), channel_id=1, source_target_pairs={{0,8},{4,12},{8,16},{12,20},{16,24},{20,28},{1,9},{5,13},{9,17},{1... | collective-permute-start | bytes 786440 | tf_op jit(solution)/shard_map/ppermute | solution.py:127
  29.8 4.2 %collective-permute-start.6 = (f32[2,8,1,128]{3,2,1,0:T(1,128)S(1)}, f32[2,8,1,128]{3,2,1,0:T(1,128)S(1)}, u32[]{:S(2)}, u32[]{:S(2)}) collective-permute-start(f32[2,8,1,128]{3,2,1,0:T(1,128)S(1)} %get-tuple-element.70), channel_id=1, source_target_pairs={{0,1},{1,0},{2,3},{3,2},{4,5},{5,4},{6,7},{7,6},{8,9},{9,8},{10,11... | collective-permute-start | bytes 24584 | tf_op jit(solution)/shard_map/ppermute | solution.py:44
  34.0 3.0 %collective-permute-start.5 = (f32[2,8,1,128]{3,2,1,0:T(1,128)S(1)}, f32[2,8,1,128]{3,2,1,0:T(1,128)S(1)}, u32[]{:S(2)}, u32[]{:S(2)}) collective-permute-start(f32[2,8,1,128]{3,2,1,0:T(1,128)S(1)} %get-tuple-element.71), channel_id=1, source_target_pairs={{1,2},{2,1},{5,6},{6,5},{9,10},{10,9},{13,14},{14,13},{17,18},{18,... | collective-permute-start | bytes 24584 | tf_op jit(solution)/shard_map/ppermute | solution.py:47
  37.1 0.0 copy-start.6
  37.1 2.6 %fusion.2 = f32[32,7,32,128]{3,2,1,0:T(8,128)S(1)} fusion(f32[32,8,32,128]{3,2,1,0:T(8,128)} %get-tuple-element.52), kind=kOutput, calls=%fused_computation.13 | output fusion | flops 5505024 | bytes 7340032 | tf_op jit(solution)/shard_map/jit(cumsum)/reduce_window_sum | solution.py:221
  39.7 0.0 copy-start.5
  39.7 0.0 collective-permute-done.6
  39.7 0.0 collective-permute-done.5
  39.7 0.0 collective-permute-done.3
  39.7 3.9 %collective-permute-done.4 = f32[16,32,128]{2,1,0:T(8,128)S(1)} collective-permute-done((f32[16,32,128]{2,1,0:T(8,128)S(1)}, f32[16,32,128]{2,1,0:T(8,128)S(1)}, u32[]{:S(2)}, u32[]{:S(2)}) %collective-permute-start.4) | collective-permute-done | bytes 262176 | tf_op jit(solution)/shard_map/ppermute | solution.py:127
  43.6 0.1 fusion.117
  43.7 0.1 add_select_fusion.1
  43.8 1.3 %collective-permute-start.7 = (f32[16,32,128]{2,1,0:T(8,128)S(1)}, f32[16,32,128]{2,1,0:T(8,128)S(1)}, u32[]{:S(2)}, u32[]{:S(2)}) collective-permute-start(f32[16,32,128]{2,1,0:T(8,128)S(1)} %add_select_fusion.1), channel_id=1, source_target_pairs={{0,4},{4,0},{8,12},{12,8},{16,20},{20,16},{24,28},{28,24},{1,5},{5... | collective-permute-start | bytes 786440 | tf_op jit(solution)/shard_map/ppermute | solution.py:127
  45.1 0.0 copy-start
  45.1 1.6 %collective-permute-start.8 = (f32[16,32,128]{2,1,0:T(8,128)S(1)}, f32[16,32,128]{2,1,0:T(8,128)S(1)}, u32[]{:S(2)}, u32[]{:S(2)}) collective-permute-start(f32[16,32,128]{2,1,0:T(8,128)S(1)} %add.223), channel_id=1, source_target_pairs={{0,16},{4,20},{8,24},{12,28},{1,17},{5,21},{9,25},{13,29},{2,18},{... | collective-permute-start | bytes 786440 | tf_op jit(solution)/shard_map/ppermute | solution.py:127
  46.7 0.3 collective-permute-start.10
  47.0 6.8 %collective-permute-start.9 = (f32[2,1,32,128]{3,2,1,0:T(8,128)S(1)}, f32[2,1,32,128]{3,2,1,0:T(8,128)S(1)}, u32[]{:S(2)}, u32[]{:S(2)}) collective-permute-start(f32[2,1,32,128]{3,2,1,0:T(8,128)S(1)} %get-tuple-element.69), channel_id=1, source_target_pairs={{4,8},{12,16},{20,24},{8,4},{16,12},{24,20},{5,9},{13,17},{21,25},... | collective-permute-start | bytes 98312 | tf_op jit(solution)/shard_map/ppermute | solution.py:47
  53.9 0.0 collective-permute-done.10
  53.9 1.5 %collective-permute-done.9 = f32[2,1,32,128]{3,2,1,0:T(8,128)S(1)} collective-permute-done((f32[2,1,32,128]{3,2,1,0:T(8,128)S(1)}, f32[2,1,32,128]{3,2,1,0:T(8,128)S(1)}, u32[]{:S(2)}, u32[]{:S(2)}) %collective-permute-start.9) | collective-permute-done | bytes 32800 | tf_op jit(solution)/shard_map/ppermute | solution.py:47
  55.4 0.0 collective-permute-done.7
  55.5 0.0 collective-permute-done.8
  55.5 0.1 fusion.116
  55.5 0.1 add_select_fusion
  55.6 2.1 %collective-permute-start.11 = (f32[16,32,128]{2,1,0:T(8,128)S(1)}, f32[16,32,128]{2,1,0:T(8,128)S(1)}, u32[]{:S(2)}, u32[]{:S(2)}) collective-permute-start(f32[16,32,128]{2,1,0:T(8,128)S(1)} %add_select_fusion), channel_id=1, source_target_pairs={{0,4},{4,0},{8,12},{12,8},{16,20},{20,16},{24,28},{28,24},{1,5},{5... | collective-permute-start | bytes 786440 | tf_op jit(solution)/shard_map/ppermute | solution.py:127
  57.7 0.1 fusion.7
  57.7 0.5 power_multiply_fusion.2
  58.3 0.2 fusion.119
  58.5 2.4 %multiply_reduce_fusion.2 = (f32[8,32,128]{2,1,0:T(8,128)S(1)}, f32[8,32,128]{2,1,0:T(8,128)S(1)}, bf16[32,8,32,128]{3,2,1,0:T(8,128)(2,1)S(1)}) fusion(f32[32,8,32,128]{3,2,1,0:T(8,128)S(1)} %copy-done, f32[32,7,32,128]{3,2,1,0:T(8,128)S(1)} %fusion.2, f32[32,32,128]{2,1,0:T(8,128)S(1)} %get-tuple-element.86, f32[32,32,128]{2,1,0:T(8,128)S(1)} %get-tuple-element.57, ...), kind=kLoop, calls=%fused_computation.4 | loop fusion | flops 13565952 | bytes 13369472 | tf_op jit(solution)/shard_map/reduce_sum | solution.py:228
  60.9 0.6 fusion.20
  61.6 0.0 collective-permute-done.11
  61.6 0.1 maximum_select_fusion.1
  61.6 0.0 copy-start.4
  61.7 2.7 %multiply_reduce_fusion.1 = (f32[8,32,128]{2,1,0:T(8,128)S(1)}, f32[8,32,128]{2,1,0:T(8,128)S(1)}, bf16[32,8,32,128]{3,2,1,0:T(8,128)(2,1)S(1)}) fusion(f32[32,7,32,128]{3,2,1,0:T(8,128)S(1)} %copy-done.2, f32[32,32,128]{2,1,0:T(8,128)S(1)} %maximum_select_fusion.1, f32[32,32,128]{2,1,0:T(8,128)S(1)} %get-tuple-element.56, f32[32]{0:T(128)S(1)} %get-tuple-element.85, ...), kind=kLoop, calls=%fused_computation.2 | loop fusion | flops 15663104 | bytes 9307264 | tf_op jit(solution)/shard_map/reduce_sum | solution.py:227
  64.4 0.8 broadcast_multiply_fusion
  65.1 0.1 fusion.112
  65.3 3.6 %collective-permute-start.12 = (f32[2,1,32,128]{3,2,1,0:T(8,128)S(1)}, f32[2,1,32,128]{3,2,1,0:T(8,128)S(1)}, u32[]{:S(2)}, u32[]{:S(2)}) collective-permute-start(f32[2,1,32,128]{3,2,1,0:T(8,128)S(1)} %get-tuple-element.66), channel_id=1, source_target_pairs={{4,8},{12,16},{20,24},{8,4},{16,12},{24,20},{5,9},{13,17},{21,25},... | collective-permute-start | bytes 98312 | tf_op jit(solution)/shard_map/ppermute | solution.py:47
  69.0 2.6 %collective-permute-start.13 = (f32[2,1,32,128]{3,2,1,0:T(8,128)S(1)}, f32[2,1,32,128]{3,2,1,0:T(8,128)S(1)}, u32[]{:S(2)}, u32[]{:S(2)}) collective-permute-start(f32[2,1,32,128]{3,2,1,0:T(8,128)S(1)} %get-tuple-element.67), channel_id=1, source_target_pairs={{0,4},{4,0},{8,12},{12,8},{16,20},{20,16},{24,28},{28,24},{1,5},{5... | collective-permute-start | bytes 98312 | tf_op jit(solution)/shard_map/ppermute | solution.py:44
  71.6 7.1 %collective-permute-start.14 = (f32[2,8,1,128]{3,2,1,0:T(1,128)S(1)}, f32[2,8,1,128]{3,2,1,0:T(1,128)S(1)}, u32[]{:S(2)}, u32[]{:S(2)}) collective-permute-start(f32[2,8,1,128]{3,2,1,0:T(1,128)S(1)} %get-tuple-element.44), channel_id=1, source_target_pairs={{1,2},{2,1},{5,6},{6,5},{9,10},{10,9},{13,14},{14,13},{17,18},{18,... | collective-permute-start | bytes 24584 | tf_op jit(solution)/shard_map/ppermute | solution.py:47
  78.7 0.1 collective-permute-start.15
  78.8 2.4 %pad_maximum_fusion = bf16[64,8,32,128]{3,2,1,0:T(8,128)(2,1)} fusion(bf16[32,8,32,128]{3,2,1,0:T(8,128)(2,1)S(1)} %get-tuple-element.53, bf16[32,8,32,128]{3,2,1,0:T(8,128)(2,1)S(1)} %get-tuple-element.30), kind=kLoop, calls=%fused_computation | loop fusion | flops 2097152 | bytes 8388608 | tf_op jit(solution)/shard_map/dynamic_update_slice | solution.py:248
  81.2 0.0 collective-permute-done.14
  81.2 0.0 collective-permute-done.15
  81.2 0.0 collective-permute-done.12
  81.2 0.0 collective-permute-done.13
  81.2 0.1 fusion.9
  81.3 0.5 power_multiply_fusion
  81.9 0.7 fusion.29
  82.5 0.9 %fusion.93 = (f32[8,32,128]{2,1,0:T(8,128)}, f32[8,32,128]{2,1,0:T(8,128)}) fusion(f32[2,8,32,128]{3,2,1,0:T(8,128)S(1)} %fusion.29, f32[8,32]{1,0:T(8,128)S(1)} %get-tuple-element.82, f32[8,32,128]{2,1,0:T(8,128)S(1)} %get-tuple-element.37, f32[8,32,128]{2,1,0:T(8,128)S(1)} %get-tuple-element.39, f32[2,8,32,128]{3,2,1,0:T(8,128)S(1)} %fusion.20, ...), kind=kLoop, calls=%fused_computation.196 | loop fusion | flops 1081344 | bytes 1442816 | tf_op jit(solution)/shard_map/add | solution.py:267
  (25 shorter events, 0.3 us)
Async XLA Ops:
  9.1 7.2 %collective-permute-start = (f32[16,32,128]{2,1,0:T(8,128)S(1)}, f32[16,32,128]{2,1,0:T(8,128)S(1)}, u32[]{:S(2)}, u32[]{:S(2)}) collective-permute-start(f32[16,32,128]{2,1,0:T(8,128)S(1)} %slice_select_fusion.2), channel_id=1, source_target_pairs={{0,4},{4,0},{8,12},{12,8},{16,20},{20,16},{24,28},{28,24},{1,5},{5... | collective-permute-start | bytes 786440 | tf_op jit(solution)/shard_map/ppermute | solution.py:127
  13.2 10.9 %copy-start.3 = (f32[8,32,128]{2,1,0:T(8,128)S(1)}, f32[8,32,128]{2,1,0:T(8,128)}, u32[]{:S(2)}) copy-start(f32[8,32,128]{2,1,0:T(8,128)} %param.8) | copy-start | bytes 393220
  13.2 10.9 %collective-permute-start.2 = (f32[16,32,128]{2,1,0:T(8,128)S(1)}, f32[16,32,128]{2,1,0:T(8,128)S(1)}, u32[]{:S(2)}, u32[]{:S(2)}) collective-permute-start(f32[16,32,128]{2,1,0:T(8,128)S(1)} %slice_select_fusion.1), channel_id=1, source_target_pairs={{0,4},{4,0},{8,12},{12,8},{16,20},{20,16},{24,28},{28,24},{1,5},{5... | collective-permute-start | bytes 786440 | tf_op jit(solution)/shard_map/ppermute | solution.py:127
  16.4 7.7 %collective-permute-start.1 = (f32[16,32,128]{2,1,0:T(8,128)S(1)}, f32[16,32,128]{2,1,0:T(8,128)S(1)}, u32[]{:S(2)}, u32[]{:S(2)}) collective-permute-start(f32[16,32,128]{2,1,0:T(8,128)S(1)} %fusion.106), channel_id=1, source_target_pairs={{0,8},{4,12},{8,16},{12,20},{16,24},{20,28},{1,9},{5,13},{9,17},{1... | collective-permute-start | bytes 786440 | tf_op jit(solution)/shard_map/ppermute | solution.py:127
  24.2 15.5 %collective-permute-start.3 = (f32[16,32,128]{2,1,0:T(8,128)S(1)}, f32[16,32,128]{2,1,0:T(8,128)S(1)}, u32[]{:S(2)}, u32[]{:S(2)}) collective-permute-start(f32[16,32,128]{2,1,0:T(8,128)S(1)} %add.218), channel_id=1, source_target_pairs={{0,16},{4,20},{8,24},{12,28},{1,17},{5,21},{9,25},{13,29},{2,18},{... | collective-permute-start | bytes 786440 | tf_op jit(solution)/shard_map/ppermute | solution.py:127
  27.9 15.7 %collective-permute-start.4 = (f32[16,32,128]{2,1,0:T(8,128)S(1)}, f32[16,32,128]{2,1,0:T(8,128)S(1)}, u32[]{:S(2)}, u32[]{:S(2)}) collective-permute-start(f32[16,32,128]{2,1,0:T(8,128)S(1)} %fusion.107), channel_id=1, source_target_pairs={{0,8},{4,12},{8,16},{12,20},{16,24},{20,28},{1,9},{5,13},{9,17},{1... | collective-permute-start | bytes 786440 | tf_op jit(solution)/shard_map/ppermute | solution.py:127
  29.8 9.9 %collective-permute-start.6 = (f32[2,8,1,128]{3,2,1,0:T(1,128)S(1)}, f32[2,8,1,128]{3,2,1,0:T(1,128)S(1)}, u32[]{:S(2)}, u32[]{:S(2)}) collective-permute-start(f32[2,8,1,128]{3,2,1,0:T(1,128)S(1)} %get-tuple-element.70), channel_id=1, source_target_pairs={{0,1},{1,0},{2,3},{3,2},{4,5},{5,4},{6,7},{7,6},{8,9},{9,8},{10,11... | collective-permute-start | bytes 24584 | tf_op jit(solution)/shard_map/ppermute | solution.py:44
  34.0 5.7 %collective-permute-start.5 = (f32[2,8,1,128]{3,2,1,0:T(1,128)S(1)}, f32[2,8,1,128]{3,2,1,0:T(1,128)S(1)}, u32[]{:S(2)}, u32[]{:S(2)}) collective-permute-start(f32[2,8,1,128]{3,2,1,0:T(1,128)S(1)} %get-tuple-element.71), channel_id=1, source_target_pairs={{1,2},{2,1},{5,6},{6,5},{9,10},{10,9},{13,14},{14,13},{17,18},{18,... | collective-permute-start | bytes 24584 | tf_op jit(solution)/shard_map/ppermute | solution.py:47
  37.1 16.8 %copy-start.6 = (f32[32,128]{1,0:T(8,128)S(1)}, f32[32,128]{1,0:T(8,128)}, u32[]{:S(2)}) copy-start(f32[32,128]{1,0:T(8,128)} %param.14) | copy-start | bytes 49156
  39.7 18.6 %copy-start.5 = (f32[64,32,128]{2,1,0:T(8,128)S(1)}, f32[64,32,128]{2,1,0:T(8,128)}, u32[]{:S(2)}) copy-start(f32[64,32,128]{2,1,0:T(8,128)} %param.12) | copy-start | bytes 3145732
  43.8 11.7 %collective-permute-start.7 = (f32[16,32,128]{2,1,0:T(8,128)S(1)}, f32[16,32,128]{2,1,0:T(8,128)S(1)}, u32[]{:S(2)}, u32[]{:S(2)}) collective-permute-start(f32[16,32,128]{2,1,0:T(8,128)S(1)} %add_select_fusion.1), channel_id=1, source_target_pairs={{0,4},{4,0},{8,12},{12,8},{16,20},{20,16},{24,28},{28,24},{1,5},{5... | collective-permute-start | bytes 786440 | tf_op jit(solution)/shard_map/ppermute | solution.py:127
  45.1 13.4 %copy-start.1 = (bf16[64,8,32,128]{3,2,1,0:T(8,128)(2,1)S(1)}, bf16[64,8,32,128]{3,2,1,0:T(8,128)(2,1)}, u32[]{:S(2)}) copy-start(bf16[64,8,32,128]{3,2,1,0:T(8,128)(2,1)} %param.11) | copy-start | bytes 12582916
  45.1 13.4 %copy-start = (f32[32,8,32,128]{3,2,1,0:T(8,128)S(1)}, f32[32,8,32,128]{3,2,1,0:T(8,128)}, u32[]{:S(2)}) copy-start(f32[32,8,32,128]{3,2,1,0:T(8,128)} %get-tuple-element.52) | copy-start | bytes 12582916
  45.1 10.3 %collective-permute-start.8 = (f32[16,32,128]{2,1,0:T(8,128)S(1)}, f32[16,32,128]{2,1,0:T(8,128)S(1)}, u32[]{:S(2)}, u32[]{:S(2)}) collective-permute-start(f32[16,32,128]{2,1,0:T(8,128)S(1)} %add.223), channel_id=1, source_target_pairs={{0,16},{4,20},{8,24},{12,28},{1,17},{5,21},{9,25},{13,29},{2,18},{... | collective-permute-start | bytes 786440 | tf_op jit(solution)/shard_map/ppermute | solution.py:127
  46.7 7.2 %collective-permute-start.10 = (f32[2,1,32,128]{3,2,1,0:T(8,128)S(1)}, f32[2,1,32,128]{3,2,1,0:T(8,128)S(1)}, u32[]{:S(2)}, u32[]{:S(2)}) collective-permute-start(f32[2,1,32,128]{3,2,1,0:T(8,128)S(1)} %get-tuple-element.68), channel_id=1, source_target_pairs={{0,4},{4,0},{8,12},{12,8},{16,20},{20,16},{24,28},{28,24},{1,5},{5... | collective-permute-start | bytes 98312 | tf_op jit(solution)/shard_map/ppermute | solution.py:44
  47.0 8.4 %collective-permute-start.9 = (f32[2,1,32,128]{3,2,1,0:T(8,128)S(1)}, f32[2,1,32,128]{3,2,1,0:T(8,128)S(1)}, u32[]{:S(2)}, u32[]{:S(2)}) collective-permute-start(f32[2,1,32,128]{3,2,1,0:T(8,128)S(1)} %get-tuple-element.69), channel_id=1, source_target_pairs={{4,8},{12,16},{20,24},{8,4},{16,12},{24,20},{5,9},{13,17},{21,25},... | collective-permute-start | bytes 98312 | tf_op jit(solution)/shard_map/ppermute | solution.py:47
  55.6 6.0 %collective-permute-start.11 = (f32[16,32,128]{2,1,0:T(8,128)S(1)}, f32[16,32,128]{2,1,0:T(8,128)S(1)}, u32[]{:S(2)}, u32[]{:S(2)}) collective-permute-start(f32[16,32,128]{2,1,0:T(8,128)S(1)} %add_select_fusion), channel_id=1, source_target_pairs={{0,4},{4,0},{8,12},{12,8},{16,20},{20,16},{24,28},{28,24},{1,5},{5... | collective-permute-start | bytes 786440 | tf_op jit(solution)/shard_map/ppermute | solution.py:127
  58.5 3.1 %copy-start.2 = (f32[32,7,32,128]{3,2,1,0:T(8,128)S(1)}, f32[32,7,32,128]{3,2,1,0:T(8,128)}, u32[]{:S(2)}) copy-start(f32[32,7,32,128]{3,2,1,0:T(8,128)} %fusion) | copy-start | bytes 11010052
  61.6 2.7 %copy-start.4 = (f32[8,32,128]{2,1,0:T(8,128)S(1)}, f32[8,32,128]{2,1,0:T(8,128)}, u32[]{:S(2)}) copy-start(f32[8,32,128]{2,1,0:T(8,128)} %param.9) | copy-start | bytes 393220
  65.3 15.9 %collective-permute-start.12 = (f32[2,1,32,128]{3,2,1,0:T(8,128)S(1)}, f32[2,1,32,128]{3,2,1,0:T(8,128)S(1)}, u32[]{:S(2)}, u32[]{:S(2)}) collective-permute-start(f32[2,1,32,128]{3,2,1,0:T(8,128)S(1)} %get-tuple-element.66), channel_id=1, source_target_pairs={{4,8},{12,16},{20,24},{8,4},{16,12},{24,20},{5,9},{13,17},{21,25},... | collective-permute-start | bytes 98312 | tf_op jit(solution)/shard_map/ppermute | solution.py:47
  69.0 12.2 %collective-permute-start.13 = (f32[2,1,32,128]{3,2,1,0:T(8,128)S(1)}, f32[2,1,32,128]{3,2,1,0:T(8,128)S(1)}, u32[]{:S(2)}, u32[]{:S(2)}) collective-permute-start(f32[2,1,32,128]{3,2,1,0:T(8,128)S(1)} %get-tuple-element.67), channel_id=1, source_target_pairs={{0,4},{4,0},{8,12},{12,8},{16,20},{20,16},{24,28},{28,24},{1,5},{5... | collective-permute-start | bytes 98312 | tf_op jit(solution)/shard_map/ppermute | solution.py:44
  71.6 9.6 %collective-permute-start.14 = (f32[2,8,1,128]{3,2,1,0:T(1,128)S(1)}, f32[2,8,1,128]{3,2,1,0:T(1,128)S(1)}, u32[]{:S(2)}, u32[]{:S(2)}) collective-permute-start(f32[2,8,1,128]{3,2,1,0:T(1,128)S(1)} %get-tuple-element.44), channel_id=1, source_target_pairs={{1,2},{2,1},{5,6},{6,5},{9,10},{10,9},{13,14},{14,13},{17,18},{18,... | collective-permute-start | bytes 24584 | tf_op jit(solution)/shard_map/ppermute | solution.py:47
  78.7 2.5 %collective-permute-start.15 = (f32[2,8,1,128]{3,2,1,0:T(1,128)S(1)}, f32[2,8,1,128]{3,2,1,0:T(1,128)S(1)}, u32[]{:S(2)}, u32[]{:S(2)}) collective-permute-start(f32[2,8,1,128]{3,2,1,0:T(1,128)S(1)} %bitcast.81), channel_id=1, source_target_pairs={{0,1},{1,0},{2,3},{3,2},{4,5},{5,4},{6,7},{7,6},{8,9},{9,8},{10,11... | collective-permute-start | bytes 24584 | tf_op jit(solution)/shard_map/ppermute | solution.py:44

commit v20 on v19

--- a/solution.py
+++ b/solution.py
@@ -93,11 +93,11 @@
     got = yield jnp.where(is_low, second, first), swap
     pair_total = mine + got
     pairs = count // 2
-    before = yield pair_total, shift_pairs(count, 2)
+    before = from_below((yield pair_total, shift_pairs(count, 2)), axis, 2)
     through = pair_total + before
     step = 2
     while step < pairs:
-        arrived = yield through, shift_pairs(count, 2 * step)
+        arrived = from_below((yield through, shift_pairs(count, 2 * step)), axis, 2 * step)
         before = before + arrived
         step *= 2
         if step < pairs:
@@ -109,7 +109,11 @@
 
 
 def shift_pairs(count, shift):
-    return [(i, i + shift) for i in range(count - shift)]
+    return [(i, (i + shift) % count) for i in range(count)]
+
+
+def from_below(arrived, axis, shift):
+    return jnp.where(lax.axis_index(axis) >= shift, arrived, jnp.zeros_like(arrived))
 
 
 def pipelined_scan(totals_of, emit, lines, axis, riders, groups=2):

time: 83.8 us -> 86.7 us (1.035)
  the two profiles are of different devices: /device:TPU:9 before, /device:TPU:0 now
where the time goes in v20:
time: 86.7 us; the launch traced here: 86.2 us
  other arithmetic  39.1 us (45%)
  starting transfers between devices  23.9 us (28%)
  waiting for transfers between devices  21.4 us (25%)
  between operations  1 us (1%)
    ppermute x8, waiting for transfers between devices, pipelined_scan(): lax.ppermute(payload, axis, pairs)  19.4 us
    ppermute x8, starting transfers between devices, pipelined_scan(): lax.ppermute(payload, axis, pairs)  13.9 us
    another operation x2, other arithmetic, emit(): jnp.cumsum(optical_depth[:, :rows - 1], axis=1)  8.97 us
    reduce_sum x2, other arithmetic, totals_of(): return jnp.sum(optical_depth, axis=1)  8.64 us
    ppermute x4, starting transfers between devices, faces(): lax.ppermute(jnp.where(is_even, last, first), axis, [(i, i ^ 1) for i in...  6.8 us
    reduce_sum x1, other arithmetic, emit(): jnp.sum(radiance * (1.0 - jnp.exp(-optical_depth)), axis=0)  4.02 us
    ppermute x4, starting transfers between devices, faces(): across = lax.ppermute(jnp.where(is_even, first, last), axis, pairs)  3.21 us
    reduce_sum x1, other arithmetic, emit(): jnp.sum(weight * radiance, axis=0)  2.68 us
  transfers between devices with their start and end apart: 16, of which 6 were waited for; matrix products, arithmetic and copies ran while one was open for 28% of the time, Pallas kernels for 0%

profile of v20, /device:TPU:0, one launch (start us, length us, event | category | flops | bytes accessed | tf_op | source)
XLA Modules:
  0.0 86.2 jit_solution(4690154898989646974)
XLA Ops:
  0.6 0.7 convert_subtract_fusion
  1.3 0.8 fusion.120
  2.1 1.1 %add_bitcast_fusion = (f32[1,8,32,128]{3,2,1,0:T(8,128)S(1)}, f32[8,32,128]{2,1,0:T(8,128)S(1)}) fusion(f32[8,32,128]{2,1,0:T(8,128)} %param.9, f32[8,32,128]{2,1,0:T(8,128)} %param.10, f32[8,32]{1,0:T(8,128)S(1)} %get-tuple-element.82), kind=kLoop, calls=%fused_computation.219 | loop fusion | flops 262144 | bytes 525312 | tf_op jit(solution)/shard_map/stack | solution.py:199
  3.2 5.9 %fusion.118 = (f32[32,32,128]{2,1,0:T(8,128)S(1)}, f32[32,8,32,128]{3,2,1,0:T(8,128)}, f32[32,8,32,128]{3,2,1,0:T(8,128)}) fusion(f32[8,32]{1,0:T(8,128)S(1)} %get-tuple-element.83, bf16[64,8,32,128]{3,2,1,0:T(8,128)(2,1)} %param.11, f32[32]{0:T(128)S(1)} %get-tuple-element.84, f32[8,32,128]{2,1,0:T(8,128)S(1)} %get-tuple-element.73, ...), kind=kLoop, calls=%fused_computation.250 | loop fusion | flops 11403264 | bytes 13239552 | tf_op jit(solution)/shard_map/reduce_sum | solution.py:220
  9.2 3.0 %collective-permute-start = (f32[16,32,128]{2,1,0:T(8,128)S(1)}, f32[16,32,128]{2,1,0:T(8,128)S(1)}, u32[]{:S(2)}, u32[]{:S(2)}) collective-permute-start(f32[16,32,128]{2,1,0:T(8,128)S(1)} %slice_select_fusion.2), channel_id=1, source_target_pairs={{0,4},{4,0},{8,12},{12,8},{16,20},{20,16},{24,28},{28,24},{1,5},{5... | collective-permute-start | bytes 786440 | tf_op jit(solution)/shard_map/ppermute | solution.py:131
  12.2 2.7 %reduce_sum.55 = f32[32,32,128]{2,1,0:T(8,128)S(1)} reduce(f32[32,8,32,128]{3,2,1,0:T(8,128)} %get-tuple-element.21, f32[]{:T(128)} %constant.67.clone.1), dimensions={1}, to_apply=%region_1.2 | reduce | flops 917504 | bytes 4718596 | tf_op jit(solution)/shard_map/reduce_sum | solution.py:220
  15.0 0.0 copy-start.3
  15.0 0.1 collective-permute-start.2
  15.1 4.2 %collective-permute-done = f32[16,32,128]{2,1,0:T(8,128)S(1)} collective-permute-done((f32[16,32,128]{2,1,0:T(8,128)S(1)}, f32[16,32,128]{2,1,0:T(8,128)S(1)}, u32[]{:S(2)}, u32[]{:S(2)}) %collective-permute-start) | collective-permute-done | bytes 262176 | tf_op jit(solution)/shard_map/ppermute | solution.py:131
  19.3 0.1 fusion.106
  19.4 2.2 %collective-permute-start.1 = (f32[16,32,128]{2,1,0:T(8,128)S(1)}, f32[16,32,128]{2,1,0:T(8,128)S(1)}, u32[]{:S(2)}, u32[]{:S(2)}) collective-permute-start(f32[16,32,128]{2,1,0:T(8,128)S(1)} %fusion.106), channel_id=1, source_target_pairs={{0,8},{4,12},{8,16},{12,20},{16,24},{20,28},{24,0},{28,4},{1,9},{5... | collective-permute-start | bytes 786440 | tf_op jit(solution)/shard_map/ppermute | solution.py:131
  21.6 4.5 %fusion = f32[32,7,32,128]{3,2,1,0:T(8,128)} fusion(f32[32,8,32,128]{3,2,1,0:T(8,128)} %get-tuple-element.21), kind=kOutput, calls=%fused_computation.11 | output fusion | flops 5505024 | bytes 7340032 | tf_op jit(solution)/shard_map/jit(cumsum)/reduce_window_sum | solution.py:225
  26.1 1.8 %collective-permute-done.1 = f32[16,32,128]{2,1,0:T(8,128)S(1)} collective-permute-done((f32[16,32,128]{2,1,0:T(8,128)S(1)}, f32[16,32,128]{2,1,0:T(8,128)S(1)}, u32[]{:S(2)}, u32[]{:S(2)}) %collective-permute-start.1) | collective-permute-done | bytes 262176 | tf_op jit(solution)/shard_map/ppermute | solution.py:131
  27.9 0.8 select_add_fusion.3
  28.7 1.0 %collective-permute-start.3 = (f32[16,32,128]{2,1,0:T(8,128)}, f32[16,32,128]{2,1,0:T(8,128)}, u32[]{:S(2)}, u32[]{:S(2)}) collective-permute-start(f32[16,32,128]{2,1,0:T(8,128)} %select_add_fusion.3), channel_id=1, source_target_pairs={{0,16},{4,20},{8,24},{12,28},{16,0},{20,4},{24,8},{28,12},{1,17},{... | collective-permute-start | bytes 786440 | tf_op jit(solution)/shard_map/ppermute | solution.py:131
  29.7 0.7 fusion.107
  30.5 1.6 %collective-permute-start.4 = (f32[16,32,128]{2,1,0:T(8,128)}, f32[16,32,128]{2,1,0:T(8,128)S(1)}, u32[]{:S(2)}, u32[]{:S(2)}) collective-permute-start(f32[16,32,128]{2,1,0:T(8,128)} %fusion.107), channel_id=1, source_target_pairs={{0,8},{4,12},{8,16},{12,20},{16,24},{20,28},{24,0},{28,4},{1,9},{5... | collective-permute-start | bytes 786440 | tf_op jit(solution)/shard_map/ppermute | solution.py:131
  32.0 0.6 broadcast_select_fusion.12
  32.7 0.0 collective-permute-start.6
  32.7 1.2 %collective-permute-start.5 = (f32[2,8,1,128]{3,2,1,0:T(1,128)}, f32[2,8,1,128]{3,2,1,0:T(1,128)}, u32[]{:S(2)}, u32[]{:S(2)}) collective-permute-start(f32[2,8,1,128]{3,2,1,0:T(1,128)} %get-tuple-element.71), channel_id=1, source_target_pairs={{1,2},{2,1},{5,6},{6,5},{9,10},{10,9},{13,14},{14,13},{17,18},{18,... | collective-permute-start | bytes 24584 | tf_op jit(solution)/shard_map/ppermute | solution.py:47
  33.9 4.5 %fusion.2 = f32[32,7,32,128]{3,2,1,0:T(8,128)} fusion(f32[32,8,32,128]{3,2,1,0:T(8,128)} %get-tuple-element.52), kind=kOutput, calls=%fused_computation.13 | output fusion | flops 5505024 | bytes 7340032 | tf_op jit(solution)/shard_map/jit(cumsum)/reduce_window_sum | solution.py:225
  38.4 0.8 broadcast_select_fusion.10
  39.2 6.9 %collective-permute-done.3 = f32[16,32,128]{2,1,0:T(8,128)} collective-permute-done((f32[16,32,128]{2,1,0:T(8,128)}, f32[16,32,128]{2,1,0:T(8,128)}, u32[]{:S(2)}, u32[]{:S(2)}) %collective-permute-start.3) | collective-permute-done | bytes 262176 | tf_op jit(solution)/shard_map/ppermute | solution.py:131
  46.1 0.0 collective-permute-done.4
  46.1 0.1 fusion.117
  46.2 0.1 add_select_fusion.1
  46.3 1.6 %collective-permute-start.7 = (f32[16,32,128]{2,1,0:T(8,128)S(1)}, f32[16,32,128]{2,1,0:T(8,128)S(1)}, u32[]{:S(2)}, u32[]{:S(2)}) collective-permute-start(f32[16,32,128]{2,1,0:T(8,128)S(1)} %add_select_fusion.1), channel_id=1, source_target_pairs={{0,4},{4,0},{8,12},{12,8},{16,20},{20,16},{24,28},{28,24},{1,5},{5... | collective-permute-start | bytes 786440 | tf_op jit(solution)/shard_map/ppermute | solution.py:131
  47.9 1.1 %select_add_fusion.2 = f32[16,32,128]{2,1,0:T(8,128)S(1)} fusion(f32[16,32,128]{2,1,0:T(8,128)} %fusion.107, f32[16,32,128]{2,1,0:T(8,128)S(1)} %collective-permute-done.4, pred[]{:T(512)S(6)} %ge.8), kind=kLoop, calls=%fused_computation.192 | loop fusion | flops 131072 | bytes 786433 | tf_op jit(solution)/shard_map/add | solution.py:97
  49.0 0.0 copy-start
  49.0 2.3 %collective-permute-start.8 = (f32[16,32,128]{2,1,0:T(8,128)S(1)}, f32[16,32,128]{2,1,0:T(8,128)S(1)}, u32[]{:S(2)}, u32[]{:S(2)}) collective-permute-start(f32[16,32,128]{2,1,0:T(8,128)S(1)} %select_add_fusion.2), channel_id=1, source_target_pairs={{0,16},{4,20},{8,24},{12,28},{16,0},{20,4},{24,8},{28,12},{1,17},{... | collective-permute-start | bytes 786440 | tf_op jit(solution)/shard_map/ppermute | solution.py:131
  51.3 0.8 slice_select_fusion.4
  52.1 0.5 collective-permute-start.10
  52.6 0.7 collective-permute-start.9
  53.2 0.7 broadcast_multiply_fusion.1
  54.0 2.0 %collective-permute-done.10 = f32[2,1,32,128]{3,2,1,0:T(8,128)S(1)} collective-permute-done((f32[2,1,32,128]{3,2,1,0:T(8,128)S(1)}, f32[2,1,32,128]{3,2,1,0:T(8,128)S(1)}, u32[]{:S(2)}, u32[]{:S(2)}) %collective-permute-start.10) | collective-permute-done | bytes 32800 | tf_op jit(solution)/shard_map/ppermute | solution.py:44
  56.0 0.0 collective-permute-done.9
  56.0 5.4 %collective-permute-done.8 = f32[16,32,128]{2,1,0:T(8,128)S(1)} collective-permute-done((f32[16,32,128]{2,1,0:T(8,128)S(1)}, f32[16,32,128]{2,1,0:T(8,128)S(1)}, u32[]{:S(2)}, u32[]{:S(2)}) %collective-permute-start.8) | collective-permute-done | bytes 262176 | tf_op jit(solution)/shard_map/ppermute | solution.py:131
  61.4 0.1 fusion.116
  61.5 0.1 add_select_fusion
  61.6 2.1 %collective-permute-start.11 = (f32[16,32,128]{2,1,0:T(8,128)S(1)}, f32[16,32,128]{2,1,0:T(8,128)S(1)}, u32[]{:S(2)}, u32[]{:S(2)}) collective-permute-start(f32[16,32,128]{2,1,0:T(8,128)S(1)} %add_select_fusion), channel_id=1, source_target_pairs={{0,4},{4,0},{8,12},{12,8},{16,20},{20,16},{24,28},{28,24},{1,5},{5... | collective-permute-start | bytes 786440 | tf_op jit(solution)/shard_map/ppermute | solution.py:131
  63.7 0.1 fusion.7
  63.8 0.5 power_multiply_fusion.2
  64.3 0.2 fusion.119
  64.6 0.0 copy-start.8
  64.6 4.0 %multiply_reduce_fusion.2 = (f32[8,32,128]{2,1,0:T(8,128)S(1)}, f32[8,32,128]{2,1,0:T(8,128)S(1)}, bf16[32,8,32,128]{3,2,1,0:T(8,128)(2,1)S(1)}) fusion(f32[32,8,32,128]{3,2,1,0:T(8,128)S(1)} %copy-done, f32[32,7,32,128]{3,2,1,0:T(8,128)} %fusion.2, f32[32,32,128]{2,1,0:T(8,128)S(1)} %get-tuple-element.86, f32[32,32,128]{2,1,0:T(8,128)S(1)} %get-tuple-element.57, ...), kind=kLoop, calls=%fused_computation.4 | loop fusion | flops 13565952 | bytes 13369472 | tf_op jit(solution)/shard_map/reduce_sum | solution.py:232
  68.6 0.6 fusion.20
  69.3 0.9 %collective-permute-done.11 = f32[16,32,128]{2,1,0:T(8,128)S(1)} collective-permute-done((f32[16,32,128]{2,1,0:T(8,128)S(1)}, f32[16,32,128]{2,1,0:T(8,128)S(1)}, u32[]{:S(2)}, u32[]{:S(2)}) %collective-permute-start.11) | collective-permute-done | bytes 262176 | tf_op jit(solution)/shard_map/ppermute | solution.py:131
  70.2 0.1 maximum_select_fusion.1
  70.3 0.0 copy-start.4
  70.3 2.7 %multiply_reduce_fusion.1 = (f32[8,32,128]{2,1,0:T(8,128)S(1)}, f32[8,32,128]{2,1,0:T(8,128)S(1)}, bf16[32,8,32,128]{3,2,1,0:T(8,128)(2,1)S(1)}) fusion(f32[32,7,32,128]{3,2,1,0:T(8,128)S(1)} %copy-done.2, f32[32,32,128]{2,1,0:T(8,128)S(1)} %maximum_select_fusion.1, f32[32,32,128]{2,1,0:T(8,128)S(1)} %get-tuple-element.56, f32[32]{0:T(128)S(1)} %copy-done.8, ...), kind=kLoop, calls=%fused_computation.2 | loop fusion | flops 15663104 | bytes 9307264 | tf_op jit(solution)/shard_map/reduce_sum | solution.py:231
  73.0 0.8 broadcast_multiply_fusion
  73.8 0.1 fusion.112
  73.9 0.7 collective-permute-start.12
  74.6 3.4 %collective-permute-start.13 = (f32[2,1,32,128]{3,2,1,0:T(8,128)S(1)}, f32[2,1,32,128]{3,2,1,0:T(8,128)S(1)}, u32[]{:S(2)}, u32[]{:S(2)}) collective-permute-start(f32[2,1,32,128]{3,2,1,0:T(8,128)S(1)} %get-tuple-element.67), channel_id=1, source_target_pairs={{0,4},{4,0},{8,12},{12,8},{16,20},{20,16},{24,28},{28,24},{1,5},{5... | collective-permute-start | bytes 98312 | tf_op jit(solution)/shard_map/ppermute | solution.py:44
  78.0 0.6 collective-permute-start.14
  78.7 2.9 %collective-permute-start.15 = (f32[2,8,1,128]{3,2,1,0:T(1,128)S(1)}, f32[2,8,1,128]{3,2,1,0:T(1,128)S(1)}, u32[]{:S(2)}, u32[]{:S(2)}) collective-permute-start(f32[2,8,1,128]{3,2,1,0:T(1,128)S(1)} %bitcast.81), channel_id=1, source_target_pairs={{0,1},{1,0},{2,3},{3,2},{4,5},{5,4},{6,7},{7,6},{8,9},{9,8},{10,11... | collective-permute-start | bytes 24584 | tf_op jit(solution)/shard_map/ppermute | solution.py:44
  81.6 2.4 %pad_maximum_fusion = bf16[64,8,32,128]{3,2,1,0:T(8,128)(2,1)} fusion(bf16[32,8,32,128]{3,2,1,0:T(8,128)(2,1)S(1)} %get-tuple-element.53, bf16[32,8,32,128]{3,2,1,0:T(8,128)(2,1)S(1)} %get-tuple-element.30), kind=kLoop, calls=%fused_computation | loop fusion | flops 2097152 | bytes 8388608 | tf_op jit(solution)/shard_map/dynamic_update_slice | solution.py:252
  84.0 0.0 collective-permute-done.14
  84.0 0.0 collective-permute-done.15
  84.0 0.0 collective-permute-done.12
  84.0 0.1 fusion.9
  84.1 0.5 power_multiply_fusion
  84.6 0.7 fusion.29
  85.3 0.9 %fusion.93 = (f32[8,32,128]{2,1,0:T(8,128)}, f32[8,32,128]{2,1,0:T(8,128)}) fusion(f32[2,8,32,128]{3,2,1,0:T(8,128)S(1)} %fusion.29, f32[8,32]{1,0:T(8,128)S(1)} %get-tuple-element.82, f32[8,32,128]{2,1,0:T(8,128)S(1)} %get-tuple-element.37, f32[8,32,128]{2,1,0:T(8,128)S(1)} %get-tuple-element.39, f32[2,8,32,128]{3,2,1,0:T(8,128)S(1)} %fusion.20, ...), kind=kLoop, calls=%fused_computation.200 | loop fusion | flops 1081344 | bytes 1442816 | tf_op jit(solution)/shard_map/add | solution.py:271
  (33 shorter events, 0.2 us)
Async XLA Ops:
  2.1 7.0 %copy-start.7 = (f32[32]{0:T(128)}, f32[32]{0:T(128)S(1)}, u32[]{:S(2)}) copy-start(f32[32]{0:T(128)S(1)} %get-tuple-element.85) | copy-start | bytes 388
  2.1 7.0 %copy-start.9 = (f32[32]{0:T(128)}, f32[32]{0:T(128)S(1)}, u32[]{:S(2)}) copy-start(f32[32]{0:T(128)S(1)} %get-tuple-element.84) | copy-start | bytes 388
  9.2 10.2 %collective-permute-start = (f32[16,32,128]{2,1,0:T(8,128)S(1)}, f32[16,32,128]{2,1,0:T(8,128)S(1)}, u32[]{:S(2)}, u32[]{:S(2)}) collective-permute-start(f32[16,32,128]{2,1,0:T(8,128)S(1)} %slice_select_fusion.2), channel_id=1, source_target_pairs={{0,4},{4,0},{8,12},{12,8},{16,20},{20,16},{24,28},{28,24},{1,5},{5... | collective-permute-start | bytes 786440 | tf_op jit(solution)/shard_map/ppermute | solution.py:131
  15.0 11.1 %copy-start.3 = (f32[8,32,128]{2,1,0:T(8,128)S(1)}, f32[8,32,128]{2,1,0:T(8,128)}, u32[]{:S(2)}) copy-start(f32[8,32,128]{2,1,0:T(8,128)} %param.8) | copy-start | bytes 393220
  15.0 11.1 %collective-permute-start.2 = (f32[16,32,128]{2,1,0:T(8,128)S(1)}, f32[16,32,128]{2,1,0:T(8,128)S(1)}, u32[]{:S(2)}, u32[]{:S(2)}) collective-permute-start(f32[16,32,128]{2,1,0:T(8,128)S(1)} %slice_select_fusion.1), channel_id=1, source_target_pairs={{0,4},{4,0},{8,12},{12,8},{16,20},{20,16},{24,28},{28,24},{1,5},{5... | collective-permute-start | bytes 786440 | tf_op jit(solution)/shard_map/ppermute | solution.py:131
  19.4 8.5 %collective-permute-start.1 = (f32[16,32,128]{2,1,0:T(8,128)S(1)}, f32[16,32,128]{2,1,0:T(8,128)S(1)}, u32[]{:S(2)}, u32[]{:S(2)}) collective-permute-start(f32[16,32,128]{2,1,0:T(8,128)S(1)} %fusion.106), channel_id=1, source_target_pairs={{0,8},{4,12},{8,16},{12,20},{16,24},{20,28},{24,0},{28,4},{1,9},{5... | collective-permute-start | bytes 786440 | tf_op jit(solution)/shard_map/ppermute | solution.py:131
  26.1 7.8 %copy-start.6 = (f32[2,8,32,128]{3,2,1,0:T(8,128)}, f32[2,8,32,128]{3,2,1,0:T(8,128)S(1)}, u32[]{:S(2)}) copy-start(f32[2,8,32,128]{3,2,1,0:T(8,128)S(1)} %pad_maximum_fusion.40) | copy-start | bytes 786436
  28.7 17.4 %collective-permute-start.3 = (f32[16,32,128]{2,1,0:T(8,128)}, f32[16,32,128]{2,1,0:T(8,128)}, u32[]{:S(2)}, u32[]{:S(2)}) collective-permute-start(f32[16,32,128]{2,1,0:T(8,128)} %select_add_fusion.3), channel_id=1, source_target_pairs={{0,16},{4,20},{8,24},{12,28},{16,0},{20,4},{24,8},{28,12},{1,17},{... | collective-permute-start | bytes 786440 | tf_op jit(solution)/shard_map/ppermute | solution.py:131
  30.5 15.7 %collective-permute-start.4 = (f32[16,32,128]{2,1,0:T(8,128)}, f32[16,32,128]{2,1,0:T(8,128)S(1)}, u32[]{:S(2)}, u32[]{:S(2)}) collective-permute-start(f32[16,32,128]{2,1,0:T(8,128)} %fusion.107), channel_id=1, source_target_pairs={{0,8},{4,12},{8,16},{12,20},{16,24},{20,28},{24,0},{28,4},{1,9},{5... | collective-permute-start | bytes 786440 | tf_op jit(solution)/shard_map/ppermute | solution.py:131
  32.7 5.7 %collective-permute-start.6 = (f32[2,8,1,128]{3,2,1,0:T(1,128)}, f32[2,8,1,128]{3,2,1,0:T(1,128)S(1)}, u32[]{:S(2)}, u32[]{:S(2)}) collective-permute-start(f32[2,8,1,128]{3,2,1,0:T(1,128)} %get-tuple-element.70), channel_id=1, source_target_pairs={{0,1},{1,0},{2,3},{3,2},{4,5},{5,4},{6,7},{7,6},{8,9},{9,8},{10,11... | collective-permute-start | bytes 24584 | tf_op jit(solution)/shard_map/ppermute | solution.py:44
  32.7 5.7 %collective-permute-start.5 = (f32[2,8,1,128]{3,2,1,0:T(1,128)}, f32[2,8,1,128]{3,2,1,0:T(1,128)}, u32[]{:S(2)}, u32[]{:S(2)}) collective-permute-start(f32[2,8,1,128]{3,2,1,0:T(1,128)} %get-tuple-element.71), channel_id=1, source_target_pairs={{1,2},{2,1},{5,6},{6,5},{9,10},{10,9},{13,14},{14,13},{17,18},{18,... | collective-permute-start | bytes 24584 | tf_op jit(solution)/shard_map/ppermute | solution.py:47
  38.4 25.9 %copy-start.5 = (f32[64,32,128]{2,1,0:T(8,128)S(1)}, f32[64,32,128]{2,1,0:T(8,128)}, u32[]{:S(2)}) copy-start(f32[64,32,128]{2,1,0:T(8,128)} %param.12) | copy-start | bytes 3145732
  46.3 9.7 %collective-permute-start.7 = (f32[16,32,128]{2,1,0:T(8,128)S(1)}, f32[16,32,128]{2,1,0:T(8,128)S(1)}, u32[]{:S(2)}, u32[]{:S(2)}) collective-permute-start(f32[16,32,128]{2,1,0:T(8,128)S(1)} %add_select_fusion.1), channel_id=1, source_target_pairs={{0,4},{4,0},{8,12},{12,8},{16,20},{20,16},{24,28},{28,24},{1,5},{5... | collective-permute-start | bytes 786440 | tf_op jit(solution)/shard_map/ppermute | solution.py:131
  47.9 16.7 %copy-start.1 = (bf16[64,8,32,128]{3,2,1,0:T(8,128)(2,1)S(1)}, bf16[64,8,32,128]{3,2,1,0:T(8,128)(2,1)}, u32[]{:S(2)}) copy-start(bf16[64,8,32,128]{3,2,1,0:T(8,128)(2,1)} %param.11) | copy-start | bytes 12582916
  49.0 15.6 %copy-start = (f32[32,8,32,128]{3,2,1,0:T(8,128)S(1)}, f32[32,8,32,128]{3,2,1,0:T(8,128)}, u32[]{:S(2)}) copy-start(f32[32,8,32,128]{3,2,1,0:T(8,128)} %get-tuple-element.52) | copy-start | bytes 12582916
  49.0 15.6 %copy-start.10 = (f32[32]{0:T(128)S(1)}, f32[32]{0:T(128)}, u32[]{:S(2)}) copy-start(f32[32]{0:T(128)} %copy-done.9) | copy-start | bytes 388
  49.0 12.4 %collective-permute-start.8 = (f32[16,32,128]{2,1,0:T(8,128)S(1)}, f32[16,32,128]{2,1,0:T(8,128)S(1)}, u32[]{:S(2)}, u32[]{:S(2)}) collective-permute-start(f32[16,32,128]{2,1,0:T(8,128)S(1)} %select_add_fusion.2), channel_id=1, source_target_pairs={{0,16},{4,20},{8,24},{12,28},{16,0},{20,4},{24,8},{28,12},{1,17},{... | collective-permute-start | bytes 786440 | tf_op jit(solution)/shard_map/ppermute | solution.py:131
  52.1 3.9 %collective-permute-start.10 = (f32[2,1,32,128]{3,2,1,0:T(8,128)S(1)}, f32[2,1,32,128]{3,2,1,0:T(8,128)S(1)}, u32[]{:S(2)}, u32[]{:S(2)}) collective-permute-start(f32[2,1,32,128]{3,2,1,0:T(8,128)S(1)} %get-tuple-element.68), channel_id=1, source_target_pairs={{0,4},{4,0},{8,12},{12,8},{16,20},{20,16},{24,28},{28,24},{1,5},{5... | collective-permute-start | bytes 98312 | tf_op jit(solution)/shard_map/ppermute | solution.py:44
  52.6 3.4 %collective-permute-start.9 = (f32[2,1,32,128]{3,2,1,0:T(8,128)S(1)}, f32[2,1,32,128]{3,2,1,0:T(8,128)S(1)}, u32[]{:S(2)}, u32[]{:S(2)}) collective-permute-start(f32[2,1,32,128]{3,2,1,0:T(8,128)S(1)} %get-tuple-element.69), channel_id=1, source_target_pairs={{4,8},{12,16},{20,24},{8,4},{16,12},{24,20},{5,9},{13,17},{21,25},... | collective-permute-start | bytes 98312 | tf_op jit(solution)/shard_map/ppermute | solution.py:47
  61.6 8.6 %collective-permute-start.11 = (f32[16,32,128]{2,1,0:T(8,128)S(1)}, f32[16,32,128]{2,1,0:T(8,128)S(1)}, u32[]{:S(2)}, u32[]{:S(2)}) collective-permute-start(f32[16,32,128]{2,1,0:T(8,128)S(1)} %add_select_fusion), channel_id=1, source_target_pairs={{0,4},{4,0},{8,12},{12,8},{16,20},{20,16},{24,28},{28,24},{1,5},{5... | collective-permute-start | bytes 786440 | tf_op jit(solution)/shard_map/ppermute | solution.py:131
  64.6 5.7 %copy-start.2 = (f32[32,7,32,128]{3,2,1,0:T(8,128)S(1)}, f32[32,7,32,128]{3,2,1,0:T(8,128)}, u32[]{:S(2)}) copy-start(f32[32,7,32,128]{3,2,1,0:T(8,128)} %fusion) | copy-start | bytes 11010052
  64.6 5.7 %copy-start.8 = (f32[32]{0:T(128)S(1)}, f32[32]{0:T(128)}, u32[]{:S(2)}) copy-start(f32[32]{0:T(128)} %copy-done.7) | copy-start | bytes 388
  70.3 2.7 %copy-start.4 = (f32[8,32,128]{2,1,0:T(8,128)S(1)}, f32[8,32,128]{2,1,0:T(8,128)}, u32[]{:S(2)}) copy-start(f32[8,32,128]{2,1,0:T(8,128)} %param.9) | copy-start | bytes 393220
  73.9 10.0 %collective-permute-start.12 = (f32[2,1,32,128]{3,2,1,0:T(8,128)S(1)}, f32[2,1,32,128]{3,2,1,0:T(8,128)S(1)}, u32[]{:S(2)}, u32[]{:S(2)}) collective-permute-start(f32[2,1,32,128]{3,2,1,0:T(8,128)S(1)} %get-tuple-element.66), channel_id=1, source_target_pairs={{4,8},{12,16},{20,24},{8,4},{16,12},{24,20},{5,9},{13,17},{21,25},... | collective-permute-start | bytes 98312 | tf_op jit(solution)/shard_map/ppermute | solution.py:47
  74.6 9.4 %collective-permute-start.13 = (f32[2,1,32,128]{3,2,1,0:T(8,128)S(1)}, f32[2,1,32,128]{3,2,1,0:T(8,128)S(1)}, u32[]{:S(2)}, u32[]{:S(2)}) collective-permute-start(f32[2,1,32,128]{3,2,1,0:T(8,128)S(1)} %get-tuple-element.67), channel_id=1, source_target_pairs={{0,4},{4,0},{8,12},{12,8},{16,20},{20,16},{24,28},{28,24},{1,5},{5... | collective-permute-start | bytes 98312 | tf_op jit(solution)/shard_map/ppermute | solution.py:44
  78.0 6.0 %collective-permute-start.14 = (f32[2,8,1,128]{3,2,1,0:T(1,128)S(1)}, f32[2,8,1,128]{3,2,1,0:T(1,128)S(1)}, u32[]{:S(2)}, u32[]{:S(2)}) collective-permute-start(f32[2,8,1,128]{3,2,1,0:T(1,128)S(1)} %get-tuple-element.44), channel_id=1, source_target_pairs={{1,2},{2,1},{5,6},{6,5},{9,10},{10,9},{13,14},{14,13},{17,18},{18,... | collective-permute-start | bytes 24584 | tf_op jit(solution)/shard_map/ppermute | solution.py:47
  78.7 5.3 %collective-permute-start.15 = (f32[2,8,1,128]{3,2,1,0:T(1,128)S(1)}, f32[2,8,1,128]{3,2,1,0:T(1,128)S(1)}, u32[]{:S(2)}, u32[]{:S(2)}) collective-permute-start(f32[2,8,1,128]{3,2,1,0:T(1,128)S(1)} %bitcast.81), channel_id=1, source_target_pairs={{0,1},{1,0},{2,3},{3,2},{4,5},{5,4},{6,7},{7,6},{8,9},{9,8},{10,11... | collective-permute-start | bytes 24584 | tf_op jit(solution)/shard_map/ppermute | solution.py:44

commit v21 on v19

--- a/solution.py
+++ b/solution.py
@@ -239,9 +239,9 @@
 
     lines = earlier_spectral_power.shape[0]
     made, first_faces = pipelined_scan(
-        totals_of, emit, lines, "beam", {2: tied_faces(cross_faces), 3: tied_faces(beam_faces)}
-    )
-    first_bordered = bordered_fields(physical_quantities, first_faces[3], first_faces[2])
+        totals_of, emit, lines, "beam", {2: tied_faces(beam_faces), 3: tied_faces(cross_faces)}
+    )
+    first_bordered = bordered_fields(physical_quantities, first_faces[2], first_faces[3])
     spectral_power = jnp.zeros(earlier_spectral_power.shape, jnp.bfloat16)
     start = 0
     for part, _, _ in made:

time: 83.8 us -> 88.2 us (1.053)
  the two profiles are of different devices: /device:TPU:9 before, /device:TPU:0 now
where the time goes in v21:
time: 88.2 us; the launch traced here: 87.6 us
  starting transfers between devices  41.2 us (47%)
  other arithmetic  37.9 us (43%)
  waiting for transfers between devices  6.56 us (7%)
  between operations  1.02 us (1%)
    ppermute x8, starting transfers between devices, pipelined_scan(): lax.ppermute(payload, axis, pairs)  28.5 us
    ppermute x4, starting transfers between devices, faces(): lax.ppermute(jnp.where(is_even, last, first), axis, [(i, i ^ 1) for i in...  9.47 us
    reduce_sum x2, other arithmetic, totals_of(): return jnp.sum(optical_depth, axis=1)  8.64 us
    another operation x2, other arithmetic, emit(): jnp.cumsum(optical_depth[:, :rows - 1], axis=1)  6.8 us
    ppermute x8, waiting for transfers between devices, pipelined_scan(): lax.ppermute(payload, axis, pairs)  6.54 us
    reduce_sum x1, other arithmetic, emit(): jnp.sum(radiance * (1.0 - jnp.exp(-optical_depth)), axis=0)  4.02 us
    ppermute x4, starting transfers between devices, faces(): across = lax.ppermute(jnp.where(is_even, first, last), axis, pairs)  3.23 us
    reduce_sum x1, other arithmetic, emit(): jnp.sum(weight * radiance, axis=0)  2.68 us
  transfers between devices with their start and end apart: 16, of which 3 were waited for; matrix products, arithmetic and copies ran while one was open for 26% of the time, Pallas kernels for 0%

profile of v21, /device:TPU:0, one launch (start us, length us, event | category | flops | bytes accessed | tf_op | source)
XLA Modules:
  0.0 87.6 jit_solution(3403292076210543108)
XLA Ops:
  0.6 0.7 convert_subtract_fusion
  1.3 0.8 fusion.120
  2.1 1.1 %add_bitcast_fusion = (f32[1,8,32,128]{3,2,1,0:T(8,128)S(1)}, f32[8,32,128]{2,1,0:T(8,128)S(1)}) fusion(f32[8,32,128]{2,1,0:T(8,128)} %param.9, f32[8,32,128]{2,1,0:T(8,128)} %param.10, f32[8,32]{1,0:T(8,128)S(1)} %get-tuple-element.82), kind=kLoop, calls=%fused_computation.215 | loop fusion | flops 262144 | bytes 525312 | tf_op jit(solution)/shard_map/stack | solution.py:195
  3.2 5.9 %fusion.118 = (f32[32,32,128]{2,1,0:T(8,128)S(1)}, f32[32,8,32,128]{3,2,1,0:T(8,128)}, f32[32,8,32,128]{3,2,1,0:T(8,128)}) fusion(f32[8,32]{1,0:T(8,128)S(1)} %get-tuple-element.83, bf16[64,8,32,128]{3,2,1,0:T(8,128)(2,1)} %param.11, f32[32]{0:T(128)S(1)} %get-tuple-element.84, f32[8,32,128]{2,1,0:T(8,128)S(1)} %get-tuple-element.73, ...), kind=kLoop, calls=%fused_computation.246 | loop fusion | flops 11403264 | bytes 13239552 | tf_op jit(solution)/shard_map/reduce_sum | solution.py:216
  9.1 3.0 %collective-permute-start = (f32[16,32,128]{2,1,0:T(8,128)S(1)}, f32[16,32,128]{2,1,0:T(8,128)S(1)}, u32[]{:S(2)}, u32[]{:S(2)}) collective-permute-start(f32[16,32,128]{2,1,0:T(8,128)S(1)} %slice_select_fusion.2), channel_id=1, source_target_pairs={{0,4},{4,0},{8,12},{12,8},{16,20},{20,16},{24,28},{28,24},{1,5},{5... | collective-permute-start | bytes 786440 | tf_op jit(solution)/shard_map/ppermute | solution.py:127
  12.2 2.7 %reduce_sum.55 = f32[32,32,128]{2,1,0:T(8,128)S(1)} reduce(f32[32,8,32,128]{3,2,1,0:T(8,128)} %get-tuple-element.21, f32[]{:T(128)} %constant.65.clone.1), dimensions={1}, to_apply=%region_1.2 | reduce | flops 917504 | bytes 4718596 | tf_op jit(solution)/shard_map/reduce_sum | solution.py:216
  15.0 0.0 copy-start.4
  15.0 0.1 collective-permute-start.2
  15.1 4.2 %collective-permute-done = f32[16,32,128]{2,1,0:T(8,128)S(1)} collective-permute-done((f32[16,32,128]{2,1,0:T(8,128)S(1)}, f32[16,32,128]{2,1,0:T(8,128)S(1)}, u32[]{:S(2)}, u32[]{:S(2)}) %collective-permute-start) | collective-permute-done | bytes 262176 | tf_op jit(solution)/shard_map/ppermute | solution.py:127
  19.3 0.1 fusion.106
  19.4 0.0 copy-start
  19.4 4.3 %collective-permute-start.1 = (f32[16,32,128]{2,1,0:T(8,128)S(1)}, f32[16,32,128]{2,1,0:T(8,128)S(1)}, u32[]{:S(2)}, u32[]{:S(2)}) collective-permute-start(f32[16,32,128]{2,1,0:T(8,128)S(1)} %fusion.106), channel_id=1, source_target_pairs={{0,8},{4,12},{8,16},{12,20},{16,24},{20,28},{1,9},{5,13},{9,17},{1... | collective-permute-start | bytes 786440 | tf_op jit(solution)/shard_map/ppermute | solution.py:127
  23.7 4.5 %fusion = f32[32,7,32,128]{3,2,1,0:T(8,128)} fusion(f32[32,8,32,128]{3,2,1,0:T(8,128)} %get-tuple-element.21), kind=kOutput, calls=%fused_computation.11 | output fusion | flops 5505024 | bytes 7340032 | tf_op jit(solution)/shard_map/jit(cumsum)/reduce_window_sum | solution.py:221
  28.2 0.0 collective-permute-done.1
  28.2 0.8 add.218
  29.0 5.4 %collective-permute-start.3 = (f32[16,32,128]{2,1,0:T(8,128)}, f32[16,32,128]{2,1,0:T(8,128)}, u32[]{:S(2)}, u32[]{:S(2)}) collective-permute-start(f32[16,32,128]{2,1,0:T(8,128)} %add.218), channel_id=1, source_target_pairs={{0,16},{4,20},{8,24},{12,28},{1,17},{5,21},{9,25},{13,29},{2,18},{... | collective-permute-start | bytes 786440 | tf_op jit(solution)/shard_map/ppermute | solution.py:127
  34.4 0.8 fusion.107
  35.2 3.5 %collective-permute-start.4 = (f32[16,32,128]{2,1,0:T(8,128)}, f32[16,32,128]{2,1,0:T(8,128)S(1)}, u32[]{:S(2)}, u32[]{:S(2)}) collective-permute-start(f32[16,32,128]{2,1,0:T(8,128)} %fusion.107), channel_id=1, source_target_pairs={{0,8},{4,12},{8,16},{12,20},{16,24},{20,28},{1,9},{5,13},{9,17},{1... | collective-permute-start | bytes 786440 | tf_op jit(solution)/shard_map/ppermute | solution.py:127
  38.7 0.6 slice_select_fusion.4
  39.3 1.5 %collective-permute-start.6 = (f32[2,1,32,128]{3,2,1,0:T(8,128)}, f32[2,1,32,128]{3,2,1,0:T(8,128)}, u32[]{:S(2)}, u32[]{:S(2)}) collective-permute-start(f32[2,1,32,128]{3,2,1,0:T(8,128)} %get-tuple-element.70), channel_id=1, source_target_pairs={{0,4},{4,0},{8,12},{12,8},{16,20},{20,16},{24,28},{28,24},{1,5},{5... | collective-permute-start | bytes 98312 | tf_op jit(solution)/shard_map/ppermute | solution.py:44
  40.8 1.3 %collective-permute-start.5 = (f32[2,1,32,128]{3,2,1,0:T(8,128)}, f32[2,1,32,128]{3,2,1,0:T(8,128)}, u32[]{:S(2)}, u32[]{:S(2)}) collective-permute-start(f32[2,1,32,128]{3,2,1,0:T(8,128)} %get-tuple-element.71), channel_id=1, source_target_pairs={{4,8},{12,16},{20,24},{8,4},{16,12},{24,20},{5,9},{13,17},{21,25},... | collective-permute-start | bytes 98312 | tf_op jit(solution)/shard_map/ppermute | solution.py:47
  42.1 2.3 %fusion.2 = f32[32,7,32,128]{3,2,1,0:T(8,128)} fusion(f32[32,8,32,128]{3,2,1,0:T(8,128)S(1)} %copy-done), kind=kOutput, calls=%fused_computation.13 | output fusion | flops 5505024 | bytes 7340032 | tf_op jit(solution)/shard_map/jit(cumsum)/reduce_window_sum | solution.py:221
  44.4 0.0 collective-permute-done.6
  44.4 0.0 collective-permute-done.5
  44.4 0.9 broadcast_select_fusion.12
  45.3 0.0 collective-permute-done.3
  45.3 1.0 %fusion.117 = (f32[16,32,128]{2,1,0:T(8,128)S(1)}, f32[16,32,128]{2,1,0:T(8,128)S(1)}) fusion(f32[16,32,128]{2,1,0:T(8,128)S(1)} %collective-permute-done, f32[16,32,128]{2,1,0:T(8,128)S(1)} %collective-permute-done.1, f32[16,32,128]{2,1,0:T(8,128)} %collective-permute-done.3), kind=kLoop, calls=%fused_computation.245 | loop fusion | flops 131072 | bytes 1310720 | tf_op jit(solution)/shard_map/add | solution.py:107
  46.3 0.1 add_select_fusion.1
  46.4 0.0 copy-start.1
  46.4 0.0 copy-start.2
  46.4 4.0 %collective-permute-start.7 = (f32[16,32,128]{2,1,0:T(8,128)S(1)}, f32[16,32,128]{2,1,0:T(8,128)S(1)}, u32[]{:S(2)}, u32[]{:S(2)}) collective-permute-start(f32[16,32,128]{2,1,0:T(8,128)S(1)} %add_select_fusion.1), channel_id=1, source_target_pairs={{0,4},{4,0},{8,12},{12,8},{16,20},{20,16},{24,28},{28,24},{1,5},{5... | collective-permute-start | bytes 786440 | tf_op jit(solution)/shard_map/ppermute | solution.py:127
  50.4 1.0 %add.222 = f32[16,32,128]{2,1,0:T(8,128)S(1)} add(f32[16,32,128]{2,1,0:T(8,128)} %fusion.107, f32[16,32,128]{2,1,0:T(8,128)S(1)} %collective-permute-done.4) | non-fusion elementwise | flops 65536 | bytes 786432 | tf_op jit(solution)/shard_map/add | solution.py:97
  51.4 6.7 %collective-permute-start.8 = (f32[16,32,128]{2,1,0:T(8,128)S(1)}, f32[16,32,128]{2,1,0:T(8,128)S(1)}, u32[]{:S(2)}, u32[]{:S(2)}) collective-permute-start(f32[16,32,128]{2,1,0:T(8,128)S(1)} %add.222), channel_id=1, source_target_pairs={{0,16},{4,20},{8,24},{12,28},{1,17},{5,21},{9,25},{13,29},{2,18},{... | collective-permute-start | bytes 786440 | tf_op jit(solution)/shard_map/ppermute | solution.py:127
  58.1 0.9 %broadcast_select_fusion.6 = (f32[2,8,1,128]{3,2,1,0:T(1,128)S(1)}, f32[2,8,1,128]{3,2,1,0:T(1,128)S(1)}) fusion(pred[]{:T(512)S(6)} %eq.18, f32[2,8,32,128]{3,2,1,0:T(8,128)} %copy-done.7), kind=kLoop, calls=%fused_computation.229 | loop fusion | flops 4096 | bytes 32769 | tf_op jit(solution)/shard_map/jit(_where)/select_n | solution.py:44
  59.0 0.1 collective-permute-start.10
  59.1 0.7 collective-permute-start.9
  59.7 0.7 broadcast_multiply_fusion.1
  60.5 0.0 collective-permute-done.10
  60.5 0.0 collective-permute-done.9
  60.5 1.6 %collective-permute-done.8 = f32[16,32,128]{2,1,0:T(8,128)S(1)} collective-permute-done((f32[16,32,128]{2,1,0:T(8,128)S(1)}, f32[16,32,128]{2,1,0:T(8,128)S(1)}, u32[]{:S(2)}, u32[]{:S(2)}) %collective-permute-start.8) | collective-permute-done | bytes 262176 | tf_op jit(solution)/shard_map/ppermute | solution.py:127
  62.1 0.1 fusion.116
  62.2 0.1 add_select_fusion
  62.3 1.5 %collective-permute-start.11 = (f32[16,32,128]{2,1,0:T(8,128)S(1)}, f32[16,32,128]{2,1,0:T(8,128)S(1)}, u32[]{:S(2)}, u32[]{:S(2)}) collective-permute-start(f32[16,32,128]{2,1,0:T(8,128)S(1)} %add_select_fusion), channel_id=1, source_target_pairs={{0,4},{4,0},{8,12},{12,8},{16,20},{20,16},{24,28},{28,24},{1,5},{5... | collective-permute-start | bytes 786440 | tf_op jit(solution)/shard_map/ppermute | solution.py:127
  63.8 0.1 fusion.7
  63.8 0.5 power_multiply_fusion.2
  64.4 0.2 fusion.119
  64.6 4.0 %multiply_reduce_fusion.2 = (f32[8,32,128]{2,1,0:T(8,128)S(1)}, f32[8,32,128]{2,1,0:T(8,128)S(1)}, bf16[32,8,32,128]{3,2,1,0:T(8,128)(2,1)S(1)}) fusion(f32[32,8,32,128]{3,2,1,0:T(8,128)S(1)} %copy-done.1, f32[32,7,32,128]{3,2,1,0:T(8,128)} %fusion.2, f32[32,32,128]{2,1,0:T(8,128)S(1)} %get-tuple-element.86, f32[32,32,128]{2,1,0:T(8,128)S(1)} %get-tuple-element.57, ...), kind=kLoop, calls=%fused_computation.4 | loop fusion | flops 13565952 | bytes 13369472 | tf_op jit(solution)/shard_map/reduce_sum | solution.py:228
  68.7 0.6 fusion.20
  69.3 0.7 collective-permute-done.11
  70.0 0.1 maximum_select_fusion.1
  70.1 0.0 copy-start.5
  70.1 2.7 %multiply_reduce_fusion.1 = (f32[8,32,128]{2,1,0:T(8,128)S(1)}, f32[8,32,128]{2,1,0:T(8,128)S(1)}, bf16[32,8,32,128]{3,2,1,0:T(8,128)(2,1)S(1)}) fusion(f32[32,7,32,128]{3,2,1,0:T(8,128)S(1)} %copy-done.3, f32[32,32,128]{2,1,0:T(8,128)S(1)} %maximum_select_fusion.1, f32[32,32,128]{2,1,0:T(8,128)S(1)} %get-tuple-element.56, f32[32]{0:T(128)S(1)} %get-tuple-element.85, ...), kind=kLoop, calls=%fused_computation.2 | loop fusion | flops 15663104 | bytes 9307264 | tf_op jit(solution)/shard_map/reduce_sum | solution.py:227
  72.8 0.8 broadcast_multiply_fusion
  73.5 0.1 fusion.112
  73.7 0.7 collective-permute-start.12
  74.4 5.0 %collective-permute-start.13 = (f32[2,1,32,128]{3,2,1,0:T(8,128)S(1)}, f32[2,1,32,128]{3,2,1,0:T(8,128)S(1)}, u32[]{:S(2)}, u32[]{:S(2)}) collective-permute-start(f32[2,1,32,128]{3,2,1,0:T(8,128)S(1)} %get-tuple-element.67), channel_id=1, source_target_pairs={{0,4},{4,0},{8,12},{12,8},{16,20},{20,16},{24,28},{28,24},{1,5},{5... | collective-permute-start | bytes 98312 | tf_op jit(solution)/shard_map/ppermute | solution.py:44
  79.4 0.6 collective-permute-start.14
  80.0 2.9 %collective-permute-start.15 = (f32[2,8,1,128]{3,2,1,0:T(1,128)S(1)}, f32[2,8,1,128]{3,2,1,0:T(1,128)S(1)}, u32[]{:S(2)}, u32[]{:S(2)}) collective-permute-start(f32[2,8,1,128]{3,2,1,0:T(1,128)S(1)} %bitcast.81), channel_id=1, source_target_pairs={{0,1},{1,0},{2,3},{3,2},{4,5},{5,4},{6,7},{7,6},{8,9},{9,8},{10,11... | collective-permute-start | bytes 24584 | tf_op jit(solution)/shard_map/ppermute | solution.py:44
  83.0 2.4 %pad_maximum_fusion = bf16[64,8,32,128]{3,2,1,0:T(8,128)(2,1)} fusion(bf16[32,8,32,128]{3,2,1,0:T(8,128)(2,1)S(1)} %get-tuple-element.53, bf16[32,8,32,128]{3,2,1,0:T(8,128)(2,1)S(1)} %get-tuple-element.30), kind=kLoop, calls=%fused_computation | loop fusion | flops 2097152 | bytes 8388608 | tf_op jit(solution)/shard_map/dynamic_update_slice | solution.py:248
  85.3 0.0 collective-permute-done.13
  85.4 0.1 fusion.9
  85.4 0.5 power_multiply_fusion
  86.0 0.7 fusion.29
  86.7 0.9 %fusion.93 = (f32[8,32,128]{2,1,0:T(8,128)}, f32[8,32,128]{2,1,0:T(8,128)}) fusion(f32[2,8,32,128]{3,2,1,0:T(8,128)S(1)} %fusion.29, f32[8,32]{1,0:T(8,128)S(1)} %get-tuple-element.82, f32[8,32,128]{2,1,0:T(8,128)S(1)} %get-tuple-element.37, f32[8,32,128]{2,1,0:T(8,128)S(1)} %get-tuple-element.39, f32[2,8,32,128]{3,2,1,0:T(8,128)S(1)} %fusion.20, ...), kind=kLoop, calls=%fused_computation.196 | loop fusion | flops 1081344 | bytes 1442816 | tf_op jit(solution)/shard_map/add | solution.py:267
  (27 shorter events, 0.2 us)
Async XLA Ops:
  9.1 10.2 %collective-permute-start = (f32[16,32,128]{2,1,0:T(8,128)S(1)}, f32[16,32,128]{2,1,0:T(8,128)S(1)}, u32[]{:S(2)}, u32[]{:S(2)}) collective-permute-start(f32[16,32,128]{2,1,0:T(8,128)S(1)} %slice_select_fusion.2), channel_id=1, source_target_pairs={{0,4},{4,0},{8,12},{12,8},{16,20},{20,16},{24,28},{28,24},{1,5},{5... | collective-permute-start | bytes 786440 | tf_op jit(solution)/shard_map/ppermute | solution.py:127
  15.0 13.2 %copy-start.4 = (f32[8,32,128]{2,1,0:T(8,128)S(1)}, f32[8,32,128]{2,1,0:T(8,128)}, u32[]{:S(2)}) copy-start(f32[8,32,128]{2,1,0:T(8,128)} %param.8) | copy-start | bytes 393220
  15.0 13.2 %collective-permute-start.2 = (f32[16,32,128]{2,1,0:T(8,128)S(1)}, f32[16,32,128]{2,1,0:T(8,128)S(1)}, u32[]{:S(2)}, u32[]{:S(2)}) collective-permute-start(f32[16,32,128]{2,1,0:T(8,128)S(1)} %slice_select_fusion.1), channel_id=1, source_target_pairs={{0,4},{4,0},{8,12},{12,8},{16,20},{20,16},{24,28},{28,24},{1,5},{5... | collective-permute-start | bytes 786440 | tf_op jit(solution)/shard_map/ppermute | solution.py:127
  19.4 22.8 %copy-start = (f32[32,8,32,128]{3,2,1,0:T(8,128)S(1)}, f32[32,8,32,128]{3,2,1,0:T(8,128)}, u32[]{:S(2)}) copy-start(f32[32,8,32,128]{3,2,1,0:T(8,128)} %get-tuple-element.52) | copy-start | bytes 12582916
  19.4 8.9 %collective-permute-start.1 = (f32[16,32,128]{2,1,0:T(8,128)S(1)}, f32[16,32,128]{2,1,0:T(8,128)S(1)}, u32[]{:S(2)}, u32[]{:S(2)}) collective-permute-start(f32[16,32,128]{2,1,0:T(8,128)S(1)} %fusion.106), channel_id=1, source_target_pairs={{0,8},{4,12},{8,16},{12,20},{16,24},{20,28},{1,9},{5,13},{9,17},{1... | collective-permute-start | bytes 786440 | tf_op jit(solution)/shard_map/ppermute | solution.py:127
  28.2 13.9 %copy-start.7 = (f32[2,8,32,128]{3,2,1,0:T(8,128)}, f32[2,8,32,128]{3,2,1,0:T(8,128)S(1)}, u32[]{:S(2)}) copy-start(f32[2,8,32,128]{3,2,1,0:T(8,128)S(1)} %pad_maximum_fusion.40) | copy-start | bytes 786436
  29.0 16.3 %collective-permute-start.3 = (f32[16,32,128]{2,1,0:T(8,128)}, f32[16,32,128]{2,1,0:T(8,128)}, u32[]{:S(2)}, u32[]{:S(2)}) collective-permute-start(f32[16,32,128]{2,1,0:T(8,128)} %add.218), channel_id=1, source_target_pairs={{0,16},{4,20},{8,24},{12,28},{1,17},{5,21},{9,25},{13,29},{2,18},{... | collective-permute-start | bytes 786440 | tf_op jit(solution)/shard_map/ppermute | solution.py:127
  35.2 10.1 %collective-permute-start.4 = (f32[16,32,128]{2,1,0:T(8,128)}, f32[16,32,128]{2,1,0:T(8,128)S(1)}, u32[]{:S(2)}, u32[]{:S(2)}) collective-permute-start(f32[16,32,128]{2,1,0:T(8,128)} %fusion.107), channel_id=1, source_target_pairs={{0,8},{4,12},{8,16},{12,20},{16,24},{20,28},{1,9},{5,13},{9,17},{1... | collective-permute-start | bytes 786440 | tf_op jit(solution)/shard_map/ppermute | solution.py:127
  39.3 5.1 %collective-permute-start.6 = (f32[2,1,32,128]{3,2,1,0:T(8,128)}, f32[2,1,32,128]{3,2,1,0:T(8,128)}, u32[]{:S(2)}, u32[]{:S(2)}) collective-permute-start(f32[2,1,32,128]{3,2,1,0:T(8,128)} %get-tuple-element.70), channel_id=1, source_target_pairs={{0,4},{4,0},{8,12},{12,8},{16,20},{20,16},{24,28},{28,24},{1,5},{5... | collective-permute-start | bytes 98312 | tf_op jit(solution)/shard_map/ppermute | solution.py:44
  40.8 3.6 %collective-permute-start.5 = (f32[2,1,32,128]{3,2,1,0:T(8,128)}, f32[2,1,32,128]{3,2,1,0:T(8,128)}, u32[]{:S(2)}, u32[]{:S(2)}) collective-permute-start(f32[2,1,32,128]{3,2,1,0:T(8,128)} %get-tuple-element.71), channel_id=1, source_target_pairs={{4,8},{12,16},{20,24},{8,4},{16,12},{24,20},{5,9},{13,17},{21,25},... | collective-permute-start | bytes 98312 | tf_op jit(solution)/shard_map/ppermute | solution.py:47
  44.4 20.0 %copy-start.6 = (f32[64,32,128]{2,1,0:T(8,128)S(1)}, f32[64,32,128]{2,1,0:T(8,128)}, u32[]{:S(2)}) copy-start(f32[64,32,128]{2,1,0:T(8,128)} %param.12) | copy-start | bytes 3145732
  46.4 18.2 %copy-start.1 = (f32[32,8,32,128]{3,2,1,0:T(8,128)S(1)}, f32[32,8,32,128]{3,2,1,0:T(8,128)}, u32[]{:S(2)}) copy-start(f32[32,8,32,128]{3,2,1,0:T(8,128)} %get-tuple-element.52) | copy-start | bytes 12582916
  46.4 18.2 %copy-start.2 = (bf16[64,8,32,128]{3,2,1,0:T(8,128)(2,1)S(1)}, bf16[64,8,32,128]{3,2,1,0:T(8,128)(2,1)}, u32[]{:S(2)}) copy-start(bf16[64,8,32,128]{3,2,1,0:T(8,128)(2,1)} %param.11) | copy-start | bytes 12582916
  46.4 14.1 %collective-permute-start.7 = (f32[16,32,128]{2,1,0:T(8,128)S(1)}, f32[16,32,128]{2,1,0:T(8,128)S(1)}, u32[]{:S(2)}, u32[]{:S(2)}) collective-permute-start(f32[16,32,128]{2,1,0:T(8,128)S(1)} %add_select_fusion.1), channel_id=1, source_target_pairs={{0,4},{4,0},{8,12},{12,8},{16,20},{20,16},{24,28},{28,24},{1,5},{5... | collective-permute-start | bytes 786440 | tf_op jit(solution)/shard_map/ppermute | solution.py:127
  51.4 10.7 %collective-permute-start.8 = (f32[16,32,128]{2,1,0:T(8,128)S(1)}, f32[16,32,128]{2,1,0:T(8,128)S(1)}, u32[]{:S(2)}, u32[]{:S(2)}) collective-permute-start(f32[16,32,128]{2,1,0:T(8,128)S(1)} %add.222), channel_id=1, source_target_pairs={{0,16},{4,20},{8,24},{12,28},{1,17},{5,21},{9,25},{13,29},{2,18},{... | collective-permute-start | bytes 786440 | tf_op jit(solution)/shard_map/ppermute | solution.py:127
  59.0 1.5 %collective-permute-start.10 = (f32[2,8,1,128]{3,2,1,0:T(1,128)S(1)}, f32[2,8,1,128]{3,2,1,0:T(1,128)S(1)}, u32[]{:S(2)}, u32[]{:S(2)}) collective-permute-start(f32[2,8,1,128]{3,2,1,0:T(1,128)S(1)} %get-tuple-element.68), channel_id=1, source_target_pairs={{0,1},{1,0},{2,3},{3,2},{4,5},{5,4},{6,7},{7,6},{8,9},{9,8},{10,11... | collective-permute-start | bytes 24584 | tf_op jit(solution)/shard_map/ppermute | solution.py:44
  59.1 1.4 %collective-permute-start.9 = (f32[2,8,1,128]{3,2,1,0:T(1,128)S(1)}, f32[2,8,1,128]{3,2,1,0:T(1,128)S(1)}, u32[]{:S(2)}, u32[]{:S(2)}) collective-permute-start(f32[2,8,1,128]{3,2,1,0:T(1,128)S(1)} %get-tuple-element.69), channel_id=1, source_target_pairs={{1,2},{2,1},{5,6},{6,5},{9,10},{10,9},{13,14},{14,13},{17,18},{18,... | collective-permute-start | bytes 24584 | tf_op jit(solution)/shard_map/ppermute | solution.py:47
  62.3 7.7 %collective-permute-start.11 = (f32[16,32,128]{2,1,0:T(8,128)S(1)}, f32[16,32,128]{2,1,0:T(8,128)S(1)}, u32[]{:S(2)}, u32[]{:S(2)}) collective-permute-start(f32[16,32,128]{2,1,0:T(8,128)S(1)} %add_select_fusion), channel_id=1, source_target_pairs={{0,4},{4,0},{8,12},{12,8},{16,20},{20,16},{24,28},{28,24},{1,5},{5... | collective-permute-start | bytes 786440 | tf_op jit(solution)/shard_map/ppermute | solution.py:127
  64.6 5.4 %copy-start.3 = (f32[32,7,32,128]{3,2,1,0:T(8,128)S(1)}, f32[32,7,32,128]{3,2,1,0:T(8,128)}, u32[]{:S(2)}) copy-start(f32[32,7,32,128]{3,2,1,0:T(8,128)} %fusion) | copy-start | bytes 11010052
  70.1 2.7 %copy-start.5 = (f32[8,32,128]{2,1,0:T(8,128)S(1)}, f32[8,32,128]{2,1,0:T(8,128)}, u32[]{:S(2)}) copy-start(f32[8,32,128]{2,1,0:T(8,128)} %param.9) | copy-start | bytes 393220
  73.7 11.6 %collective-permute-start.12 = (f32[2,1,32,128]{3,2,1,0:T(8,128)S(1)}, f32[2,1,32,128]{3,2,1,0:T(8,128)S(1)}, u32[]{:S(2)}, u32[]{:S(2)}) collective-permute-start(f32[2,1,32,128]{3,2,1,0:T(8,128)S(1)} %get-tuple-element.66), channel_id=1, source_target_pairs={{4,8},{12,16},{20,24},{8,4},{16,12},{24,20},{5,9},{13,17},{21,25},... | collective-permute-start | bytes 98312 | tf_op jit(solution)/shard_map/ppermute | solution.py:47
  74.4 11.0 %collective-permute-start.13 = (f32[2,1,32,128]{3,2,1,0:T(8,128)S(1)}, f32[2,1,32,128]{3,2,1,0:T(8,128)S(1)}, u32[]{:S(2)}, u32[]{:S(2)}) collective-permute-start(f32[2,1,32,128]{3,2,1,0:T(8,128)S(1)} %get-tuple-element.67), channel_id=1, source_target_pairs={{0,4},{4,0},{8,12},{12,8},{16,20},{20,16},{24,28},{28,24},{1,5},{5... | collective-permute-start | bytes 98312 | tf_op jit(solution)/shard_map/ppermute | solution.py:44
  79.4 6.0 %collective-permute-start.14 = (f32[2,8,1,128]{3,2,1,0:T(1,128)S(1)}, f32[2,8,1,128]{3,2,1,0:T(1,128)S(1)}, u32[]{:S(2)}, u32[]{:S(2)}) collective-permute-start(f32[2,8,1,128]{3,2,1,0:T(1,128)S(1)} %get-tuple-element.44), channel_id=1, source_target_pairs={{1,2},{2,1},{5,6},{6,5},{9,10},{10,9},{13,14},{14,13},{17,18},{18,... | collective-permute-start | bytes 24584 | tf_op jit(solution)/shard_map/ppermute | solution.py:47
  80.0 5.3 %collective-permute-start.15 = (f32[2,8,1,128]{3,2,1,0:T(1,128)S(1)}, f32[2,8,1,128]{3,2,1,0:T(1,128)S(1)}, u32[]{:S(2)}, u32[]{:S(2)}) collective-permute-start(f32[2,8,1,128]{3,2,1,0:T(1,128)S(1)} %bitcast.81), channel_id=1, source_target_pairs={{0,1},{1,0},{2,3},{3,2},{4,5},{5,4},{6,7},{7,6},{8,9},{9,8},{10,11... | collective-permute-start | bytes 24584 | tf_op jit(solution)/shard_map/ppermute | solution.py:44

commit v22 on v21

--- a/solution.py
+++ b/solution.py
@@ -112,11 +112,12 @@
     return [(i, i + shift) for i in range(count - shift)]
 
 
-def pipelined_scan(totals_of, emit, lines, axis, riders, groups=2):
+def pipelined_scan(totals_of, emit, lines, axis, riders, passenger, groups=2):
     count = lax.axis_size(axis)
     if count % 2 or count <= 2 or lines % (2 * groups):
         earlier = exclusive_scan(totals_of(0, lines, None), axis)
-        return [emit(0, lines, earlier)], {stage: rider(None) for stage, rider in riders.items()}
+        carried = {stage: rider(None) for stage, rider in riders.items()}
+        return [emit(0, lines, earlier)], carried, None
     size = lines // groups
     steps = [None] * groups
     steps[0] = paired_steps(totals_of(0, size, None), axis)
@@ -124,7 +125,15 @@
     while stage < groups or live:
         if stage < groups:
             live[stage] = next(steps[stage])
-        arrived = {g: lax.ppermute(payload, axis, pairs) for g, (payload, pairs) in live.items()}
+        sent = dict(live)
+        if stage == 0:
+            payload, pairs = live[0]
+            sent[0] = jnp.concatenate([payload, passenger.reshape((-1,) + payload.shape[1:])]), pairs
+        arrived = {g: lax.ppermute(payload, axis, pairs) for g, (payload, pairs) in sent.items()}
+        if stage == 0:
+            held = live[0][0].shape[0]
+            passenger = arrived[0][held:].reshape(passenger.shape)
+            arrived[0] = arrived[0][:held]
         if stage == 0:
             for g in range(1, groups):
                 steps[g] = paired_steps(totals_of(g * size, size, live[0][0]), axis)
@@ -142,7 +151,7 @@
                 made = made + [emit(g * size, size, finished.value)]
         live = following
         stage += 1
-    return made, carried
+    return made, carried, passenger
 
 
 def window(source, step_beam, step_cross, step_depth):
@@ -238,10 +247,31 @@
         return exchange
 
     lines = earlier_spectral_power.shape[0]
-    made, first_faces = pipelined_scan(
-        totals_of, emit, lines, "beam", {2: tied_faces(beam_faces), 3: tied_faces(cross_faces)}
-    )
-    first_bordered = bordered_fields(physical_quantities, first_faces[2], first_faces[3])
+    count = lax.axis_size("beam")
+    is_even = lax.axis_index("beam") % 2 == 0
+    last, first = physical_quantities[:, rows - 1 :], physical_quantities[:, :1]
+
+    def across_pairs(fields):
+        pairs = [(i, i + 1) for i in range(1, count - 1, 2)]
+        pairs += [(target, source) for source, target in pairs]
+        size = fields.shape[1]
+        return lax.ppermute(jnp.where(is_even, fields[:, :1], fields[:, size - 1 :]), "beam", pairs)
+
+    paired = count % 2 == 0 and count > 2 and lines % 4 == 0
+    made, first_faces, within = pipelined_scan(
+        totals_of,
+        emit,
+        lines,
+        "beam",
+        {2: tied_faces(cross_faces), 3: tied_faces(across_pairs if paired else beam_faces)},
+        jnp.where(is_even, last, first),
+    )
+    if paired:
+        across = first_faces[3]
+        beam = (jnp.where(is_even, across, within), jnp.where(is_even, within, across))
+    else:
+        beam = first_faces[3]
+    first_bordered = bordered_fields(physical_quantities, beam, first_faces[2])
     spectral_power = jnp.zeros(earlier_spectral_power.shape, jnp.bfloat16)
     start = 0
     for part, _, _ in made:

time: 88.2 us -> 84.6 us (0.959)
  the two profiles are of different devices: /device:TPU:0 before, /device:TPU:9 now
where the time goes in v22:
time: 84.6 us; the launch traced here: 84.2 us
  starting transfers between devices  42 us (50%)
  other arithmetic  30.2 us (36%)
  waiting for transfers between devices  10.1 us (12%)
  between operations  1.13 us (1%)
  local copies, waits for them, and re-layouts  0.86 us (1%)
    ppermute x8, starting transfers between devices, pipelined_scan(): lax.ppermute(payload, axis, pairs)  15.5 us
    ppermute x3, starting transfers between devices, faces(): across = lax.ppermute(jnp.where(is_even, first, last), axis, pairs)  12.5 us
    reduce_sum x2, other arithmetic, totals_of(): return jnp.sum(optical_depth, axis=1)  8.68 us
    ppermute x3, starting transfers between devices, faces(): lax.ppermute(jnp.where(is_even, last, first), axis, [(i, i ^ 1) for i in...  8.18 us
    ppermute x8, waiting for transfers between devices, pipelined_scan(): lax.ppermute(payload, axis, pairs)  7.44 us
    another operation x2, other arithmetic, emit(): jnp.cumsum(optical_depth[:, :rows - 1], axis=1)  7.09 us
    ppermute x1, starting transfers between devices, across_pairs(): lax.ppermute(jnp.where(is_even, fields[:, :1], fields[:, size - 1:]), 'be...  5.85 us
    reduce_sum x1, other arithmetic, emit(): jnp.sum(weight * radiance, axis=0)  2.68 us
  transfers between devices with their start and end apart: 15, of which 3 were waited for; matrix products, arithmetic and copies ran while one was open for 19% of the time, Pallas kernels for 0%

profile of v22, /device:TPU:9, one launch (start us, length us, event | category | flops | bytes accessed | tf_op | source)
XLA Modules:
  0.0 84.2 jit_solution(13181809207362427249)
XLA Ops:
  0.6 0.7 convert_subtract_fusion
  1.3 0.8 fusion.126
  2.1 1.1 %add_bitcast_fusion = (f32[1,8,32,128]{3,2,1,0:T(8,128)S(1)}, f32[8,32,128]{2,1,0:T(8,128)S(1)}) fusion(f32[8,32,128]{2,1,0:T(8,128)} %param.9, f32[8,32,128]{2,1,0:T(8,128)} %param.10, f32[8,32]{1,0:T(8,128)S(1)} %get-tuple-element.78), kind=kLoop, calls=%fused_computation.220 | loop fusion | flops 262144 | bytes 525312 | tf_op jit(solution)/shard_map/stack | solution.py:204
  3.2 0.0 copy-start.3
  3.2 5.9 %fusion.124 = (f32[32,32,128]{2,1,0:T(8,128)S(1)}, f32[32,8,32,128]{3,2,1,0:T(8,128)}, f32[32,8,32,128]{3,2,1,0:T(8,128)}) fusion(f32[8,32]{1,0:T(8,128)S(1)} %get-tuple-element.79, bf16[64,8,32,128]{3,2,1,0:T(8,128)(2,1)} %param.11, f32[32]{0:T(128)S(1)} %get-tuple-element.80, f32[8,32,128]{2,1,0:T(8,128)S(1)} %get-tuple-element.71, ...), kind=kLoop, calls=%fused_computation.255 | loop fusion | flops 11403264 | bytes 13239552 | tf_op jit(solution)/shard_map/reduce_sum | solution.py:225
  9.2 0.0 copy-done.3
  9.2 1.3 %collective-permute-start = (f32[18,32,128]{2,1,0:T(8,128)S(1)}, f32[18,32,128]{2,1,0:T(8,128)S(1)}, u32[]{:S(2)}, u32[]{:S(2)}) collective-permute-start(f32[18,32,128]{2,1,0:T(8,128)S(1)} %pad_maximum_fusion.19), channel_id=1, source_target_pairs={{0,4},{4,0},{8,12},{12,8},{16,20},{20,16},{24,28},{28,24},{1,5},{5... | collective-permute-start | bytes 884744 | tf_op jit(solution)/shard_map/ppermute | solution.py:132
  10.5 2.7 %reduce_sum.55 = f32[32,32,128]{2,1,0:T(8,128)S(1)} reduce(f32[32,8,32,128]{3,2,1,0:T(8,128)} %get-tuple-element.20, f32[]{:T(128)} %constant.65.clone.1), dimensions={1}, to_apply=%region_1.2 | reduce | flops 917504 | bytes 4718596 | tf_op jit(solution)/shard_map/reduce_sum | solution.py:225
  13.3 0.3 collective-permute-start.2
  13.6 3.5 %collective-permute-done = f32[18,32,128]{2,1,0:T(8,128)S(1)} collective-permute-done((f32[18,32,128]{2,1,0:T(8,128)S(1)}, f32[18,32,128]{2,1,0:T(8,128)S(1)}, u32[]{:S(2)}, u32[]{:S(2)}) %collective-permute-start) | collective-permute-done | bytes 294944 | tf_op jit(solution)/shard_map/ppermute | solution.py:132
  17.2 0.1 fusion.106
  17.3 3.2 %collective-permute-start.1 = (f32[16,32,128]{2,1,0:T(8,128)S(1)}, f32[16,32,128]{2,1,0:T(8,128)S(1)}, u32[]{:S(2)}, u32[]{:S(2)}) collective-permute-start(f32[16,32,128]{2,1,0:T(8,128)S(1)} %fusion.106), channel_id=1, source_target_pairs={{0,8},{4,12},{8,16},{12,20},{16,24},{20,28},{1,9},{5,13},{9,17},{1... | collective-permute-start | bytes 786440 | tf_op jit(solution)/shard_map/ppermute | solution.py:132
  20.5 4.5 %fusion = f32[32,7,32,128]{3,2,1,0:T(8,128)} fusion(f32[32,8,32,128]{3,2,1,0:T(8,128)} %get-tuple-element.20), kind=kOutput, calls=%fused_computation.11 | output fusion | flops 5505024 | bytes 7340032 | tf_op jit(solution)/shard_map/jit(cumsum)/reduce_window_sum | solution.py:230
  25.0 0.0 collective-permute-done.2
  25.0 0.0 collective-permute-done.1
  25.0 3.6 %collective-permute-start.3 = (f32[16,32,128]{2,1,0:T(8,128)S(1)}, f32[16,32,128]{2,1,0:T(8,128)S(1)}, u32[]{:S(2)}, u32[]{:S(2)}) collective-permute-start(f32[16,32,128]{2,1,0:T(8,128)S(1)} %add.218), channel_id=1, source_target_pairs={{0,16},{4,20},{8,24},{12,28},{1,17},{5,21},{9,25},{13,29},{2,18},{... | collective-permute-start | bytes 786440 | tf_op jit(solution)/shard_map/ppermute | solution.py:132
  28.7 0.1 fusion.107
  28.7 1.9 %collective-permute-start.4 = (f32[16,32,128]{2,1,0:T(8,128)S(1)}, f32[16,32,128]{2,1,0:T(8,128)S(1)}, u32[]{:S(2)}, u32[]{:S(2)}) collective-permute-start(f32[16,32,128]{2,1,0:T(8,128)S(1)} %fusion.107), channel_id=1, source_target_pairs={{0,8},{4,12},{8,16},{12,20},{16,24},{20,28},{1,9},{5,13},{9,17},{1... | collective-permute-start | bytes 786440 | tf_op jit(solution)/shard_map/ppermute | solution.py:132
  30.7 4.2 %collective-permute-start.6 = (f32[2,8,1,128]{3,2,1,0:T(1,128)S(1)}, f32[2,8,1,128]{3,2,1,0:T(1,128)S(1)}, u32[]{:S(2)}, u32[]{:S(2)}) collective-permute-start(f32[2,8,1,128]{3,2,1,0:T(1,128)S(1)} %get-tuple-element.68), channel_id=1, source_target_pairs={{0,1},{1,0},{2,3},{3,2},{4,5},{5,4},{6,7},{7,6},{8,9},{9,8},{10,11... | collective-permute-start | bytes 24584 | tf_op jit(solution)/shard_map/ppermute | solution.py:44
  34.9 3.0 %collective-permute-start.5 = (f32[2,8,1,128]{3,2,1,0:T(1,128)S(1)}, f32[2,8,1,128]{3,2,1,0:T(1,128)S(1)}, u32[]{:S(2)}, u32[]{:S(2)}) collective-permute-start(f32[2,8,1,128]{3,2,1,0:T(1,128)S(1)} %get-tuple-element.69), channel_id=1, source_target_pairs={{1,2},{2,1},{5,6},{6,5},{9,10},{10,9},{13,14},{14,13},{17,18},{18,... | collective-permute-start | bytes 24584 | tf_op jit(solution)/shard_map/ppermute | solution.py:47
  37.9 0.0 copy-start.6
  37.9 2.6 %fusion.2 = f32[32,7,32,128]{3,2,1,0:T(8,128)S(1)} fusion(f32[32,8,32,128]{3,2,1,0:T(8,128)} %get-tuple-element.50), kind=kOutput, calls=%fused_computation.13 | output fusion | flops 5505024 | bytes 7340032 | tf_op jit(solution)/shard_map/jit(cumsum)/reduce_window_sum | solution.py:230
  40.5 0.0 copy-start.5
  40.5 0.0 collective-permute-done.6
  40.5 0.0 collective-permute-done.5
  40.6 0.0 collective-permute-done.3
  40.6 3.9 %collective-permute-done.4 = f32[16,32,128]{2,1,0:T(8,128)S(1)} collective-permute-done((f32[16,32,128]{2,1,0:T(8,128)S(1)}, f32[16,32,128]{2,1,0:T(8,128)S(1)}, u32[]{:S(2)}, u32[]{:S(2)}) %collective-permute-start.4) | collective-permute-done | bytes 262176 | tf_op jit(solution)/shard_map/ppermute | solution.py:132
  44.5 0.1 fusion.123
  44.5 0.1 add_select_fusion.1
  44.6 1.3 %collective-permute-start.7 = (f32[16,32,128]{2,1,0:T(8,128)S(1)}, f32[16,32,128]{2,1,0:T(8,128)S(1)}, u32[]{:S(2)}, u32[]{:S(2)}) collective-permute-start(f32[16,32,128]{2,1,0:T(8,128)S(1)} %add_select_fusion.1), channel_id=1, source_target_pairs={{0,4},{4,0},{8,12},{12,8},{16,20},{20,16},{24,28},{28,24},{1,5},{5... | collective-permute-start | bytes 786440 | tf_op jit(solution)/shard_map/ppermute | solution.py:132
  45.9 0.0 copy-start
  45.9 1.6 %collective-permute-start.8 = (f32[16,32,128]{2,1,0:T(8,128)S(1)}, f32[16,32,128]{2,1,0:T(8,128)S(1)}, u32[]{:S(2)}, u32[]{:S(2)}) collective-permute-start(f32[16,32,128]{2,1,0:T(8,128)S(1)} %add.223), channel_id=1, source_target_pairs={{0,16},{4,20},{8,24},{12,28},{1,17},{5,21},{9,25},{13,29},{2,18},{... | collective-permute-start | bytes 786440 | tf_op jit(solution)/shard_map/ppermute | solution.py:132
  47.5 5.8 %collective-permute-start.9 = (f32[2,1,32,128]{3,2,1,0:T(8,128)S(1)}, f32[2,1,32,128]{3,2,1,0:T(8,128)S(1)}, u32[]{:S(2)}, u32[]{:S(2)}) collective-permute-start(f32[2,1,32,128]{3,2,1,0:T(8,128)S(1)} %slice_select_fusion.4), channel_id=1, source_target_pairs={{4,8},{12,16},{20,24},{8,4},{16,12},{24,20},{5,9},{13,17},{21,25},... | collective-permute-start | bytes 98312 | tf_op jit(solution)/shard_map/ppermute | solution.py:258
  53.4 0.0 copy-done.6
  53.4 2.6 %collective-permute-done.9 = f32[2,1,32,128]{3,2,1,0:T(8,128)S(1)} collective-permute-done((f32[2,1,32,128]{3,2,1,0:T(8,128)S(1)}, f32[2,1,32,128]{3,2,1,0:T(8,128)S(1)}, u32[]{:S(2)}, u32[]{:S(2)}) %collective-permute-start.9) | collective-permute-done | bytes 32800 | tf_op jit(solution)/shard_map/ppermute | solution.py:258
  56.0 0.0 collective-permute-done.7
  56.0 0.0 collective-permute-done.8
  56.0 0.1 fusion.122
  56.1 0.1 add_select_fusion
  56.2 2.3 %collective-permute-start.10 = (f32[16,32,128]{2,1,0:T(8,128)S(1)}, f32[16,32,128]{2,1,0:T(8,128)S(1)}, u32[]{:S(2)}, u32[]{:S(2)}) collective-permute-start(f32[16,32,128]{2,1,0:T(8,128)S(1)} %add_select_fusion), channel_id=1, source_target_pairs={{0,4},{4,0},{8,12},{12,8},{16,20},{20,16},{24,28},{28,24},{1,5},{5... | collective-permute-start | bytes 786440 | tf_op jit(solution)/shard_map/ppermute | solution.py:132
  58.5 0.1 fusion.7
  58.5 0.5 power_multiply_fusion.2
  59.1 0.2 fusion.125
  59.4 2.4 %multiply_reduce_fusion.2 = (f32[8,32,128]{2,1,0:T(8,128)S(1)}, f32[8,32,128]{2,1,0:T(8,128)S(1)}, bf16[32,8,32,128]{3,2,1,0:T(8,128)(2,1)S(1)}) fusion(f32[32,8,32,128]{3,2,1,0:T(8,128)S(1)} %copy-done, f32[32,7,32,128]{3,2,1,0:T(8,128)S(1)} %fusion.2, f32[32,32,128]{2,1,0:T(8,128)S(1)} %get-tuple-element.82, f32[32,32,128]{2,1,0:T(8,128)S(1)} %get-tuple-element.55, ...), kind=kLoop, calls=%fused_computation.4 | loop fusion | flops 13565952 | bytes 13369472 | tf_op jit(solution)/shard_map/reduce_sum | solution.py:237
  61.7 0.6 fusion.20
  62.4 0.0 collective-permute-done.10
  62.4 0.1 maximum_select_fusion.1
  62.5 0.0 copy-start.4
  62.5 2.7 %multiply_reduce_fusion.1 = (f32[8,32,128]{2,1,0:T(8,128)S(1)}, f32[8,32,128]{2,1,0:T(8,128)S(1)}, bf16[32,8,32,128]{3,2,1,0:T(8,128)(2,1)S(1)}) fusion(f32[32,7,32,128]{3,2,1,0:T(8,128)S(1)} %copy-done.2, f32[32,32,128]{2,1,0:T(8,128)S(1)} %maximum_select_fusion.1, f32[32,32,128]{2,1,0:T(8,128)S(1)} %get-tuple-element.54, f32[32]{0:T(128)S(1)} %get-tuple-element.81, ...), kind=kLoop, calls=%fused_computation.2 | loop fusion | flops 15663104 | bytes 9307264 | tf_op jit(solution)/shard_map/reduce_sum | solution.py:236
  65.2 0.8 broadcast_multiply_fusion
  66.0 0.1 fusion.118
  66.2 2.3 %collective-permute-start.11 = (f32[2,1,32,128]{3,2,1,0:T(8,128)S(1)}, f32[2,1,32,128]{3,2,1,0:T(8,128)S(1)}, u32[]{:S(2)}, u32[]{:S(2)}) collective-permute-start(f32[2,1,32,128]{3,2,1,0:T(8,128)S(1)} %get-tuple-element.66), channel_id=1, source_target_pairs={{4,8},{12,16},{20,24},{8,4},{16,12},{24,20},{5,9},{13,17},{21,25},... | collective-permute-start | bytes 98312 | tf_op jit(solution)/shard_map/ppermute | solution.py:47
  68.5 3.9 %collective-permute-start.12 = (f32[2,1,32,128]{3,2,1,0:T(8,128)S(1)}, f32[2,1,32,128]{3,2,1,0:T(8,128)S(1)}, u32[]{:S(2)}, u32[]{:S(2)}) collective-permute-start(f32[2,1,32,128]{3,2,1,0:T(8,128)S(1)} %get-tuple-element.67), channel_id=1, source_target_pairs={{0,4},{4,0},{8,12},{12,8},{16,20},{20,16},{24,28},{28,24},{1,5},{5... | collective-permute-start | bytes 98312 | tf_op jit(solution)/shard_map/ppermute | solution.py:44
  72.4 7.1 %collective-permute-start.13 = (f32[2,8,1,128]{3,2,1,0:T(1,128)S(1)}, f32[2,8,1,128]{3,2,1,0:T(1,128)S(1)}, u32[]{:S(2)}, u32[]{:S(2)}) collective-permute-start(f32[2,8,1,128]{3,2,1,0:T(1,128)S(1)} %get-tuple-element.42), channel_id=1, source_target_pairs={{1,2},{2,1},{5,6},{6,5},{9,10},{10,9},{13,14},{14,13},{17,18},{18,... | collective-permute-start | bytes 24584 | tf_op jit(solution)/shard_map/ppermute | solution.py:47
  79.5 0.1 collective-permute-start.14
  79.6 2.4 %pad_maximum_fusion = bf16[64,8,32,128]{3,2,1,0:T(8,128)(2,1)} fusion(bf16[32,8,32,128]{3,2,1,0:T(8,128)(2,1)S(1)} %get-tuple-element.51, bf16[32,8,32,128]{3,2,1,0:T(8,128)(2,1)S(1)} %get-tuple-element.29), kind=kLoop, calls=%fused_computation | loop fusion | flops 2097152 | bytes 8388608 | tf_op jit(solution)/shard_map/dynamic_update_slice | solution.py:278
  82.0 0.0 collective-permute-done.13
  82.0 0.0 collective-permute-done.14
  82.0 0.0 collective-permute-done.11
  82.0 0.0 collective-permute-done.12
  82.0 0.1 fusion.9
  82.1 0.5 power_multiply_fusion
  82.7 0.7 fusion.29
  83.3 0.9 %fusion.93 = (f32[8,32,128]{2,1,0:T(8,128)}, f32[8,32,128]{2,1,0:T(8,128)}) fusion(f32[2,8,32,128]{3,2,1,0:T(8,128)S(1)} %fusion.29, f32[8,32]{1,0:T(8,128)S(1)} %get-tuple-element.78, f32[8,32,128]{2,1,0:T(8,128)S(1)} %get-tuple-element.35, f32[8,32,128]{2,1,0:T(8,128)S(1)} %get-tuple-element.37, f32[2,8,32,128]{3,2,1,0:T(8,128)S(1)} %fusion.20, ...), kind=kLoop, calls=%fused_computation.201 | loop fusion | flops 1081344 | bytes 1442816 | tf_op jit(solution)/shard_map/add | solution.py:297
  (26 shorter events, 0.3 us)
Async XLA Ops:
  3.2 6.0 %copy-start.3 = (f32[8,32,128]{2,1,0:T(8,128)S(1)}, f32[8,32,128]{2,1,0:T(8,128)}, u32[]{:S(2)}) copy-start(f32[8,32,128]{2,1,0:T(8,128)} %param.8) | copy-start | bytes 393220
  9.2 7.9 %collective-permute-start = (f32[18,32,128]{2,1,0:T(8,128)S(1)}, f32[18,32,128]{2,1,0:T(8,128)S(1)}, u32[]{:S(2)}, u32[]{:S(2)}) collective-permute-start(f32[18,32,128]{2,1,0:T(8,128)S(1)} %pad_maximum_fusion.19), channel_id=1, source_target_pairs={{0,4},{4,0},{8,12},{12,8},{16,20},{20,16},{24,28},{28,24},{1,5},{5... | collective-permute-start | bytes 884744 | tf_op jit(solution)/shard_map/ppermute | solution.py:132
  13.3 11.6 %collective-permute-start.2 = (f32[16,32,128]{2,1,0:T(8,128)S(1)}, f32[16,32,128]{2,1,0:T(8,128)S(1)}, u32[]{:S(2)}, u32[]{:S(2)}) collective-permute-start(f32[16,32,128]{2,1,0:T(8,128)S(1)} %slice_select_fusion.1), channel_id=1, source_target_pairs={{0,4},{4,0},{8,12},{12,8},{16,20},{20,16},{24,28},{28,24},{1,5},{5... | collective-permute-start | bytes 786440 | tf_op jit(solution)/shard_map/ppermute | solution.py:132
  17.3 7.7 %collective-permute-start.1 = (f32[16,32,128]{2,1,0:T(8,128)S(1)}, f32[16,32,128]{2,1,0:T(8,128)S(1)}, u32[]{:S(2)}, u32[]{:S(2)}) collective-permute-start(f32[16,32,128]{2,1,0:T(8,128)S(1)} %fusion.106), channel_id=1, source_target_pairs={{0,8},{4,12},{8,16},{12,20},{16,24},{20,28},{1,9},{5,13},{9,17},{1... | collective-permute-start | bytes 786440 | tf_op jit(solution)/shard_map/ppermute | solution.py:132
  25.0 15.5 %collective-permute-start.3 = (f32[16,32,128]{2,1,0:T(8,128)S(1)}, f32[16,32,128]{2,1,0:T(8,128)S(1)}, u32[]{:S(2)}, u32[]{:S(2)}) collective-permute-start(f32[16,32,128]{2,1,0:T(8,128)S(1)} %add.218), channel_id=1, source_target_pairs={{0,16},{4,20},{8,24},{12,28},{1,17},{5,21},{9,25},{13,29},{2,18},{... | collective-permute-start | bytes 786440 | tf_op jit(solution)/shard_map/ppermute | solution.py:132
  28.7 15.7 %collective-permute-start.4 = (f32[16,32,128]{2,1,0:T(8,128)S(1)}, f32[16,32,128]{2,1,0:T(8,128)S(1)}, u32[]{:S(2)}, u32[]{:S(2)}) collective-permute-start(f32[16,32,128]{2,1,0:T(8,128)S(1)} %fusion.107), channel_id=1, source_target_pairs={{0,8},{4,12},{8,16},{12,20},{16,24},{20,28},{1,9},{5,13},{9,17},{1... | collective-permute-start | bytes 786440 | tf_op jit(solution)/shard_map/ppermute | solution.py:132
  30.7 9.9 %collective-permute-start.6 = (f32[2,8,1,128]{3,2,1,0:T(1,128)S(1)}, f32[2,8,1,128]{3,2,1,0:T(1,128)S(1)}, u32[]{:S(2)}, u32[]{:S(2)}) collective-permute-start(f32[2,8,1,128]{3,2,1,0:T(1,128)S(1)} %get-tuple-element.68), channel_id=1, source_target_pairs={{0,1},{1,0},{2,3},{3,2},{4,5},{5,4},{6,7},{7,6},{8,9},{9,8},{10,11... | collective-permute-start | bytes 24584 | tf_op jit(solution)/shard_map/ppermute | solution.py:44
  34.9 5.7 %collective-permute-start.5 = (f32[2,8,1,128]{3,2,1,0:T(1,128)S(1)}, f32[2,8,1,128]{3,2,1,0:T(1,128)S(1)}, u32[]{:S(2)}, u32[]{:S(2)}) collective-permute-start(f32[2,8,1,128]{3,2,1,0:T(1,128)S(1)} %get-tuple-element.69), channel_id=1, source_target_pairs={{1,2},{2,1},{5,6},{6,5},{9,10},{10,9},{13,14},{14,13},{17,18},{18,... | collective-permute-start | bytes 24584 | tf_op jit(solution)/shard_map/ppermute | solution.py:47
  37.9 15.5 %copy-start.6 = (f32[32,128]{1,0:T(8,128)S(1)}, f32[32,128]{1,0:T(8,128)}, u32[]{:S(2)}) copy-start(f32[32,128]{1,0:T(8,128)} %param.14) | copy-start | bytes 49156
  40.5 18.6 %copy-start.5 = (f32[64,32,128]{2,1,0:T(8,128)S(1)}, f32[64,32,128]{2,1,0:T(8,128)}, u32[]{:S(2)}) copy-start(f32[64,32,128]{2,1,0:T(8,128)} %param.12) | copy-start | bytes 3145732
  44.6 11.5 %collective-permute-start.7 = (f32[16,32,128]{2,1,0:T(8,128)S(1)}, f32[16,32,128]{2,1,0:T(8,128)S(1)}, u32[]{:S(2)}, u32[]{:S(2)}) collective-permute-start(f32[16,32,128]{2,1,0:T(8,128)S(1)} %add_select_fusion.1), channel_id=1, source_target_pairs={{0,4},{4,0},{8,12},{12,8},{16,20},{20,16},{24,28},{28,24},{1,5},{5... | collective-permute-start | bytes 786440 | tf_op jit(solution)/shard_map/ppermute | solution.py:132
  45.9 13.4 %copy-start.1 = (bf16[64,8,32,128]{3,2,1,0:T(8,128)(2,1)S(1)}, bf16[64,8,32,128]{3,2,1,0:T(8,128)(2,1)}, u32[]{:S(2)}) copy-start(bf16[64,8,32,128]{3,2,1,0:T(8,128)(2,1)} %param.11) | copy-start | bytes 12582916
  45.9 13.4 %copy-start = (f32[32,8,32,128]{3,2,1,0:T(8,128)S(1)}, f32[32,8,32,128]{3,2,1,0:T(8,128)}, u32[]{:S(2)}) copy-start(f32[32,8,32,128]{3,2,1,0:T(8,128)} %get-tuple-element.50) | copy-start | bytes 12582916
  45.9 10.1 %collective-permute-start.8 = (f32[16,32,128]{2,1,0:T(8,128)S(1)}, f32[16,32,128]{2,1,0:T(8,128)S(1)}, u32[]{:S(2)}, u32[]{:S(2)}) collective-permute-start(f32[16,32,128]{2,1,0:T(8,128)S(1)} %add.223), channel_id=1, source_target_pairs={{0,16},{4,20},{8,24},{12,28},{1,17},{5,21},{9,25},{13,29},{2,18},{... | collective-permute-start | bytes 786440 | tf_op jit(solution)/shard_map/ppermute | solution.py:132
  47.5 8.5 %collective-permute-start.9 = (f32[2,1,32,128]{3,2,1,0:T(8,128)S(1)}, f32[2,1,32,128]{3,2,1,0:T(8,128)S(1)}, u32[]{:S(2)}, u32[]{:S(2)}) collective-permute-start(f32[2,1,32,128]{3,2,1,0:T(8,128)S(1)} %slice_select_fusion.4), channel_id=1, source_target_pairs={{4,8},{12,16},{20,24},{8,4},{16,12},{24,20},{5,9},{13,17},{21,25},... | collective-permute-start | bytes 98312 | tf_op jit(solution)/shard_map/ppermute | solution.py:258
  56.2 6.2 %collective-permute-start.10 = (f32[16,32,128]{2,1,0:T(8,128)S(1)}, f32[16,32,128]{2,1,0:T(8,128)S(1)}, u32[]{:S(2)}, u32[]{:S(2)}) collective-permute-start(f32[16,32,128]{2,1,0:T(8,128)S(1)} %add_select_fusion), channel_id=1, source_target_pairs={{0,4},{4,0},{8,12},{12,8},{16,20},{20,16},{24,28},{28,24},{1,5},{5... | collective-permute-start | bytes 786440 | tf_op jit(solution)/shard_map/ppermute | solution.py:132
  59.3 3.1 %copy-start.2 = (f32[32,7,32,128]{3,2,1,0:T(8,128)S(1)}, f32[32,7,32,128]{3,2,1,0:T(8,128)}, u32[]{:S(2)}) copy-start(f32[32,7,32,128]{3,2,1,0:T(8,128)} %fusion) | copy-start | bytes 11010052
  62.5 2.7 %copy-start.4 = (f32[8,32,128]{2,1,0:T(8,128)S(1)}, f32[8,32,128]{2,1,0:T(8,128)}, u32[]{:S(2)}) copy-start(f32[8,32,128]{2,1,0:T(8,128)} %param.9) | copy-start | bytes 393220
  66.2 15.9 %collective-permute-start.11 = (f32[2,1,32,128]{3,2,1,0:T(8,128)S(1)}, f32[2,1,32,128]{3,2,1,0:T(8,128)S(1)}, u32[]{:S(2)}, u32[]{:S(2)}) collective-permute-start(f32[2,1,32,128]{3,2,1,0:T(8,128)S(1)} %get-tuple-element.66), channel_id=1, source_target_pairs={{4,8},{12,16},{20,24},{8,4},{16,12},{24,20},{5,9},{13,17},{21,25},... | collective-permute-start | bytes 98312 | tf_op jit(solution)/shard_map/ppermute | solution.py:47
  68.5 13.6 %collective-permute-start.12 = (f32[2,1,32,128]{3,2,1,0:T(8,128)S(1)}, f32[2,1,32,128]{3,2,1,0:T(8,128)S(1)}, u32[]{:S(2)}, u32[]{:S(2)}) collective-permute-start(f32[2,1,32,128]{3,2,1,0:T(8,128)S(1)} %get-tuple-element.67), channel_id=1, source_target_pairs={{0,4},{4,0},{8,12},{12,8},{16,20},{20,16},{24,28},{28,24},{1,5},{5... | collective-permute-start | bytes 98312 | tf_op jit(solution)/shard_map/ppermute | solution.py:44
  72.4 9.6 %collective-permute-start.13 = (f32[2,8,1,128]{3,2,1,0:T(1,128)S(1)}, f32[2,8,1,128]{3,2,1,0:T(1,128)S(1)}, u32[]{:S(2)}, u32[]{:S(2)}) collective-permute-start(f32[2,8,1,128]{3,2,1,0:T(1,128)S(1)} %get-tuple-element.42), channel_id=1, source_target_pairs={{1,2},{2,1},{5,6},{6,5},{9,10},{10,9},{13,14},{14,13},{17,18},{18,... | collective-permute-start | bytes 24584 | tf_op jit(solution)/shard_map/ppermute | solution.py:47
  79.5 2.5 %collective-permute-start.14 = (f32[2,8,1,128]{3,2,1,0:T(1,128)S(1)}, f32[2,8,1,128]{3,2,1,0:T(1,128)S(1)}, u32[]{:S(2)}, u32[]{:S(2)}) collective-permute-start(f32[2,8,1,128]{3,2,1,0:T(1,128)S(1)} %bitcast.90), channel_id=1, source_target_pairs={{0,1},{1,0},{2,3},{3,2},{4,5},{5,4},{6,7},{7,6},{8,9},{9,8},{10,11... | collective-permute-start | bytes 24584 | tf_op jit(solution)/shard_map/ppermute | solution.py:44

commit v23 on v21

--- a/solution.py
+++ b/solution.py
@@ -239,9 +239,9 @@
 
     lines = earlier_spectral_power.shape[0]
     made, first_faces = pipelined_scan(
-        totals_of, emit, lines, "beam", {2: tied_faces(beam_faces), 3: tied_faces(cross_faces)}
-    )
-    first_bordered = bordered_fields(physical_quantities, first_faces[2], first_faces[3])
+        totals_of, emit, lines, "beam", {1: tied_faces(cross_faces), 3: tied_faces(beam_faces)}
+    )
+    first_bordered = bordered_fields(physical_quantities, first_faces[3], first_faces[1])
     spectral_power = jnp.zeros(earlier_spectral_power.shape, jnp.bfloat16)
     start = 0
     for part, _, _ in made:

time: 88.2 us -> 84.9 us (0.963)
  the two profiles are of different devices: /device:TPU:0 before, /device:TPU:9 now
where the time goes in v23:
time: 84.9 us; the launch traced here: 84.5 us
  starting transfers between devices  39.2 us (46%)
  other arithmetic  26.5 us (31%)
  waiting for transfers between devices  16.9 us (20%)
  between operations  1.09 us (1%)
    ppermute x4, starting transfers between devices, faces(): across = lax.ppermute(jnp.where(is_even, first, last), axis, pairs)  19 us
    ppermute x8, waiting for transfers between devices, pipelined_scan(): lax.ppermute(payload, axis, pairs)  15.3 us
    ppermute x8, starting transfers between devices, pipelined_scan(): lax.ppermute(payload, axis, pairs)  14.2 us
    reduce_sum x2, other arithmetic, totals_of(): return jnp.sum(optical_depth, axis=1)  8.65 us
    ppermute x4, starting transfers between devices, faces(): lax.ppermute(jnp.where(is_even, last, first), axis, [(i, i ^ 1) for i in...  6.01 us
    another operation x2, other arithmetic, emit(): jnp.cumsum(optical_depth[:, :rows - 1], axis=1)  3.4 us
    reduce_sum x1, other arithmetic, emit(): jnp.sum(weight * radiance, axis=0)  2.68 us
    reduce_sum x1, other arithmetic, emit(): jnp.sum(radiance * (1.0 - jnp.exp(-optical_depth)), axis=0)  2.4 us
  transfers between devices with their start and end apart: 16, of which 4 were waited for; matrix products, arithmetic and copies ran while one was open for 15% of the time, Pallas kernels for 0%

profile of v23, /device:TPU:9, one launch (start us, length us, event | category | flops | bytes accessed | tf_op | source)
XLA Modules:
  0.0 84.5 jit_solution(9914858137861484190)
XLA Ops:
  0.6 0.7 convert_subtract_fusion
  1.3 0.8 fusion.120
  2.1 1.1 %add_bitcast_fusion = (f32[1,8,32,128]{3,2,1,0:T(8,128)S(1)}, f32[8,32,128]{2,1,0:T(8,128)S(1)}) fusion(f32[8,32,128]{2,1,0:T(8,128)} %param.9, f32[8,32,128]{2,1,0:T(8,128)} %param.10, f32[8,32]{1,0:T(8,128)S(1)} %get-tuple-element.82), kind=kLoop, calls=%fused_computation.215 | loop fusion | flops 262144 | bytes 525312 | tf_op jit(solution)/shard_map/stack | solution.py:195
  3.2 5.9 %fusion.118 = (f32[32,32,128]{2,1,0:T(8,128)S(1)}, f32[32,8,32,128]{3,2,1,0:T(8,128)}, f32[32,8,32,128]{3,2,1,0:T(8,128)}) fusion(f32[8,32]{1,0:T(8,128)S(1)} %get-tuple-element.83, bf16[64,8,32,128]{3,2,1,0:T(8,128)(2,1)} %param.11, f32[32]{0:T(128)S(1)} %get-tuple-element.84, f32[8,32,128]{2,1,0:T(8,128)S(1)} %get-tuple-element.73, ...), kind=kLoop, calls=%fused_computation.246 | loop fusion | flops 11403264 | bytes 13239552 | tf_op jit(solution)/shard_map/reduce_sum | solution.py:216
  9.1 1.3 %collective-permute-start = (f32[16,32,128]{2,1,0:T(8,128)S(1)}, f32[16,32,128]{2,1,0:T(8,128)S(1)}, u32[]{:S(2)}, u32[]{:S(2)}) collective-permute-start(f32[16,32,128]{2,1,0:T(8,128)S(1)} %slice_select_fusion.2), channel_id=1, source_target_pairs={{0,4},{4,0},{8,12},{12,8},{16,20},{20,16},{24,28},{28,24},{1,5},{5... | collective-permute-start | bytes 786440 | tf_op jit(solution)/shard_map/ppermute | solution.py:127
  10.5 2.7 %reduce_sum.55 = f32[32,32,128]{2,1,0:T(8,128)S(1)} reduce(f32[32,8,32,128]{3,2,1,0:T(8,128)} %get-tuple-element.21, f32[]{:T(128)} %constant.65.clone.1), dimensions={1}, to_apply=%region_1.2 | reduce | flops 917504 | bytes 4718596 | tf_op jit(solution)/shard_map/reduce_sum | solution.py:216
  13.2 0.3 collective-permute-start.2
  13.6 2.8 %collective-permute-done = f32[16,32,128]{2,1,0:T(8,128)S(1)} collective-permute-done((f32[16,32,128]{2,1,0:T(8,128)S(1)}, f32[16,32,128]{2,1,0:T(8,128)S(1)}, u32[]{:S(2)}, u32[]{:S(2)}) %collective-permute-start) | collective-permute-done | bytes 262176 | tf_op jit(solution)/shard_map/ppermute | solution.py:127
  16.4 0.1 fusion.106
  16.4 3.2 %collective-permute-start.1 = (f32[16,32,128]{2,1,0:T(8,128)S(1)}, f32[16,32,128]{2,1,0:T(8,128)S(1)}, u32[]{:S(2)}, u32[]{:S(2)}) collective-permute-start(f32[16,32,128]{2,1,0:T(8,128)S(1)} %fusion.106), channel_id=1, source_target_pairs={{0,8},{4,12},{8,16},{12,20},{16,24},{20,28},{1,9},{5,13},{9,17},{1... | collective-permute-start | bytes 786440 | tf_op jit(solution)/shard_map/ppermute | solution.py:127
  19.7 3.0 %collective-permute-start.4 = (f32[2,8,1,128]{3,2,1,0:T(1,128)S(1)}, f32[2,8,1,128]{3,2,1,0:T(1,128)S(1)}, u32[]{:S(2)}, u32[]{:S(2)}) collective-permute-start(f32[2,8,1,128]{3,2,1,0:T(1,128)S(1)} %get-tuple-element.70), channel_id=1, source_target_pairs={{0,1},{1,0},{2,3},{3,2},{4,5},{5,4},{6,7},{7,6},{8,9},{9,8},{10,11... | collective-permute-start | bytes 24584 | tf_op jit(solution)/shard_map/ppermute | solution.py:44
  22.7 3.3 %collective-permute-start.3 = (f32[2,8,1,128]{3,2,1,0:T(1,128)S(1)}, f32[2,8,1,128]{3,2,1,0:T(1,128)S(1)}, u32[]{:S(2)}, u32[]{:S(2)}) collective-permute-start(f32[2,8,1,128]{3,2,1,0:T(1,128)S(1)} %get-tuple-element.71), channel_id=1, source_target_pairs={{1,2},{2,1},{5,6},{6,5},{9,10},{10,9},{13,14},{14,13},{17,18},{18,... | collective-permute-start | bytes 24584 | tf_op jit(solution)/shard_map/ppermute | solution.py:47
  26.0 2.5 %fusion = f32[32,7,32,128]{3,2,1,0:T(8,128)S(1)} fusion(f32[32,8,32,128]{3,2,1,0:T(8,128)} %get-tuple-element.21), kind=kOutput, calls=%fused_computation.11 | output fusion | flops 5505024 | bytes 7340032 | tf_op jit(solution)/shard_map/jit(cumsum)/reduce_window_sum | solution.py:221
  28.6 0.0 collective-permute-done.4
  28.6 0.0 collective-permute-done.3
  28.6 0.0 collective-permute-done.2
  28.6 0.0 collective-permute-done.1
  28.7 2.0 %collective-permute-start.5 = (f32[16,32,128]{2,1,0:T(8,128)S(1)}, f32[16,32,128]{2,1,0:T(8,128)S(1)}, u32[]{:S(2)}, u32[]{:S(2)}) collective-permute-start(f32[16,32,128]{2,1,0:T(8,128)S(1)} %add.219), channel_id=1, source_target_pairs={{0,16},{4,20},{8,24},{12,28},{1,17},{5,21},{9,25},{13,29},{2,18},{... | collective-permute-start | bytes 786440 | tf_op jit(solution)/shard_map/ppermute | solution.py:127
  30.7 0.1 fusion.107
  30.8 2.5 %collective-permute-start.6 = (f32[16,32,128]{2,1,0:T(8,128)S(1)}, f32[16,32,128]{2,1,0:T(8,128)S(1)}, u32[]{:S(2)}, u32[]{:S(2)}) collective-permute-start(f32[16,32,128]{2,1,0:T(8,128)S(1)} %fusion.107), channel_id=1, source_target_pairs={{0,8},{4,12},{8,16},{12,20},{16,24},{20,28},{1,9},{5,13},{9,17},{1... | collective-permute-start | bytes 786440 | tf_op jit(solution)/shard_map/ppermute | solution.py:127
  33.3 0.0 copy-start.5
  33.3 0.9 %fusion.2 = f32[32,7,32,128]{3,2,1,0:T(8,128)S(1)} fusion(f32[32,8,32,128]{3,2,1,0:T(8,128)S(1)} %copy-done), kind=kOutput, calls=%fused_computation.13 | output fusion | flops 5505024 | bytes 7340032 | tf_op jit(solution)/shard_map/jit(cumsum)/reduce_window_sum | solution.py:221
  34.1 0.0 copy-start.4
  34.1 6.8 %collective-permute-done.5 = f32[16,32,128]{2,1,0:T(8,128)S(1)} collective-permute-done((f32[16,32,128]{2,1,0:T(8,128)S(1)}, f32[16,32,128]{2,1,0:T(8,128)S(1)}, u32[]{:S(2)}, u32[]{:S(2)}) %collective-permute-start.5) | collective-permute-done | bytes 262176 | tf_op jit(solution)/shard_map/ppermute | solution.py:127
  41.0 5.6 %collective-permute-done.6 = f32[16,32,128]{2,1,0:T(8,128)S(1)} collective-permute-done((f32[16,32,128]{2,1,0:T(8,128)S(1)}, f32[16,32,128]{2,1,0:T(8,128)S(1)}, u32[]{:S(2)}, u32[]{:S(2)}) %collective-permute-start.6) | collective-permute-done | bytes 262176 | tf_op jit(solution)/shard_map/ppermute | solution.py:127
  46.6 0.1 fusion.117
  46.7 0.1 add_select_fusion.1
  46.7 1.3 %collective-permute-start.7 = (f32[16,32,128]{2,1,0:T(8,128)S(1)}, f32[16,32,128]{2,1,0:T(8,128)S(1)}, u32[]{:S(2)}, u32[]{:S(2)}) collective-permute-start(f32[16,32,128]{2,1,0:T(8,128)S(1)} %add_select_fusion.1), channel_id=1, source_target_pairs={{0,4},{4,0},{8,12},{12,8},{16,20},{20,16},{24,28},{28,24},{1,5},{5... | collective-permute-start | bytes 786440 | tf_op jit(solution)/shard_map/ppermute | solution.py:127
  48.1 0.0 copy-start.1
  48.1 1.6 %collective-permute-start.8 = (f32[16,32,128]{2,1,0:T(8,128)S(1)}, f32[16,32,128]{2,1,0:T(8,128)S(1)}, u32[]{:S(2)}, u32[]{:S(2)}) collective-permute-start(f32[16,32,128]{2,1,0:T(8,128)S(1)} %add.223), channel_id=1, source_target_pairs={{0,16},{4,20},{8,24},{12,28},{1,17},{5,21},{9,25},{13,29},{2,18},{... | collective-permute-start | bytes 786440 | tf_op jit(solution)/shard_map/ppermute | solution.py:127
  49.7 0.3 collective-permute-start.10
  50.0 6.8 %collective-permute-start.9 = (f32[2,1,32,128]{3,2,1,0:T(8,128)S(1)}, f32[2,1,32,128]{3,2,1,0:T(8,128)S(1)}, u32[]{:S(2)}, u32[]{:S(2)}) collective-permute-start(f32[2,1,32,128]{3,2,1,0:T(8,128)S(1)} %get-tuple-element.69), channel_id=1, source_target_pairs={{4,8},{12,16},{20,24},{8,4},{16,12},{24,20},{5,9},{13,17},{21,25},... | collective-permute-start | bytes 98312 | tf_op jit(solution)/shard_map/ppermute | solution.py:47
  56.8 0.0 collective-permute-done.10
  56.9 1.6 %collective-permute-done.9 = f32[2,1,32,128]{3,2,1,0:T(8,128)S(1)} collective-permute-done((f32[2,1,32,128]{3,2,1,0:T(8,128)S(1)}, f32[2,1,32,128]{3,2,1,0:T(8,128)S(1)}, u32[]{:S(2)}, u32[]{:S(2)}) %collective-permute-start.9) | collective-permute-done | bytes 32800 | tf_op jit(solution)/shard_map/ppermute | solution.py:47
  58.4 0.0 collective-permute-done.7
  58.4 0.0 collective-permute-done.8
  58.4 0.1 fusion.116
  58.5 0.1 add_select_fusion
  58.6 2.1 %collective-permute-start.11 = (f32[16,32,128]{2,1,0:T(8,128)S(1)}, f32[16,32,128]{2,1,0:T(8,128)S(1)}, u32[]{:S(2)}, u32[]{:S(2)}) collective-permute-start(f32[16,32,128]{2,1,0:T(8,128)S(1)} %add_select_fusion), channel_id=1, source_target_pairs={{0,4},{4,0},{8,12},{12,8},{16,20},{20,16},{24,28},{28,24},{1,5},{5... | collective-permute-start | bytes 786440 | tf_op jit(solution)/shard_map/ppermute | solution.py:127
  60.6 0.1 fusion.7
  60.7 0.5 power_multiply_fusion.2
  61.2 0.0 copy-done.4
  61.3 0.2 fusion.119
  61.5 2.4 %multiply_reduce_fusion.2 = (f32[8,32,128]{2,1,0:T(8,128)S(1)}, f32[8,32,128]{2,1,0:T(8,128)S(1)}, bf16[32,8,32,128]{3,2,1,0:T(8,128)(2,1)S(1)}) fusion(f32[32,8,32,128]{3,2,1,0:T(8,128)S(1)} %copy-done, f32[32,7,32,128]{3,2,1,0:T(8,128)S(1)} %fusion.2, f32[32,32,128]{2,1,0:T(8,128)S(1)} %get-tuple-element.86, f32[32,32,128]{2,1,0:T(8,128)S(1)} %get-tuple-element.57, ...), kind=kLoop, calls=%fused_computation.4 | loop fusion | flops 13565952 | bytes 13369472 | tf_op jit(solution)/shard_map/reduce_sum | solution.py:228
  63.9 0.6 fusion.20
  64.5 0.0 collective-permute-done.11
  64.5 0.1 maximum_select_fusion.1
  64.6 0.0 copy-start.3
  64.6 2.7 %multiply_reduce_fusion.1 = (f32[8,32,128]{2,1,0:T(8,128)S(1)}, f32[8,32,128]{2,1,0:T(8,128)S(1)}, bf16[32,8,32,128]{3,2,1,0:T(8,128)(2,1)S(1)}) fusion(f32[32,7,32,128]{3,2,1,0:T(8,128)S(1)} %fusion, f32[32,32,128]{2,1,0:T(8,128)S(1)} %maximum_select_fusion.1, f32[32,32,128]{2,1,0:T(8,128)S(1)} %get-tuple-element.56, f32[32]{0:T(128)S(1)} %get-tuple-element.85, ...), kind=kLoop, calls=%fused_computation.2 | loop fusion | flops 15663104 | bytes 9307264 | tf_op jit(solution)/shard_map/reduce_sum | solution.py:227
  67.3 0.8 broadcast_multiply_fusion
  68.1 0.2 fusion.112
  68.3 3.6 %collective-permute-start.12 = (f32[2,1,32,128]{3,2,1,0:T(8,128)S(1)}, f32[2,1,32,128]{3,2,1,0:T(8,128)S(1)}, u32[]{:S(2)}, u32[]{:S(2)}) collective-permute-start(f32[2,1,32,128]{3,2,1,0:T(8,128)S(1)} %get-tuple-element.66), channel_id=1, source_target_pairs={{4,8},{12,16},{20,24},{8,4},{16,12},{24,20},{5,9},{13,17},{21,25},... | collective-permute-start | bytes 98312 | tf_op jit(solution)/shard_map/ppermute | solution.py:47
  71.9 2.6 %collective-permute-start.13 = (f32[2,1,32,128]{3,2,1,0:T(8,128)S(1)}, f32[2,1,32,128]{3,2,1,0:T(8,128)S(1)}, u32[]{:S(2)}, u32[]{:S(2)}) collective-permute-start(f32[2,1,32,128]{3,2,1,0:T(8,128)S(1)} %get-tuple-element.67), channel_id=1, source_target_pairs={{0,4},{4,0},{8,12},{12,8},{16,20},{20,16},{24,28},{28,24},{1,5},{5... | collective-permute-start | bytes 98312 | tf_op jit(solution)/shard_map/ppermute | solution.py:44
  74.5 5.2 %collective-permute-start.14 = (f32[2,8,1,128]{3,2,1,0:T(1,128)S(1)}, f32[2,8,1,128]{3,2,1,0:T(1,128)S(1)}, u32[]{:S(2)}, u32[]{:S(2)}) collective-permute-start(f32[2,8,1,128]{3,2,1,0:T(1,128)S(1)} %get-tuple-element.44), channel_id=1, source_target_pairs={{1,2},{2,1},{5,6},{6,5},{9,10},{10,9},{13,14},{14,13},{17,18},{18,... | collective-permute-start | bytes 24584 | tf_op jit(solution)/shard_map/ppermute | solution.py:47
  79.8 0.1 collective-permute-start.15
  79.9 2.4 %pad_maximum_fusion = bf16[64,8,32,128]{3,2,1,0:T(8,128)(2,1)} fusion(bf16[32,8,32,128]{3,2,1,0:T(8,128)(2,1)S(1)} %get-tuple-element.53, bf16[32,8,32,128]{3,2,1,0:T(8,128)(2,1)S(1)} %get-tuple-element.30), kind=kLoop, calls=%fused_computation | loop fusion | flops 2097152 | bytes 8388608 | tf_op jit(solution)/shard_map/dynamic_update_slice | solution.py:248
  82.3 0.0 collective-permute-done.14
  82.3 0.0 collective-permute-done.15
  82.3 0.0 collective-permute-done.12
  82.3 0.0 collective-permute-done.13
  82.3 0.1 fusion.9
  82.4 0.5 power_multiply_fusion
  82.9 0.7 fusion.29
  83.6 0.9 %fusion.93 = (f32[8,32,128]{2,1,0:T(8,128)}, f32[8,32,128]{2,1,0:T(8,128)}) fusion(f32[2,8,32,128]{3,2,1,0:T(8,128)S(1)} %fusion.29, f32[8,32]{1,0:T(8,128)S(1)} %get-tuple-element.82, f32[8,32,128]{2,1,0:T(8,128)S(1)} %get-tuple-element.37, f32[8,32,128]{2,1,0:T(8,128)S(1)} %get-tuple-element.39, f32[2,8,32,128]{3,2,1,0:T(8,128)S(1)} %fusion.20, ...), kind=kLoop, calls=%fused_computation.196 | loop fusion | flops 1081344 | bytes 1442816 | tf_op jit(solution)/shard_map/add | solution.py:267
  (23 shorter events, 0.3 us)
Async XLA Ops:
  9.1 4.4 %copy-start.2 = (f32[8,32,128]{2,1,0:T(8,128)S(1)}, f32[8,32,128]{2,1,0:T(8,128)}, u32[]{:S(2)}) copy-start(f32[8,32,128]{2,1,0:T(8,128)} %param.8) | copy-start | bytes 393220
  9.1 7.2 %collective-permute-start = (f32[16,32,128]{2,1,0:T(8,128)S(1)}, f32[16,32,128]{2,1,0:T(8,128)S(1)}, u32[]{:S(2)}, u32[]{:S(2)}) collective-permute-start(f32[16,32,128]{2,1,0:T(8,128)S(1)} %slice_select_fusion.2), channel_id=1, source_target_pairs={{0,4},{4,0},{8,12},{12,8},{16,20},{20,16},{24,28},{28,24},{1,5},{5... | collective-permute-start | bytes 786440 | tf_op jit(solution)/shard_map/ppermute | solution.py:127
  13.2 15.4 %collective-permute-start.2 = (f32[16,32,128]{2,1,0:T(8,128)S(1)}, f32[16,32,128]{2,1,0:T(8,128)S(1)}, u32[]{:S(2)}, u32[]{:S(2)}) collective-permute-start(f32[16,32,128]{2,1,0:T(8,128)S(1)} %slice_select_fusion.1), channel_id=1, source_target_pairs={{0,4},{4,0},{8,12},{12,8},{16,20},{20,16},{24,28},{28,24},{1,5},{5... | collective-permute-start | bytes 786440 | tf_op jit(solution)/shard_map/ppermute | solution.py:127
  16.4 12.2 %collective-permute-start.1 = (f32[16,32,128]{2,1,0:T(8,128)S(1)}, f32[16,32,128]{2,1,0:T(8,128)S(1)}, u32[]{:S(2)}, u32[]{:S(2)}) collective-permute-start(f32[16,32,128]{2,1,0:T(8,128)S(1)} %fusion.106), channel_id=1, source_target_pairs={{0,8},{4,12},{8,16},{12,20},{16,24},{20,28},{1,9},{5,13},{9,17},{1... | collective-permute-start | bytes 786440 | tf_op jit(solution)/shard_map/ppermute | solution.py:127
  19.7 8.9 %collective-permute-start.4 = (f32[2,8,1,128]{3,2,1,0:T(1,128)S(1)}, f32[2,8,1,128]{3,2,1,0:T(1,128)S(1)}, u32[]{:S(2)}, u32[]{:S(2)}) collective-permute-start(f32[2,8,1,128]{3,2,1,0:T(1,128)S(1)} %get-tuple-element.70), channel_id=1, source_target_pairs={{0,1},{1,0},{2,3},{3,2},{4,5},{5,4},{6,7},{7,6},{8,9},{9,8},{10,11... | collective-permute-start | bytes 24584 | tf_op jit(solution)/shard_map/ppermute | solution.py:44
  22.7 10.5 %copy-start = (f32[32,8,32,128]{3,2,1,0:T(8,128)S(1)}, f32[32,8,32,128]{3,2,1,0:T(8,128)}, u32[]{:S(2)}) copy-start(f32[32,8,32,128]{3,2,1,0:T(8,128)} %get-tuple-element.52) | copy-start | bytes 12582916
  22.7 5.9 %collective-permute-start.3 = (f32[2,8,1,128]{3,2,1,0:T(1,128)S(1)}, f32[2,8,1,128]{3,2,1,0:T(1,128)S(1)}, u32[]{:S(2)}, u32[]{:S(2)}) collective-permute-start(f32[2,8,1,128]{3,2,1,0:T(1,128)S(1)} %get-tuple-element.71), channel_id=1, source_target_pairs={{1,2},{2,1},{5,6},{6,5},{9,10},{10,9},{13,14},{14,13},{17,18},{18,... | collective-permute-start | bytes 24584 | tf_op jit(solution)/shard_map/ppermute | solution.py:47
  28.7 12.3 %collective-permute-start.5 = (f32[16,32,128]{2,1,0:T(8,128)S(1)}, f32[16,32,128]{2,1,0:T(8,128)S(1)}, u32[]{:S(2)}, u32[]{:S(2)}) collective-permute-start(f32[16,32,128]{2,1,0:T(8,128)S(1)} %add.219), channel_id=1, source_target_pairs={{0,16},{4,20},{8,24},{12,28},{1,17},{5,21},{9,25},{13,29},{2,18},{... | collective-permute-start | bytes 786440 | tf_op jit(solution)/shard_map/ppermute | solution.py:127
  30.8 15.8 %collective-permute-start.6 = (f32[16,32,128]{2,1,0:T(8,128)S(1)}, f32[16,32,128]{2,1,0:T(8,128)S(1)}, u32[]{:S(2)}, u32[]{:S(2)}) collective-permute-start(f32[16,32,128]{2,1,0:T(8,128)S(1)} %fusion.107), channel_id=1, source_target_pairs={{0,8},{4,12},{8,16},{12,20},{16,24},{20,28},{1,9},{5,13},{9,17},{1... | collective-permute-start | bytes 786440 | tf_op jit(solution)/shard_map/ppermute | solution.py:127
  33.3 23.6 %copy-start.5 = (f32[32,128]{1,0:T(8,128)S(1)}, f32[32,128]{1,0:T(8,128)}, u32[]{:S(2)}) copy-start(f32[32,128]{1,0:T(8,128)} %param.14) | copy-start | bytes 49156
  34.1 27.1 %copy-start.4 = (f32[64,32,128]{2,1,0:T(8,128)S(1)}, f32[64,32,128]{2,1,0:T(8,128)}, u32[]{:S(2)}) copy-start(f32[64,32,128]{2,1,0:T(8,128)} %param.12) | copy-start | bytes 3145732
  46.7 11.7 %collective-permute-start.7 = (f32[16,32,128]{2,1,0:T(8,128)S(1)}, f32[16,32,128]{2,1,0:T(8,128)S(1)}, u32[]{:S(2)}, u32[]{:S(2)}) collective-permute-start(f32[16,32,128]{2,1,0:T(8,128)S(1)} %add_select_fusion.1), channel_id=1, source_target_pairs={{0,4},{4,0},{8,12},{12,8},{16,20},{20,16},{24,28},{28,24},{1,5},{5... | collective-permute-start | bytes 786440 | tf_op jit(solution)/shard_map/ppermute | solution.py:127
  48.1 13.4 %copy-start.1 = (bf16[64,8,32,128]{3,2,1,0:T(8,128)(2,1)S(1)}, bf16[64,8,32,128]{3,2,1,0:T(8,128)(2,1)}, u32[]{:S(2)}) copy-start(bf16[64,8,32,128]{3,2,1,0:T(8,128)(2,1)} %param.11) | copy-start | bytes 12582916
  48.1 10.4 %collective-permute-start.8 = (f32[16,32,128]{2,1,0:T(8,128)S(1)}, f32[16,32,128]{2,1,0:T(8,128)S(1)}, u32[]{:S(2)}, u32[]{:S(2)}) collective-permute-start(f32[16,32,128]{2,1,0:T(8,128)S(1)} %add.223), channel_id=1, source_target_pairs={{0,16},{4,20},{8,24},{12,28},{1,17},{5,21},{9,25},{13,29},{2,18},{... | collective-permute-start | bytes 786440 | tf_op jit(solution)/shard_map/ppermute | solution.py:127
  49.7 7.2 %collective-permute-start.10 = (f32[2,1,32,128]{3,2,1,0:T(8,128)S(1)}, f32[2,1,32,128]{3,2,1,0:T(8,128)S(1)}, u32[]{:S(2)}, u32[]{:S(2)}) collective-permute-start(f32[2,1,32,128]{3,2,1,0:T(8,128)S(1)} %get-tuple-element.68), channel_id=1, source_target_pairs={{0,4},{4,0},{8,12},{12,8},{16,20},{20,16},{24,28},{28,24},{1,5},{5... | collective-permute-start | bytes 98312 | tf_op jit(solution)/shard_map/ppermute | solution.py:44
  50.0 8.4 %collective-permute-start.9 = (f32[2,1,32,128]{3,2,1,0:T(8,128)S(1)}, f32[2,1,32,128]{3,2,1,0:T(8,128)S(1)}, u32[]{:S(2)}, u32[]{:S(2)}) collective-permute-start(f32[2,1,32,128]{3,2,1,0:T(8,128)S(1)} %get-tuple-element.69), channel_id=1, source_target_pairs={{4,8},{12,16},{20,24},{8,4},{16,12},{24,20},{5,9},{13,17},{21,25},... | collective-permute-start | bytes 98312 | tf_op jit(solution)/shard_map/ppermute | solution.py:47
  58.6 6.0 %collective-permute-start.11 = (f32[16,32,128]{2,1,0:T(8,128)S(1)}, f32[16,32,128]{2,1,0:T(8,128)S(1)}, u32[]{:S(2)}, u32[]{:S(2)}) collective-permute-start(f32[16,32,128]{2,1,0:T(8,128)S(1)} %add_select_fusion), channel_id=1, source_target_pairs={{0,4},{4,0},{8,12},{12,8},{16,20},{20,16},{24,28},{28,24},{1,5},{5... | collective-permute-start | bytes 786440 | tf_op jit(solution)/shard_map/ppermute | solution.py:127
  64.6 2.7 %copy-start.3 = (f32[8,32,128]{2,1,0:T(8,128)S(1)}, f32[8,32,128]{2,1,0:T(8,128)}, u32[]{:S(2)}) copy-start(f32[8,32,128]{2,1,0:T(8,128)} %param.9) | copy-start | bytes 393220
  68.3 14.0 %collective-permute-start.12 = (f32[2,1,32,128]{3,2,1,0:T(8,128)S(1)}, f32[2,1,32,128]{3,2,1,0:T(8,128)S(1)}, u32[]{:S(2)}, u32[]{:S(2)}) collective-permute-start(f32[2,1,32,128]{3,2,1,0:T(8,128)S(1)} %get-tuple-element.66), channel_id=1, source_target_pairs={{4,8},{12,16},{20,24},{8,4},{16,12},{24,20},{5,9},{13,17},{21,25},... | collective-permute-start | bytes 98312 | tf_op jit(solution)/shard_map/ppermute | solution.py:47
  71.9 10.3 %collective-permute-start.13 = (f32[2,1,32,128]{3,2,1,0:T(8,128)S(1)}, f32[2,1,32,128]{3,2,1,0:T(8,128)S(1)}, u32[]{:S(2)}, u32[]{:S(2)}) collective-permute-start(f32[2,1,32,128]{3,2,1,0:T(8,128)S(1)} %get-tuple-element.67), channel_id=1, source_target_pairs={{0,4},{4,0},{8,12},{12,8},{16,20},{20,16},{24,28},{28,24},{1,5},{5... | collective-permute-start | bytes 98312 | tf_op jit(solution)/shard_map/ppermute | solution.py:44
  74.5 7.7 %collective-permute-start.14 = (f32[2,8,1,128]{3,2,1,0:T(1,128)S(1)}, f32[2,8,1,128]{3,2,1,0:T(1,128)S(1)}, u32[]{:S(2)}, u32[]{:S(2)}) collective-permute-start(f32[2,8,1,128]{3,2,1,0:T(1,128)S(1)} %get-tuple-element.44), channel_id=1, source_target_pairs={{1,2},{2,1},{5,6},{6,5},{9,10},{10,9},{13,14},{14,13},{17,18},{18,... | collective-permute-start | bytes 24584 | tf_op jit(solution)/shard_map/ppermute | solution.py:47
  79.8 2.5 %collective-permute-start.15 = (f32[2,8,1,128]{3,2,1,0:T(1,128)S(1)}, f32[2,8,1,128]{3,2,1,0:T(1,128)S(1)}, u32[]{:S(2)}, u32[]{:S(2)}) collective-permute-start(f32[2,8,1,128]{3,2,1,0:T(1,128)S(1)} %bitcast.81), channel_id=1, source_target_pairs={{0,1},{1,0},{2,3},{3,2},{4,5},{5,4},{6,7},{7,6},{8,9},{9,8},{10,11... | collective-permute-start | bytes 24584 | tf_op jit(solution)/shard_map/ppermute | solution.py:44
